TPU v7x, 32 devices: a whole 2x2x4 slice. The times are simulated.
32 devices in a mesh: groups: 2 (over y), lat: 8 (over z, x), seed: 2 (over core).
Axes of the slice: x: 2, y: 2, z: 4, core: 2. Of those that a mesh axis runs over, the one named last changes fastest.
Arguments:
- activations: bfloat16 [512, 2048], P(('groups', 'seed'), 'lat'), parts along dimension 0, may hold values from -6 to 6
- bag_rows: int32 [4, 256], P(('groups', 'seed')), parts along dimension 0, may hold values from 0 to 255
- keep_cols: int32 [4, 2048], P(('groups', 'seed')), parts along dimension 0, may hold values 0 or 1
- enc_weight: bfloat16 [4, 16384, 2048], P(('groups', 'seed'), 'lat'), parts along dimension 0, may hold values from -0.125 to 0.125
- enc_bias: float32 [4, 16384], P(('groups', 'seed'), 'lat'), parts along dimension 0, may hold values from -3 to 3
- dec_weight: bfloat16 [4, 16384, 2048], P(('groups', 'seed'), 'lat'), parts along dimension 0, may hold values from -0.0625 to 0.0625
- dec_bias: float32 [4, 2048], P(('groups', 'seed')), parts along dimension 0, may hold values from -3 to 3
- first_moment: bfloat16 [4, 16384, 2048], P(('groups', 'seed'), 'lat'), parts along dimension 0, may hold values from -0.3125 to 0.3125
- second_moment: bfloat16 [4, 16384, 2048], P(('groups', 'seed'), 'lat'), parts along dimension 0, may hold values from 9.9658966e-05 to 0.0099487305
Outputs:
- new_weight: bfloat16 [4, 16384, 2048], P(('groups', 'seed'), 'lat'), parts along dimension 0
- new_first: bfloat16 [4, 16384, 2048], P(('groups', 'seed'), 'lat'), parts along dimension 0
- new_second: bfloat16 [4, 16384, 2048], P(('groups', 'seed'), 'lat'), parts along dimension 0
There are 2 independent parts, one for each index of `groups`. A program takes and returns all parts, laid end to end along the dimension named above; each array names one. Nothing has to cross between parts.
All inputs are finite; a program needn't handle non-finite values. No bound on the sum of `keep_cols` on one device may be relied on, other than what follows from the above.
Results may differ from a plain program's by a relative error of at most 0.012.
The roundings to bfloat16 on the way count: a program that leaves them out, or rounds other values in their place, can miss the bound.
Values may be sent and summed in bfloat16 or wider, within the bound.
No kernel may reach another device: no remote copies, remote signals or barrier semaphores. Data moves between devices by JAX's collectives and lax.ppermute only.
A program may use at most 128 MiB of HBM per device.

v0:
```python
import jax
import jax.numpy as jnp
from jax import lax
from jax.sharding import PartitionSpec as P

sparsity = 0.2
beta_one = 0.9
beta_two = 0.95
corr_one = 1.0 - 0.9**10
corr_two = 1.0 - 0.95**10
adam_eps = 1e-08
rate_step = 0.001
decay_rate = 0.1


def local(
    activations,
    bag_rows,
    keep_cols,
    enc_weight,
    enc_bias,
    dec_weight,
    dec_bias,
    first_moment,
    second_moment,
):
    half_rows = lax.all_gather(activations, "lat", axis=1, tiled=True)
    gathered = lax.all_gather(half_rows, "seed", axis=0, tiled=True)
    row_order = bag_rows[0]
    sample = jnp.take(gathered, row_order, axis=0)
    weight_in = enc_weight[0]
    decoder = dec_weight[0]
    bias_dec = dec_bias[0]
    keep = keep_cols[0].astype(jnp.float32)
    centered = (sample.astype(jnp.float32) - bias_dec).astype(jnp.bfloat16)
    pre_t = lax.dot_general(
        weight_in, centered, (((1,), (1,)), ((), ())), preferred_element_type=jnp.float32
    )
    pre_t = pre_t + enc_bias[0][:, None]
    latent_t = jnp.maximum(pre_t, 0.0).astype(jnp.bfloat16)
    partial_sum = lax.dot_general(
        latent_t, decoder, (((0,), (0,)), ((), ())), preferred_element_type=jnp.float32
    )
    total = lax.psum(partial_sum, "lat")
    error = ((total + bias_dec - sample.astype(jnp.float32)) * keep).astype(jnp.bfloat16)
    back_t = lax.dot_general(
        decoder, error, (((1,), (1,)), ((), ())), preferred_element_type=jnp.float32
    )
    row_norm = jnp.sqrt(jnp.sum(jnp.square(decoder.astype(jnp.float32)), axis=1) + 1e-06)
    token_total = sample.shape[0]
    d_pre_t = (
        jnp.where(pre_t > 0, 2.0 * back_t + sparsity * row_norm[:, None], 0.0) / token_total
    ).astype(jnp.bfloat16)
    grad = jnp.dot(d_pre_t, centered, preferred_element_type=jnp.float32)
    moment_one = beta_one * first_moment[0].astype(jnp.float32) + (1.0 - beta_one) * grad
    moment_two = beta_two * second_moment[0].astype(jnp.float32) + (1.0 - beta_two) * grad * grad
    direction = moment_one / corr_one / (jnp.sqrt(moment_two / corr_two) + adam_eps)
    old = weight_in.astype(jnp.float32)
    updated = (old - rate_step * (direction + decay_rate * old)).astype(jnp.bfloat16)
    return (
        updated[None],
        moment_one.astype(jnp.bfloat16)[None],
        moment_two.astype(jnp.bfloat16)[None],
    )


def solution(mesh):
    return jax.shard_map(
        local,
        mesh=mesh,
        in_specs=(
            P(("groups", "seed"), "lat"),
            P(("groups", "seed"), None),
            P(("groups", "seed"), None),
            P(("groups", "seed"), "lat", None),
            P(("groups", "seed"), "lat"),
            P(("groups", "seed"), "lat", None),
            P(("groups", "seed"), None),
            P(("groups", "seed"), "lat", None),
            P(("groups", "seed"), "lat", None),
        ),
        out_specs=(
            P(("groups", "seed"), "lat", None),
            P(("groups", "seed"), "lat", None),
            P(("groups", "seed"), "lat", None),
        ),
        check_vma=False,
    )
```

profile of v0, /device:TPU:0, one launch (start us, length us, event | category | flops | bytes accessed | tf_op | source)
XLA Modules:
  0.0 222.0 jit_solution(16715430085450274316)
XLA Ops:
  7.2 0.0 copy-start
  7.2 0.0 copy-start.2
  7.2 0.0 all-gather.2.cloned.1.call-start
  7.2 35.4 %all_gather.6 = bf16[128,2048]{1,0:T(8,128)(2,1)} all-gather(bf16[128,256]{1,0:T(8,128)(2,1)} %param.9), channel_id=1, replica_groups=mesh['groups'=2,'lat'=8,'seed'=2] {'lat'}, dimensions={1}, use_global_device_ids=true | all-gather | bytes 589824 | tf_op jit(solution)/shard_map/all_gather | solution.py:27
  42.6 0.0 all-gather.2.cloned.1.call-update
  42.7 0.0 all-reduce.2.cloned.1.call-start
  42.7 0.7 compare_select_fusion
  43.4 0.7 compare_and_fusion
  44.1 8.8 %all-gather.2.cloned.1.call-done = bf16[256,2048]{1,0:T(8,128)(2,1)} async-done(((bf16[128,2048]{1,0:T(8,128)(2,1)}), bf16[256,2048]{1,0:T(8,128)(2,1)}) %all-gather.2.cloned.1.call-update) | async-done | bytes 1048592 | tf_op jit(solution)/shard_map/all_gather | solution.py:28
  52.9 3.7 %gather_fusion = bf16[256,2048]{1,0:T(8,128)(2,1)S(1)} fusion(bf16[256,2048]{1,0:T(8,128)(2,1)} %all-gather.2.cloned.1.call-done, s32[1024]{0:T(1024)S(1)} %pad_clamp_fusion), kind=kCustom, calls=%fused_computation | custom fusion | bytes 2098176 | tf_op jit(solution)/shard_map/jit(_take)/gather | solution.py:30
  56.6 0.0 copy-done
  56.6 0.0 copy-done.2
  56.7 5.8 %fusion.27 = f32[256,2048]{1,0:T(8,128)S(1)} fusion(bf16[1,2048,2048]{2,1,0:T(8,128)(2,1)} %param.12, f32[2048]{0:T(1024)S(1)} %bitcast.64, f32[2048]{0:T(1024)S(1)} %bitcast.59, bf16[256,2048]{1,0:T(8,128)(2,1)S(1)} %gather_fusion, pred[256]{0:T(512)(128)(4,1)S(1)} %compare_and_fusion), kind=kOutput, calls=%fused_computation.27 | convolution fusion | flops 2150105088 | bytes 11550976 | tf_op jit(solution)/shard_map/dot_general | solution.py:36
  62.4 0.0 copy-start.1
  62.5 7.0 %fusion.10 = f32[256,2048]{1,0:T(8,128)} fusion(bf16[1,2048,2048]{2,1,0:T(8,128)(2,1)} %param.14, f32[256,2048]{1,0:T(8,128)S(1)} %fusion.27), kind=kOutput, calls=%fused_computation.16 | convolution fusion | flops 2148532224 | bytes 12582912 | tf_op jit(solution)/shard_map/dot_general | solution.py:41
  69.5 0.0 all-reduce.2.cloned.1.call-update
  69.5 0.0 copy-done.1
  69.5 5.1 %multiply_reduce_fusion = f32[2048]{0:T(1024)S(1)} fusion(bf16[1,2048,2048]{2,1,0:T(8,128)(2,1)} %param.14), kind=kLoop, calls=%fused_computation.9 | loop fusion | flops 12580864 | bytes 8396800 | tf_op jit(solution)/shard_map/reduce_sum | solution.py:49
  74.6 98.0 %all-reduce.2.cloned.1.call-done = f32[256,2048]{1,0:T(8,128)} async-done(((f32[256,2048]{1,0:T(8,128)}), f32[256,2048]{1,0:T(8,128)}) %all-reduce.2.cloned.1.call-update) | async-done | bytes 2097168 | tf_op jit(solution)/shard_map/psum | solution.py:44
  172.7 14.7 %fusion.34 = f32[2048,2048]{1,0:T(8,128)} fusion(bf16[1,2048,2048]{2,1,0:T(8,128)(2,1)} %param.14, f32[256,2048]{1,0:T(8,128)S(1)} %fusion.27, f32[256,2048]{1,0:T(8,128)} %all-reduce.2.cloned.1.call-done, f32[2048]{0:T(1024)S(1)} %sqrt_multiply_fusion, f32[2048]{0:T(1024)S(1)} %bitcast.61, f32[2048]{0:T(1024)S(1)} %bitcast.60, ...), kind=kOutput, calls=%fused_computation.29 | convolution fusion | flops 4303355904 | bytes 30433536 | tf_op jit(solution)/shard_map/dot_general | solution.py:54
  187.3 27.9 %fusion.6 = (bf16[1,2048,2048]{2,1,0:T(8,128)(2,1)}, bf16[1,2048,2048]{2,1,0:T(8,128)(2,1)}, bf16[1,2048,2048]{2,1,0:T(8,128)(2,1)}) fusion(f32[2048,2048]{1,0:T(8,128)} %fusion.34, bf16[1,2048,2048]{2,1,0:T(8,128)(2,1)} %param.17, bf16[1,2048,2048]{2,1,0:T(8,128)(2,1)} %param.16, bf16[1,2048,2048]{2,1,0:T(8,128)(2,1)} %param.12), kind=kLoop, calls=%fused_computation.12 | loop fusion | flops 88080384 | bytes 67108864 | tf_op jit(solution)/shard_map/broadcast_in_dim | solution.py:63
  (3 shorter events, 0.0 us)
Async XLA Ops:
  7.2 49.5 %copy-start = (f32[1,2048]{1,0:T(1,128)S(1)}, f32[1,2048]{1,0:T(1,128)}, u32[]{:S(2)}) copy-start(f32[1,2048]{1,0:T(1,128)} %param.15) | copy-start | bytes 24580
  7.2 49.5 %copy-start.2 = (f32[1,2048]{1,0:T(1,128)S(1)}, f32[1,2048]{1,0:T(1,128)}, u32[]{:S(2)}) copy-start(f32[1,2048]{1,0:T(1,128)} %param.13) | copy-start | bytes 24580
  7.2 45.7 %all-gather.2.cloned.1.call-start = ((), (), s32[]{:S(2)}) async-start(), calls=%async_computation | async-start | bytes 1572864 | tf_op jit(solution)/shard_map/all_gather | solution.py:28
  42.7 130.0 %all-reduce.2.cloned.1.call-start = ((), (), s32[]{:S(2)}) async-start(), calls=%async_computation.1 | async-start | bytes 4194304 | tf_op jit(solution)/shard_map/psum | solution.py:44
  62.4 7.1 %copy-start.1 = (s32[1,2048]{1,0:T(1,128)S(1)}, s32[1,2048]{1,0:T(1,128)}, u32[]{:S(2)}) copy-start(s32[1,2048]{1,0:T(1,128)} %param.11) | copy-start | bytes 24580
Sparse Core Ops, SparseCore 0:
  42.8 10.0 all-gather.1
  69.6 103.0 all-reduce.1
where the time goes:
time: 222 us
  waiting for transfers between devices  107 us (48%)
  blocking collectives  35.4 us (16%)
  other arithmetic  34.3 us (15%)
  matrix products  27.5 us (12%)
  between operations  14.1 us (6%)
  local copies, waits for them, and re-layouts  3.74 us (2%)
    psum x1, waiting for transfers between devices, local(): total = lax.psum(partial_sum, 'lat')  98 us
    all_gather x1, blocking collectives, local(): half_rows = lax.all_gather(activations, 'lat', axis=1, tiled=True)  35.4 us
    broadcast_in_dim x1, other arithmetic, local(): moment_two.astype(jnp.bfloat16)[None]  27.9 us
    dot_general x1, matrix products, local(): grad = jnp.dot(d_pre_t, centered, preferred_element_type=jnp.float32)  14.7 us
    all_gather x1, waiting for transfers between devices, local(): gathered = lax.all_gather(half_rows, 'seed', axis=0, tiled=True)  8.8 us
    dot_general x1, matrix products, local(): lax.dot_general(latent_t, decoder, (((0,), (0,)), ((), ())), preferred_el...  7.04 us
    dot_general x1, matrix products, local(): lax.dot_general(weight_in, centered, (((1,), (1,)), ((), ())), preferred_...  5.77 us
    reduce_sum x1, other arithmetic, local(): jnp.sum(jnp.square(decoder.astype(jnp.float32)), axis=1) + 1e-06  5.08 us
  transfers between devices with their start and end apart: 2, of which 2 were waited for; matrix products, arithmetic and copies ran while one was open for 3% of the time, Pallas kernels for 0%

commit v1 on v0

--- a/solution.py
+++ b/solution.py
@@ -38,11 +38,20 @@
     )
     pre_t = pre_t + enc_bias[0][:, None]
     latent_t = jnp.maximum(pre_t, 0.0).astype(jnp.bfloat16)
-    partial_sum = lax.dot_general(
-        latent_t, decoder, (((0,), (0,)), ((), ())), preferred_element_type=jnp.float32
+    lat_size = lax.psum(1, "lat")
+    width = bias_dec.shape[0] // lat_size
+    start = lax.axis_index("lat") * width
+    decoder_blocks = decoder.reshape(decoder.shape[0], lat_size, width)
+    partial_sum = jnp.einsum(
+        "lt,lbf->btf", latent_t, decoder_blocks, preferred_element_type=jnp.float32
     )
-    total = lax.psum(partial_sum, "lat")
-    error = ((total + bias_dec - sample.astype(jnp.float32)) * keep).astype(jnp.bfloat16)
+    total = lax.psum_scatter(partial_sum, "lat", scatter_dimension=0, tiled=True)[0]
+    sample_cols = lax.dynamic_slice_in_dim(sample, start, width, axis=1).astype(jnp.float32)
+    bias_cols = lax.dynamic_slice_in_dim(bias_dec, start, width)
+    keep_cols_f = lax.dynamic_slice_in_dim(keep, start, width)
+    error_cols = ((total + bias_cols - sample_cols) * keep_cols_f).astype(jnp.bfloat16)
+    error_blocks = lax.all_gather(error_cols, "lat", axis=0, tiled=False)
+    error = jnp.transpose(error_blocks, (1, 0, 2)).reshape(error_cols.shape[0], -1)
     back_t = lax.dot_general(
         decoder, error, (((1,), (1,)), ((), ())), preferred_element_type=jnp.float32
     )

time: 222 us -> 215 us (0.968)
  other arithmetic: 34.3 us -> 7.62 us
  local copies, waits for them, and re-layouts: 3.74 us -> 17 us
  matrix products: 27.5 us -> 36.9 us
  waiting for transfers between devices: 107 us -> 103 us
    psum x1 -> x0, waiting for transfers between devices: 98 us -> none  [local(): total = lax.psum(partial_sum, 'lat')]
    reduce_scatter x0 -> x1, waiting for transfers between devices: none -> 68 us  [local(): lax.psum_scatter(partial_sum, 'lat', scatter_dimension=0, tiled=True)[0]]
    all_gather x0 -> x1, waiting for transfers between devices: none -> 35.1 us  [local(): error_blocks = lax.all_gather(error_cols, 'lat', axis=0, tiled=False)]
    broadcast_in_dim x1 -> x0, other arithmetic: 27.9 us -> none  [local(): moment_two.astype(jnp.bfloat16)[None]]
    dot_general x1, matrix products: 14.7 us -> 27.3 us  [local(): grad = jnp.dot(d_pre_t, centered, preferred_element_type=jnp.float32)]
    unnamed x6 -> x13, local copies, waits for them, and re-layouts: 0.01 us -> 11.8 us
    all_gather x1, waiting for transfers between devices: 8.8 us -> 0.02 us  [local(): gathered = lax.all_gather(half_rows, 'seed', axis=0, tiled=True)]
    dot_general x1, matrix products: 7.04 us -> 3.67 us  [local(): jnp.einsum('lt,lbf->btf', latent_t, decoder_blocks, preferred_element_typ...]
  transfers between devices with their start and end apart: 2 -> 3, of which waited for: 2 -> 2; matrix products, arithmetic and copies ran while one was open for 3% -> 8% of each run, Pallas kernels for 0% -> 0%
where the time goes in v1:
time: 215 us; the launch traced here: 214 us
  waiting for transfers between devices  103 us (48%)
  matrix products  36.9 us (17%)
  blocking collectives  35.4 us (16%)
  local copies, waits for them, and re-layouts  17 us (8%)
  between operations  13.9 us (6%)
  other arithmetic  7.62 us (4%)
    reduce_scatter x1, waiting for transfers between devices, local(): lax.psum_scatter(partial_sum, 'lat', scatter_dimension=0, tiled=True)[0]  68 us
    all_gather x1, blocking collectives, local(): half_rows = lax.all_gather(activations, 'lat', axis=1, tiled=True)  35.4 us
    all_gather x1, waiting for transfers between devices, local(): error_blocks = lax.all_gather(error_cols, 'lat', axis=0, tiled=False)  35.1 us
    dot_general x1, matrix products, local(): grad = jnp.dot(d_pre_t, centered, preferred_element_type=jnp.float32)  27.3 us
    unnamed x13, local copies, waits for them, and re-layouts  11.8 us
    dot_general x1, matrix products, local(): lax.dot_general(weight_in, centered, (((1,), (1,)), ((), ())), preferred_...  5.91 us
    reduce_sum x1, other arithmetic, local(): jnp.sum(jnp.square(decoder.astype(jnp.float32)), axis=1) + 1e-06  5.08 us
  transfers between devices with their start and end apart: 3, of which 2 were waited for; matrix products, arithmetic and copies ran while one was open for 8% of the time, Pallas kernels for 0%

profile of v1, /device:TPU:0, one launch (start us, length us, event | category | flops | bytes accessed | tf_op | source)
XLA Modules:
  0.0 214.3 jit_solution(8274398981548980554)
XLA Ops:
  7.2 0.0 all-gather.4.cloned.1.call-start
  7.2 35.4 %all_gather.12 = bf16[128,2048]{1,0:T(8,128)(2,1)} all-gather(bf16[128,256]{1,0:T(8,128)(2,1)} %param.9), channel_id=1, replica_groups=mesh['groups'=2,'lat'=8,'seed'=2] {'lat'}, dimensions={1}, use_global_device_ids=true | all-gather | bytes 589824 | tf_op jit(solution)/shard_map/all_gather | solution.py:27
  42.6 0.0 all-gather.4.cloned.1.call-update
  42.7 0.0 reduce-scatter.2.cloned.1.call-start
  42.7 0.0 copy-start
  42.7 10.5 %copy.15 = bf16[256,8,8,256]{3,2,1,0:T(8,128)(2,1)} copy(bf16[256,8,8,256]{3,1,2,0:T(8,128)(2,1)} %bitcast.81) | data formatting | bytes 16777216
  53.2 0.0 all-gather.4.cloned.1.call-done
  53.2 3.7 %gather_fusion = bf16[256,2048]{1,0:T(8,128)(2,1)S(1)} fusion(bf16[256,2048]{1,0:T(8,128)(2,1)} %all-gather.4.cloned.1.call-done, s32[1024]{0:T(1024)S(1)} %pad_clamp_fusion), kind=kCustom, calls=%fused_computation | custom fusion | bytes 2098176 | tf_op jit(solution)/shard_map/jit(_take)/gather | solution.py:30
  57.0 0.0 slice-start
  57.0 0.2 broadcast_select_fusion
  57.2 0.0 slice-start.1
  57.2 5.9 %fusion.27 = f32[256,2048]{1,0:T(8,128)S(1)} fusion(bf16[1,2048,2048]{2,1,0:T(8,128)(2,1)} %param.12, f32[2048]{0:T(1024)S(1)} %bitcast.93, bf16[256,2048]{1,0:T(8,128)(2,1)S(1)} %broadcast_select_fusion, f32[2048]{0:T(1024)S(1)} %bitcast.91), kind=kOutput, calls=%fused_computation.25 | convolution fusion | flops 2149580800 | bytes 11550720 | tf_op jit(solution)/shard_map/dot_general | solution.py:36
  63.1 1.3 copy-done.3
  64.5 3.7 %fusion.37 = f32[8,256,256]{2,1,0:T(8,128)} fusion(bf16[2048,8,256]{2,1,0:T(8,128)(2,1)S(1)} %bitcast.84, f32[256,2048]{1,0:T(8,128)S(1)} %fusion.27), kind=kOutput, calls=%fused_computation.31 | convolution fusion | flops 2148532224 | bytes 12582912 | tf_op jit(solution)/shard_map/lt,lbf->btf/dot_general | solution.py:45
  68.1 0.0 reduce-scatter.2.cloned.1.call-update
  68.2 0.2 all-gather.6.cloned.1.call-start
  68.4 0.7 dynamic-slice_convert_fusion
  69.1 68.0 %reduce-scatter.2.cloned.1.call-done = f32[1,256,256]{2,1,0:T(8,128)} async-done(((f32[8,256,256]{2,1,0:T(8,128)}), f32[1,256,256]{2,1,0:T(8,128)}) %reduce-scatter.2.cloned.1.call-update) | async-done | bytes 262160 | tf_op jit(solution)/shard_map/reduce_scatter | solution.py:48
  137.1 1.7 fusion.49
  138.8 0.0 all-gather.6.cloned.1.call-update
  138.8 5.1 %multiply_reduce_fusion = f32[2048]{0:T(1024)S(1)} fusion(bf16[1,2048,2048]{2,1,0:T(8,128)(2,1)} %param.14), kind=kLoop, calls=%fused_computation.9 | loop fusion | flops 12580864 | bytes 8396800 | tf_op jit(solution)/shard_map/reduce_sum | solution.py:58
  143.9 35.1 %all-gather.6.cloned.1.call-done = bf16[2048,256]{1,0:T(8,128)(2,1)} async-done(((bf16[256,256]{1,0:T(8,128)(2,1)}), bf16[2048,256]{1,0:T(8,128)(2,1)}) %all-gather.6.cloned.1.call-update) | async-done | bytes 1048592 | tf_op jit(solution)/shard_map/all_gather | solution.py:53
  179.0 1.5 copy.14
  180.5 27.3 %fusion.6 = (bf16[1,2048,2048]{2,1,0:T(8,128)(2,1)}, bf16[1,2048,2048]{2,1,0:T(8,128)(2,1)}, bf16[1,2048,2048]{2,1,0:T(8,128)(2,1)}) fusion(bf16[1,2048,2048]{2,1,0:T(8,128)(2,1)} %param.17, bf16[1,2048,2048]{2,1,0:T(8,128)(2,1)} %param.16, bf16[1,2048,2048]{2,1,0:T(8,128)(2,1)} %param.12, bf16[256,2048]{1,0:T(8,128)(2,1)S(1)} %broadcast_select_fusion, ...), kind=kOutput, calls=%fused_computation.12 | convolution fusion | flops 4387766272 | bytes 62930944 | tf_op jit(solution)/shard_map/dot_general | solution.py:63
  (14 shorter events, 0.1 us)
Async XLA Ops:
  7.2 46.1 %all-gather.4.cloned.1.call-start = ((), (), s32[]{:S(2)}) async-start(), calls=%async_computation.1 | async-start | bytes 1572864 | tf_op jit(solution)/shard_map/all_gather | solution.py:28
  42.7 94.5 %reduce-scatter.2.cloned.1.call-start = ((), (), s32[]{:S(2)}) async-start(), calls=%async_computation.2 | async-start | bytes 2359296 | tf_op jit(solution)/shard_map/reduce_scatter | solution.py:48
  42.7 10.5 %copy-start = (s32[1,256]{1,0:T(1,128)S(1)}, s32[1,256]{1,0:T(1,128)}, u32[]{:S(2)}) copy-start(s32[1,256]{1,0:T(1,128)} %param.10) | copy-start | bytes 3076
  53.2 4.0 %copy-start.1 = (f32[1,2048]{1,0:T(1,128)S(1)}, f32[1,2048]{1,0:T(1,128)}, u32[]{:S(2)}) copy-start(f32[1,2048]{1,0:T(1,128)} %param.15) | copy-start | bytes 24580
  53.2 4.0 %copy-start.2 = (f32[1,2048]{1,0:T(1,128)S(1)}, f32[1,2048]{1,0:T(1,128)}, u32[]{:S(2)}) copy-start(f32[1,2048]{1,0:T(1,128)} %param.13) | copy-start | bytes 24580
  57.0 7.5 %slice-start = ((s8[8388608]{0:T(1024)(128)(4,1)}), s8[4194304]{0:T(1024)(128)(4,1)S(1)}, s32[]{:S(2)}) async-start(s8[8388608]{0:T(1024)(128)(4,1)} %bitcast.82), calls=%async_computation.4 | async-start | bytes 8388608
  57.2 7.3 %slice-start.1 = ((s8[8388608]{0:T(1024)(128)(4,1)}), s8[4194304]{0:T(1024)(128)(4,1)S(1)}, s32[]{:S(2)}) async-start(s8[8388608]{0:T(1024)(128)(4,1)} %bitcast.82), calls=%async_computation.5 | async-start | bytes 8388608
  63.1 1.3 copy-start.3
  68.2 110.9 %all-gather.6.cloned.1.call-start = ((), (), s32[]{:S(2)}) async-start(), calls=%async_computation.3 | async-start | bytes 1179648 | tf_op jit(solution)/shard_map/all_gather | solution.py:53
Sparse Core Ops, SparseCore 0:
  42.8 10.0 all-gather.3
  68.3 68.8 reduce-scatter.1
  139.8 39.1 all-gather.5

commit v2 on v1

--- a/solution.py
+++ b/solution.py
@@ -13,6 +13,66 @@
 decay_rate = 0.1
 
 
+def _pair_swap(value, axis, mask, size):
+    return lax.ppermute(value, axis, [(i, i ^ mask) for i in range(size)])
+
+
+def _halving_sum(blocks, axis, size, order):
+    nbits = size.bit_length() - 1
+    me = lax.axis_index(axis)
+    cur = blocks.reshape((2,) * nbits + blocks.shape[1:])
+    bits = list(range(nbits - 1, -1, -1))
+    for bit in order:
+        pos = bits.index(bit)
+        mine_bit = (me >> bit) & 1
+        keep_part = lax.dynamic_index_in_dim(cur, mine_bit, pos, keepdims=False)
+        send_part = lax.dynamic_index_in_dim(cur, 1 - mine_bit, pos, keepdims=False)
+        cur = keep_part + _pair_swap(send_part, axis, 1 << bit, size)
+        bits.pop(pos)
+    return cur
+
+
+def _doubling_gather(value, axis, size, order):
+    me = lax.axis_index(axis)
+    cur = value
+    bits = []
+    for bit in order:
+        other = _pair_swap(cur, axis, 1 << bit, size)
+        low_is_me = ((me >> bit) & 1) == 0
+        low = jnp.where(low_is_me, cur, other)
+        high = jnp.where(low_is_me, other, cur)
+        cur = jnp.stack([low, high], axis=0)
+        bits.insert(0, bit)
+    want = sorted(bits, reverse=True)
+    cur = jnp.transpose(cur, [bits.index(b) for b in want] + list(range(len(bits), cur.ndim)))
+    return cur.reshape((size,) + value.shape)
+
+
+def _orders(size):
+    nbits = size.bit_length() - 1
+    first = list(range(nbits))
+    second = first[:]
+    if nbits >= 2:
+        second[0], second[1] = 1, 0
+    return first, second
+
+
+def _reduce_scatter(blocks, axis, size):
+    first, second = _orders(size)
+    half = blocks.shape[1] // 2
+    a = _halving_sum(blocks[:, :half], axis, size, first)
+    b = _halving_sum(blocks[:, half:], axis, size, second)
+    return jnp.concatenate([a, b], axis=0)
+
+
+def _all_gather(value, axis, size):
+    first, second = _orders(size)
+    half = value.shape[0] // 2
+    a = _doubling_gather(value[:half], axis, size, first[::-1])
+    b = _doubling_gather(value[half:], axis, size, second[::-1])
+    return jnp.concatenate([a, b], axis=1)
+
+
 def local(
     activations,
     bag_rows,
@@ -24,7 +84,9 @@
     first_moment,
     second_moment,
 ):
-    half_rows = lax.all_gather(activations, "lat", axis=1, tiled=True)
+    lat_size = LAT_SIZE[0]
+    act_blocks = _all_gather(activations, "lat", lat_size)
+    half_rows = jnp.transpose(act_blocks, (1, 0, 2)).reshape(activations.shape[0], -1)
     gathered = lax.all_gather(half_rows, "seed", axis=0, tiled=True)
     row_order = bag_rows[0]
     sample = jnp.take(gathered, row_order, axis=0)
@@ -38,19 +100,18 @@
     )
     pre_t = pre_t + enc_bias[0][:, None]
     latent_t = jnp.maximum(pre_t, 0.0).astype(jnp.bfloat16)
-    lat_size = lax.psum(1, "lat")
     width = bias_dec.shape[0] // lat_size
     start = lax.axis_index("lat") * width
     decoder_blocks = decoder.reshape(decoder.shape[0], lat_size, width)
     partial_sum = jnp.einsum(
         "lt,lbf->btf", latent_t, decoder_blocks, preferred_element_type=jnp.float32
     )
-    total = lax.psum_scatter(partial_sum, "lat", scatter_dimension=0, tiled=True)[0]
+    total = _reduce_scatter(partial_sum, "lat", lat_size)
     sample_cols = lax.dynamic_slice_in_dim(sample, start, width, axis=1).astype(jnp.float32)
     bias_cols = lax.dynamic_slice_in_dim(bias_dec, start, width)
     keep_cols_f = lax.dynamic_slice_in_dim(keep, start, width)
     error_cols = ((total + bias_cols - sample_cols) * keep_cols_f).astype(jnp.bfloat16)
-    error_blocks = lax.all_gather(error_cols, "lat", axis=0, tiled=False)
+    error_blocks = _all_gather(error_cols, "lat", lat_size)
     error = jnp.transpose(error_blocks, (1, 0, 2)).reshape(error_cols.shape[0], -1)
     back_t = lax.dot_general(
         decoder, error, (((1,), (1,)), ((), ())), preferred_element_type=jnp.float32
@@ -73,7 +134,11 @@
     )
 
 
+LAT_SIZE = [8]
+
+
 def solution(mesh):
+    LAT_SIZE[0] = mesh.shape["lat"]
     return jax.shard_map(
         local,
         mesh=mesh,

time: 215 us -> 152 us (0.71)
  waiting for transfers between devices: 103 us -> 45.3 us
  blocking collectives: 35.4 us -> 0 us
  starting transfers between devices: 0.3 us -> 30.4 us
    reduce_scatter x1 -> x0, waiting for transfers between devices: 68 us -> none  [local(): lax.psum_scatter(partial_sum, 'lat', scatter_dimension=0, tiled=True)[0]]
    ppermute x0 -> x18, waiting for transfers between devices: none -> 45.1 us  [_pair_swap(): return lax.ppermute(value, axis, [(i, i ^ mask) for i in range(size)])]
    all_gather x1 -> x0, blocking collectives: 35.4 us -> none  [local(): half_rows = lax.all_gather(activations, 'lat', axis=1, tiled=True)]
    all_gather x1 -> x0, waiting for transfers between devices: 35.1 us -> none  [local(): error_blocks = lax.all_gather(error_cols, 'lat', axis=0, tiled=False)]
    ppermute x0 -> x18, starting transfers between devices: none -> 30.4 us  [_pair_swap(): return lax.ppermute(value, axis, [(i, i ^ mask) for i in range(size)])]
    reduce_sum x1, other arithmetic: 5.08 us -> 1.87 us  [local(): jnp.sum(jnp.square(decoder.astype(jnp.float32)), axis=1) + 1e-06]
    add x0 -> x6, other arithmetic: none -> 2.32 us  [_halving_sum(): cur = keep_part + _pair_swap(send_part, axis, 1 << bit, size)]
    unnamed x13 -> x17, local copies, waits for them, and re-layouts: 11.8 us -> 10.5 us
  transfers between devices with their start and end apart: 3 -> 19, of which waited for: 2 -> 17; matrix products, arithmetic and copies ran while one was open for 8% -> 12% of each run, Pallas kernels for 0% -> 0%
where the time goes in v2:
time: 152 us
  waiting for transfers between devices  45.3 us (30%)
  matrix products  35.7 us (23%)
  starting transfers between devices  30.4 us (20%)
  local copies, waits for them, and re-layouts  18.4 us (12%)
  between operations  14.5 us (10%)
  other arithmetic  7.3 us (5%)
    ppermute x18, waiting for transfers between devices, _pair_swap(): return lax.ppermute(value, axis, [(i, i ^ mask) for i in range(size)])  45.1 us
    ppermute x18, starting transfers between devices, _pair_swap(): return lax.ppermute(value, axis, [(i, i ^ mask) for i in range(size)])  30.4 us
    dot_general x1, matrix products, local(): grad = jnp.dot(d_pre_t, centered, preferred_element_type=jnp.float32)  27.5 us
    unnamed x17, local copies, waits for them, and re-layouts  10.5 us
    dot_general x1, matrix products, local(): lax.dot_general(weight_in, centered, (((1,), (1,)), ((), ())), preferred_...  5.9 us
    gather x1, local copies, waits for them, and re-layouts, local(): sample = jnp.take(gathered, row_order, axis=0)  3.72 us
  transfers between devices with their start and end apart: 19, of which 17 were waited for; matrix products, arithmetic and copies ran while one was open for 12% of the time, Pallas kernels for 0%

profile of v2, /device:TPU:0, one launch (start us, length us, event | category | flops | bytes accessed | tf_op | source)
XLA Modules:
  0.0 151.6 jit_solution(2629475500519459501)
XLA Ops:
  8.0 4.0 %collective-permute-start = (bf16[64,256]{1,0:T(8,128)(2,1)S(1)}, bf16[64,256]{1,0:T(8,128)(2,1)S(1)}, u32[]{:S(2)}, u32[]{:S(2)}) collective-permute-start(bf16[64,256]{1,0:T(8,128)(2,1)S(1)} %slice.18), channel_id=1, source_target_pairs={{0,8},{2,10},{4,12},{6,14},{8,0},{10,2},{12,4},{14,6},{1,9},{3,11}... | collective-permute-start | bytes 98312 | tf_op jit(solution)/shard_map/ppermute | solution.py:17
  12.0 2.2 %collective-permute-done = bf16[64,256]{1,0:T(8,128)(2,1)S(1)} collective-permute-done((bf16[64,256]{1,0:T(8,128)(2,1)S(1)}, bf16[64,256]{1,0:T(8,128)(2,1)S(1)}, u32[]{:S(2)}, u32[]{:S(2)}) %collective-permute-start) | collective-permute-done | bytes 32800 | tf_op jit(solution)/shard_map/ppermute | solution.py:17
  15.0 2.7 %collective-permute-start.3 = (bf16[64,256]{1,0:T(8,128)(2,1)S(1)}, bf16[64,256]{1,0:T(8,128)(2,1)S(1)}, u32[]{:S(2)}, u32[]{:S(2)}) collective-permute-start(bf16[64,256]{1,0:T(8,128)(2,1)S(1)} %get-tuple-element.33), channel_id=1, source_target_pairs={{0,8},{2,10},{4,12},{6,14},{8,0},{10,2},{12,4},{14,6},{1,9},{3,11}... | collective-permute-start | bytes 98312 | tf_op jit(solution)/shard_map/ppermute | solution.py:17
  17.7 1.9 %collective-permute-start.1 = (bf16[2,64,256]{2,1,0:T(8,128)(2,1)S(1)}, bf16[2,64,256]{2,1,0:T(8,128)(2,1)S(1)}, u32[]{:S(2)}, u32[]{:S(2)}) collective-permute-start(bf16[2,64,256]{2,1,0:T(8,128)(2,1)S(1)} %pad_maximum_fusion.7), channel_id=1, source_target_pairs={{0,4},{2,6},{4,0},{6,2},{8,12},{10,14},{12,8},{14,10},{1,5},{3,7},... | collective-permute-start | bytes 196616 | tf_op jit(solution)/shard_map/ppermute | solution.py:17
  27.6 2.5 %collective-permute-done.5 = bf16[2,2,64,256]{3,2,1,0:T(8,128)(2,1)S(1)} collective-permute-done((bf16[2,2,64,256]{3,2,1,0:T(8,128)(2,1)S(1)}, bf16[2,2,64,256]{3,2,1,0:T(8,128)(2,1)S(1)}, u32[]{:S(2)}, u32[]{:S(2)}) %collective-permute-start.5) | collective-permute-done | bytes 131104 | tf_op jit(solution)/shard_map/ppermute | solution.py:17
  31.1 10.5 %copy.22 = bf16[256,8,8,256]{3,2,1,0:T(8,128)(2,1)} copy(bf16[256,8,8,256]{3,1,2,0:T(8,128)(2,1)} %bitcast.166) | data formatting | bytes 16777216
  41.8 3.7 %gather_fusion = bf16[256,2048]{1,0:T(8,128)(2,1)S(1)} fusion(bf16[256,2048]{1,0:T(8,128)(2,1)} %all-gather.2.cloned.1.call-done, s32[1024]{0:T(1024)S(1)} %pad_clamp_fusion), kind=kCustom, calls=%fused_computation | custom fusion | bytes 2098176 | tf_op jit(solution)/shard_map/jit(_take)/gather | solution.py:92
  45.7 5.9 %fusion.27 = f32[256,2048]{1,0:T(8,128)S(1)} fusion(bf16[1,2048,2048]{2,1,0:T(8,128)(2,1)} %param.12, f32[2048]{0:T(1024)S(1)} %bitcast.188, bf16[256,2048]{1,0:T(8,128)(2,1)S(1)} %broadcast_select_fusion, f32[2048]{0:T(1024)S(1)} %bitcast.186), kind=kOutput, calls=%fused_computation.25 | convolution fusion | flops 2149580800 | bytes 11550720 | tf_op jit(solution)/shard_map/dot_general | solution.py:98
  51.7 2.4 %fusion.37 = f32[8,256,256]{2,1,0:T(8,128)S(1)} fusion(bf16[2048,8,256]{2,1,0:T(8,128)(2,1)S(1)} %bitcast.171, f32[256,2048]{1,0:T(8,128)S(1)} %fusion.27), kind=kOutput, calls=%fused_computation.31 | convolution fusion | flops 2148532224 | bytes 12582912 | tf_op jit(solution)/shard_map/lt,lbf->btf/dot_general | solution.py:106
  56.9 1.9 %multiply_reduce_fusion = f32[2048]{0:T(1024)S(1)} fusion(bf16[1,2048,2048]{2,1,0:T(8,128)(2,1)S(1)} %bitcast.168), kind=kLoop, calls=%fused_computation.9 | loop fusion | flops 12580864 | bytes 8396800 | tf_op jit(solution)/shard_map/reduce_sum | solution.py:119
  61.8 7.8 %collective-permute-done.6 = f32[2,2,128,256]{3,2,1,0:T(8,128)} collective-permute-done((f32[2,2,128,256]{3,2,1,0:T(8,128)}, f32[2,2,128,256]{3,2,1,0:T(8,128)}, u32[]{:S(2)}, u32[]{:S(2)}) %collective-permute-start.6) | collective-permute-done | bytes 524320 | tf_op jit(solution)/shard_map/ppermute | solution.py:17
  70.7 1.8 %collective-permute-start.7 = (f32[2,128,256]{2,1,0:T(8,128)S(1)}, f32[2,128,256]{2,1,0:T(8,128)S(1)}, u32[]{:S(2)}, u32[]{:S(2)}) collective-permute-start(f32[2,128,256]{2,1,0:T(8,128)S(1)} %dynamic-slice_bitcast_fusion.3), channel_id=1, source_target_pairs={{0,4},{2,6},{4,0},{6,2},{8,12},{10,14},{12,8},{14,10},{1,5},{3,7},... | collective-permute-start | bytes 786440 | tf_op jit(solution)/shard_map/ppermute | solution.py:17
  72.5 1.9 %collective-permute-done.9 = f32[2,2,128,256]{3,2,1,0:T(8,128)} collective-permute-done((f32[2,2,128,256]{3,2,1,0:T(8,128)}, f32[2,2,128,256]{3,2,1,0:T(8,128)}, u32[]{:S(2)}, u32[]{:S(2)}) %collective-permute-start.9) | collective-permute-done | bytes 524320 | tf_op jit(solution)/shard_map/ppermute | solution.py:17
  76.3 3.0 %collective-permute-done.7 = f32[2,128,256]{2,1,0:T(8,128)S(1)} collective-permute-done((f32[2,128,256]{2,1,0:T(8,128)S(1)}, f32[2,128,256]{2,1,0:T(8,128)S(1)}, u32[]{:S(2)}, u32[]{:S(2)}) %collective-permute-start.7) | collective-permute-done | bytes 262176 | tf_op jit(solution)/shard_map/ppermute | solution.py:17
  79.3 2.5 %collective-permute-start.8 = (f32[128,256]{1,0:T(8,128)S(1)}, f32[128,256]{1,0:T(8,128)S(1)}, u32[]{:S(2)}, u32[]{:S(2)}) collective-permute-start(f32[128,256]{1,0:T(8,128)S(1)} %dynamic-slice_bitcast_fusion.5), channel_id=1, source_target_pairs={{0,8},{2,10},{4,12},{6,14},{8,0},{10,2},{12,4},{14,6},{1,9},{3,11}... | collective-permute-start | bytes 393224 | tf_op jit(solution)/shard_map/ppermute | solution.py:17
  82.4 2.5 %collective-permute-start.11 = (f32[128,256]{1,0:T(8,128)S(1)}, f32[128,256]{1,0:T(8,128)S(1)}, u32[]{:S(2)}, u32[]{:S(2)}) collective-permute-start(f32[128,256]{1,0:T(8,128)S(1)} %dynamic-slice_bitcast_fusion.4), channel_id=1, source_target_pairs={{0,8},{2,10},{4,12},{6,14},{8,0},{10,2},{12,4},{14,6},{1,9},{3,11}... | collective-permute-start | bytes 393224 | tf_op jit(solution)/shard_map/ppermute | solution.py:17
  84.9 6.6 %collective-permute-done.8 = f32[128,256]{1,0:T(8,128)S(1)} collective-permute-done((f32[128,256]{1,0:T(8,128)S(1)}, f32[128,256]{1,0:T(8,128)S(1)}, u32[]{:S(2)}, u32[]{:S(2)}) %collective-permute-start.8) | collective-permute-done | bytes 131104 | tf_op jit(solution)/shard_map/ppermute | solution.py:17
  91.5 2.0 %collective-permute-done.11 = f32[128,256]{1,0:T(8,128)S(1)} collective-permute-done((f32[128,256]{1,0:T(8,128)S(1)}, f32[128,256]{1,0:T(8,128)S(1)}, u32[]{:S(2)}, u32[]{:S(2)}) %collective-permute-start.11) | collective-permute-done | bytes 131104 | tf_op jit(solution)/shard_map/ppermute | solution.py:17
  93.7 5.8 %collective-permute-done.12 = bf16[128,256]{1,0:T(8,128)(2,1)S(1)} collective-permute-done((bf16[128,256]{1,0:T(8,128)(2,1)S(1)}, bf16[128,256]{1,0:T(8,128)(2,1)S(1)}, u32[]{:S(2)}, u32[]{:S(2)}) %collective-permute-start.12) | collective-permute-done | bytes 65568 | tf_op jit(solution)/shard_map/ppermute | solution.py:17
  99.6 2.9 %collective-permute-start.13 = (bf16[2,128,256]{2,1,0:T(8,128)(2,1)S(1)}, bf16[2,128,256]{2,1,0:T(8,128)(2,1)S(1)}, u32[]{:S(2)}, u32[]{:S(2)}) collective-permute-start(bf16[2,128,256]{2,1,0:T(8,128)(2,1)S(1)} %pad_maximum_fusion.5), channel_id=1, source_target_pairs={{0,4},{2,6},{4,0},{6,2},{8,12},{10,14},{12,8},{14,10},{1,5},{3,7},... | collective-permute-start | bytes 393224 | tf_op jit(solution)/shard_map/ppermute | solution.py:17
  102.6 2.4 %collective-permute-done.15 = bf16[128,256]{1,0:T(8,128)(2,1)S(1)} collective-permute-done((bf16[128,256]{1,0:T(8,128)(2,1)S(1)}, bf16[128,256]{1,0:T(8,128)(2,1)S(1)}, u32[]{:S(2)}, u32[]{:S(2)}) %collective-permute-start.15) | collective-permute-done | bytes 65568 | tf_op jit(solution)/shard_map/ppermute | solution.py:17
  107.5 2.6 %collective-permute-done.16 = bf16[2,128,256]{2,1,0:T(8,128)(2,1)S(1)} collective-permute-done((bf16[2,128,256]{2,1,0:T(8,128)(2,1)S(1)}, bf16[2,128,256]{2,1,0:T(8,128)(2,1)S(1)}, u32[]{:S(2)}, u32[]{:S(2)}) %collective-permute-start.16) | collective-permute-done | bytes 131104 | tf_op jit(solution)/shard_map/ppermute | solution.py:17
  113.0 3.5 %collective-permute-done.17 = bf16[2,2,128,256]{3,2,1,0:T(8,128)(2,1)S(1)} collective-permute-done((bf16[2,2,128,256]{3,2,1,0:T(8,128)(2,1)S(1)}, bf16[2,2,128,256]{3,2,1,0:T(8,128)(2,1)S(1)}, u32[]{:S(2)}, u32[]{:S(2)}) %collective-permute-start.17) | collective-permute-done | bytes 262176 | tf_op jit(solution)/shard_map/ppermute | solution.py:17
  117.3 27.5 %fusion.6 = (bf16[1,2048,2048]{2,1,0:T(8,128)(2,1)}, bf16[1,2048,2048]{2,1,0:T(8,128)(2,1)}, bf16[1,2048,2048]{2,1,0:T(8,128)(2,1)}) fusion(bf16[1,2048,2048]{2,1,0:T(8,128)(2,1)} %param.17, bf16[1,2048,2048]{2,1,0:T(8,128)(2,1)} %param.16, bf16[1,2048,2048]{2,1,0:T(8,128)(2,1)} %param.12, bf16[256,2048]{1,0:T(8,128)(2,1)S(1)} %broadcast_select_fusion, ...), kind=kOutput, calls=%fused_computation.12 | convolution fusion | flops 4387766272 | bytes 62930944 | tf_op jit(solution)/shard_map/dot_general | solution.py:124
  (93 shorter events, 26.7 us)
Async XLA Ops:
  7.2 34.6 %all-gather.2.cloned.1.call-start = ((), (), s32[]{:S(2)}) async-start(), calls=%async_computation | async-start | bytes 1572864 | tf_op jit(solution)/shard_map/all_gather | solution.py:90
  8.0 6.3 %collective-permute-start = (bf16[64,256]{1,0:T(8,128)(2,1)S(1)}, bf16[64,256]{1,0:T(8,128)(2,1)S(1)}, u32[]{:S(2)}, u32[]{:S(2)}) collective-permute-start(bf16[64,256]{1,0:T(8,128)(2,1)S(1)} %slice.18), channel_id=1, source_target_pairs={{0,8},{2,10},{4,12},{6,14},{8,0},{10,2},{12,4},{14,6},{1,9},{3,11}... | collective-permute-start | bytes 98312 | tf_op jit(solution)/shard_map/ppermute | solution.py:17
  15.0 4.9 %collective-permute-start.3 = (bf16[64,256]{1,0:T(8,128)(2,1)S(1)}, bf16[64,256]{1,0:T(8,128)(2,1)S(1)}, u32[]{:S(2)}, u32[]{:S(2)}) collective-permute-start(bf16[64,256]{1,0:T(8,128)(2,1)S(1)} %get-tuple-element.33), channel_id=1, source_target_pairs={{0,8},{2,10},{4,12},{6,14},{8,0},{10,2},{12,4},{14,6},{1,9},{3,11}... | collective-permute-start | bytes 98312 | tf_op jit(solution)/shard_map/ppermute | solution.py:17
  17.7 4.8 %collective-permute-start.1 = (bf16[2,64,256]{2,1,0:T(8,128)(2,1)S(1)}, bf16[2,64,256]{2,1,0:T(8,128)(2,1)S(1)}, u32[]{:S(2)}, u32[]{:S(2)}) collective-permute-start(bf16[2,64,256]{2,1,0:T(8,128)(2,1)S(1)} %pad_maximum_fusion.7), channel_id=1, source_target_pairs={{0,4},{2,6},{4,0},{6,2},{8,12},{10,14},{12,8},{14,10},{1,5},{3,7},... | collective-permute-start | bytes 196616 | tf_op jit(solution)/shard_map/ppermute | solution.py:17
  20.7 4.3 %collective-permute-start.4 = (bf16[2,64,256]{2,1,0:T(8,128)(2,1)S(1)}, bf16[2,64,256]{2,1,0:T(8,128)(2,1)S(1)}, u32[]{:S(2)}, u32[]{:S(2)}) collective-permute-start(bf16[2,64,256]{2,1,0:T(8,128)(2,1)S(1)} %pad_maximum_fusion.8), channel_id=1, source_target_pairs={{0,2},{2,0},{4,6},{6,4},{8,10},{10,8},{12,14},{14,12},{1,3},{3,1},... | collective-permute-start | bytes 196616 | tf_op jit(solution)/shard_map/ppermute | solution.py:17
  22.5 5.0 %collective-permute-start.2 = (bf16[2,2,64,256]{3,2,0,1:T(8,128)(2,1)S(1)}, bf16[2,2,64,256]{3,2,0,1:T(8,128)(2,1)S(1)}, u32[]{:S(2)}, u32[]{:S(2)}) collective-permute-start(bf16[2,2,64,256]{3,2,0,1:T(8,128)(2,1)S(1)} %pad_maximum_fusion.3), channel_id=1, source_target_pairs={{0,2},{2,0},{4,6},{6,4},{8,10},{10,8},{12,14},{14,12},{1,3},{3,1},... | collective-permute-start | bytes 393224 | tf_op jit(solution)/shard_map/ppermute | solution.py:17
  25.1 5.0 %collective-permute-start.5 = (bf16[2,2,64,256]{3,2,1,0:T(8,128)(2,1)S(1)}, bf16[2,2,64,256]{3,2,1,0:T(8,128)(2,1)S(1)}, u32[]{:S(2)}, u32[]{:S(2)}) collective-permute-start(bf16[2,2,64,256]{3,2,1,0:T(8,128)(2,1)S(1)} %pad_maximum_fusion.4), channel_id=1, source_target_pairs={{0,4},{2,6},{4,0},{6,2},{8,12},{10,14},{12,8},{14,10},{1,5},{3,7},... | collective-permute-start | bytes 393224 | tf_op jit(solution)/shard_map/ppermute | solution.py:17
  31.1 10.5 %copy-start = (s32[1,256]{1,0:T(1,128)S(1)}, s32[1,256]{1,0:T(1,128)}, u32[]{:S(2)}) copy-start(s32[1,256]{1,0:T(1,128)} %param.10) | copy-start | bytes 3076
  45.5 6.1 %slice-start.2 = ((s8[8388608]{0:T(1024)(128)(4,1)}), s8[4194304]{0:T(1024)(128)(4,1)S(1)}, s32[]{:S(2)}) async-start(s8[8388608]{0:T(1024)(128)(4,1)} %bitcast.169), calls=%async_computation.3 | async-start | bytes 8388608
  45.7 6.0 %slice-start.3 = ((s8[8388608]{0:T(1024)(128)(4,1)}), s8[4194304]{0:T(1024)(128)(4,1)S(1)}, s32[]{:S(2)}) async-start(s8[8388608]{0:T(1024)(128)(4,1)} %bitcast.169), calls=%async_computation.4 | async-start | bytes 8388608
  51.7 5.2 %slice-start = ((s8[8388608]{0:T(1024)(128)(4,1)}), s8[4194304]{0:T(1024)(128)(4,1)S(1)}, s32[]{:S(2)}) async-start(s8[8388608]{0:T(1024)(128)(4,1)} %bitcast.167), calls=%async_computation.1 | async-start | bytes 8388608
  51.7 5.2 %slice-start.1 = ((s8[8388608]{0:T(1024)(128)(4,1)}), s8[4194304]{0:T(1024)(128)(4,1)S(1)}, s32[]{:S(2)}) async-start(s8[8388608]{0:T(1024)(128)(4,1)} %bitcast.167), calls=%async_computation.2 | async-start | bytes 8388608
  55.1 14.4 %collective-permute-start.6 = (f32[2,2,128,256]{3,2,1,0:T(8,128)}, f32[2,2,128,256]{3,2,1,0:T(8,128)}, u32[]{:S(2)}, u32[]{:S(2)}) collective-permute-start(f32[2,2,128,256]{3,2,1,0:T(8,128)} %dynamic-slice_bitcast_fusion.1), channel_id=1, source_target_pairs={{0,2},{2,0},{4,6},{6,4},{8,10},{10,8},{12,14},{14,12},{1,3},{3,1},... | collective-permute-start | bytes 1572872 | tf_op jit(solution)/shard_map/ppermute | solution.py:17
  59.6 14.9 %collective-permute-start.9 = (f32[2,2,128,256]{3,2,1,0:T(8,128)}, f32[2,2,128,256]{3,2,1,0:T(8,128)}, u32[]{:S(2)}, u32[]{:S(2)}) collective-permute-start(f32[2,2,128,256]{3,2,1,0:T(8,128)} %dynamic-slice_bitcast_fusion), channel_id=1, source_target_pairs={{0,4},{2,6},{4,0},{6,2},{8,12},{10,14},{12,8},{14,10},{1,5},{3,7},... | collective-permute-start | bytes 1572872 | tf_op jit(solution)/shard_map/ppermute | solution.py:17
  70.7 8.5 %collective-permute-start.7 = (f32[2,128,256]{2,1,0:T(8,128)S(1)}, f32[2,128,256]{2,1,0:T(8,128)S(1)}, u32[]{:S(2)}, u32[]{:S(2)}) collective-permute-start(f32[2,128,256]{2,1,0:T(8,128)S(1)} %dynamic-slice_bitcast_fusion.3), channel_id=1, source_target_pairs={{0,4},{2,6},{4,0},{6,2},{8,12},{10,14},{12,8},{14,10},{1,5},{3,7},... | collective-permute-start | bytes 786440 | tf_op jit(solution)/shard_map/ppermute | solution.py:17
  75.6 6.8 %collective-permute-start.10 = (f32[2,128,256]{2,1,0:T(8,128)S(1)}, f32[2,128,256]{2,1,0:T(8,128)S(1)}, u32[]{:S(2)}, u32[]{:S(2)}) collective-permute-start(f32[2,128,256]{2,1,0:T(8,128)S(1)} %dynamic-slice_bitcast_fusion.2), channel_id=1, source_target_pairs={{0,2},{2,0},{4,6},{6,4},{8,10},{10,8},{12,14},{14,12},{1,3},{3,1},... | collective-permute-start | bytes 786440 | tf_op jit(solution)/shard_map/ppermute | solution.py:17
  79.3 12.1 %collective-permute-start.8 = (f32[128,256]{1,0:T(8,128)S(1)}, f32[128,256]{1,0:T(8,128)S(1)}, u32[]{:S(2)}, u32[]{:S(2)}) collective-permute-start(f32[128,256]{1,0:T(8,128)S(1)} %dynamic-slice_bitcast_fusion.5), channel_id=1, source_target_pairs={{0,8},{2,10},{4,12},{6,14},{8,0},{10,2},{12,4},{14,6},{1,9},{3,11}... | collective-permute-start | bytes 393224 | tf_op jit(solution)/shard_map/ppermute | solution.py:17
  82.4 11.0 %collective-permute-start.11 = (f32[128,256]{1,0:T(8,128)S(1)}, f32[128,256]{1,0:T(8,128)S(1)}, u32[]{:S(2)}, u32[]{:S(2)}) collective-permute-start(f32[128,256]{1,0:T(8,128)S(1)} %dynamic-slice_bitcast_fusion.4), channel_id=1, source_target_pairs={{0,8},{2,10},{4,12},{6,14},{8,0},{10,2},{12,4},{14,6},{1,9},{3,11}... | collective-permute-start | bytes 393224 | tf_op jit(solution)/shard_map/ppermute | solution.py:17
  93.6 5.9 %collective-permute-start.12 = (bf16[128,256]{1,0:T(8,128)(2,1)S(1)}, bf16[128,256]{1,0:T(8,128)(2,1)S(1)}, u32[]{:S(2)}, u32[]{:S(2)}) collective-permute-start(bf16[128,256]{1,0:T(8,128)(2,1)S(1)} %slice.28), channel_id=1, source_target_pairs={{0,8},{2,10},{4,12},{6,14},{8,0},{10,2},{12,4},{14,6},{1,9},{3,11}... | collective-permute-start | bytes 196616 | tf_op jit(solution)/shard_map/ppermute | solution.py:17
  99.5 5.5 %collective-permute-start.15 = (bf16[128,256]{1,0:T(8,128)(2,1)S(1)}, bf16[128,256]{1,0:T(8,128)(2,1)S(1)}, u32[]{:S(2)}, u32[]{:S(2)}) collective-permute-start(bf16[128,256]{1,0:T(8,128)(2,1)S(1)} %get-tuple-element.24), channel_id=1, source_target_pairs={{0,8},{2,10},{4,12},{6,14},{8,0},{10,2},{12,4},{14,6},{1,9},{3,11}... | collective-permute-start | bytes 196616 | tf_op jit(solution)/shard_map/ppermute | solution.py:17
  99.6 6.7 %collective-permute-start.13 = (bf16[2,128,256]{2,1,0:T(8,128)(2,1)S(1)}, bf16[2,128,256]{2,1,0:T(8,128)(2,1)S(1)}, u32[]{:S(2)}, u32[]{:S(2)}) collective-permute-start(bf16[2,128,256]{2,1,0:T(8,128)(2,1)S(1)} %pad_maximum_fusion.5), channel_id=1, source_target_pairs={{0,4},{2,6},{4,0},{6,2},{8,12},{10,14},{12,8},{14,10},{1,5},{3,7},... | collective-permute-start | bytes 393224 | tf_op jit(solution)/shard_map/ppermute | solution.py:17
  105.0 5.0 %collective-permute-start.16 = (bf16[2,128,256]{2,1,0:T(8,128)(2,1)S(1)}, bf16[2,128,256]{2,1,0:T(8,128)(2,1)S(1)}, u32[]{:S(2)}, u32[]{:S(2)}) collective-permute-start(bf16[2,128,256]{2,1,0:T(8,128)(2,1)S(1)} %pad_maximum_fusion.6), channel_id=1, source_target_pairs={{0,2},{2,0},{4,6},{6,4},{8,10},{10,8},{12,14},{14,12},{1,3},{3,1},... | collective-permute-start | bytes 393224 | tf_op jit(solution)/shard_map/ppermute | solution.py:17
  106.4 6.5 %collective-permute-start.14 = (bf16[2,2,128,256]{3,2,1,0:T(8,128)(2,1)S(1)}, bf16[2,2,128,256]{3,2,1,0:T(8,128)(2,1)S(1)}, u32[]{:S(2)}, u32[]{:S(2)}) collective-permute-start(bf16[2,2,128,256]{3,2,1,0:T(8,128)(2,1)S(1)} %pad_maximum_fusion.1), channel_id=1, source_target_pairs={{0,2},{2,0},{4,6},{6,4},{8,10},{10,8},{12,14},{14,12},{1,3},{3,1},... | collective-permute-start | bytes 786440 | tf_op jit(solution)/shard_map/ppermute | solution.py:17
  110.1 6.4 %collective-permute-start.17 = (bf16[2,2,128,256]{3,2,1,0:T(8,128)(2,1)S(1)}, bf16[2,2,128,256]{3,2,1,0:T(8,128)(2,1)S(1)}, u32[]{:S(2)}, u32[]{:S(2)}) collective-permute-start(bf16[2,2,128,256]{3,2,1,0:T(8,128)(2,1)S(1)} %pad_maximum_fusion.2), channel_id=1, source_target_pairs={{0,4},{2,6},{4,0},{6,2},{8,12},{10,14},{12,8},{14,10},{1,5},{3,7},... | collective-permute-start | bytes 786440 | tf_op jit(solution)/shard_map/ppermute | solution.py:17
  (3 other events, 10.7 us)
Sparse Core Ops, SparseCore 0:
  31.2 10.5 all-gather.1

commit v3 on v2

--- a/solution.py
+++ b/solution.py
@@ -57,20 +57,31 @@
     return first, second
 
 
-def _reduce_scatter(blocks, axis, size):
-    first, second = _orders(size)
-    half = blocks.shape[1] // 2
-    a = _halving_sum(blocks[:, :half], axis, size, first)
-    b = _halving_sum(blocks[:, half:], axis, size, second)
-    return jnp.concatenate([a, b], axis=0)
+def _halving_cols(cols, axis, size, order):
+    nbits = size.bit_length() - 1
+    me = lax.axis_index(axis)
+    cur = cols
+    block = 0
+    for step, bit in enumerate(order):
+        half = cur.shape[1] // 2
+        mine_bit = (me >> bit) & 1
+        keep_part = lax.dynamic_slice_in_dim(cur, mine_bit * half, half, axis=1)
+        send_part = lax.dynamic_slice_in_dim(cur, (1 - mine_bit) * half, half, axis=1)
+        cur = keep_part + _pair_swap(send_part, axis, 1 << bit, size)
+        block = block + (mine_bit << (nbits - 1 - step))
+    return cur, block
 
 
-def _all_gather(value, axis, size):
-    first, second = _orders(size)
-    half = value.shape[0] // 2
-    a = _doubling_gather(value[:half], axis, size, first[::-1])
-    b = _doubling_gather(value[half:], axis, size, second[::-1])
-    return jnp.concatenate([a, b], axis=1)
+def _doubling_cols(cols, axis, size, order):
+    me = lax.axis_index(axis)
+    cur = cols
+    for bit in order[::-1]:
+        other = _pair_swap(cur, axis, 1 << bit, size)
+        low_is_me = ((me >> bit) & 1) == 0
+        low = jnp.where(low_is_me, cur, other)
+        high = jnp.where(low_is_me, other, cur)
+        cur = jnp.concatenate([low, high], axis=1)
+    return cur
 
 
 def local(
@@ -85,7 +96,8 @@
     second_moment,
 ):
     lat_size = LAT_SIZE[0]
-    act_blocks = _all_gather(activations, "lat", lat_size)
+    first, second = _orders(lat_size)
+    act_blocks = _doubling_gather(activations, "lat", lat_size, first[::-1])
     half_rows = jnp.transpose(act_blocks, (1, 0, 2)).reshape(activations.shape[0], -1)
     gathered = lax.all_gather(half_rows, "seed", axis=0, tiled=True)
     row_order = bag_rows[0]
@@ -101,18 +113,22 @@
     pre_t = pre_t + enc_bias[0][:, None]
     latent_t = jnp.maximum(pre_t, 0.0).astype(jnp.bfloat16)
     width = bias_dec.shape[0] // lat_size
-    start = lax.axis_index("lat") * width
-    decoder_blocks = decoder.reshape(decoder.shape[0], lat_size, width)
-    partial_sum = jnp.einsum(
-        "lt,lbf->btf", latent_t, decoder_blocks, preferred_element_type=jnp.float32
+    partial_sum = lax.dot_general(
+        latent_t, decoder, (((0,), (0,)), ((), ())), preferred_element_type=jnp.float32
     )
-    total = _reduce_scatter(partial_sum, "lat", lat_size)
-    sample_cols = lax.dynamic_slice_in_dim(sample, start, width, axis=1).astype(jnp.float32)
-    bias_cols = lax.dynamic_slice_in_dim(bias_dec, start, width)
-    keep_cols_f = lax.dynamic_slice_in_dim(keep, start, width)
-    error_cols = ((total + bias_cols - sample_cols) * keep_cols_f).astype(jnp.bfloat16)
-    error_blocks = _all_gather(error_cols, "lat", lat_size)
-    error = jnp.transpose(error_blocks, (1, 0, 2)).reshape(error_cols.shape[0], -1)
+    half = partial_sum.shape[0] // 2
+    error_parts = []
+    for rows, order in ((slice(0, half), first), (slice(half, None), second)):
+        total, block = _halving_cols(partial_sum[rows], "lat", lat_size, order)
+        start = block * width
+        sample_cols = lax.dynamic_slice_in_dim(sample[rows], start, width, axis=1)
+        bias_cols = lax.dynamic_slice_in_dim(bias_dec, start, width)
+        keep_cols_f = lax.dynamic_slice_in_dim(keep, start, width)
+        error_cols = (
+            (total + bias_cols - sample_cols.astype(jnp.float32)) * keep_cols_f
+        ).astype(jnp.bfloat16)
+        error_parts.append(_doubling_cols(error_cols, "lat", lat_size, order))
+    error = jnp.concatenate(error_parts, axis=0)
     back_t = lax.dot_general(
         decoder, error, (((1,), (1,)), ((), ())), preferred_element_type=jnp.float32
     )

time: 152 us -> 157 us (1.033)
  other arithmetic: 7.3 us -> 38.4 us
  matrix products: 35.7 us -> 22.5 us
  local copies, waits for them, and re-layouts: 18.4 us -> 5.81 us
  starting transfers between devices: 30.4 us -> 24.6 us
  waiting for transfers between devices: 45.3 us -> 50.7 us
    broadcast_in_dim x0 -> x1, other arithmetic: none -> 27.9 us  [local(): moment_two.astype(jnp.bfloat16)[None]]
    dot_general x1, matrix products: 27.5 us -> 14.3 us  [local(): grad = jnp.dot(d_pre_t, centered, preferred_element_type=jnp.float32)]
    unnamed x17 -> x8, local copies, waits for them, and re-layouts: 10.5 us -> 0.02 us
    ppermute x18 -> x15, starting transfers between devices: 30.4 us -> 24.6 us  [_pair_swap(): return lax.ppermute(value, axis, [(i, i ^ mask) for i in range(size)])]
    all_gather x1, waiting for transfers between devices: 0.17 us -> 4.36 us  [local(): gathered = lax.all_gather(half_rows, 'seed', axis=0, tiled=True)]
    reduce_sum x1, other arithmetic: 1.87 us -> 5.1 us  [local(): jnp.sum(jnp.square(decoder.astype(jnp.float32)), axis=1) + 1e-06]
    add x6 -> x4, other arithmetic: 2.32 us -> 0.24 us  [_halving_cols(): cur = keep_part + _pair_swap(send_part, axis, 1 << bit, size)]
    select_n x0 -> x6, other arithmetic: none -> 1.84 us  [_doubling_cols(): low = jnp.where(low_is_me, cur, other)]
  transfers between devices with their start and end apart: 19 -> 16, of which waited for: 17 -> 13; matrix products, arithmetic and copies ran while one was open for 12% -> 6% of each run, Pallas kernels for 0% -> 0%
where the time goes in v3:
time: 157 us; the launch traced here: 156 us
  waiting for transfers between devices  50.7 us (32%)
  other arithmetic  38.4 us (24%)
  starting transfers between devices  24.6 us (16%)
  matrix products  22.5 us (14%)
  between operations  14.3 us (9%)
  local copies, waits for them, and re-layouts  5.81 us (4%)
    ppermute x15, waiting for transfers between devices, _pair_swap(): return lax.ppermute(value, axis, [(i, i ^ mask) for i in range(size)])  46.3 us
    broadcast_in_dim x1, other arithmetic, local(): moment_two.astype(jnp.bfloat16)[None]  27.9 us
    ppermute x15, starting transfers between devices, _pair_swap(): return lax.ppermute(value, axis, [(i, i ^ mask) for i in range(size)])  24.6 us
    dot_general x1, matrix products, local(): grad = jnp.dot(d_pre_t, centered, preferred_element_type=jnp.float32)  14.3 us
    dot_general x1, matrix products, local(): lax.dot_general(weight_in, centered, (((1,), (1,)), ((), ())), preferred_...  5.9 us
    reduce_sum x1, other arithmetic, local(): jnp.sum(jnp.square(decoder.astype(jnp.float32)), axis=1) + 1e-06  5.1 us
    all_gather x1, waiting for transfers between devices, local(): gathered = lax.all_gather(half_rows, 'seed', axis=0, tiled=True)  4.36 us
    gather x1, local copies, waits for them, and re-layouts, local(): sample = jnp.take(gathered, row_order, axis=0)  3.72 us
  transfers between devices with their start and end apart: 16, of which 13 were waited for; matrix products, arithmetic and copies ran while one was open for 6% of the time, Pallas kernels for 0%

profile of v3, /device:TPU:0, one launch (start us, length us, event | category | flops | bytes accessed | tf_op | source)
XLA Modules:
  0.0 156.3 jit_solution(4936165760401323648)
XLA Ops:
  7.2 4.1 %collective-permute-start = (bf16[128,256]{1,0:T(8,128)(2,1)}, bf16[128,256]{1,0:T(8,128)(2,1)S(1)}, u32[]{:S(2)}, u32[]{:S(2)}) collective-permute-start(bf16[128,256]{1,0:T(8,128)(2,1)} %param.9), channel_id=1, source_target_pairs={{0,8},{2,10},{4,12},{6,14},{8,0},{10,2},{12,4},{14,6},{1,9},{3,11}... | collective-permute-start | bytes 196616 | tf_op jit(solution)/shard_map/ppermute | solution.py:17
  11.3 3.9 %collective-permute-done = bf16[128,256]{1,0:T(8,128)(2,1)S(1)} collective-permute-done((bf16[128,256]{1,0:T(8,128)(2,1)}, bf16[128,256]{1,0:T(8,128)(2,1)S(1)}, u32[]{:S(2)}, u32[]{:S(2)}) %collective-permute-start) | collective-permute-done | bytes 65568 | tf_op jit(solution)/shard_map/ppermute | solution.py:17
  16.8 4.3 %collective-permute-done.1 = bf16[2,128,256]{2,1,0:T(8,128)(2,1)S(1)} collective-permute-done((bf16[2,128,256]{2,1,0:T(8,128)(2,1)S(1)}, bf16[2,128,256]{2,1,0:T(8,128)(2,1)S(1)}, u32[]{:S(2)}, u32[]{:S(2)}) %collective-permute-start.1) | collective-permute-done | bytes 131104 | tf_op jit(solution)/shard_map/ppermute | solution.py:17
  21.1 1.8 %collective-permute-start.2 = (bf16[2,2,128,256]{3,2,1,0:T(8,128)(2,1)S(1)}, bf16[2,2,128,256]{3,2,1,0:T(8,128)(2,1)S(1)}, u32[]{:S(2)}, u32[]{:S(2)}) collective-permute-start(bf16[2,2,128,256]{3,2,1,0:T(8,128)(2,1)S(1)} %pad_maximum_fusion), channel_id=1, source_target_pairs={{0,2},{2,0},{4,6},{6,4},{8,10},{10,8},{12,14},{14,12},{1,3},{3,1},... | collective-permute-start | bytes 786440 | tf_op jit(solution)/shard_map/ppermute | solution.py:17
  24.3 3.3 %collective-permute-done.2 = bf16[2,2,128,256]{3,2,1,0:T(8,128)(2,1)S(1)} collective-permute-done((bf16[2,2,128,256]{3,2,1,0:T(8,128)(2,1)S(1)}, bf16[2,2,128,256]{3,2,1,0:T(8,128)(2,1)S(1)}, u32[]{:S(2)}, u32[]{:S(2)}) %collective-permute-start.2) | collective-permute-done | bytes 262176 | tf_op jit(solution)/shard_map/ppermute | solution.py:17
  30.1 5.1 %multiply_reduce_fusion = f32[2048]{0:T(1024)S(1)} fusion(bf16[1,2048,2048]{2,1,0:T(8,128)(2,1)} %param.14), kind=kLoop, calls=%fused_computation.9 | loop fusion | flops 12580864 | bytes 8396800 | tf_op jit(solution)/shard_map/reduce_sum | solution.py:135
  35.2 4.4 %all-gather.2.cloned.1.call-done = bf16[256,2048]{1,0:T(8,128)(2,1)} async-done(((bf16[128,2048]{1,0:T(8,128)(2,1)}), bf16[256,2048]{1,0:T(8,128)(2,1)}) %all-gather.2.cloned.1.call-update) | async-done | bytes 1048592 | tf_op jit(solution)/shard_map/all_gather | solution.py:102
  39.5 3.7 %gather_fusion = bf16[256,2048]{1,0:T(8,128)(2,1)S(1)} fusion(bf16[256,2048]{1,0:T(8,128)(2,1)} %all-gather.2.cloned.1.call-done, s32[1024]{0:T(1024)S(1)} %pad_clamp_fusion), kind=kCustom, calls=%fused_computation | custom fusion | bytes 2098176 | tf_op jit(solution)/shard_map/jit(_take)/gather | solution.py:104
  43.5 5.9 %fusion.27 = f32[256,2048]{1,0:T(8,128)S(1)} fusion(bf16[1,2048,2048]{2,1,0:T(8,128)(2,1)} %param.12, f32[2048]{0:T(1024)S(1)} %bitcast.93, bf16[256,2048]{1,0:T(8,128)(2,1)S(1)} %broadcast_select_fusion, f32[2048]{0:T(1024)S(1)} %bitcast.85), kind=kOutput, calls=%fused_computation.25 | convolution fusion | flops 2149580800 | bytes 11550720 | tf_op jit(solution)/shard_map/dot_general | solution.py:110
  49.4 2.3 %fusion.10 = f32[256,2048]{1,0:T(8,128)S(1)} fusion(bf16[1,2048,2048]{2,1,0:T(8,128)(2,1)S(1)} %bitcast.82, f32[256,2048]{1,0:T(8,128)S(1)} %fusion.27), kind=kOutput, calls=%fused_computation.16 | convolution fusion | flops 2148532224 | bytes 12582912 | tf_op jit(solution)/shard_map/dot_general | solution.py:116
  52.0 1.8 %collective-permute-start.9 = (f32[128,1024]{1,0:T(8,128)S(1)}, f32[128,1024]{1,0:T(8,128)S(1)}, u32[]{:S(2)}, u32[]{:S(2)}) collective-permute-start(f32[128,1024]{1,0:T(8,128)S(1)} %constant_dynamic-slice_fusion.3), channel_id=1, source_target_pairs={{0,4},{2,6},{4,0},{6,2},{8,12},{10,14},{12,8},{14,10},{1,5},{3,7},... | collective-permute-start | bytes 1572872 | tf_op jit(solution)/shard_map/ppermute | solution.py:17
  55.5 10.7 %collective-permute-done.9 = f32[128,1024]{1,0:T(8,128)S(1)} collective-permute-done((f32[128,1024]{1,0:T(8,128)S(1)}, f32[128,1024]{1,0:T(8,128)S(1)}, u32[]{:S(2)}, u32[]{:S(2)}) %collective-permute-start.9) | collective-permute-done | bytes 524320 | tf_op jit(solution)/shard_map/ppermute | solution.py:17
  66.3 1.8 %collective-permute-start.10 = (f32[128,512]{1,0:T(8,128)S(1)}, f32[128,512]{1,0:T(8,128)S(1)}, u32[]{:S(2)}, u32[]{:S(2)}) collective-permute-start(f32[128,512]{1,0:T(8,128)S(1)} %constant_dynamic-slice_fusion.2), channel_id=1, source_target_pairs={{0,2},{2,0},{4,6},{6,4},{8,10},{10,8},{12,14},{14,12},{1,3},{3,1},... | collective-permute-start | bytes 786440 | tf_op jit(solution)/shard_map/ppermute | solution.py:17
  68.2 1.6 collective-permute-start.4
  69.7 4.3 %collective-permute-done.10 = f32[128,512]{1,0:T(8,128)S(1)} collective-permute-done((f32[128,512]{1,0:T(8,128)S(1)}, f32[128,512]{1,0:T(8,128)S(1)}, u32[]{:S(2)}, u32[]{:S(2)}) %collective-permute-start.10) | collective-permute-done | bytes 262176 | tf_op jit(solution)/shard_map/ppermute | solution.py:17
  74.1 2.7 %collective-permute-start.11 = (f32[128,256]{1,0:T(8,128)S(1)}, f32[128,256]{1,0:T(8,128)S(1)}, u32[]{:S(2)}, u32[]{:S(2)}) collective-permute-start(f32[128,256]{1,0:T(8,128)S(1)} %constant_dynamic-slice_fusion.1), channel_id=1, source_target_pairs={{0,8},{2,10},{4,12},{6,14},{8,0},{10,2},{12,4},{14,6},{1,9},{3,11}... | collective-permute-start | bytes 393224 | tf_op jit(solution)/shard_map/ppermute | solution.py:17
  78.2 7.9 %collective-permute-done.11 = f32[128,256]{1,0:T(8,128)S(1)} collective-permute-done((f32[128,256]{1,0:T(8,128)S(1)}, f32[128,256]{1,0:T(8,128)S(1)}, u32[]{:S(2)}, u32[]{:S(2)}) %collective-permute-start.11) | collective-permute-done | bytes 131104 | tf_op jit(solution)/shard_map/ppermute | solution.py:17
  86.2 2.0 %collective-permute-done.5 = f32[128,256]{1,0:T(8,128)S(1)} collective-permute-done((f32[128,256]{1,0:T(8,128)S(1)}, f32[128,256]{1,0:T(8,128)S(1)}, u32[]{:S(2)}, u32[]{:S(2)}) %collective-permute-start.5) | collective-permute-done | bytes 131104 | tf_op jit(solution)/shard_map/ppermute | solution.py:17
  89.2 3.4 %collective-permute-done.12 = bf16[128,256]{1,0:T(8,128)(2,1)S(1)} collective-permute-done((bf16[128,256]{1,0:T(8,128)(2,1)S(1)}, bf16[128,256]{1,0:T(8,128)(2,1)S(1)}, u32[]{:S(2)}, u32[]{:S(2)}) %collective-permute-start.12) | collective-permute-done | bytes 65568 | tf_op jit(solution)/shard_map/ppermute | solution.py:17
  92.7 1.6 %collective-permute-start.13 = (bf16[128,512]{1,0:T(8,128)(2,1)S(1)}, bf16[128,512]{1,0:T(8,128)(2,1)S(1)}, u32[]{:S(2)}, u32[]{:S(2)}) collective-permute-start(bf16[128,512]{1,0:T(8,128)(2,1)S(1)} %pad_maximum_fusion.5), channel_id=1, source_target_pairs={{0,2},{2,0},{4,6},{6,4},{8,10},{10,8},{12,14},{14,12},{1,3},{3,1},... | collective-permute-start | bytes 393224 | tf_op jit(solution)/shard_map/ppermute | solution.py:17
  94.3 1.9 %collective-permute-start.7 = (bf16[128,512]{1,0:T(8,128)(2,1)S(1)}, bf16[128,512]{1,0:T(8,128)(2,1)S(1)}, u32[]{:S(2)}, u32[]{:S(2)}) collective-permute-start(bf16[128,512]{1,0:T(8,128)(2,1)S(1)} %pad_maximum_fusion.4), channel_id=1, source_target_pairs={{0,4},{2,6},{4,0},{6,2},{8,12},{10,14},{12,8},{14,10},{1,5},{3,7},... | collective-permute-start | bytes 393224 | tf_op jit(solution)/shard_map/ppermute | solution.py:17
  101.2 3.8 %collective-permute-done.14 = bf16[128,1024]{1,0:T(8,128)(2,1)S(1)} collective-permute-done((bf16[128,1024]{1,0:T(8,128)(2,1)S(1)}, bf16[128,1024]{1,0:T(8,128)(2,1)S(1)}, u32[]{:S(2)}, u32[]{:S(2)}) %collective-permute-start.14) | collective-permute-done | bytes 262176 | tf_op jit(solution)/shard_map/ppermute | solution.py:17
  107.4 14.3 %fusion.34 = f32[2048,2048]{1,0:T(8,128)} fusion(bf16[1,2048,2048]{2,1,0:T(8,128)(2,1)} %param.14, f32[256,2048]{1,0:T(8,128)S(1)} %fusion.27, bf16[128,1024]{1,0:T(8,128)(2,1)} %get-tuple-element.13, bf16[128,1024]{1,0:T(8,128)(2,1)S(1)} %get-tuple-element.12, bf16[128,1024]{1,0:T(8,128)(2,1)} %get-tuple-element.11, ...), kind=kOutput, calls=%fused_computation.27 | convolution fusion | flops 4303880192 | bytes 29376512 | tf_op jit(solution)/shard_map/dot_general | solution.py:140
  121.6 27.9 %fusion.6 = (bf16[1,2048,2048]{2,1,0:T(8,128)(2,1)}, bf16[1,2048,2048]{2,1,0:T(8,128)(2,1)}, bf16[1,2048,2048]{2,1,0:T(8,128)(2,1)}) fusion(f32[2048,2048]{1,0:T(8,128)} %fusion.34, bf16[1,2048,2048]{2,1,0:T(8,128)(2,1)} %param.17, bf16[1,2048,2048]{2,1,0:T(8,128)(2,1)} %param.16, bf16[1,2048,2048]{2,1,0:T(8,128)(2,1)} %param.12), kind=kLoop, calls=%fused_computation.12 | loop fusion | flops 88080384 | bytes 67108864 | tf_op jit(solution)/shard_map/broadcast_in_dim | solution.py:149
  (63 shorter events, 17.7 us)
Async XLA Ops:
  7.2 32.4 %all-gather.2.cloned.1.call-start = ((), (), s32[]{:S(2)}) async-start(), calls=%async_computation | async-start | bytes 1572864 | tf_op jit(solution)/shard_map/all_gather | solution.py:102
  7.2 8.0 %collective-permute-start = (bf16[128,256]{1,0:T(8,128)(2,1)}, bf16[128,256]{1,0:T(8,128)(2,1)S(1)}, u32[]{:S(2)}, u32[]{:S(2)}) collective-permute-start(bf16[128,256]{1,0:T(8,128)(2,1)} %param.9), channel_id=1, source_target_pairs={{0,8},{2,10},{4,12},{6,14},{8,0},{10,2},{12,4},{14,6},{1,9},{3,11}... | collective-permute-start | bytes 196616 | tf_op jit(solution)/shard_map/ppermute | solution.py:17
  16.1 5.0 %collective-permute-start.1 = (bf16[2,128,256]{2,1,0:T(8,128)(2,1)S(1)}, bf16[2,128,256]{2,1,0:T(8,128)(2,1)S(1)}, u32[]{:S(2)}, u32[]{:S(2)}) collective-permute-start(bf16[2,128,256]{2,1,0:T(8,128)(2,1)S(1)} %pad_maximum_fusion.3), channel_id=1, source_target_pairs={{0,4},{2,6},{4,0},{6,2},{8,12},{10,14},{12,8},{14,10},{1,5},{3,7},... | collective-permute-start | bytes 393224 | tf_op jit(solution)/shard_map/ppermute | solution.py:17
  21.1 6.4 %collective-permute-start.2 = (bf16[2,2,128,256]{3,2,1,0:T(8,128)(2,1)S(1)}, bf16[2,2,128,256]{3,2,1,0:T(8,128)(2,1)S(1)}, u32[]{:S(2)}, u32[]{:S(2)}) collective-permute-start(bf16[2,2,128,256]{3,2,1,0:T(8,128)(2,1)S(1)} %pad_maximum_fusion), channel_id=1, source_target_pairs={{0,2},{2,0},{4,6},{6,4},{8,10},{10,8},{12,14},{14,12},{1,3},{3,1},... | collective-permute-start | bytes 786440 | tf_op jit(solution)/shard_map/ppermute | solution.py:17
  30.1 13.4 %copy-start = (f32[1,2048]{1,0:T(1,128)S(1)}, f32[1,2048]{1,0:T(1,128)}, u32[]{:S(2)}) copy-start(f32[1,2048]{1,0:T(1,128)} %param.15) | copy-start | bytes 24580
  30.1 13.4 %copy-start.1 = (f32[1,2048]{1,0:T(1,128)S(1)}, f32[1,2048]{1,0:T(1,128)}, u32[]{:S(2)}) copy-start(f32[1,2048]{1,0:T(1,128)} %param.13) | copy-start | bytes 24580
  43.3 6.1 %slice-start = ((s8[8388608]{0:T(1024)(128)(4,1)}), s8[4194304]{0:T(1024)(128)(4,1)S(1)}, s32[]{:S(2)}) async-start(s8[8388608]{0:T(1024)(128)(4,1)} %bitcast.81), calls=%async_computation.1 | async-start | bytes 8388608
  43.5 5.9 %slice-start.1 = ((s8[8388608]{0:T(1024)(128)(4,1)}), s8[4194304]{0:T(1024)(128)(4,1)S(1)}, s32[]{:S(2)}) async-start(s8[8388608]{0:T(1024)(128)(4,1)} %bitcast.81), calls=%async_computation.2 | async-start | bytes 8388608
  52.0 14.2 %collective-permute-start.9 = (f32[128,1024]{1,0:T(8,128)S(1)}, f32[128,1024]{1,0:T(8,128)S(1)}, u32[]{:S(2)}, u32[]{:S(2)}) collective-permute-start(f32[128,1024]{1,0:T(8,128)S(1)} %constant_dynamic-slice_fusion.3), channel_id=1, source_target_pairs={{0,4},{2,6},{4,0},{6,2},{8,12},{10,14},{12,8},{14,10},{1,5},{3,7},... | collective-permute-start | bytes 1572872 | tf_op jit(solution)/shard_map/ppermute | solution.py:17
  53.8 14.3 %collective-permute-start.3 = (f32[128,1024]{1,0:T(8,128)S(1)}, f32[128,1024]{1,0:T(8,128)S(1)}, u32[]{:S(2)}, u32[]{:S(2)}) collective-permute-start(f32[128,1024]{1,0:T(8,128)S(1)} %constant_dynamic-slice_fusion.9), channel_id=1, source_target_pairs={{0,2},{2,0},{4,6},{6,4},{8,10},{10,8},{12,14},{14,12},{1,3},{3,1},... | collective-permute-start | bytes 1572872 | tf_op jit(solution)/shard_map/ppermute | solution.py:17
  66.3 7.8 %collective-permute-start.10 = (f32[128,512]{1,0:T(8,128)S(1)}, f32[128,512]{1,0:T(8,128)S(1)}, u32[]{:S(2)}, u32[]{:S(2)}) collective-permute-start(f32[128,512]{1,0:T(8,128)S(1)} %constant_dynamic-slice_fusion.2), channel_id=1, source_target_pairs={{0,2},{2,0},{4,6},{6,4},{8,10},{10,8},{12,14},{14,12},{1,3},{3,1},... | collective-permute-start | bytes 786440 | tf_op jit(solution)/shard_map/ppermute | solution.py:17
  68.2 8.7 %collective-permute-start.4 = (f32[128,512]{1,0:T(8,128)S(1)}, f32[128,512]{1,0:T(8,128)S(1)}, u32[]{:S(2)}, u32[]{:S(2)}) collective-permute-start(f32[128,512]{1,0:T(8,128)S(1)} %constant_dynamic-slice_fusion.8), channel_id=1, source_target_pairs={{0,4},{2,6},{4,0},{6,2},{8,12},{10,14},{12,8},{14,10},{1,5},{3,7},... | collective-permute-start | bytes 786440 | tf_op jit(solution)/shard_map/ppermute | solution.py:17
  74.1 12.0 %collective-permute-start.11 = (f32[128,256]{1,0:T(8,128)S(1)}, f32[128,256]{1,0:T(8,128)S(1)}, u32[]{:S(2)}, u32[]{:S(2)}) collective-permute-start(f32[128,256]{1,0:T(8,128)S(1)} %constant_dynamic-slice_fusion.1), channel_id=1, source_target_pairs={{0,8},{2,10},{4,12},{6,14},{8,0},{10,2},{12,4},{14,6},{1,9},{3,11}... | collective-permute-start | bytes 393224 | tf_op jit(solution)/shard_map/ppermute | solution.py:17
  76.9 11.3 %collective-permute-start.5 = (f32[128,256]{1,0:T(8,128)S(1)}, f32[128,256]{1,0:T(8,128)S(1)}, u32[]{:S(2)}, u32[]{:S(2)}) collective-permute-start(f32[128,256]{1,0:T(8,128)S(1)} %constant_dynamic-slice_fusion.7), channel_id=1, source_target_pairs={{0,8},{2,10},{4,12},{6,14},{8,0},{10,2},{12,4},{14,6},{1,9},{3,11}... | collective-permute-start | bytes 393224 | tf_op jit(solution)/shard_map/ppermute | solution.py:17
  86.1 6.5 %collective-permute-start.12 = (bf16[128,256]{1,0:T(8,128)(2,1)S(1)}, bf16[128,256]{1,0:T(8,128)(2,1)S(1)}, u32[]{:S(2)}, u32[]{:S(2)}) collective-permute-start(bf16[128,256]{1,0:T(8,128)(2,1)S(1)} %multiply_convert_fusion), channel_id=1, source_target_pairs={{0,8},{2,10},{4,12},{6,14},{8,0},{10,2},{12,4},{14,6},{1,9},{3,11}... | collective-permute-start | bytes 196616 | tf_op jit(solution)/shard_map/ppermute | solution.py:17
  88.3 6.0 %collective-permute-start.6 = (bf16[128,256]{1,0:T(8,128)(2,1)S(1)}, bf16[128,256]{1,0:T(8,128)(2,1)S(1)}, u32[]{:S(2)}, u32[]{:S(2)}) collective-permute-start(bf16[128,256]{1,0:T(8,128)(2,1)S(1)} %multiply_convert_fusion.1), channel_id=1, source_target_pairs={{0,8},{2,10},{4,12},{6,14},{8,0},{10,2},{12,4},{14,6},{1,9},{3,11}... | collective-permute-start | bytes 196616 | tf_op jit(solution)/shard_map/ppermute | solution.py:17
  92.7 5.0 %collective-permute-start.13 = (bf16[128,512]{1,0:T(8,128)(2,1)S(1)}, bf16[128,512]{1,0:T(8,128)(2,1)S(1)}, u32[]{:S(2)}, u32[]{:S(2)}) collective-permute-start(bf16[128,512]{1,0:T(8,128)(2,1)S(1)} %pad_maximum_fusion.5), channel_id=1, source_target_pairs={{0,2},{2,0},{4,6},{6,4},{8,10},{10,8},{12,14},{14,12},{1,3},{3,1},... | collective-permute-start | bytes 393224 | tf_op jit(solution)/shard_map/ppermute | solution.py:17
  94.3 5.6 %collective-permute-start.7 = (bf16[128,512]{1,0:T(8,128)(2,1)S(1)}, bf16[128,512]{1,0:T(8,128)(2,1)S(1)}, u32[]{:S(2)}, u32[]{:S(2)}) collective-permute-start(bf16[128,512]{1,0:T(8,128)(2,1)S(1)} %pad_maximum_fusion.4), channel_id=1, source_target_pairs={{0,4},{2,6},{4,0},{6,2},{8,12},{10,14},{12,8},{14,10},{1,5},{3,7},... | collective-permute-start | bytes 393224 | tf_op jit(solution)/shard_map/ppermute | solution.py:17
  97.8 7.2 %collective-permute-start.14 = (bf16[128,1024]{1,0:T(8,128)(2,1)S(1)}, bf16[128,1024]{1,0:T(8,128)(2,1)S(1)}, u32[]{:S(2)}, u32[]{:S(2)}) collective-permute-start(bf16[128,1024]{1,0:T(8,128)(2,1)S(1)} %pad_maximum_fusion.2), channel_id=1, source_target_pairs={{0,4},{2,6},{4,0},{6,2},{8,12},{10,14},{12,8},{14,10},{1,5},{3,7},... | collective-permute-start | bytes 786440 | tf_op jit(solution)/shard_map/ppermute | solution.py:17
  100.0 6.4 %collective-permute-start.8 = (bf16[128,1024]{1,0:T(8,128)(2,1)S(1)}, bf16[128,1024]{1,0:T(8,128)(2,1)S(1)}, u32[]{:S(2)}, u32[]{:S(2)}) collective-permute-start(bf16[128,1024]{1,0:T(8,128)(2,1)S(1)} %pad_maximum_fusion.1), channel_id=1, source_target_pairs={{0,2},{2,0},{4,6},{6,4},{8,10},{10,8},{12,14},{14,12},{1,3},{3,1},... | collective-permute-start | bytes 786440 | tf_op jit(solution)/shard_map/ppermute | solution.py:17
Sparse Core Ops, SparseCore 0:
  28.7 10.7 all-gather.1

commit v4 on v3

--- a/solution.py
+++ b/solution.py
@@ -72,6 +72,15 @@
     return cur, block
 
 
+def _block_owners(size, order):
+    nbits = size.bit_length() - 1
+    owned = [
+        sum(((d >> bit) & 1) << (nbits - 1 - step) for step, bit in enumerate(order))
+        for d in range(size)
+    ]
+    return [owned.index(k) for k in range(size)]
+
+
 def _doubling_cols(cols, axis, size, order):
     me = lax.axis_index(axis)
     cur = cols
@@ -127,8 +136,10 @@
         error_cols = (
             (total + bias_cols - sample_cols.astype(jnp.float32)) * keep_cols_f
         ).astype(jnp.bfloat16)
-        error_parts.append(_doubling_cols(error_cols, "lat", lat_size, order))
-    error = jnp.concatenate(error_parts, axis=0)
+        stacked = _doubling_gather(error_cols, "lat", lat_size, order[::-1])
+        error_parts.append(stacked[jnp.array(_block_owners(lat_size, order))])
+    error_blocks = jnp.concatenate(error_parts, axis=1)
+    error = jnp.transpose(error_blocks, (1, 0, 2)).reshape(error_blocks.shape[1], -1)
     back_t = lax.dot_general(
         decoder, error, (((1,), (1,)), ((), ())), preferred_element_type=jnp.float32
     )

time: 157 us -> 143 us (0.911)
  other arithmetic: 38.4 us -> 10.4 us
  matrix products: 22.5 us -> 35.5 us
  local copies, waits for them, and re-layouts: 5.81 us -> 7.75 us
    broadcast_in_dim x1 -> x0, other arithmetic: 27.9 us -> none  [local(): moment_two.astype(jnp.bfloat16)[None]]
    dot_general x1, matrix products: 14.3 us -> 27.3 us  [local(): grad = jnp.dot(d_pre_t, centered, preferred_element_type=jnp.float32)]
    select_n x6 -> x0, other arithmetic: 1.84 us -> none  [_doubling_cols(): low = jnp.where(low_is_me, cur, other)]
  transfers between devices with their start and end apart: 16 -> 16, of which waited for: 13 -> 13; matrix products, arithmetic and copies ran while one was open for 6% -> 7% of each run, Pallas kernels for 0% -> 0%
where the time goes in v4:
time: 143 us
  waiting for transfers between devices  50.1 us (35%)
  matrix products  35.5 us (25%)
  starting transfers between devices  24.6 us (17%)
  between operations  14.4 us (10%)
  other arithmetic  10.4 us (7%)
  local copies, waits for them, and re-layouts  7.75 us (5%)
    ppermute x15, waiting for transfers between devices, _pair_swap(): return lax.ppermute(value, axis, [(i, i ^ mask) for i in range(size)])  44.9 us
    dot_general x1, matrix products, local(): grad = jnp.dot(d_pre_t, centered, preferred_element_type=jnp.float32)  27.3 us
    ppermute x15, starting transfers between devices, _pair_swap(): return lax.ppermute(value, axis, [(i, i ^ mask) for i in range(size)])  24.6 us
    dot_general x1, matrix products, local(): lax.dot_general(weight_in, centered, (((1,), (1,)), ((), ())), preferred_...  5.9 us
    all_gather x1, waiting for transfers between devices, local(): gathered = lax.all_gather(half_rows, 'seed', axis=0, tiled=True)  5.12 us
    reduce_sum x1, other arithmetic, local(): jnp.sum(jnp.square(decoder.astype(jnp.float32)), axis=1) + 1e-06  5.1 us
    gather x1, local copies, waits for them, and re-layouts, local(): sample = jnp.take(gathered, row_order, axis=0)  3.72 us
  transfers between devices with their start and end apart: 16, of which 13 were waited for; matrix products, arithmetic and copies ran while one was open for 7% of the time, Pallas kernels for 0%

profile of v4, /device:TPU:0, one launch (start us, length us, event | category | flops | bytes accessed | tf_op | source)
XLA Modules:
  0.0 142.7 jit_solution(12228044460641383015)
XLA Ops:
  7.2 4.1 %collective-permute-start = (bf16[128,256]{1,0:T(8,128)(2,1)}, bf16[128,256]{1,0:T(8,128)(2,1)S(1)}, u32[]{:S(2)}, u32[]{:S(2)}) collective-permute-start(bf16[128,256]{1,0:T(8,128)(2,1)} %param.11), channel_id=1, source_target_pairs={{0,8},{2,10},{4,12},{6,14},{8,0},{10,2},{12,4},{14,6},{1,9},{3,11}... | collective-permute-start | bytes 196616 | tf_op jit(solution)/shard_map/ppermute | solution.py:17
  11.3 3.9 %collective-permute-done = bf16[128,256]{1,0:T(8,128)(2,1)S(1)} collective-permute-done((bf16[128,256]{1,0:T(8,128)(2,1)}, bf16[128,256]{1,0:T(8,128)(2,1)S(1)}, u32[]{:S(2)}, u32[]{:S(2)}) %collective-permute-start) | collective-permute-done | bytes 65568 | tf_op jit(solution)/shard_map/ppermute | solution.py:17
  17.5 3.6 %collective-permute-done.1 = bf16[2,128,256]{2,1,0:T(8,128)(2,1)S(1)} collective-permute-done((bf16[2,128,256]{2,1,0:T(8,128)(2,1)S(1)}, bf16[2,128,256]{2,1,0:T(8,128)(2,1)S(1)}, u32[]{:S(2)}, u32[]{:S(2)}) %collective-permute-start.1) | collective-permute-done | bytes 131104 | tf_op jit(solution)/shard_map/ppermute | solution.py:17
  21.1 1.8 %collective-permute-start.2 = (bf16[2,2,128,256]{3,2,1,0:T(8,128)(2,1)S(1)}, bf16[2,2,128,256]{3,2,1,0:T(8,128)(2,1)S(1)}, u32[]{:S(2)}, u32[]{:S(2)}) collective-permute-start(bf16[2,2,128,256]{3,2,1,0:T(8,128)(2,1)S(1)} %pad_maximum_fusion), channel_id=1, source_target_pairs={{0,2},{2,0},{4,6},{6,4},{8,10},{10,8},{12,14},{14,12},{1,3},{3,1},... | collective-permute-start | bytes 786440 | tf_op jit(solution)/shard_map/ppermute | solution.py:17
  25.7 1.9 %collective-permute-done.2 = bf16[2,2,128,256]{3,2,1,0:T(8,128)(2,1)S(1)} collective-permute-done((bf16[2,2,128,256]{3,2,1,0:T(8,128)(2,1)S(1)}, bf16[2,2,128,256]{3,2,1,0:T(8,128)(2,1)S(1)}, u32[]{:S(2)}, u32[]{:S(2)}) %collective-permute-start.2) | collective-permute-done | bytes 262176 | tf_op jit(solution)/shard_map/ppermute | solution.py:17
  29.3 5.1 %multiply_reduce_fusion = f32[2048]{0:T(1024)S(1)} fusion(bf16[1,2048,2048]{2,1,0:T(8,128)(2,1)} %param.16), kind=kLoop, calls=%fused_computation.11 | loop fusion | flops 12580864 | bytes 8396800 | tf_op jit(solution)/shard_map/reduce_sum | solution.py:146
  34.4 5.1 %all-gather.2.cloned.1.call-done = bf16[256,2048]{1,0:T(8,128)(2,1)} async-done(((bf16[128,2048]{1,0:T(8,128)(2,1)}), bf16[256,2048]{1,0:T(8,128)(2,1)}) %all-gather.2.cloned.1.call-update) | async-done | bytes 1048592 | tf_op jit(solution)/shard_map/all_gather | solution.py:111
  39.5 3.7 %gather_fusion = bf16[256,2048]{1,0:T(8,128)(2,1)S(1)} fusion(bf16[256,2048]{1,0:T(8,128)(2,1)} %all-gather.2.cloned.1.call-done, s32[1024]{0:T(1024)S(1)} %pad_clamp_fusion.2), kind=kCustom, calls=%fused_computation | custom fusion | bytes 2098176 | tf_op jit(solution)/shard_map/jit(_take)/gather | solution.py:113
  43.5 5.9 %fusion.27 = f32[256,2048]{1,0:T(8,128)S(1)} fusion(bf16[1,2048,2048]{2,1,0:T(8,128)(2,1)} %param.14, f32[2048]{0:T(1024)S(1)} %bitcast.132, bf16[256,2048]{1,0:T(8,128)(2,1)S(1)} %broadcast_select_fusion, f32[2048]{0:T(1024)S(1)} %bitcast.130), kind=kOutput, calls=%fused_computation.27 | convolution fusion | flops 2149580800 | bytes 11550720 | tf_op jit(solution)/shard_map/dot_general | solution.py:119
  49.4 2.3 %fusion.10 = f32[256,2048]{1,0:T(8,128)S(1)} fusion(bf16[1,2048,2048]{2,1,0:T(8,128)(2,1)S(1)} %bitcast.118, f32[256,2048]{1,0:T(8,128)S(1)} %fusion.27), kind=kOutput, calls=%fused_computation.18 | convolution fusion | flops 2148532224 | bytes 12582912 | tf_op jit(solution)/shard_map/dot_general | solution.py:125
  52.0 1.8 %collective-permute-start.9 = (f32[128,1024]{1,0:T(8,128)S(1)}, f32[128,1024]{1,0:T(8,128)S(1)}, u32[]{:S(2)}, u32[]{:S(2)}) collective-permute-start(f32[128,1024]{1,0:T(8,128)S(1)} %constant_dynamic-slice_fusion.2), channel_id=1, source_target_pairs={{0,4},{2,6},{4,0},{6,2},{8,12},{10,14},{12,8},{14,10},{1,5},{3,7},... | collective-permute-start | bytes 1572872 | tf_op jit(solution)/shard_map/ppermute | solution.py:17
  53.8 1.5 %collective-permute-start.3 = (f32[128,1024]{1,0:T(8,128)S(1)}, f32[128,1024]{1,0:T(8,128)S(1)}, u32[]{:S(2)}, u32[]{:S(2)}) collective-permute-start(f32[128,1024]{1,0:T(8,128)S(1)} %constant_dynamic-slice_fusion.9), channel_id=1, source_target_pairs={{0,2},{2,0},{4,6},{6,4},{8,10},{10,8},{12,14},{14,12},{1,3},{3,1},... | collective-permute-start | bytes 1572872 | tf_op jit(solution)/shard_map/ppermute | solution.py:17
  55.5 10.7 %collective-permute-done.9 = f32[128,1024]{1,0:T(8,128)S(1)} collective-permute-done((f32[128,1024]{1,0:T(8,128)S(1)}, f32[128,1024]{1,0:T(8,128)S(1)}, u32[]{:S(2)}, u32[]{:S(2)}) %collective-permute-start.9) | collective-permute-done | bytes 524320 | tf_op jit(solution)/shard_map/ppermute | solution.py:17
  66.3 1.8 %collective-permute-start.10 = (f32[128,512]{1,0:T(8,128)S(1)}, f32[128,512]{1,0:T(8,128)S(1)}, u32[]{:S(2)}, u32[]{:S(2)}) collective-permute-start(f32[128,512]{1,0:T(8,128)S(1)} %constant_dynamic-slice_fusion.1), channel_id=1, source_target_pairs={{0,2},{2,0},{4,6},{6,4},{8,10},{10,8},{12,14},{14,12},{1,3},{3,1},... | collective-permute-start | bytes 786440 | tf_op jit(solution)/shard_map/ppermute | solution.py:17
  68.2 1.6 %collective-permute-start.4 = (f32[128,512]{1,0:T(8,128)S(1)}, f32[128,512]{1,0:T(8,128)S(1)}, u32[]{:S(2)}, u32[]{:S(2)}) collective-permute-start(f32[128,512]{1,0:T(8,128)S(1)} %constant_dynamic-slice_fusion.8), channel_id=1, source_target_pairs={{0,4},{2,6},{4,0},{6,2},{8,12},{10,14},{12,8},{14,10},{1,5},{3,7},... | collective-permute-start | bytes 786440 | tf_op jit(solution)/shard_map/ppermute | solution.py:17
  69.8 4.3 %collective-permute-done.10 = f32[128,512]{1,0:T(8,128)S(1)} collective-permute-done((f32[128,512]{1,0:T(8,128)S(1)}, f32[128,512]{1,0:T(8,128)S(1)}, u32[]{:S(2)}, u32[]{:S(2)}) %collective-permute-start.10) | collective-permute-done | bytes 262176 | tf_op jit(solution)/shard_map/ppermute | solution.py:17
  74.1 2.7 %collective-permute-start.11 = (f32[128,256]{1,0:T(8,128)S(1)}, f32[128,256]{1,0:T(8,128)S(1)}, u32[]{:S(2)}, u32[]{:S(2)}) collective-permute-start(f32[128,256]{1,0:T(8,128)S(1)} %constant_dynamic-slice_fusion), channel_id=1, source_target_pairs={{0,8},{2,10},{4,12},{6,14},{8,0},{10,2},{12,4},{14,6},{1,9},{3,11}... | collective-permute-start | bytes 393224 | tf_op jit(solution)/shard_map/ppermute | solution.py:17
  78.2 7.9 %collective-permute-done.11 = f32[128,256]{1,0:T(8,128)S(1)} collective-permute-done((f32[128,256]{1,0:T(8,128)S(1)}, f32[128,256]{1,0:T(8,128)S(1)}, u32[]{:S(2)}, u32[]{:S(2)}) %collective-permute-start.11) | collective-permute-done | bytes 131104 | tf_op jit(solution)/shard_map/ppermute | solution.py:17
  86.2 2.0 %collective-permute-done.5 = f32[128,256]{1,0:T(8,128)S(1)} collective-permute-done((f32[128,256]{1,0:T(8,128)S(1)}, f32[128,256]{1,0:T(8,128)S(1)}, u32[]{:S(2)}, u32[]{:S(2)}) %collective-permute-start.5) | collective-permute-done | bytes 131104 | tf_op jit(solution)/shard_map/ppermute | solution.py:17
  89.3 3.4 %collective-permute-done.12 = bf16[128,256]{1,0:T(8,128)(2,1)S(1)} collective-permute-done((bf16[128,256]{1,0:T(8,128)(2,1)S(1)}, bf16[128,256]{1,0:T(8,128)(2,1)S(1)}, u32[]{:S(2)}, u32[]{:S(2)}) %collective-permute-start.12) | collective-permute-done | bytes 65568 | tf_op jit(solution)/shard_map/ppermute | solution.py:17
  92.7 1.6 %collective-permute-start.13 = (bf16[2,128,256]{2,1,0:T(8,128)(2,1)S(1)}, bf16[2,128,256]{2,1,0:T(8,128)(2,1)S(1)}, u32[]{:S(2)}, u32[]{:S(2)}) collective-permute-start(bf16[2,128,256]{2,1,0:T(8,128)(2,1)S(1)} %pad_maximum_fusion.5), channel_id=1, source_target_pairs={{0,2},{2,0},{4,6},{6,4},{8,10},{10,8},{12,14},{14,12},{1,3},{3,1},... | collective-permute-start | bytes 393224 | tf_op jit(solution)/shard_map/ppermute | solution.py:17
  94.4 1.9 %collective-permute-start.7 = (bf16[2,128,256]{2,1,0:T(8,128)(2,1)S(1)}, bf16[2,128,256]{2,1,0:T(8,128)(2,1)S(1)}, u32[]{:S(2)}, u32[]{:S(2)}) collective-permute-start(bf16[2,128,256]{2,1,0:T(8,128)(2,1)S(1)} %pad_maximum_fusion.4), channel_id=1, source_target_pairs={{0,4},{2,6},{4,0},{6,2},{8,12},{10,14},{12,8},{14,10},{1,5},{3,7},... | collective-permute-start | bytes 393224 | tf_op jit(solution)/shard_map/ppermute | solution.py:17
  101.3 3.8 %collective-permute-done.14 = bf16[2,2,128,256]{3,2,1,0:T(8,128)(2,1)S(1)} collective-permute-done((bf16[2,2,128,256]{3,2,1,0:T(8,128)(2,1)S(1)}, bf16[2,2,128,256]{3,2,1,0:T(8,128)(2,1)S(1)}, u32[]{:S(2)}, u32[]{:S(2)}) %collective-permute-start.14) | collective-permute-done | bytes 262176 | tf_op jit(solution)/shard_map/ppermute | solution.py:17
  108.6 27.3 %fusion.6 = (bf16[1,2048,2048]{2,1,0:T(8,128)(2,1)}, bf16[1,2048,2048]{2,1,0:T(8,128)(2,1)}, bf16[1,2048,2048]{2,1,0:T(8,128)(2,1)}) fusion(bf16[1,2048,2048]{2,1,0:T(8,128)(2,1)} %param.19, bf16[1,2048,2048]{2,1,0:T(8,128)(2,1)} %param.18, bf16[1,2048,2048]{2,1,0:T(8,128)(2,1)} %param.14, bf16[256,2048]{1,0:T(8,128)(2,1)S(1)} %broadcast_select_fusion, ...), kind=kOutput, calls=%fused_computation.14 | convolution fusion | flops 4387766272 | bytes 62930944 | tf_op jit(solution)/shard_map/dot_general | solution.py:151
  (74 shorter events, 18.6 us)
Async XLA Ops:
  7.2 32.4 %all-gather.2.cloned.1.call-start = ((), (), s32[]{:S(2)}) async-start(), calls=%async_computation | async-start | bytes 1572864 | tf_op jit(solution)/shard_map/all_gather | solution.py:111
  7.2 8.0 %collective-permute-start = (bf16[128,256]{1,0:T(8,128)(2,1)}, bf16[128,256]{1,0:T(8,128)(2,1)S(1)}, u32[]{:S(2)}, u32[]{:S(2)}) collective-permute-start(bf16[128,256]{1,0:T(8,128)(2,1)} %param.11), channel_id=1, source_target_pairs={{0,8},{2,10},{4,12},{6,14},{8,0},{10,2},{12,4},{14,6},{1,9},{3,11}... | collective-permute-start | bytes 196616 | tf_op jit(solution)/shard_map/ppermute | solution.py:17
  16.1 5.0 %collective-permute-start.1 = (bf16[2,128,256]{2,1,0:T(8,128)(2,1)S(1)}, bf16[2,128,256]{2,1,0:T(8,128)(2,1)S(1)}, u32[]{:S(2)}, u32[]{:S(2)}) collective-permute-start(bf16[2,128,256]{2,1,0:T(8,128)(2,1)S(1)} %pad_maximum_fusion.3), channel_id=1, source_target_pairs={{0,4},{2,6},{4,0},{6,2},{8,12},{10,14},{12,8},{14,10},{1,5},{3,7},... | collective-permute-start | bytes 393224 | tf_op jit(solution)/shard_map/ppermute | solution.py:17
  21.1 6.4 %collective-permute-start.2 = (bf16[2,2,128,256]{3,2,1,0:T(8,128)(2,1)S(1)}, bf16[2,2,128,256]{3,2,1,0:T(8,128)(2,1)S(1)}, u32[]{:S(2)}, u32[]{:S(2)}) collective-permute-start(bf16[2,2,128,256]{3,2,1,0:T(8,128)(2,1)S(1)} %pad_maximum_fusion), channel_id=1, source_target_pairs={{0,2},{2,0},{4,6},{6,4},{8,10},{10,8},{12,14},{14,12},{1,3},{3,1},... | collective-permute-start | bytes 786440 | tf_op jit(solution)/shard_map/ppermute | solution.py:17
  29.3 14.2 %copy-start = (f32[1,2048]{1,0:T(1,128)S(1)}, f32[1,2048]{1,0:T(1,128)}, u32[]{:S(2)}) copy-start(f32[1,2048]{1,0:T(1,128)} %param.17) | copy-start | bytes 24580
  29.3 14.2 %copy-start.1 = (f32[1,2048]{1,0:T(1,128)S(1)}, f32[1,2048]{1,0:T(1,128)}, u32[]{:S(2)}) copy-start(f32[1,2048]{1,0:T(1,128)} %param.15) | copy-start | bytes 24580
  43.3 6.1 %slice-start = ((s8[8388608]{0:T(1024)(128)(4,1)}), s8[4194304]{0:T(1024)(128)(4,1)S(1)}, s32[]{:S(2)}) async-start(s8[8388608]{0:T(1024)(128)(4,1)} %bitcast.117), calls=%async_computation.1 | async-start | bytes 8388608
  43.5 5.9 %slice-start.1 = ((s8[8388608]{0:T(1024)(128)(4,1)}), s8[4194304]{0:T(1024)(128)(4,1)S(1)}, s32[]{:S(2)}) async-start(s8[8388608]{0:T(1024)(128)(4,1)} %bitcast.117), calls=%async_computation.2 | async-start | bytes 8388608
  49.4 2.3 %copy-start.2 = (f32[256,2048]{1,0:T(8,128)}, f32[256,2048]{1,0:T(8,128)S(1)}, u32[]{:S(2)}) copy-start(f32[256,2048]{1,0:T(8,128)S(1)} %fusion.27) | copy-start | bytes 6291460
  52.0 14.2 %collective-permute-start.9 = (f32[128,1024]{1,0:T(8,128)S(1)}, f32[128,1024]{1,0:T(8,128)S(1)}, u32[]{:S(2)}, u32[]{:S(2)}) collective-permute-start(f32[128,1024]{1,0:T(8,128)S(1)} %constant_dynamic-slice_fusion.2), channel_id=1, source_target_pairs={{0,4},{2,6},{4,0},{6,2},{8,12},{10,14},{12,8},{14,10},{1,5},{3,7},... | collective-permute-start | bytes 1572872 | tf_op jit(solution)/shard_map/ppermute | solution.py:17
  53.8 14.3 %collective-permute-start.3 = (f32[128,1024]{1,0:T(8,128)S(1)}, f32[128,1024]{1,0:T(8,128)S(1)}, u32[]{:S(2)}, u32[]{:S(2)}) collective-permute-start(f32[128,1024]{1,0:T(8,128)S(1)} %constant_dynamic-slice_fusion.9), channel_id=1, source_target_pairs={{0,2},{2,0},{4,6},{6,4},{8,10},{10,8},{12,14},{14,12},{1,3},{3,1},... | collective-permute-start | bytes 1572872 | tf_op jit(solution)/shard_map/ppermute | solution.py:17
  66.3 7.8 %collective-permute-start.10 = (f32[128,512]{1,0:T(8,128)S(1)}, f32[128,512]{1,0:T(8,128)S(1)}, u32[]{:S(2)}, u32[]{:S(2)}) collective-permute-start(f32[128,512]{1,0:T(8,128)S(1)} %constant_dynamic-slice_fusion.1), channel_id=1, source_target_pairs={{0,2},{2,0},{4,6},{6,4},{8,10},{10,8},{12,14},{14,12},{1,3},{3,1},... | collective-permute-start | bytes 786440 | tf_op jit(solution)/shard_map/ppermute | solution.py:17
  68.2 8.7 %collective-permute-start.4 = (f32[128,512]{1,0:T(8,128)S(1)}, f32[128,512]{1,0:T(8,128)S(1)}, u32[]{:S(2)}, u32[]{:S(2)}) collective-permute-start(f32[128,512]{1,0:T(8,128)S(1)} %constant_dynamic-slice_fusion.8), channel_id=1, source_target_pairs={{0,4},{2,6},{4,0},{6,2},{8,12},{10,14},{12,8},{14,10},{1,5},{3,7},... | collective-permute-start | bytes 786440 | tf_op jit(solution)/shard_map/ppermute | solution.py:17
  74.1 12.0 %collective-permute-start.11 = (f32[128,256]{1,0:T(8,128)S(1)}, f32[128,256]{1,0:T(8,128)S(1)}, u32[]{:S(2)}, u32[]{:S(2)}) collective-permute-start(f32[128,256]{1,0:T(8,128)S(1)} %constant_dynamic-slice_fusion), channel_id=1, source_target_pairs={{0,8},{2,10},{4,12},{6,14},{8,0},{10,2},{12,4},{14,6},{1,9},{3,11}... | collective-permute-start | bytes 393224 | tf_op jit(solution)/shard_map/ppermute | solution.py:17
  76.9 11.3 %collective-permute-start.5 = (f32[128,256]{1,0:T(8,128)S(1)}, f32[128,256]{1,0:T(8,128)S(1)}, u32[]{:S(2)}, u32[]{:S(2)}) collective-permute-start(f32[128,256]{1,0:T(8,128)S(1)} %constant_dynamic-slice_fusion.7), channel_id=1, source_target_pairs={{0,8},{2,10},{4,12},{6,14},{8,0},{10,2},{12,4},{14,6},{1,9},{3,11}... | collective-permute-start | bytes 393224 | tf_op jit(solution)/shard_map/ppermute | solution.py:17
  86.2 6.5 %collective-permute-start.12 = (bf16[128,256]{1,0:T(8,128)(2,1)S(1)}, bf16[128,256]{1,0:T(8,128)(2,1)S(1)}, u32[]{:S(2)}, u32[]{:S(2)}) collective-permute-start(bf16[128,256]{1,0:T(8,128)(2,1)S(1)} %multiply_convert_fusion), channel_id=1, source_target_pairs={{0,8},{2,10},{4,12},{6,14},{8,0},{10,2},{12,4},{14,6},{1,9},{3,11}... | collective-permute-start | bytes 196616 | tf_op jit(solution)/shard_map/ppermute | solution.py:17
  88.3 6.0 %collective-permute-start.6 = (bf16[128,256]{1,0:T(8,128)(2,1)S(1)}, bf16[128,256]{1,0:T(8,128)(2,1)S(1)}, u32[]{:S(2)}, u32[]{:S(2)}) collective-permute-start(bf16[128,256]{1,0:T(8,128)(2,1)S(1)} %multiply_convert_fusion.1), channel_id=1, source_target_pairs={{0,8},{2,10},{4,12},{6,14},{8,0},{10,2},{12,4},{14,6},{1,9},{3,11}... | collective-permute-start | bytes 196616 | tf_op jit(solution)/shard_map/ppermute | solution.py:17
  92.7 5.0 %collective-permute-start.13 = (bf16[2,128,256]{2,1,0:T(8,128)(2,1)S(1)}, bf16[2,128,256]{2,1,0:T(8,128)(2,1)S(1)}, u32[]{:S(2)}, u32[]{:S(2)}) collective-permute-start(bf16[2,128,256]{2,1,0:T(8,128)(2,1)S(1)} %pad_maximum_fusion.5), channel_id=1, source_target_pairs={{0,2},{2,0},{4,6},{6,4},{8,10},{10,8},{12,14},{14,12},{1,3},{3,1},... | collective-permute-start | bytes 393224 | tf_op jit(solution)/shard_map/ppermute | solution.py:17
  94.4 5.6 %collective-permute-start.7 = (bf16[2,128,256]{2,1,0:T(8,128)(2,1)S(1)}, bf16[2,128,256]{2,1,0:T(8,128)(2,1)S(1)}, u32[]{:S(2)}, u32[]{:S(2)}) collective-permute-start(bf16[2,128,256]{2,1,0:T(8,128)(2,1)S(1)} %pad_maximum_fusion.4), channel_id=1, source_target_pairs={{0,4},{2,6},{4,0},{6,2},{8,12},{10,14},{12,8},{14,10},{1,5},{3,7},... | collective-permute-start | bytes 393224 | tf_op jit(solution)/shard_map/ppermute | solution.py:17
  97.8 7.2 %collective-permute-start.14 = (bf16[2,2,128,256]{3,2,1,0:T(8,128)(2,1)S(1)}, bf16[2,2,128,256]{3,2,1,0:T(8,128)(2,1)S(1)}, u32[]{:S(2)}, u32[]{:S(2)}) collective-permute-start(bf16[2,2,128,256]{3,2,1,0:T(8,128)(2,1)S(1)} %pad_maximum_fusion.2), channel_id=1, source_target_pairs={{0,4},{2,6},{4,0},{6,2},{8,12},{10,14},{12,8},{14,10},{1,5},{3,7},... | collective-permute-start | bytes 786440 | tf_op jit(solution)/shard_map/ppermute | solution.py:17
  100.1 6.4 %collective-permute-start.8 = (bf16[2,2,128,256]{3,2,1,0:T(8,128)(2,1)S(1)}, bf16[2,2,128,256]{3,2,1,0:T(8,128)(2,1)S(1)}, u32[]{:S(2)}, u32[]{:S(2)}) collective-permute-start(bf16[2,2,128,256]{3,2,1,0:T(8,128)(2,1)S(1)} %pad_maximum_fusion.1), channel_id=1, source_target_pairs={{0,2},{2,0},{4,6},{6,4},{8,10},{10,8},{12,14},{14,12},{1,3},{3,1},... | collective-permute-start | bytes 786440 | tf_op jit(solution)/shard_map/ppermute | solution.py:17
Sparse Core Ops, SparseCore 0:
  28.7 10.7 all-gather.1

commit v5 on v4

--- a/solution.py
+++ b/solution.py
@@ -46,6 +46,16 @@
     want = sorted(bits, reverse=True)
     cur = jnp.transpose(cur, [bits.index(b) for b in want] + list(range(len(bits), cur.ndim)))
     return cur.reshape((size,) + value.shape)
+
+
+def _direct_gather(value, axis, size):
+    me = lax.axis_index(axis)
+    parts = [value] + [
+        lax.ppermute(value, axis, [(i, (i + k) % size) for i in range(size)])
+        for k in range(1, size)
+    ]
+    stacked = jnp.stack(parts, axis=0)
+    return jnp.take(stacked, (me - jnp.arange(size)) % size, axis=0)
 
 
 def _orders(size):
@@ -106,9 +116,17 @@
 ):
     lat_size = LAT_SIZE[0]
     first, second = _orders(lat_size)
-    act_blocks = _doubling_gather(activations, "lat", lat_size, first[::-1])
+    if lat_size <= 8:
+        act_blocks = _direct_gather(activations, "lat", lat_size)
+    else:
+        act_blocks = _doubling_gather(activations, "lat", lat_size, first[::-1])
     half_rows = jnp.transpose(act_blocks, (1, 0, 2)).reshape(activations.shape[0], -1)
-    gathered = lax.all_gather(half_rows, "seed", axis=0, tiled=True)
+    other_rows = lax.ppermute(half_rows, "seed", [(0, 1), (1, 0)])
+    seed_first = lax.axis_index("seed") == 0
+    gathered = jnp.concatenate(
+        [jnp.where(seed_first, half_rows, other_rows), jnp.where(seed_first, other_rows, half_rows)],
+        axis=0,
+    )
     row_order = bag_rows[0]
     sample = jnp.take(gathered, row_order, axis=0)
     weight_in = enc_weight[0]

time: 143 us -> 124 us (0.87)
  between operations: 14.4 us -> 1.24 us
  other arithmetic: 10.4 us -> 7.68 us
  local copies, waits for them, and re-layouts: 7.75 us -> 5.33 us
  starting transfers between devices: 24.6 us -> 22.4 us
    ppermute x15 -> x12, starting transfers between devices: 24.6 us -> 8.04 us  [_pair_swap(): return lax.ppermute(value, axis, [(i, i ^ mask) for i in range(size)])]
    ppermute x0 -> x8, starting transfers between devices: none -> 14.4 us  [the longest x7 14.3 us: _direct_gather(): lax.ppermute(value, axis, [(i, (i + k) % size) for i in range(size)])]
    ppermute x0 -> x8, waiting for transfers between devices: none -> 6 us  [the longest x7 4.18 us: _direct_gather(): lax.ppermute(value, axis, [(i, (i + k) % size) for i in range(size)])]
    all_gather x1 -> x0, waiting for transfers between devices: 5.12 us -> none  [local(): gathered = lax.all_gather(half_rows, 'seed', axis=0, tiled=True)]
    gather x1, local copies, waits for them, and re-layouts: 3.72 us -> 1.36 us  [local(): sample = jnp.take(gathered, row_order, axis=0)]
    ppermute x15 -> x12, waiting for transfers between devices: 44.9 us -> 45.2 us  [_pair_swap(): return lax.ppermute(value, axis, [(i, i ^ mask) for i in range(size)])]
  transfers between devices with their start and end apart: 16 -> 20, of which waited for: 13 -> 12; matrix products, arithmetic and copies ran while one was open for 7% -> 7% of each run, Pallas kernels for 0% -> 0%
where the time goes in v5:
time: 124 us; the launch traced here: 123 us
  waiting for transfers between devices  51.2 us (41%)
  matrix products  35.5 us (29%)
  starting transfers between devices  22.4 us (18%)
  other arithmetic  7.68 us (6%)
  local copies, waits for them, and re-layouts  5.33 us (4%)
  between operations  1.24 us (1%)
    ppermute x12, waiting for transfers between devices, _pair_swap(): return lax.ppermute(value, axis, [(i, i ^ mask) for i in range(size)])  45.2 us
    dot_general x1, matrix products, local(): grad = jnp.dot(d_pre_t, centered, preferred_element_type=jnp.float32)  27.3 us
    ppermute x7, starting transfers between devices, _direct_gather(): lax.ppermute(value, axis, [(i, (i + k) % size) for i in range(size)])  14.3 us
    ppermute x12, starting transfers between devices, _pair_swap(): return lax.ppermute(value, axis, [(i, i ^ mask) for i in range(size)])  8.04 us
    dot_general x1, matrix products, local(): lax.dot_general(weight_in, centered, (((1,), (1,)), ((), ())), preferred_...  5.9 us
    reduce_sum x1, other arithmetic, local(): jnp.sum(jnp.square(decoder.astype(jnp.float32)), axis=1) + 1e-06  5.08 us
    ppermute x7, waiting for transfers between devices, _direct_gather(): lax.ppermute(value, axis, [(i, (i + k) % size) for i in range(size)])  4.18 us
  transfers between devices with their start and end apart: 20, of which 12 were waited for; matrix products, arithmetic and copies ran while one was open for 7% of the time, Pallas kernels for 0%

profile of v5, /device:TPU:0, one launch (start us, length us, event | category | flops | bytes accessed | tf_op | source)
XLA Modules:
  0.0 123.4 jit_solution(1096688105059293116)
XLA Ops:
  0.7 5.0 %collective-permute-start.4 = (bf16[128,256]{1,0:T(8,128)(2,1)}, bf16[128,256]{1,0:T(8,128)(2,1)S(1)}, u32[]{:S(2)}, u32[]{:S(2)}) collective-permute-start(bf16[128,256]{1,0:T(8,128)(2,1)} %param.11), channel_id=1, source_target_pairs={{0,10},{2,12},{4,14},{6,0},{8,2},{10,4},{12,6},{14,8},{1,11},{3,13... | collective-permute-start | bytes 196616 | tf_op jit(solution)/shard_map/ppermute | solution.py:54
  6.0 1.7 %collective-permute-start.2 = (bf16[128,256]{1,0:T(8,128)(2,1)}, bf16[128,256]{1,0:T(8,128)(2,1)S(1)}, u32[]{:S(2)}, u32[]{:S(2)}) collective-permute-start(bf16[128,256]{1,0:T(8,128)(2,1)} %param.11), channel_id=1, source_target_pairs={{0,6},{2,8},{4,10},{6,12},{8,14},{10,0},{12,2},{14,4},{1,7},{3,9},... | collective-permute-start | bytes 196616 | tf_op jit(solution)/shard_map/ppermute | solution.py:54
  7.7 2.5 %collective-permute-start.1 = (bf16[128,256]{1,0:T(8,128)(2,1)}, bf16[128,256]{1,0:T(8,128)(2,1)S(1)}, u32[]{:S(2)}, u32[]{:S(2)}) collective-permute-start(bf16[128,256]{1,0:T(8,128)(2,1)} %param.11), channel_id=1, source_target_pairs={{0,4},{2,6},{4,8},{6,10},{8,12},{10,14},{12,0},{14,2},{1,5},{3,7},... | collective-permute-start | bytes 196616 | tf_op jit(solution)/shard_map/ppermute | solution.py:54
  10.2 1.5 %collective-permute-start = (bf16[128,256]{1,0:T(8,128)(2,1)}, bf16[128,256]{1,0:T(8,128)(2,1)S(1)}, u32[]{:S(2)}, u32[]{:S(2)}) collective-permute-start(bf16[128,256]{1,0:T(8,128)(2,1)} %param.11), channel_id=1, source_target_pairs={{0,2},{2,4},{4,6},{6,8},{8,10},{10,12},{12,14},{14,0},{1,3},{3,5},... | collective-permute-start | bytes 196616 | tf_op jit(solution)/shard_map/ppermute | solution.py:54
  14.0 5.1 %multiply_reduce_fusion = f32[2048]{0:T(1024)S(1)} fusion(bf16[1,2048,2048]{2,1,0:T(8,128)(2,1)} %param.16), kind=kLoop, calls=%fused_computation.12 | loop fusion | flops 12580864 | bytes 8396800 | tf_op jit(solution)/shard_map/reduce_sum | solution.py:164
  19.1 3.3 %collective-permute-start.6 = (bf16[128,256]{1,0:T(8,128)(2,1)S(1)}, bf16[128,256]{1,0:T(8,128)(2,1)S(1)}, u32[]{:S(2)}, u32[]{:S(2)}) collective-permute-start(bf16[128,256]{1,0:T(8,128)(2,1)S(1)} %copy-done), channel_id=1, source_target_pairs={{0,14},{2,0},{4,2},{6,4},{8,6},{10,8},{12,10},{14,12},{1,15},{3,1}... | collective-permute-start | bytes 196616 | tf_op jit(solution)/shard_map/ppermute | solution.py:54
  22.6 4.2 %collective-permute-done.5 = bf16[128,256]{1,0:T(8,128)(2,1)S(1)} collective-permute-done((bf16[128,256]{1,0:T(8,128)(2,1)S(1)}, bf16[128,256]{1,0:T(8,128)(2,1)S(1)}, u32[]{:S(2)}, u32[]{:S(2)}) %collective-permute-start.5) | collective-permute-done | bytes 65568 | tf_op jit(solution)/shard_map/ppermute | solution.py:54
  27.7 1.8 %collective-permute-done.7 = bf16[128,2048]{1,0:T(8,128)(2,1)S(1)} collective-permute-done((bf16[128,2048]{1,0:T(8,128)(2,1)S(1)}, bf16[128,2048]{1,0:T(8,128)(2,1)S(1)}, u32[]{:S(2)}, u32[]{:S(2)}) %collective-permute-start.7) | collective-permute-done | bytes 524320 | tf_op jit(solution)/shard_map/ppermute | solution.py:124
  29.7 1.4 %gather_fusion.1 = bf16[256,2048]{1,0:T(8,128)(2,1)S(1)} fusion(bf16[256,2048]{1,0:T(8,128)(2,1)S(1)} %pad_maximum_fusion, s32[1024]{0:T(1024)S(1)} %pad_clamp_fusion.2), kind=kCustom, calls=%fused_computation.1 | custom fusion | bytes 2098176 | tf_op jit(solution)/shard_map/jit(_take)/gather | solution.py:131
  31.2 5.9 %fusion.27 = f32[256,2048]{1,0:T(8,128)S(1)} fusion(bf16[1,2048,2048]{2,1,0:T(8,128)(2,1)} %param.14, f32[2048]{0:T(1024)S(1)} %bitcast.135, bf16[256,2048]{1,0:T(8,128)(2,1)S(1)} %broadcast_select_fusion, f32[2048]{0:T(1024)S(1)} %bitcast.133), kind=kOutput, calls=%fused_computation.28 | convolution fusion | flops 2149580800 | bytes 11550720 | tf_op jit(solution)/shard_map/dot_general | solution.py:137
  37.2 2.3 %fusion.10 = f32[256,2048]{1,0:T(8,128)S(1)} fusion(bf16[1,2048,2048]{2,1,0:T(8,128)(2,1)S(1)} %bitcast.121, f32[256,2048]{1,0:T(8,128)S(1)} %fusion.27), kind=kOutput, calls=%fused_computation.19 | convolution fusion | flops 2148532224 | bytes 12582912 | tf_op jit(solution)/shard_map/dot_general | solution.py:143
  40.0 13.7 %collective-permute-done.14 = f32[128,1024]{1,0:T(8,128)S(1)} collective-permute-done((f32[128,1024]{1,0:T(8,128)S(1)}, f32[128,1024]{1,0:T(8,128)S(1)}, u32[]{:S(2)}, u32[]{:S(2)}) %collective-permute-start.14) | collective-permute-done | bytes 524320 | tf_op jit(solution)/shard_map/ppermute | solution.py:17
  54.1 1.7 %collective-permute-start.9 = (f32[128,512]{1,0:T(8,128)S(1)}, f32[128,512]{1,0:T(8,128)S(1)}, u32[]{:S(2)}, u32[]{:S(2)}) collective-permute-start(f32[128,512]{1,0:T(8,128)S(1)} %constant_dynamic-slice_fusion.8), channel_id=1, source_target_pairs={{0,4},{2,6},{4,0},{6,2},{8,12},{10,14},{12,8},{14,10},{1,5},{3,7},... | collective-permute-start | bytes 786440 | tf_op jit(solution)/shard_map/ppermute | solution.py:17
  55.8 5.7 %collective-permute-done.15 = f32[128,512]{1,0:T(8,128)S(1)} collective-permute-done((f32[128,512]{1,0:T(8,128)S(1)}, f32[128,512]{1,0:T(8,128)S(1)}, u32[]{:S(2)}, u32[]{:S(2)}) %collective-permute-start.15) | collective-permute-done | bytes 262176 | tf_op jit(solution)/shard_map/ppermute | solution.py:17
  61.5 1.6 %collective-permute-start.16 = (f32[128,256]{1,0:T(8,128)S(1)}, f32[128,256]{1,0:T(8,128)S(1)}, u32[]{:S(2)}, u32[]{:S(2)}) collective-permute-start(f32[128,256]{1,0:T(8,128)S(1)} %constant_dynamic-slice_fusion.1), channel_id=1, source_target_pairs={{0,8},{2,10},{4,12},{6,14},{8,0},{10,2},{12,4},{14,6},{1,9},{3,11}... | collective-permute-start | bytes 393224 | tf_op jit(solution)/shard_map/ppermute | solution.py:17
  63.2 1.4 %collective-permute-start.10 = (f32[128,256]{1,0:T(8,128)S(1)}, f32[128,256]{1,0:T(8,128)S(1)}, u32[]{:S(2)}, u32[]{:S(2)}) collective-permute-start(f32[128,256]{1,0:T(8,128)S(1)} %constant_dynamic-slice_fusion.7), channel_id=1, source_target_pairs={{0,8},{2,10},{4,12},{6,14},{8,0},{10,2},{12,4},{14,6},{1,9},{3,11}... | collective-permute-start | bytes 393224 | tf_op jit(solution)/shard_map/ppermute | solution.py:17
  64.7 8.2 %collective-permute-done.16 = f32[128,256]{1,0:T(8,128)S(1)} collective-permute-done((f32[128,256]{1,0:T(8,128)S(1)}, f32[128,256]{1,0:T(8,128)S(1)}, u32[]{:S(2)}, u32[]{:S(2)}) %collective-permute-start.16) | collective-permute-done | bytes 131104 | tf_op jit(solution)/shard_map/ppermute | solution.py:17
  73.0 1.7 %collective-permute-done.10 = f32[128,256]{1,0:T(8,128)S(1)} collective-permute-done((f32[128,256]{1,0:T(8,128)S(1)}, f32[128,256]{1,0:T(8,128)S(1)}, u32[]{:S(2)}, u32[]{:S(2)}) %collective-permute-start.10) | collective-permute-done | bytes 131104 | tf_op jit(solution)/shard_map/ppermute | solution.py:17
  76.0 3.5 %collective-permute-done.17 = bf16[128,256]{1,0:T(8,128)(2,1)S(1)} collective-permute-done((bf16[128,256]{1,0:T(8,128)(2,1)S(1)}, bf16[128,256]{1,0:T(8,128)(2,1)S(1)}, u32[]{:S(2)}, u32[]{:S(2)}) %collective-permute-start.17) | collective-permute-done | bytes 65568 | tf_op jit(solution)/shard_map/ppermute | solution.py:17
  81.2 3.3 %collective-permute-done.18 = bf16[2,128,256]{2,1,0:T(8,128)(2,1)S(1)} collective-permute-done((bf16[2,128,256]{2,1,0:T(8,128)(2,1)S(1)}, bf16[2,128,256]{2,1,0:T(8,128)(2,1)S(1)}, u32[]{:S(2)}, u32[]{:S(2)}) %collective-permute-start.18) | collective-permute-done | bytes 131104 | tf_op jit(solution)/shard_map/ppermute | solution.py:17
  84.7 2.8 %collective-permute-done.12 = bf16[2,128,256]{2,1,0:T(8,128)(2,1)S(1)} collective-permute-done((bf16[2,128,256]{2,1,0:T(8,128)(2,1)S(1)}, bf16[2,128,256]{2,1,0:T(8,128)(2,1)S(1)}, u32[]{:S(2)}, u32[]{:S(2)}) %collective-permute-start.12) | collective-permute-done | bytes 131104 | tf_op jit(solution)/shard_map/ppermute | solution.py:17
  88.3 2.8 %collective-permute-done.19 = bf16[2,2,128,256]{3,2,1,0:T(8,128)(2,1)S(1)} collective-permute-done((bf16[2,2,128,256]{3,2,1,0:T(8,128)(2,1)S(1)}, bf16[2,2,128,256]{3,2,1,0:T(8,128)(2,1)S(1)}, u32[]{:S(2)}, u32[]{:S(2)}) %collective-permute-start.19) | collective-permute-done | bytes 262176 | tf_op jit(solution)/shard_map/ppermute | solution.py:17
  91.2 2.8 %collective-permute-done.13 = bf16[2,2,128,256]{3,2,1,0:T(8,128)(2,1)S(1)} collective-permute-done((bf16[2,2,128,256]{3,2,1,0:T(8,128)(2,1)S(1)}, bf16[2,2,128,256]{3,2,1,0:T(8,128)(2,1)S(1)}, u32[]{:S(2)}, u32[]{:S(2)}) %collective-permute-start.13) | collective-permute-done | bytes 262176 | tf_op jit(solution)/shard_map/ppermute | solution.py:17
  96.1 27.3 %fusion.6 = (bf16[1,2048,2048]{2,1,0:T(8,128)(2,1)}, bf16[1,2048,2048]{2,1,0:T(8,128)(2,1)}, bf16[1,2048,2048]{2,1,0:T(8,128)(2,1)}) fusion(bf16[1,2048,2048]{2,1,0:T(8,128)(2,1)} %param.19, bf16[1,2048,2048]{2,1,0:T(8,128)(2,1)} %param.18, bf16[1,2048,2048]{2,1,0:T(8,128)(2,1)} %param.14, bf16[256,2048]{1,0:T(8,128)(2,1)S(1)} %broadcast_select_fusion, ...), kind=kOutput, calls=%fused_computation.15 | convolution fusion | flops 4387766272 | bytes 62930944 | tf_op jit(solution)/shard_map/dot_general | solution.py:169
  (96 shorter events, 11.1 us)
Async XLA Ops:
  0.6 18.4 %copy-start.2 = (s32[8]{0:T(128)S(1)}, s32[8]{0:T(128)}, u32[]{:S(2)}) copy-start(s32[8]{0:T(128)} %constant.123) | copy-start | bytes 100
  0.7 18.4 %copy-start = (bf16[128,256]{1,0:T(8,128)(2,1)S(1)}, bf16[128,256]{1,0:T(8,128)(2,1)}, u32[]{:S(2)}) copy-start(bf16[128,256]{1,0:T(8,128)(2,1)} %param.11) | copy-start | bytes 196612
  0.7 27.0 %copy-start.1 = (s32[1,256]{1,0:T(1,128)S(1)}, s32[1,256]{1,0:T(1,128)}, u32[]{:S(2)}) copy-start(s32[1,256]{1,0:T(1,128)} %param.12) | copy-start | bytes 3076
  0.7 26.9 %copy-start.4 = (f32[1,2048]{1,0:T(1,128)S(1)}, f32[1,2048]{1,0:T(1,128)}, u32[]{:S(2)}) copy-start(f32[1,2048]{1,0:T(1,128)} %param.17) | copy-start | bytes 24580
  0.7 21.8 %collective-permute-start.4 = (bf16[128,256]{1,0:T(8,128)(2,1)}, bf16[128,256]{1,0:T(8,128)(2,1)S(1)}, u32[]{:S(2)}, u32[]{:S(2)}) collective-permute-start(bf16[128,256]{1,0:T(8,128)(2,1)} %param.11), channel_id=1, source_target_pairs={{0,10},{2,12},{4,14},{6,0},{8,2},{10,4},{12,6},{14,8},{1,11},{3,13... | collective-permute-start | bytes 196616 | tf_op jit(solution)/shard_map/ppermute | solution.py:54
  5.7 16.8 %collective-permute-start.3 = (bf16[128,256]{1,0:T(8,128)(2,1)}, bf16[128,256]{1,0:T(8,128)(2,1)S(1)}, u32[]{:S(2)}, u32[]{:S(2)}) collective-permute-start(bf16[128,256]{1,0:T(8,128)(2,1)} %param.11), channel_id=1, source_target_pairs={{0,8},{2,10},{4,12},{6,14},{8,0},{10,2},{12,4},{14,6},{1,9},{3,11}... | collective-permute-start | bytes 196616 | tf_op jit(solution)/shard_map/ppermute | solution.py:54
  6.0 16.4 %collective-permute-start.2 = (bf16[128,256]{1,0:T(8,128)(2,1)}, bf16[128,256]{1,0:T(8,128)(2,1)S(1)}, u32[]{:S(2)}, u32[]{:S(2)}) collective-permute-start(bf16[128,256]{1,0:T(8,128)(2,1)} %param.11), channel_id=1, source_target_pairs={{0,6},{2,8},{4,10},{6,12},{8,14},{10,0},{12,2},{14,4},{1,7},{3,9},... | collective-permute-start | bytes 196616 | tf_op jit(solution)/shard_map/ppermute | solution.py:54
  7.7 14.7 %collective-permute-start.1 = (bf16[128,256]{1,0:T(8,128)(2,1)}, bf16[128,256]{1,0:T(8,128)(2,1)S(1)}, u32[]{:S(2)}, u32[]{:S(2)}) collective-permute-start(bf16[128,256]{1,0:T(8,128)(2,1)} %param.11), channel_id=1, source_target_pairs={{0,4},{2,6},{4,8},{6,10},{8,12},{10,14},{12,0},{14,2},{1,5},{3,7},... | collective-permute-start | bytes 196616 | tf_op jit(solution)/shard_map/ppermute | solution.py:54
  10.2 8.9 %collective-permute-start = (bf16[128,256]{1,0:T(8,128)(2,1)}, bf16[128,256]{1,0:T(8,128)(2,1)S(1)}, u32[]{:S(2)}, u32[]{:S(2)}) collective-permute-start(bf16[128,256]{1,0:T(8,128)(2,1)} %param.11), channel_id=1, source_target_pairs={{0,2},{2,4},{4,6},{6,8},{8,10},{10,12},{12,14},{14,0},{1,3},{3,5},... | collective-permute-start | bytes 196616 | tf_op jit(solution)/shard_map/ppermute | solution.py:54
  19.1 7.6 %collective-permute-start.6 = (bf16[128,256]{1,0:T(8,128)(2,1)S(1)}, bf16[128,256]{1,0:T(8,128)(2,1)S(1)}, u32[]{:S(2)}, u32[]{:S(2)}) collective-permute-start(bf16[128,256]{1,0:T(8,128)(2,1)S(1)} %copy-done), channel_id=1, source_target_pairs={{0,14},{2,0},{4,2},{6,4},{8,6},{10,8},{12,10},{14,12},{1,15},{3,1}... | collective-permute-start | bytes 196616 | tf_op jit(solution)/shard_map/ppermute | solution.py:54
  22.4 4.3 %collective-permute-start.5 = (bf16[128,256]{1,0:T(8,128)(2,1)S(1)}, bf16[128,256]{1,0:T(8,128)(2,1)S(1)}, u32[]{:S(2)}, u32[]{:S(2)}) collective-permute-start(bf16[128,256]{1,0:T(8,128)(2,1)S(1)} %copy-done), channel_id=1, source_target_pairs={{0,12},{2,14},{4,0},{6,2},{8,4},{10,6},{12,8},{14,10},{1,13},{3,15... | collective-permute-start | bytes 196616 | tf_op jit(solution)/shard_map/ppermute | solution.py:54
  27.5 2.0 %collective-permute-start.7 = (bf16[128,2048]{1,0:T(8,128)(2,1)S(1)}, bf16[128,2048]{1,0:T(8,128)(2,1)S(1)}, u32[]{:S(2)}, u32[]{:S(2)}) collective-permute-start(bf16[128,2048]{1,0:T(8,128)(2,1)S(1)} %bitcast.122), channel_id=1, source_target_pairs={{0,1},{1,0},{2,3},{3,2},{4,5},{5,4},{6,7},{7,6},{8,9},{9,8},{10,11... | collective-permute-start | bytes 1572872 | tf_op jit(solution)/shard_map/ppermute | solution.py:124
  39.7 14.0 %collective-permute-start.14 = (f32[128,1024]{1,0:T(8,128)S(1)}, f32[128,1024]{1,0:T(8,128)S(1)}, u32[]{:S(2)}, u32[]{:S(2)}) collective-permute-start(f32[128,1024]{1,0:T(8,128)S(1)} %constant_dynamic-slice_fusion.3), channel_id=1, source_target_pairs={{0,4},{2,6},{4,0},{6,2},{8,12},{10,14},{12,8},{14,10},{1,5},{3,7},... | collective-permute-start | bytes 1572872 | tf_op jit(solution)/shard_map/ppermute | solution.py:17
  39.9 14.1 %collective-permute-start.8 = (f32[128,1024]{1,0:T(8,128)S(1)}, f32[128,1024]{1,0:T(8,128)S(1)}, u32[]{:S(2)}, u32[]{:S(2)}) collective-permute-start(f32[128,1024]{1,0:T(8,128)S(1)} %constant_dynamic-slice_fusion.9), channel_id=1, source_target_pairs={{0,2},{2,0},{4,6},{6,4},{8,10},{10,8},{12,14},{14,12},{1,3},{3,1},... | collective-permute-start | bytes 1572872 | tf_op jit(solution)/shard_map/ppermute | solution.py:17
  53.9 7.6 %collective-permute-start.15 = (f32[128,512]{1,0:T(8,128)S(1)}, f32[128,512]{1,0:T(8,128)S(1)}, u32[]{:S(2)}, u32[]{:S(2)}) collective-permute-start(f32[128,512]{1,0:T(8,128)S(1)} %constant_dynamic-slice_fusion.2), channel_id=1, source_target_pairs={{0,2},{2,0},{4,6},{6,4},{8,10},{10,8},{12,14},{14,12},{1,3},{3,1},... | collective-permute-start | bytes 786440 | tf_op jit(solution)/shard_map/ppermute | solution.py:17
  54.1 9.1 %collective-permute-start.9 = (f32[128,512]{1,0:T(8,128)S(1)}, f32[128,512]{1,0:T(8,128)S(1)}, u32[]{:S(2)}, u32[]{:S(2)}) collective-permute-start(f32[128,512]{1,0:T(8,128)S(1)} %constant_dynamic-slice_fusion.8), channel_id=1, source_target_pairs={{0,4},{2,6},{4,0},{6,2},{8,12},{10,14},{12,8},{14,10},{1,5},{3,7},... | collective-permute-start | bytes 786440 | tf_op jit(solution)/shard_map/ppermute | solution.py:17
  61.5 11.3 %collective-permute-start.16 = (f32[128,256]{1,0:T(8,128)S(1)}, f32[128,256]{1,0:T(8,128)S(1)}, u32[]{:S(2)}, u32[]{:S(2)}) collective-permute-start(f32[128,256]{1,0:T(8,128)S(1)} %constant_dynamic-slice_fusion.1), channel_id=1, source_target_pairs={{0,8},{2,10},{4,12},{6,14},{8,0},{10,2},{12,4},{14,6},{1,9},{3,11}... | collective-permute-start | bytes 393224 | tf_op jit(solution)/shard_map/ppermute | solution.py:17
  63.2 11.5 %collective-permute-start.10 = (f32[128,256]{1,0:T(8,128)S(1)}, f32[128,256]{1,0:T(8,128)S(1)}, u32[]{:S(2)}, u32[]{:S(2)}) collective-permute-start(f32[128,256]{1,0:T(8,128)S(1)} %constant_dynamic-slice_fusion.7), channel_id=1, source_target_pairs={{0,8},{2,10},{4,12},{6,14},{8,0},{10,2},{12,4},{14,6},{1,9},{3,11}... | collective-permute-start | bytes 393224 | tf_op jit(solution)/shard_map/ppermute | solution.py:17
  72.9 6.6 %collective-permute-start.17 = (bf16[128,256]{1,0:T(8,128)(2,1)S(1)}, bf16[128,256]{1,0:T(8,128)(2,1)S(1)}, u32[]{:S(2)}, u32[]{:S(2)}) collective-permute-start(bf16[128,256]{1,0:T(8,128)(2,1)S(1)} %multiply_convert_fusion), channel_id=1, source_target_pairs={{0,8},{2,10},{4,12},{6,14},{8,0},{10,2},{12,4},{14,6},{1,9},{3,11}... | collective-permute-start | bytes 196616 | tf_op jit(solution)/shard_map/ppermute | solution.py:17
  74.7 6.2 %collective-permute-start.11 = (bf16[128,256]{1,0:T(8,128)(2,1)S(1)}, bf16[128,256]{1,0:T(8,128)(2,1)S(1)}, u32[]{:S(2)}, u32[]{:S(2)}) collective-permute-start(bf16[128,256]{1,0:T(8,128)(2,1)S(1)} %multiply_convert_fusion.1), channel_id=1, source_target_pairs={{0,8},{2,10},{4,12},{6,14},{8,0},{10,2},{12,4},{14,6},{1,9},{3,11}... | collective-permute-start | bytes 196616 | tf_op jit(solution)/shard_map/ppermute | solution.py:17
  79.5 5.0 %collective-permute-start.18 = (bf16[2,128,256]{2,1,0:T(8,128)(2,1)S(1)}, bf16[2,128,256]{2,1,0:T(8,128)(2,1)S(1)}, u32[]{:S(2)}, u32[]{:S(2)}) collective-permute-start(bf16[2,128,256]{2,1,0:T(8,128)(2,1)S(1)} %pad_maximum_fusion.4), channel_id=1, source_target_pairs={{0,2},{2,0},{4,6},{6,4},{8,10},{10,8},{12,14},{14,12},{1,3},{3,1},... | collective-permute-start | bytes 393224 | tf_op jit(solution)/shard_map/ppermute | solution.py:17
  81.0 6.5 %collective-permute-start.12 = (bf16[2,128,256]{2,1,0:T(8,128)(2,1)S(1)}, bf16[2,128,256]{2,1,0:T(8,128)(2,1)S(1)}, u32[]{:S(2)}, u32[]{:S(2)}) collective-permute-start(bf16[2,128,256]{2,1,0:T(8,128)(2,1)S(1)} %pad_maximum_fusion.3), channel_id=1, source_target_pairs={{0,4},{2,6},{4,0},{6,2},{8,12},{10,14},{12,8},{14,10},{1,5},{3,7},... | collective-permute-start | bytes 393224 | tf_op jit(solution)/shard_map/ppermute | solution.py:17
  84.6 6.4 %collective-permute-start.19 = (bf16[2,2,128,256]{3,2,1,0:T(8,128)(2,1)S(1)}, bf16[2,2,128,256]{3,2,1,0:T(8,128)(2,1)S(1)}, u32[]{:S(2)}, u32[]{:S(2)}) collective-permute-start(bf16[2,2,128,256]{3,2,1,0:T(8,128)(2,1)S(1)} %pad_maximum_fusion.2), channel_id=1, source_target_pairs={{0,4},{2,6},{4,0},{6,2},{8,12},{10,14},{12,8},{14,10},{1,5},{3,7},... | collective-permute-start | bytes 786440 | tf_op jit(solution)/shard_map/ppermute | solution.py:17
  87.5 6.4 %collective-permute-start.13 = (bf16[2,2,128,256]{3,2,1,0:T(8,128)(2,1)S(1)}, bf16[2,2,128,256]{3,2,1,0:T(8,128)(2,1)S(1)}, u32[]{:S(2)}, u32[]{:S(2)}) collective-permute-start(bf16[2,2,128,256]{3,2,1,0:T(8,128)(2,1)S(1)} %pad_maximum_fusion.1), channel_id=1, source_target_pairs={{0,2},{2,0},{4,6},{6,4},{8,10},{10,8},{12,14},{14,12},{1,3},{3,1},... | collective-permute-start | bytes 786440 | tf_op jit(solution)/shard_map/ppermute | solution.py:17
  (5 other events, 36.6 us)

commit v6 on v5

--- a/solution.py
+++ b/solution.py
@@ -2,6 +2,8 @@
 import jax.numpy as jnp
 from jax import lax
 from jax.sharding import PartitionSpec as P
+from jax.experimental import pallas as pl
+from jax.experimental.pallas import tpu as pltpu
 
 sparsity = 0.2
 beta_one = 0.9
@@ -11,6 +13,51 @@
 adam_eps = 1e-08
 rate_step = 0.001
 decay_rate = 0.1
+
+
+def _tail_kernel(pre_ref, err_ref, cen_ref, dec_ref, enc_ref, m1_ref, m2_ref, w_out, m1_out, m2_out):
+    dec = dec_ref[...]
+    dec32 = dec.astype(jnp.float32)
+    row_norm = jnp.sqrt(jnp.sum(dec32 * dec32, axis=1, keepdims=True) + 1e-06)
+    back_t = lax.dot_general(
+        dec, err_ref[...], (((1,), (1,)), ((), ())), preferred_element_type=jnp.float32
+    )
+    tokens = err_ref.shape[0]
+    d_pre = (
+        jnp.where(pre_ref[...] > 0, 2.0 * back_t + sparsity * row_norm, 0.0) / tokens
+    ).astype(jnp.bfloat16)
+    grad = jnp.dot(d_pre, cen_ref[...], preferred_element_type=jnp.float32)
+    moment_one = beta_one * m1_ref[...].astype(jnp.float32) + (1.0 - beta_one) * grad
+    moment_two = beta_two * m2_ref[...].astype(jnp.float32) + (1.0 - beta_two) * grad * grad
+    direction = moment_one / corr_one / (jnp.sqrt(moment_two / corr_two) + adam_eps)
+    old = enc_ref[...].astype(jnp.float32)
+    w_out[...] = (old - rate_step * (direction + decay_rate * old)).astype(jnp.bfloat16)
+    m1_out[...] = moment_one.astype(jnp.bfloat16)
+    m2_out[...] = moment_two.astype(jnp.bfloat16)
+
+
+def tail(pre_t, error, centered, decoder, weight_in, first, second, tile=256):
+    n_lat, width = decoder.shape
+    tokens = error.shape[0]
+    row_block = pl.BlockSpec((tile, width), lambda i: (i, 0))
+    whole = pl.BlockSpec((tokens, width), lambda i: (0, 0))
+    out = jax.ShapeDtypeStruct((n_lat, width), jnp.bfloat16)
+    return pl.pallas_call(
+        _tail_kernel,
+        grid=(n_lat // tile,),
+        in_specs=[
+            pl.BlockSpec((tile, tokens), lambda i: (i, 0)),
+            whole,
+            whole,
+            row_block,
+            row_block,
+            row_block,
+            row_block,
+        ],
+        out_specs=[row_block, row_block, row_block],
+        out_shape=[out, out, out],
+        compiler_params=pltpu.CompilerParams(vmem_limit_bytes=56 * 1024 * 1024),
+    )(pre_t, error, centered, decoder, weight_in, first, second)
 
 
 def _pair_swap(value, axis, mask, size):
@@ -158,25 +205,10 @@
         error_parts.append(stacked[jnp.array(_block_owners(lat_size, order))])
     error_blocks = jnp.concatenate(error_parts, axis=1)
     error = jnp.transpose(error_blocks, (1, 0, 2)).reshape(error_blocks.shape[1], -1)
-    back_t = lax.dot_general(
-        decoder, error, (((1,), (1,)), ((), ())), preferred_element_type=jnp.float32
-    )
-    row_norm = jnp.sqrt(jnp.sum(jnp.square(decoder.astype(jnp.float32)), axis=1) + 1e-06)
-    token_total = sample.shape[0]
-    d_pre_t = (
-        jnp.where(pre_t > 0, 2.0 * back_t + sparsity * row_norm[:, None], 0.0) / token_total
-    ).astype(jnp.bfloat16)
-    grad = jnp.dot(d_pre_t, centered, preferred_element_type=jnp.float32)
-    moment_one = beta_one * first_moment[0].astype(jnp.float32) + (1.0 - beta_one) * grad
-    moment_two = beta_two * second_moment[0].astype(jnp.float32) + (1.0 - beta_two) * grad * grad
-    direction = moment_one / corr_one / (jnp.sqrt(moment_two / corr_two) + adam_eps)
-    old = weight_in.astype(jnp.float32)
-    updated = (old - rate_step * (direction + decay_rate * old)).astype(jnp.bfloat16)
-    return (
-        updated[None],
-        moment_one.astype(jnp.bfloat16)[None],
-        moment_two.astype(jnp.bfloat16)[None],
-    )
+    updated, moment_one, moment_two = tail(
+        pre_t, error, centered, decoder, weight_in, first_moment[0], second_moment[0]
+    )
+    return updated[None], moment_one[None], moment_two[None]
 
 
 LAT_SIZE = [8]

time: 124 us -> 123 us (level)
  Pallas kernels: 0 us -> 29.6 us
  matrix products: 35.5 us -> 8.83 us
  other arithmetic: 7.68 us -> 2.82 us
  starting transfers between devices: 22.4 us -> 25.9 us
  waiting for transfers between devices: 51.2 us -> 48.5 us
    pallas_call x0 -> x1, Pallas kernels: none -> 29.6 us  [tail(): pl.pallas_call(_tail_kernel, grid=(n_lat // tile,), in_specs=[pl.BlockSpe...]
    dot_general x1 -> x0, matrix products: 27.3 us -> none  [local(): grad = jnp.dot(d_pre_t, centered, preferred_element_type=jnp.float32)]
    ppermute x12, starting transfers between devices: 8.04 us -> 13.5 us  [_pair_swap(): return lax.ppermute(value, axis, [(i, i ^ mask) for i in range(size)])]
    ppermute x12, waiting for transfers between devices: 45.2 us -> 39.8 us  [_pair_swap(): return lax.ppermute(value, axis, [(i, i ^ mask) for i in range(size)])]
    reduce_sum x1 -> x0, other arithmetic: 5.08 us -> none  [local(): jnp.sum(jnp.square(decoder.astype(jnp.float32)), axis=1) + 1e-06]
    ppermute x7, waiting for transfers between devices: 4.18 us -> 6.9 us  [_direct_gather(): lax.ppermute(value, axis, [(i, (i + k) % size) for i in range(size)])]
    ppermute x7, starting transfers between devices: 14.3 us -> 12.3 us  [_direct_gather(): lax.ppermute(value, axis, [(i, (i + k) % size) for i in range(size)])]
  transfers between devices with their start and end apart: 20 -> 20, of which waited for: 12 -> 12; matrix products, arithmetic and copies ran while one was open for 7% -> 3% of each run, Pallas kernels for 0% -> 0%
where the time goes in v6:
time: 123 us
  waiting for transfers between devices  48.5 us (39%)
  Pallas kernels  29.6 us (24%)
  starting transfers between devices  25.9 us (21%)
  matrix products  8.83 us (7%)
  local copies, waits for them, and re-layouts  6.09 us (5%)
  other arithmetic  2.82 us (2%)
    ppermute x12, waiting for transfers between devices, _pair_swap(): return lax.ppermute(value, axis, [(i, i ^ mask) for i in range(size)])  39.8 us
    pallas_call x1, Pallas kernels, tail(): pl.pallas_call(_tail_kernel, grid=(n_lat // tile,), in_specs=[pl.BlockSpe...  29.6 us
    ppermute x12, starting transfers between devices, _pair_swap(): return lax.ppermute(value, axis, [(i, i ^ mask) for i in range(size)])  13.5 us
    ppermute x7, starting transfers between devices, _direct_gather(): lax.ppermute(value, axis, [(i, (i + k) % size) for i in range(size)])  12.3 us
    ppermute x7, waiting for transfers between devices, _direct_gather(): lax.ppermute(value, axis, [(i, (i + k) % size) for i in range(size)])  6.9 us
    dot_general x1, matrix products, local(): lax.dot_general(weight_in, centered, (((1,), (1,)), ((), ())), preferred_...  6.49 us
  transfers between devices with their start and end apart: 20, of which 12 were waited for; matrix products, arithmetic and copies ran while one was open for 3% of the time, Pallas kernels for 0%

profile of v6, /device:TPU:0, one launch (start us, length us, event | category | flops | bytes accessed | tf_op | source)
XLA Modules:
  0.0 122.8 jit_solution(8974586277716638277)
XLA Ops:
  0.6 5.0 %collective-permute-start.4 = (bf16[128,256]{1,0:T(8,128)(2,1)}, bf16[128,256]{1,0:T(8,128)(2,1)S(1)}, u32[]{:S(2)}, u32[]{:S(2)}) collective-permute-start(bf16[128,256]{1,0:T(8,128)(2,1)} %param.11), channel_id=1, source_target_pairs={{0,10},{2,12},{4,14},{6,0},{8,2},{10,4},{12,6},{14,8},{1,11},{3,13... | collective-permute-start | bytes 196616 | tf_op jit(solution)/shard_map/ppermute | solution.py:101
  6.0 1.7 %collective-permute-start.2 = (bf16[128,256]{1,0:T(8,128)(2,1)}, bf16[128,256]{1,0:T(8,128)(2,1)S(1)}, u32[]{:S(2)}, u32[]{:S(2)}) collective-permute-start(bf16[128,256]{1,0:T(8,128)(2,1)} %param.11), channel_id=1, source_target_pairs={{0,6},{2,8},{4,10},{6,12},{8,14},{10,0},{12,2},{14,4},{1,7},{3,9},... | collective-permute-start | bytes 196616 | tf_op jit(solution)/shard_map/ppermute | solution.py:101
  7.6 2.5 %collective-permute-start.1 = (bf16[128,256]{1,0:T(8,128)(2,1)}, bf16[128,256]{1,0:T(8,128)(2,1)S(1)}, u32[]{:S(2)}, u32[]{:S(2)}) collective-permute-start(bf16[128,256]{1,0:T(8,128)(2,1)} %param.11), channel_id=1, source_target_pairs={{0,4},{2,6},{4,8},{6,10},{8,12},{10,14},{12,0},{14,2},{1,5},{3,7},... | collective-permute-start | bytes 196616 | tf_op jit(solution)/shard_map/ppermute | solution.py:101
  10.1 1.5 %collective-permute-start = (bf16[128,256]{1,0:T(8,128)(2,1)}, bf16[128,256]{1,0:T(8,128)(2,1)S(1)}, u32[]{:S(2)}, u32[]{:S(2)}) collective-permute-start(bf16[128,256]{1,0:T(8,128)(2,1)} %param.11), channel_id=1, source_target_pairs={{0,2},{2,4},{4,6},{6,8},{8,10},{10,12},{12,14},{14,0},{1,3},{3,5},... | collective-permute-start | bytes 196616 | tf_op jit(solution)/shard_map/ppermute | solution.py:101
  14.0 3.4 %collective-permute-done = bf16[128,256]{1,0:T(8,128)(2,1)S(1)} collective-permute-done((bf16[128,256]{1,0:T(8,128)(2,1)}, bf16[128,256]{1,0:T(8,128)(2,1)S(1)}, u32[]{:S(2)}, u32[]{:S(2)}) %collective-permute-start) | collective-permute-done | bytes 65568 | tf_op jit(solution)/shard_map/ppermute | solution.py:101
  18.8 3.5 %collective-permute-done.5 = bf16[128,256]{1,0:T(8,128)(2,1)S(1)} collective-permute-done((bf16[128,256]{1,0:T(8,128)(2,1)}, bf16[128,256]{1,0:T(8,128)(2,1)S(1)}, u32[]{:S(2)}, u32[]{:S(2)}) %collective-permute-start.5) | collective-permute-done | bytes 65568 | tf_op jit(solution)/shard_map/ppermute | solution.py:101
  23.3 1.8 %collective-permute-done.7 = bf16[128,2048]{1,0:T(8,128)(2,1)S(1)} collective-permute-done((bf16[128,2048]{1,0:T(8,128)(2,1)S(1)}, bf16[128,2048]{1,0:T(8,128)(2,1)S(1)}, u32[]{:S(2)}, u32[]{:S(2)}) %collective-permute-start.7) | collective-permute-done | bytes 524320 | tf_op jit(solution)/shard_map/ppermute | solution.py:171
  25.2 1.4 %gather_fusion.1 = bf16[256,2048]{1,0:T(8,128)(2,1)S(1)} fusion(bf16[256,2048]{1,0:T(8,128)(2,1)S(1)} %pad_maximum_fusion, s32[1024]{0:T(1024)S(1)} %pad_clamp_fusion.2), kind=kCustom, calls=%fused_computation.1 | custom fusion | bytes 2098176 | tf_op jit(solution)/shard_map/jit(_take)/gather | solution.py:178
  27.3 6.5 %fusion.pre_ref = f32[2048,256]{1,0:T(8,128)S(1)} fusion(bf16[256,2048]{1,0:T(8,128)(2,1)S(1)} %get-tuple-element.9.cen_ref, f32[2048]{0:T(1024)S(1)} %bitcast.101, bf16[1,2048,2048]{2,1,0:T(8,128)(2,1)} %param.14), kind=kOutput, calls=%fused_computation.5 | convolution fusion | flops 2148007936 | bytes 11542528 | tf_op jit(solution)/shard_map/dot_general | solution.py:184
  33.8 2.3 %fusion.1 = f32[256,2048]{1,0:T(8,128)S(1)} fusion(f32[2048,256]{1,0:T(8,128)S(1)} %fusion.pre_ref, bf16[1,2048,2048]{2,1,0:T(8,128)(2,1)S(1)} %bitcast.82), kind=kOutput, calls=%fused_computation.8 | convolution fusion | flops 2148532224 | bytes 12582912 | tf_op jit(solution)/shard_map/dot_general | solution.py:190
  38.9 11.6 %collective-permute-done.14 = f32[128,1024]{1,0:T(8,128)S(1)} collective-permute-done((f32[128,1024]{1,0:T(8,128)S(1)}, f32[128,1024]{1,0:T(8,128)S(1)}, u32[]{:S(2)}, u32[]{:S(2)}) %collective-permute-start.14) | collective-permute-done | bytes 524320 | tf_op jit(solution)/shard_map/ppermute | solution.py:64
  50.6 1.7 %collective-permute-start.15 = (f32[128,512]{1,0:T(8,128)S(1)}, f32[128,512]{1,0:T(8,128)S(1)}, u32[]{:S(2)}, u32[]{:S(2)}) collective-permute-start(f32[128,512]{1,0:T(8,128)S(1)} %constant_dynamic-slice_fusion.2), channel_id=1, source_target_pairs={{0,2},{2,0},{4,6},{6,4},{8,10},{10,8},{12,14},{14,12},{1,3},{3,1},... | collective-permute-start | bytes 786440 | tf_op jit(solution)/shard_map/ppermute | solution.py:64
  53.0 5.2 %collective-permute-done.15 = f32[128,512]{1,0:T(8,128)S(1)} collective-permute-done((f32[128,512]{1,0:T(8,128)S(1)}, f32[128,512]{1,0:T(8,128)S(1)}, u32[]{:S(2)}, u32[]{:S(2)}) %collective-permute-start.15) | collective-permute-done | bytes 262176 | tf_op jit(solution)/shard_map/ppermute | solution.py:64
  58.3 1.9 %collective-permute-start.16 = (f32[128,256]{1,0:T(8,128)S(1)}, f32[128,256]{1,0:T(8,128)S(1)}, u32[]{:S(2)}, u32[]{:S(2)}) collective-permute-start(f32[128,256]{1,0:T(8,128)S(1)} %constant_dynamic-slice_fusion.1), channel_id=1, source_target_pairs={{0,8},{2,10},{4,12},{6,14},{8,0},{10,2},{12,4},{14,6},{1,9},{3,11}... | collective-permute-start | bytes 393224 | tf_op jit(solution)/shard_map/ppermute | solution.py:64
  60.2 2.0 %collective-permute-start.10 = (f32[128,256]{1,0:T(8,128)S(1)}, f32[128,256]{1,0:T(8,128)S(1)}, u32[]{:S(2)}, u32[]{:S(2)}) collective-permute-start(f32[128,256]{1,0:T(8,128)S(1)} %constant_dynamic-slice_fusion.7), channel_id=1, source_target_pairs={{0,8},{2,10},{4,12},{6,14},{8,0},{10,2},{12,4},{14,6},{1,9},{3,11}... | collective-permute-start | bytes 393224 | tf_op jit(solution)/shard_map/ppermute | solution.py:64
  62.2 7.6 %collective-permute-done.16 = f32[128,256]{1,0:T(8,128)S(1)} collective-permute-done((f32[128,256]{1,0:T(8,128)S(1)}, f32[128,256]{1,0:T(8,128)S(1)}, u32[]{:S(2)}, u32[]{:S(2)}) %collective-permute-start.16) | collective-permute-done | bytes 131104 | tf_op jit(solution)/shard_map/ppermute | solution.py:64
  70.0 1.7 %collective-permute-done.10 = f32[128,256]{1,0:T(8,128)S(1)} collective-permute-done((f32[128,256]{1,0:T(8,128)S(1)}, f32[128,256]{1,0:T(8,128)S(1)}, u32[]{:S(2)}, u32[]{:S(2)}) %collective-permute-start.10) | collective-permute-done | bytes 131104 | tf_op jit(solution)/shard_map/ppermute | solution.py:64
  73.0 2.4 %collective-permute-done.17 = bf16[128,256]{1,0:T(8,128)(2,1)S(1)} collective-permute-done((bf16[128,256]{1,0:T(8,128)(2,1)S(1)}, bf16[128,256]{1,0:T(8,128)(2,1)S(1)}, u32[]{:S(2)}, u32[]{:S(2)}) %collective-permute-start.17) | collective-permute-done | bytes 65568 | tf_op jit(solution)/shard_map/ppermute | solution.py:64
  75.5 2.3 %collective-permute-start.18 = (bf16[2,128,256]{2,1,0:T(8,128)(2,1)S(1)}, bf16[2,128,256]{2,1,0:T(8,128)(2,1)S(1)}, u32[]{:S(2)}, u32[]{:S(2)}) collective-permute-start(bf16[2,128,256]{2,1,0:T(8,128)(2,1)S(1)} %pad_maximum_fusion.4), channel_id=1, source_target_pairs={{0,2},{2,0},{4,6},{6,4},{8,10},{10,8},{12,14},{14,12},{1,3},{3,1},... | collective-permute-start | bytes 393224 | tf_op jit(solution)/shard_map/ppermute | solution.py:64
  78.0 2.8 %collective-permute-done.18 = bf16[2,128,256]{2,1,0:T(8,128)(2,1)S(1)} collective-permute-done((bf16[2,128,256]{2,1,0:T(8,128)(2,1)S(1)}, bf16[2,128,256]{2,1,0:T(8,128)(2,1)S(1)}, u32[]{:S(2)}, u32[]{:S(2)}) %collective-permute-start.18) | collective-permute-done | bytes 131104 | tf_op jit(solution)/shard_map/ppermute | solution.py:64
  80.9 3.3 %collective-permute-done.12 = bf16[2,128,256]{2,1,0:T(8,128)(2,1)S(1)} collective-permute-done((bf16[2,128,256]{2,1,0:T(8,128)(2,1)S(1)}, bf16[2,128,256]{2,1,0:T(8,128)(2,1)S(1)}, u32[]{:S(2)}, u32[]{:S(2)}) %collective-permute-start.12) | collective-permute-done | bytes 131104 | tf_op jit(solution)/shard_map/ppermute | solution.py:64
  85.5 1.8 %collective-permute-done.19 = bf16[2,2,128,256]{3,2,1,0:T(8,128)(2,1)S(1)} collective-permute-done((bf16[2,2,128,256]{3,2,1,0:T(8,128)(2,1)S(1)}, bf16[2,2,128,256]{3,2,1,0:T(8,128)(2,1)S(1)}, u32[]{:S(2)}, u32[]{:S(2)}) %collective-permute-start.19) | collective-permute-done | bytes 262176 | tf_op jit(solution)/shard_map/ppermute | solution.py:64
  87.4 3.2 %collective-permute-done.13 = bf16[2,2,128,256]{3,2,1,0:T(8,128)(2,1)S(1)} collective-permute-done((bf16[2,2,128,256]{3,2,1,0:T(8,128)(2,1)S(1)}, bf16[2,2,128,256]{3,2,1,0:T(8,128)(2,1)S(1)}, u32[]{:S(2)}, u32[]{:S(2)}) %collective-permute-start.13) | collective-permute-done | bytes 262176 | tf_op jit(solution)/shard_map/ppermute | solution.py:64
  93.2 29.6 %shard_map.130 = (bf16[2048,2048]{1,0:T(8,128)(2,1)}, bf16[2048,2048]{1,0:T(8,128)(2,1)}, bf16[2048,2048]{1,0:T(8,128)(2,1)}) custom-call(f32[2048,256]{1,0:T(8,128)} %copy-done, bf16[256,2048]{1,0:T(8,128)(2,1)} %bitcast.86, bf16[256,2048]{1,0:T(8,128)(2,1)} %copy-done.1, bf16[2048,2048]{1,0:T(8,128)(2,1)} %bitcast.80, bf16[2048,2048]{1,0:T(8,128)(2,1)} %bitcast.83, ...), custom_call_target="tpu_custom_call" | custom-call | tf_op jit(solution)/shard_map/pallas_call | solution.py:45
  (94 shorter events, 14.9 us)
Async XLA Ops:
  0.6 18.2 %collective-permute-start.4 = (bf16[128,256]{1,0:T(8,128)(2,1)}, bf16[128,256]{1,0:T(8,128)(2,1)S(1)}, u32[]{:S(2)}, u32[]{:S(2)}) collective-permute-start(bf16[128,256]{1,0:T(8,128)(2,1)} %param.11), channel_id=1, source_target_pairs={{0,10},{2,12},{4,14},{6,0},{8,2},{10,4},{12,6},{14,8},{1,11},{3,13... | collective-permute-start | bytes 196616 | tf_op jit(solution)/shard_map/ppermute | solution.py:101
  5.6 13.1 %collective-permute-start.3 = (bf16[128,256]{1,0:T(8,128)(2,1)}, bf16[128,256]{1,0:T(8,128)(2,1)S(1)}, u32[]{:S(2)}, u32[]{:S(2)}) collective-permute-start(bf16[128,256]{1,0:T(8,128)(2,1)} %param.11), channel_id=1, source_target_pairs={{0,8},{2,10},{4,12},{6,14},{8,0},{10,2},{12,4},{14,6},{1,9},{3,11}... | collective-permute-start | bytes 196616 | tf_op jit(solution)/shard_map/ppermute | solution.py:101
  6.0 12.8 %collective-permute-start.2 = (bf16[128,256]{1,0:T(8,128)(2,1)}, bf16[128,256]{1,0:T(8,128)(2,1)S(1)}, u32[]{:S(2)}, u32[]{:S(2)}) collective-permute-start(bf16[128,256]{1,0:T(8,128)(2,1)} %param.11), channel_id=1, source_target_pairs={{0,6},{2,8},{4,10},{6,12},{8,14},{10,0},{12,2},{14,4},{1,7},{3,9},... | collective-permute-start | bytes 196616 | tf_op jit(solution)/shard_map/ppermute | solution.py:101
  7.6 10.1 %collective-permute-start.1 = (bf16[128,256]{1,0:T(8,128)(2,1)}, bf16[128,256]{1,0:T(8,128)(2,1)S(1)}, u32[]{:S(2)}, u32[]{:S(2)}) collective-permute-start(bf16[128,256]{1,0:T(8,128)(2,1)} %param.11), channel_id=1, source_target_pairs={{0,4},{2,6},{4,8},{6,10},{8,12},{10,14},{12,0},{14,2},{1,5},{3,7},... | collective-permute-start | bytes 196616 | tf_op jit(solution)/shard_map/ppermute | solution.py:101
  10.1 7.3 %collective-permute-start = (bf16[128,256]{1,0:T(8,128)(2,1)}, bf16[128,256]{1,0:T(8,128)(2,1)S(1)}, u32[]{:S(2)}, u32[]{:S(2)}) collective-permute-start(bf16[128,256]{1,0:T(8,128)(2,1)} %param.11), channel_id=1, source_target_pairs={{0,2},{2,4},{4,6},{6,8},{8,10},{10,12},{12,14},{14,0},{1,3},{3,5},... | collective-permute-start | bytes 196616 | tf_op jit(solution)/shard_map/ppermute | solution.py:101
  11.6 11.6 %copy-start.2 = (f32[1,2048]{1,0:T(1,128)S(1)}, f32[1,2048]{1,0:T(1,128)}, u32[]{:S(2)}) copy-start(f32[1,2048]{1,0:T(1,128)} %param.17) | copy-start | bytes 24580
  12.5 10.7 %copy-start.4 = (s32[8]{0:T(128)S(1)}, s32[8]{0:T(128)}, u32[]{:S(2)}) copy-start(s32[8]{0:T(128)} %constant.95) | copy-start | bytes 100
  12.5 10.7 %copy-start.5 = (s32[8]{0:T(128)S(1)}, s32[8]{0:T(128)}, u32[]{:S(2)}) copy-start(s32[8]{0:T(128)} %constant.94) | copy-start | bytes 100
  12.5 10.8 %copy-start.3 = (s32[1,256]{1,0:T(1,128)S(1)}, s32[1,256]{1,0:T(1,128)}, u32[]{:S(2)}) copy-start(s32[1,256]{1,0:T(1,128)} %param.12) | copy-start | bytes 3076
  17.4 4.9 %collective-permute-start.6 = (bf16[128,256]{1,0:T(8,128)(2,1)}, bf16[128,256]{1,0:T(8,128)(2,1)S(1)}, u32[]{:S(2)}, u32[]{:S(2)}) collective-permute-start(bf16[128,256]{1,0:T(8,128)(2,1)} %param.11), channel_id=1, source_target_pairs={{0,14},{2,0},{4,2},{6,4},{8,6},{10,8},{12,10},{14,12},{1,15},{3,1}... | collective-permute-start | bytes 196616 | tf_op jit(solution)/shard_map/ppermute | solution.py:101
  17.8 4.5 %collective-permute-start.5 = (bf16[128,256]{1,0:T(8,128)(2,1)}, bf16[128,256]{1,0:T(8,128)(2,1)S(1)}, u32[]{:S(2)}, u32[]{:S(2)}) collective-permute-start(bf16[128,256]{1,0:T(8,128)(2,1)} %param.11), channel_id=1, source_target_pairs={{0,12},{2,14},{4,0},{6,2},{8,4},{10,6},{12,8},{14,10},{1,13},{3,15... | collective-permute-start | bytes 196616 | tf_op jit(solution)/shard_map/ppermute | solution.py:101
  23.1 2.0 %collective-permute-start.7 = (bf16[128,2048]{1,0:T(8,128)(2,1)S(1)}, bf16[128,2048]{1,0:T(8,128)(2,1)S(1)}, u32[]{:S(2)}, u32[]{:S(2)}) collective-permute-start(bf16[128,2048]{1,0:T(8,128)(2,1)S(1)} %bitcast.87), channel_id=1, source_target_pairs={{0,1},{1,0},{2,3},{3,2},{4,5},{5,4},{6,7},{7,6},{8,9},{9,8},{10,11... | collective-permute-start | bytes 1572872 | tf_op jit(solution)/shard_map/ppermute | solution.py:171
  36.5 14.0 %collective-permute-start.14 = (f32[128,1024]{1,0:T(8,128)S(1)}, f32[128,1024]{1,0:T(8,128)S(1)}, u32[]{:S(2)}, u32[]{:S(2)}) collective-permute-start(f32[128,1024]{1,0:T(8,128)S(1)} %constant_dynamic-slice_fusion.3), channel_id=1, source_target_pairs={{0,4},{2,6},{4,0},{6,2},{8,12},{10,14},{12,8},{14,10},{1,5},{3,7},... | collective-permute-start | bytes 1572872 | tf_op jit(solution)/shard_map/ppermute | solution.py:64
  37.5 14.8 %collective-permute-start.8 = (f32[128,1024]{1,0:T(8,128)S(1)}, f32[128,1024]{1,0:T(8,128)S(1)}, u32[]{:S(2)}, u32[]{:S(2)}) collective-permute-start(f32[128,1024]{1,0:T(8,128)S(1)} %constant_dynamic-slice_fusion.9), channel_id=1, source_target_pairs={{0,2},{2,0},{4,6},{6,4},{8,10},{10,8},{12,14},{14,12},{1,3},{3,1},... | collective-permute-start | bytes 1572872 | tf_op jit(solution)/shard_map/ppermute | solution.py:64
  50.6 7.6 %collective-permute-start.15 = (f32[128,512]{1,0:T(8,128)S(1)}, f32[128,512]{1,0:T(8,128)S(1)}, u32[]{:S(2)}, u32[]{:S(2)}) collective-permute-start(f32[128,512]{1,0:T(8,128)S(1)} %constant_dynamic-slice_fusion.2), channel_id=1, source_target_pairs={{0,2},{2,0},{4,6},{6,4},{8,10},{10,8},{12,14},{14,12},{1,3},{3,1},... | collective-permute-start | bytes 786440 | tf_op jit(solution)/shard_map/ppermute | solution.py:64
  52.5 7.7 %collective-permute-start.9 = (f32[128,512]{1,0:T(8,128)S(1)}, f32[128,512]{1,0:T(8,128)S(1)}, u32[]{:S(2)}, u32[]{:S(2)}) collective-permute-start(f32[128,512]{1,0:T(8,128)S(1)} %constant_dynamic-slice_fusion.8), channel_id=1, source_target_pairs={{0,4},{2,6},{4,0},{6,2},{8,12},{10,14},{12,8},{14,10},{1,5},{3,7},... | collective-permute-start | bytes 786440 | tf_op jit(solution)/shard_map/ppermute | solution.py:64
  58.3 11.6 %collective-permute-start.16 = (f32[128,256]{1,0:T(8,128)S(1)}, f32[128,256]{1,0:T(8,128)S(1)}, u32[]{:S(2)}, u32[]{:S(2)}) collective-permute-start(f32[128,256]{1,0:T(8,128)S(1)} %constant_dynamic-slice_fusion.1), channel_id=1, source_target_pairs={{0,8},{2,10},{4,12},{6,14},{8,0},{10,2},{12,4},{14,6},{1,9},{3,11}... | collective-permute-start | bytes 393224 | tf_op jit(solution)/shard_map/ppermute | solution.py:64
  60.2 11.5 %collective-permute-start.10 = (f32[128,256]{1,0:T(8,128)S(1)}, f32[128,256]{1,0:T(8,128)S(1)}, u32[]{:S(2)}, u32[]{:S(2)}) collective-permute-start(f32[128,256]{1,0:T(8,128)S(1)} %constant_dynamic-slice_fusion.7), channel_id=1, source_target_pairs={{0,8},{2,10},{4,12},{6,14},{8,0},{10,2},{12,4},{14,6},{1,9},{3,11}... | collective-permute-start | bytes 393224 | tf_op jit(solution)/shard_map/ppermute | solution.py:64
  69.9 5.5 %collective-permute-start.17 = (bf16[128,256]{1,0:T(8,128)(2,1)S(1)}, bf16[128,256]{1,0:T(8,128)(2,1)S(1)}, u32[]{:S(2)}, u32[]{:S(2)}) collective-permute-start(bf16[128,256]{1,0:T(8,128)(2,1)S(1)} %multiply_convert_fusion), channel_id=1, source_target_pairs={{0,8},{2,10},{4,12},{6,14},{8,0},{10,2},{12,4},{14,6},{1,9},{3,11}... | collective-permute-start | bytes 196616 | tf_op jit(solution)/shard_map/ppermute | solution.py:64
  71.8 6.1 %collective-permute-start.11 = (bf16[128,256]{1,0:T(8,128)(2,1)S(1)}, bf16[128,256]{1,0:T(8,128)(2,1)S(1)}, u32[]{:S(2)}, u32[]{:S(2)}) collective-permute-start(bf16[128,256]{1,0:T(8,128)(2,1)S(1)} %multiply_convert_fusion.1), channel_id=1, source_target_pairs={{0,8},{2,10},{4,12},{6,14},{8,0},{10,2},{12,4},{14,6},{1,9},{3,11}... | collective-permute-start | bytes 196616 | tf_op jit(solution)/shard_map/ppermute | solution.py:64
  75.5 5.3 %collective-permute-start.18 = (bf16[2,128,256]{2,1,0:T(8,128)(2,1)S(1)}, bf16[2,128,256]{2,1,0:T(8,128)(2,1)S(1)}, u32[]{:S(2)}, u32[]{:S(2)}) collective-permute-start(bf16[2,128,256]{2,1,0:T(8,128)(2,1)S(1)} %pad_maximum_fusion.4), channel_id=1, source_target_pairs={{0,2},{2,0},{4,6},{6,4},{8,10},{10,8},{12,14},{14,12},{1,3},{3,1},... | collective-permute-start | bytes 393224 | tf_op jit(solution)/shard_map/ppermute | solution.py:64
  77.9 6.3 %collective-permute-start.12 = (bf16[2,128,256]{2,1,0:T(8,128)(2,1)S(1)}, bf16[2,128,256]{2,1,0:T(8,128)(2,1)S(1)}, u32[]{:S(2)}, u32[]{:S(2)}) collective-permute-start(bf16[2,128,256]{2,1,0:T(8,128)(2,1)S(1)} %pad_maximum_fusion.3), channel_id=1, source_target_pairs={{0,4},{2,6},{4,0},{6,2},{8,12},{10,14},{12,8},{14,10},{1,5},{3,7},... | collective-permute-start | bytes 393224 | tf_op jit(solution)/shard_map/ppermute | solution.py:64
  80.8 6.4 %collective-permute-start.19 = (bf16[2,2,128,256]{3,2,1,0:T(8,128)(2,1)S(1)}, bf16[2,2,128,256]{3,2,1,0:T(8,128)(2,1)S(1)}, u32[]{:S(2)}, u32[]{:S(2)}) collective-permute-start(bf16[2,2,128,256]{3,2,1,0:T(8,128)(2,1)S(1)} %pad_maximum_fusion.2), channel_id=1, source_target_pairs={{0,4},{2,6},{4,0},{6,2},{8,12},{10,14},{12,8},{14,10},{1,5},{3,7},... | collective-permute-start | bytes 786440 | tf_op jit(solution)/shard_map/ppermute | solution.py:64
  84.2 6.4 %collective-permute-start.13 = (bf16[2,2,128,256]{3,2,1,0:T(8,128)(2,1)S(1)}, bf16[2,2,128,256]{3,2,1,0:T(8,128)(2,1)S(1)}, u32[]{:S(2)}, u32[]{:S(2)}) collective-permute-start(bf16[2,2,128,256]{3,2,1,0:T(8,128)(2,1)S(1)} %pad_maximum_fusion.1), channel_id=1, source_target_pairs={{0,2},{2,0},{4,6},{6,4},{8,10},{10,8},{12,14},{14,12},{1,3},{3,1},... | collective-permute-start | bytes 786440 | tf_op jit(solution)/shard_map/ppermute | solution.py:64
  (5 other events, 23.6 us)

commit v7 on v6

--- a/solution.py
+++ b/solution.py
@@ -19,17 +19,17 @@
     dec = dec_ref[...]
     dec32 = dec.astype(jnp.float32)
     row_norm = jnp.sqrt(jnp.sum(dec32 * dec32, axis=1, keepdims=True) + 1e-06)
-    back_t = lax.dot_general(
-        dec, err_ref[...], (((1,), (1,)), ((), ())), preferred_element_type=jnp.float32
-    )
-    tokens = err_ref.shape[0]
+    back_t = jnp.dot(dec, err_ref[...], preferred_element_type=jnp.float32)
+    tokens = err_ref.shape[1]
     d_pre = (
         jnp.where(pre_ref[...] > 0, 2.0 * back_t + sparsity * row_norm, 0.0) / tokens
     ).astype(jnp.bfloat16)
     grad = jnp.dot(d_pre, cen_ref[...], preferred_element_type=jnp.float32)
     moment_one = beta_one * m1_ref[...].astype(jnp.float32) + (1.0 - beta_one) * grad
     moment_two = beta_two * m2_ref[...].astype(jnp.float32) + (1.0 - beta_two) * grad * grad
-    direction = moment_one / corr_one / (jnp.sqrt(moment_two / corr_two) + adam_eps)
+    direction = (moment_one * (1.0 / corr_one)) / (
+        jnp.sqrt(moment_two * (1.0 / corr_two)) + adam_eps
+    )
     old = enc_ref[...].astype(jnp.float32)
     w_out[...] = (old - rate_step * (direction + decay_rate * old)).astype(jnp.bfloat16)
     m1_out[...] = moment_one.astype(jnp.bfloat16)
@@ -39,6 +39,7 @@
 def tail(pre_t, error, centered, decoder, weight_in, first, second, tile=256):
     n_lat, width = decoder.shape
     tokens = error.shape[0]
+    error_t = error.T
     row_block = pl.BlockSpec((tile, width), lambda i: (i, 0))
     whole = pl.BlockSpec((tokens, width), lambda i: (0, 0))
     out = jax.ShapeDtypeStruct((n_lat, width), jnp.bfloat16)
@@ -47,7 +48,7 @@
         grid=(n_lat // tile,),
         in_specs=[
             pl.BlockSpec((tile, tokens), lambda i: (i, 0)),
-            whole,
+            pl.BlockSpec((width, tokens), lambda i: (0, 0)),
             whole,
             row_block,
             row_block,
@@ -57,7 +58,7 @@
         out_specs=[row_block, row_block, row_block],
         out_shape=[out, out, out],
         compiler_params=pltpu.CompilerParams(vmem_limit_bytes=56 * 1024 * 1024),
-    )(pre_t, error, centered, decoder, weight_in, first, second)
+    )(pre_t, error_t, centered, decoder, weight_in, first, second)
 
 
 def _pair_swap(value, axis, mask, size):

time: 123 us -> 123 us (level)
    transpose x0 -> x1, local copies, waits for them, and re-layouts: none -> 1.34 us  [local(): jnp.transpose(error_blocks, (1, 0, 2)).reshape(error_blocks.shape[1], -1)]
where the time goes in v7:
time: 123 us
  waiting for transfers between devices  48.5 us (39%)
  Pallas kernels  29.4 us (24%)
  starting transfers between devices  25.9 us (21%)
  matrix products  8.83 us (7%)
  local copies, waits for them, and re-layouts  6.3 us (5%)
  other arithmetic  2.82 us (2%)
    ppermute x12, waiting for transfers between devices, _pair_swap(): return lax.ppermute(value, axis, [(i, i ^ mask) for i in range(size)])  39.8 us
    pallas_call x1, Pallas kernels, tail(): pl.pallas_call(_tail_kernel, grid=(n_lat // tile,), in_specs=[pl.BlockSpe...  29.4 us
    ppermute x12, starting transfers between devices, _pair_swap(): return lax.ppermute(value, axis, [(i, i ^ mask) for i in range(size)])  13.5 us
    ppermute x7, starting transfers between devices, _direct_gather(): lax.ppermute(value, axis, [(i, (i + k) % size) for i in range(size)])  12.3 us
    ppermute x7, waiting for transfers between devices, _direct_gather(): lax.ppermute(value, axis, [(i, (i + k) % size) for i in range(size)])  6.9 us
    dot_general x1, matrix products, local(): lax.dot_general(weight_in, centered, (((1,), (1,)), ((), ())), preferred_...  6.49 us
  transfers between devices with their start and end apart: 20, of which 12 were waited for; matrix products, arithmetic and copies ran while one was open for 3% of the time, Pallas kernels for 0%

profile of v7, /device:TPU:0, one launch (start us, length us, event | category | flops | bytes accessed | tf_op | source)
XLA Modules:
  0.0 122.8 jit_solution(260984078189511111)
XLA Ops:
  0.6 5.0 %collective-permute-start.4 = (bf16[128,256]{1,0:T(8,128)(2,1)}, bf16[128,256]{1,0:T(8,128)(2,1)S(1)}, u32[]{:S(2)}, u32[]{:S(2)}) collective-permute-start(bf16[128,256]{1,0:T(8,128)(2,1)} %param.11), channel_id=1, source_target_pairs={{0,10},{2,12},{4,14},{6,0},{8,2},{10,4},{12,6},{14,8},{1,11},{3,13... | collective-permute-start | bytes 196616 | tf_op jit(solution)/shard_map/ppermute | solution.py:102
  6.0 1.7 %collective-permute-start.2 = (bf16[128,256]{1,0:T(8,128)(2,1)}, bf16[128,256]{1,0:T(8,128)(2,1)S(1)}, u32[]{:S(2)}, u32[]{:S(2)}) collective-permute-start(bf16[128,256]{1,0:T(8,128)(2,1)} %param.11), channel_id=1, source_target_pairs={{0,6},{2,8},{4,10},{6,12},{8,14},{10,0},{12,2},{14,4},{1,7},{3,9},... | collective-permute-start | bytes 196616 | tf_op jit(solution)/shard_map/ppermute | solution.py:102
  7.6 2.5 %collective-permute-start.1 = (bf16[128,256]{1,0:T(8,128)(2,1)}, bf16[128,256]{1,0:T(8,128)(2,1)S(1)}, u32[]{:S(2)}, u32[]{:S(2)}) collective-permute-start(bf16[128,256]{1,0:T(8,128)(2,1)} %param.11), channel_id=1, source_target_pairs={{0,4},{2,6},{4,8},{6,10},{8,12},{10,14},{12,0},{14,2},{1,5},{3,7},... | collective-permute-start | bytes 196616 | tf_op jit(solution)/shard_map/ppermute | solution.py:102
  10.1 1.5 %collective-permute-start = (bf16[128,256]{1,0:T(8,128)(2,1)}, bf16[128,256]{1,0:T(8,128)(2,1)S(1)}, u32[]{:S(2)}, u32[]{:S(2)}) collective-permute-start(bf16[128,256]{1,0:T(8,128)(2,1)} %param.11), channel_id=1, source_target_pairs={{0,2},{2,4},{4,6},{6,8},{8,10},{10,12},{12,14},{14,0},{1,3},{3,5},... | collective-permute-start | bytes 196616 | tf_op jit(solution)/shard_map/ppermute | solution.py:102
  14.0 3.4 %collective-permute-done = bf16[128,256]{1,0:T(8,128)(2,1)S(1)} collective-permute-done((bf16[128,256]{1,0:T(8,128)(2,1)}, bf16[128,256]{1,0:T(8,128)(2,1)S(1)}, u32[]{:S(2)}, u32[]{:S(2)}) %collective-permute-start) | collective-permute-done | bytes 65568 | tf_op jit(solution)/shard_map/ppermute | solution.py:102
  18.8 3.5 %collective-permute-done.5 = bf16[128,256]{1,0:T(8,128)(2,1)S(1)} collective-permute-done((bf16[128,256]{1,0:T(8,128)(2,1)}, bf16[128,256]{1,0:T(8,128)(2,1)S(1)}, u32[]{:S(2)}, u32[]{:S(2)}) %collective-permute-start.5) | collective-permute-done | bytes 65568 | tf_op jit(solution)/shard_map/ppermute | solution.py:102
  23.3 1.8 %collective-permute-done.7 = bf16[128,2048]{1,0:T(8,128)(2,1)S(1)} collective-permute-done((bf16[128,2048]{1,0:T(8,128)(2,1)S(1)}, bf16[128,2048]{1,0:T(8,128)(2,1)S(1)}, u32[]{:S(2)}, u32[]{:S(2)}) %collective-permute-start.7) | collective-permute-done | bytes 524320 | tf_op jit(solution)/shard_map/ppermute | solution.py:172
  25.2 1.4 %gather_fusion.1 = bf16[256,2048]{1,0:T(8,128)(2,1)S(1)} fusion(bf16[256,2048]{1,0:T(8,128)(2,1)S(1)} %pad_maximum_fusion, s32[1024]{0:T(1024)S(1)} %pad_clamp_fusion.2), kind=kCustom, calls=%fused_computation.1 | custom fusion | bytes 2098176 | tf_op jit(solution)/shard_map/jit(_take)/gather | solution.py:179
  27.3 6.5 %fusion.pre_ref = f32[2048,256]{1,0:T(8,128)S(1)} fusion(bf16[256,2048]{1,0:T(8,128)(2,1)S(1)} %get-tuple-element.9.cen_ref, f32[2048]{0:T(1024)S(1)} %bitcast.102, bf16[1,2048,2048]{2,1,0:T(8,128)(2,1)} %param.14), kind=kOutput, calls=%fused_computation.5 | convolution fusion | flops 2148007936 | bytes 11542528 | tf_op jit(solution)/shard_map/dot_general | solution.py:185
  33.8 2.3 %fusion.1 = f32[256,2048]{1,0:T(8,128)S(1)} fusion(f32[2048,256]{1,0:T(8,128)S(1)} %fusion.pre_ref, bf16[1,2048,2048]{2,1,0:T(8,128)(2,1)S(1)} %bitcast.83), kind=kOutput, calls=%fused_computation.8 | convolution fusion | flops 2148532224 | bytes 12582912 | tf_op jit(solution)/shard_map/dot_general | solution.py:191
  38.9 11.6 %collective-permute-done.14 = f32[128,1024]{1,0:T(8,128)S(1)} collective-permute-done((f32[128,1024]{1,0:T(8,128)S(1)}, f32[128,1024]{1,0:T(8,128)S(1)}, u32[]{:S(2)}, u32[]{:S(2)}) %collective-permute-start.14) | collective-permute-done | bytes 524320 | tf_op jit(solution)/shard_map/ppermute | solution.py:65
  50.6 1.7 %collective-permute-start.15 = (f32[128,512]{1,0:T(8,128)S(1)}, f32[128,512]{1,0:T(8,128)S(1)}, u32[]{:S(2)}, u32[]{:S(2)}) collective-permute-start(f32[128,512]{1,0:T(8,128)S(1)} %constant_dynamic-slice_fusion.2), channel_id=1, source_target_pairs={{0,2},{2,0},{4,6},{6,4},{8,10},{10,8},{12,14},{14,12},{1,3},{3,1},... | collective-permute-start | bytes 786440 | tf_op jit(solution)/shard_map/ppermute | solution.py:65
  53.0 5.2 %collective-permute-done.15 = f32[128,512]{1,0:T(8,128)S(1)} collective-permute-done((f32[128,512]{1,0:T(8,128)S(1)}, f32[128,512]{1,0:T(8,128)S(1)}, u32[]{:S(2)}, u32[]{:S(2)}) %collective-permute-start.15) | collective-permute-done | bytes 262176 | tf_op jit(solution)/shard_map/ppermute | solution.py:65
  58.3 1.9 %collective-permute-start.16 = (f32[128,256]{1,0:T(8,128)S(1)}, f32[128,256]{1,0:T(8,128)S(1)}, u32[]{:S(2)}, u32[]{:S(2)}) collective-permute-start(f32[128,256]{1,0:T(8,128)S(1)} %constant_dynamic-slice_fusion.1), channel_id=1, source_target_pairs={{0,8},{2,10},{4,12},{6,14},{8,0},{10,2},{12,4},{14,6},{1,9},{3,11}... | collective-permute-start | bytes 393224 | tf_op jit(solution)/shard_map/ppermute | solution.py:65
  60.2 2.0 %collective-permute-start.10 = (f32[128,256]{1,0:T(8,128)S(1)}, f32[128,256]{1,0:T(8,128)S(1)}, u32[]{:S(2)}, u32[]{:S(2)}) collective-permute-start(f32[128,256]{1,0:T(8,128)S(1)} %constant_dynamic-slice_fusion.7), channel_id=1, source_target_pairs={{0,8},{2,10},{4,12},{6,14},{8,0},{10,2},{12,4},{14,6},{1,9},{3,11}... | collective-permute-start | bytes 393224 | tf_op jit(solution)/shard_map/ppermute | solution.py:65
  62.2 7.6 %collective-permute-done.16 = f32[128,256]{1,0:T(8,128)S(1)} collective-permute-done((f32[128,256]{1,0:T(8,128)S(1)}, f32[128,256]{1,0:T(8,128)S(1)}, u32[]{:S(2)}, u32[]{:S(2)}) %collective-permute-start.16) | collective-permute-done | bytes 131104 | tf_op jit(solution)/shard_map/ppermute | solution.py:65
  70.0 1.7 %collective-permute-done.10 = f32[128,256]{1,0:T(8,128)S(1)} collective-permute-done((f32[128,256]{1,0:T(8,128)S(1)}, f32[128,256]{1,0:T(8,128)S(1)}, u32[]{:S(2)}, u32[]{:S(2)}) %collective-permute-start.10) | collective-permute-done | bytes 131104 | tf_op jit(solution)/shard_map/ppermute | solution.py:65
  73.0 2.4 %collective-permute-done.17 = bf16[128,256]{1,0:T(8,128)(2,1)S(1)} collective-permute-done((bf16[128,256]{1,0:T(8,128)(2,1)S(1)}, bf16[128,256]{1,0:T(8,128)(2,1)S(1)}, u32[]{:S(2)}, u32[]{:S(2)}) %collective-permute-start.17) | collective-permute-done | bytes 65568 | tf_op jit(solution)/shard_map/ppermute | solution.py:65
  75.5 2.3 %collective-permute-start.18 = (bf16[2,128,256]{2,1,0:T(8,128)(2,1)S(1)}, bf16[2,128,256]{2,1,0:T(8,128)(2,1)S(1)}, u32[]{:S(2)}, u32[]{:S(2)}) collective-permute-start(bf16[2,128,256]{2,1,0:T(8,128)(2,1)S(1)} %pad_maximum_fusion.4), channel_id=1, source_target_pairs={{0,2},{2,0},{4,6},{6,4},{8,10},{10,8},{12,14},{14,12},{1,3},{3,1},... | collective-permute-start | bytes 393224 | tf_op jit(solution)/shard_map/ppermute | solution.py:65
  78.0 2.8 %collective-permute-done.18 = bf16[2,128,256]{2,1,0:T(8,128)(2,1)S(1)} collective-permute-done((bf16[2,128,256]{2,1,0:T(8,128)(2,1)S(1)}, bf16[2,128,256]{2,1,0:T(8,128)(2,1)S(1)}, u32[]{:S(2)}, u32[]{:S(2)}) %collective-permute-start.18) | collective-permute-done | bytes 131104 | tf_op jit(solution)/shard_map/ppermute | solution.py:65
  80.9 3.3 %collective-permute-done.12 = bf16[2,128,256]{2,1,0:T(8,128)(2,1)S(1)} collective-permute-done((bf16[2,128,256]{2,1,0:T(8,128)(2,1)S(1)}, bf16[2,128,256]{2,1,0:T(8,128)(2,1)S(1)}, u32[]{:S(2)}, u32[]{:S(2)}) %collective-permute-start.12) | collective-permute-done | bytes 131104 | tf_op jit(solution)/shard_map/ppermute | solution.py:65
  85.5 1.8 %collective-permute-done.19 = bf16[2,2,128,256]{3,2,1,0:T(8,128)(2,1)S(1)} collective-permute-done((bf16[2,2,128,256]{3,2,1,0:T(8,128)(2,1)S(1)}, bf16[2,2,128,256]{3,2,1,0:T(8,128)(2,1)S(1)}, u32[]{:S(2)}, u32[]{:S(2)}) %collective-permute-start.19) | collective-permute-done | bytes 262176 | tf_op jit(solution)/shard_map/ppermute | solution.py:65
  87.4 3.2 %collective-permute-done.13 = bf16[2,2,128,256]{3,2,1,0:T(8,128)(2,1)S(1)} collective-permute-done((bf16[2,2,128,256]{3,2,1,0:T(8,128)(2,1)S(1)}, bf16[2,2,128,256]{3,2,1,0:T(8,128)(2,1)S(1)}, u32[]{:S(2)}, u32[]{:S(2)}) %collective-permute-start.13) | collective-permute-done | bytes 262176 | tf_op jit(solution)/shard_map/ppermute | solution.py:65
  93.4 29.4 %shard_map.130 = (bf16[2048,2048]{1,0:T(8,128)(2,1)}, bf16[2048,2048]{1,0:T(8,128)(2,1)}, bf16[2048,2048]{1,0:T(8,128)(2,1)}) custom-call(f32[2048,256]{1,0:T(8,128)} %copy-done, bf16[2048,256]{1,0:T(8,128)(2,1)} %bitcast.87, bf16[256,2048]{1,0:T(8,128)(2,1)} %copy-done.1, bf16[2048,2048]{1,0:T(8,128)(2,1)} %bitcast.81, bf16[2048,2048]{1,0:T(8,128)(2,1)} %bitcast.84, ...), custom_call_target="tpu_custom_call" | custom-call | tf_op jit(solution)/shard_map/pallas_call | solution.py:46
  (94 shorter events, 15.1 us)
Async XLA Ops:
  0.6 18.2 %collective-permute-start.4 = (bf16[128,256]{1,0:T(8,128)(2,1)}, bf16[128,256]{1,0:T(8,128)(2,1)S(1)}, u32[]{:S(2)}, u32[]{:S(2)}) collective-permute-start(bf16[128,256]{1,0:T(8,128)(2,1)} %param.11), channel_id=1, source_target_pairs={{0,10},{2,12},{4,14},{6,0},{8,2},{10,4},{12,6},{14,8},{1,11},{3,13... | collective-permute-start | bytes 196616 | tf_op jit(solution)/shard_map/ppermute | solution.py:102
  5.6 13.1 %collective-permute-start.3 = (bf16[128,256]{1,0:T(8,128)(2,1)}, bf16[128,256]{1,0:T(8,128)(2,1)S(1)}, u32[]{:S(2)}, u32[]{:S(2)}) collective-permute-start(bf16[128,256]{1,0:T(8,128)(2,1)} %param.11), channel_id=1, source_target_pairs={{0,8},{2,10},{4,12},{6,14},{8,0},{10,2},{12,4},{14,6},{1,9},{3,11}... | collective-permute-start | bytes 196616 | tf_op jit(solution)/shard_map/ppermute | solution.py:102
  6.0 12.8 %collective-permute-start.2 = (bf16[128,256]{1,0:T(8,128)(2,1)}, bf16[128,256]{1,0:T(8,128)(2,1)S(1)}, u32[]{:S(2)}, u32[]{:S(2)}) collective-permute-start(bf16[128,256]{1,0:T(8,128)(2,1)} %param.11), channel_id=1, source_target_pairs={{0,6},{2,8},{4,10},{6,12},{8,14},{10,0},{12,2},{14,4},{1,7},{3,9},... | collective-permute-start | bytes 196616 | tf_op jit(solution)/shard_map/ppermute | solution.py:102
  7.6 10.1 %collective-permute-start.1 = (bf16[128,256]{1,0:T(8,128)(2,1)}, bf16[128,256]{1,0:T(8,128)(2,1)S(1)}, u32[]{:S(2)}, u32[]{:S(2)}) collective-permute-start(bf16[128,256]{1,0:T(8,128)(2,1)} %param.11), channel_id=1, source_target_pairs={{0,4},{2,6},{4,8},{6,10},{8,12},{10,14},{12,0},{14,2},{1,5},{3,7},... | collective-permute-start | bytes 196616 | tf_op jit(solution)/shard_map/ppermute | solution.py:102
  10.1 7.3 %collective-permute-start = (bf16[128,256]{1,0:T(8,128)(2,1)}, bf16[128,256]{1,0:T(8,128)(2,1)S(1)}, u32[]{:S(2)}, u32[]{:S(2)}) collective-permute-start(bf16[128,256]{1,0:T(8,128)(2,1)} %param.11), channel_id=1, source_target_pairs={{0,2},{2,4},{4,6},{6,8},{8,10},{10,12},{12,14},{14,0},{1,3},{3,5},... | collective-permute-start | bytes 196616 | tf_op jit(solution)/shard_map/ppermute | solution.py:102
  11.6 11.6 %copy-start.2 = (f32[1,2048]{1,0:T(1,128)S(1)}, f32[1,2048]{1,0:T(1,128)}, u32[]{:S(2)}) copy-start(f32[1,2048]{1,0:T(1,128)} %param.17) | copy-start | bytes 24580
  12.5 10.7 %copy-start.4 = (s32[8]{0:T(128)S(1)}, s32[8]{0:T(128)}, u32[]{:S(2)}) copy-start(s32[8]{0:T(128)} %constant.95) | copy-start | bytes 100
  12.5 10.7 %copy-start.5 = (s32[8]{0:T(128)S(1)}, s32[8]{0:T(128)}, u32[]{:S(2)}) copy-start(s32[8]{0:T(128)} %constant.94) | copy-start | bytes 100
  12.5 10.8 %copy-start.3 = (s32[1,256]{1,0:T(1,128)S(1)}, s32[1,256]{1,0:T(1,128)}, u32[]{:S(2)}) copy-start(s32[1,256]{1,0:T(1,128)} %param.12) | copy-start | bytes 3076
  17.4 4.9 %collective-permute-start.6 = (bf16[128,256]{1,0:T(8,128)(2,1)}, bf16[128,256]{1,0:T(8,128)(2,1)S(1)}, u32[]{:S(2)}, u32[]{:S(2)}) collective-permute-start(bf16[128,256]{1,0:T(8,128)(2,1)} %param.11), channel_id=1, source_target_pairs={{0,14},{2,0},{4,2},{6,4},{8,6},{10,8},{12,10},{14,12},{1,15},{3,1}... | collective-permute-start | bytes 196616 | tf_op jit(solution)/shard_map/ppermute | solution.py:102
  17.8 4.5 %collective-permute-start.5 = (bf16[128,256]{1,0:T(8,128)(2,1)}, bf16[128,256]{1,0:T(8,128)(2,1)S(1)}, u32[]{:S(2)}, u32[]{:S(2)}) collective-permute-start(bf16[128,256]{1,0:T(8,128)(2,1)} %param.11), channel_id=1, source_target_pairs={{0,12},{2,14},{4,0},{6,2},{8,4},{10,6},{12,8},{14,10},{1,13},{3,15... | collective-permute-start | bytes 196616 | tf_op jit(solution)/shard_map/ppermute | solution.py:102
  23.1 2.0 %collective-permute-start.7 = (bf16[128,2048]{1,0:T(8,128)(2,1)S(1)}, bf16[128,2048]{1,0:T(8,128)(2,1)S(1)}, u32[]{:S(2)}, u32[]{:S(2)}) collective-permute-start(bf16[128,2048]{1,0:T(8,128)(2,1)S(1)} %bitcast.88), channel_id=1, source_target_pairs={{0,1},{1,0},{2,3},{3,2},{4,5},{5,4},{6,7},{7,6},{8,9},{9,8},{10,11... | collective-permute-start | bytes 1572872 | tf_op jit(solution)/shard_map/ppermute | solution.py:172
  36.5 14.0 %collective-permute-start.14 = (f32[128,1024]{1,0:T(8,128)S(1)}, f32[128,1024]{1,0:T(8,128)S(1)}, u32[]{:S(2)}, u32[]{:S(2)}) collective-permute-start(f32[128,1024]{1,0:T(8,128)S(1)} %constant_dynamic-slice_fusion.3), channel_id=1, source_target_pairs={{0,4},{2,6},{4,0},{6,2},{8,12},{10,14},{12,8},{14,10},{1,5},{3,7},... | collective-permute-start | bytes 1572872 | tf_op jit(solution)/shard_map/ppermute | solution.py:65
  37.5 14.8 %collective-permute-start.8 = (f32[128,1024]{1,0:T(8,128)S(1)}, f32[128,1024]{1,0:T(8,128)S(1)}, u32[]{:S(2)}, u32[]{:S(2)}) collective-permute-start(f32[128,1024]{1,0:T(8,128)S(1)} %constant_dynamic-slice_fusion.9), channel_id=1, source_target_pairs={{0,2},{2,0},{4,6},{6,4},{8,10},{10,8},{12,14},{14,12},{1,3},{3,1},... | collective-permute-start | bytes 1572872 | tf_op jit(solution)/shard_map/ppermute | solution.py:65
  50.6 7.6 %collective-permute-start.15 = (f32[128,512]{1,0:T(8,128)S(1)}, f32[128,512]{1,0:T(8,128)S(1)}, u32[]{:S(2)}, u32[]{:S(2)}) collective-permute-start(f32[128,512]{1,0:T(8,128)S(1)} %constant_dynamic-slice_fusion.2), channel_id=1, source_target_pairs={{0,2},{2,0},{4,6},{6,4},{8,10},{10,8},{12,14},{14,12},{1,3},{3,1},... | collective-permute-start | bytes 786440 | tf_op jit(solution)/shard_map/ppermute | solution.py:65
  52.5 7.7 %collective-permute-start.9 = (f32[128,512]{1,0:T(8,128)S(1)}, f32[128,512]{1,0:T(8,128)S(1)}, u32[]{:S(2)}, u32[]{:S(2)}) collective-permute-start(f32[128,512]{1,0:T(8,128)S(1)} %constant_dynamic-slice_fusion.8), channel_id=1, source_target_pairs={{0,4},{2,6},{4,0},{6,2},{8,12},{10,14},{12,8},{14,10},{1,5},{3,7},... | collective-permute-start | bytes 786440 | tf_op jit(solution)/shard_map/ppermute | solution.py:65
  58.3 11.6 %collective-permute-start.16 = (f32[128,256]{1,0:T(8,128)S(1)}, f32[128,256]{1,0:T(8,128)S(1)}, u32[]{:S(2)}, u32[]{:S(2)}) collective-permute-start(f32[128,256]{1,0:T(8,128)S(1)} %constant_dynamic-slice_fusion.1), channel_id=1, source_target_pairs={{0,8},{2,10},{4,12},{6,14},{8,0},{10,2},{12,4},{14,6},{1,9},{3,11}... | collective-permute-start | bytes 393224 | tf_op jit(solution)/shard_map/ppermute | solution.py:65
  60.2 11.5 %collective-permute-start.10 = (f32[128,256]{1,0:T(8,128)S(1)}, f32[128,256]{1,0:T(8,128)S(1)}, u32[]{:S(2)}, u32[]{:S(2)}) collective-permute-start(f32[128,256]{1,0:T(8,128)S(1)} %constant_dynamic-slice_fusion.7), channel_id=1, source_target_pairs={{0,8},{2,10},{4,12},{6,14},{8,0},{10,2},{12,4},{14,6},{1,9},{3,11}... | collective-permute-start | bytes 393224 | tf_op jit(solution)/shard_map/ppermute | solution.py:65
  69.9 5.5 %collective-permute-start.17 = (bf16[128,256]{1,0:T(8,128)(2,1)S(1)}, bf16[128,256]{1,0:T(8,128)(2,1)S(1)}, u32[]{:S(2)}, u32[]{:S(2)}) collective-permute-start(bf16[128,256]{1,0:T(8,128)(2,1)S(1)} %multiply_convert_fusion), channel_id=1, source_target_pairs={{0,8},{2,10},{4,12},{6,14},{8,0},{10,2},{12,4},{14,6},{1,9},{3,11}... | collective-permute-start | bytes 196616 | tf_op jit(solution)/shard_map/ppermute | solution.py:65
  71.8 6.1 %collective-permute-start.11 = (bf16[128,256]{1,0:T(8,128)(2,1)S(1)}, bf16[128,256]{1,0:T(8,128)(2,1)S(1)}, u32[]{:S(2)}, u32[]{:S(2)}) collective-permute-start(bf16[128,256]{1,0:T(8,128)(2,1)S(1)} %multiply_convert_fusion.1), channel_id=1, source_target_pairs={{0,8},{2,10},{4,12},{6,14},{8,0},{10,2},{12,4},{14,6},{1,9},{3,11}... | collective-permute-start | bytes 196616 | tf_op jit(solution)/shard_map/ppermute | solution.py:65
  75.5 5.3 %collective-permute-start.18 = (bf16[2,128,256]{2,1,0:T(8,128)(2,1)S(1)}, bf16[2,128,256]{2,1,0:T(8,128)(2,1)S(1)}, u32[]{:S(2)}, u32[]{:S(2)}) collective-permute-start(bf16[2,128,256]{2,1,0:T(8,128)(2,1)S(1)} %pad_maximum_fusion.4), channel_id=1, source_target_pairs={{0,2},{2,0},{4,6},{6,4},{8,10},{10,8},{12,14},{14,12},{1,3},{3,1},... | collective-permute-start | bytes 393224 | tf_op jit(solution)/shard_map/ppermute | solution.py:65
  77.9 6.3 %collective-permute-start.12 = (bf16[2,128,256]{2,1,0:T(8,128)(2,1)S(1)}, bf16[2,128,256]{2,1,0:T(8,128)(2,1)S(1)}, u32[]{:S(2)}, u32[]{:S(2)}) collective-permute-start(bf16[2,128,256]{2,1,0:T(8,128)(2,1)S(1)} %pad_maximum_fusion.3), channel_id=1, source_target_pairs={{0,4},{2,6},{4,0},{6,2},{8,12},{10,14},{12,8},{14,10},{1,5},{3,7},... | collective-permute-start | bytes 393224 | tf_op jit(solution)/shard_map/ppermute | solution.py:65
  80.8 6.4 %collective-permute-start.19 = (bf16[2,2,128,256]{3,2,1,0:T(8,128)(2,1)S(1)}, bf16[2,2,128,256]{3,2,1,0:T(8,128)(2,1)S(1)}, u32[]{:S(2)}, u32[]{:S(2)}) collective-permute-start(bf16[2,2,128,256]{3,2,1,0:T(8,128)(2,1)S(1)} %pad_maximum_fusion.2), channel_id=1, source_target_pairs={{0,4},{2,6},{4,0},{6,2},{8,12},{10,14},{12,8},{14,10},{1,5},{3,7},... | collective-permute-start | bytes 786440 | tf_op jit(solution)/shard_map/ppermute | solution.py:65
  84.2 6.4 %collective-permute-start.13 = (bf16[2,2,128,256]{3,2,1,0:T(8,128)(2,1)S(1)}, bf16[2,2,128,256]{3,2,1,0:T(8,128)(2,1)S(1)}, u32[]{:S(2)}, u32[]{:S(2)}) collective-permute-start(bf16[2,2,128,256]{3,2,1,0:T(8,128)(2,1)S(1)} %pad_maximum_fusion.1), channel_id=1, source_target_pairs={{0,2},{2,0},{4,6},{6,4},{8,10},{10,8},{12,14},{14,12},{1,3},{3,1},... | collective-permute-start | bytes 786440 | tf_op jit(solution)/shard_map/ppermute | solution.py:65
  (5 other events, 23.6 us)

commit v8 on v7

--- a/solution.py
+++ b/solution.py
@@ -15,11 +15,11 @@
 decay_rate = 0.1
 
 
-def _tail_kernel(pre_ref, err_ref, cen_ref, dec_ref, enc_ref, m1_ref, m2_ref, w_out, m1_out, m2_out):
-    dec = dec_ref[...]
-    dec32 = dec.astype(jnp.float32)
-    row_norm = jnp.sqrt(jnp.sum(dec32 * dec32, axis=1, keepdims=True) + 1e-06)
-    back_t = jnp.dot(dec, err_ref[...], preferred_element_type=jnp.float32)
+def _tail_kernel(
+    pre_ref, norm_ref, err_ref, cen_ref, dec_ref, enc_ref, m1_ref, m2_ref, w_out, m1_out, m2_out
+):
+    row_norm = norm_ref[...]
+    back_t = jnp.dot(dec_ref[...], err_ref[...], preferred_element_type=jnp.float32)
     tokens = err_ref.shape[1]
     d_pre = (
         jnp.where(pre_ref[...] > 0, 2.0 * back_t + sparsity * row_norm, 0.0) / tokens
@@ -27,16 +27,18 @@
     grad = jnp.dot(d_pre, cen_ref[...], preferred_element_type=jnp.float32)
     moment_one = beta_one * m1_ref[...].astype(jnp.float32) + (1.0 - beta_one) * grad
     moment_two = beta_two * m2_ref[...].astype(jnp.float32) + (1.0 - beta_two) * grad * grad
-    direction = (moment_one * (1.0 / corr_one)) / (
-        jnp.sqrt(moment_two * (1.0 / corr_two)) + adam_eps
+    direction = moment_one / (
+        jnp.sqrt(moment_two * (corr_one * corr_one / corr_two)) + corr_one * adam_eps
     )
     old = enc_ref[...].astype(jnp.float32)
-    w_out[...] = (old - rate_step * (direction + decay_rate * old)).astype(jnp.bfloat16)
+    w_out[...] = (old * (1.0 - rate_step * decay_rate) - rate_step * direction).astype(
+        jnp.bfloat16
+    )
     m1_out[...] = moment_one.astype(jnp.bfloat16)
     m2_out[...] = moment_two.astype(jnp.bfloat16)
 
 
-def tail(pre_t, error, centered, decoder, weight_in, first, second, tile=256):
+def tail(pre_t, row_norm, error, centered, decoder, weight_in, first, second, tile=256):
     n_lat, width = decoder.shape
     tokens = error.shape[0]
     error_t = error.T
@@ -48,6 +50,7 @@
         grid=(n_lat // tile,),
         in_specs=[
             pl.BlockSpec((tile, tokens), lambda i: (i, 0)),
+            pl.BlockSpec((tile, 1), lambda i: (i, 0)),
             pl.BlockSpec((width, tokens), lambda i: (0, 0)),
             whole,
             row_block,
@@ -58,7 +61,7 @@
         out_specs=[row_block, row_block, row_block],
         out_shape=[out, out, out],
         compiler_params=pltpu.CompilerParams(vmem_limit_bytes=56 * 1024 * 1024),
-    )(pre_t, error_t, centered, decoder, weight_in, first, second)
+    )(pre_t, row_norm, error_t, centered, decoder, weight_in, first, second)
 
 
 def _pair_swap(value, axis, mask, size):
@@ -206,8 +209,9 @@
         error_parts.append(stacked[jnp.array(_block_owners(lat_size, order))])
     error_blocks = jnp.concatenate(error_parts, axis=1)
     error = jnp.transpose(error_blocks, (1, 0, 2)).reshape(error_blocks.shape[1], -1)
+    row_norm = jnp.sqrt(jnp.sum(jnp.square(decoder.astype(jnp.float32)), axis=1) + 1e-06)
     updated, moment_one, moment_two = tail(
-        pre_t, error, centered, decoder, weight_in, first_moment[0], second_moment[0]
+        pre_t, row_norm[:, None], error, centered, decoder, weight_in, first_moment[0], second_moment[0]
     )
     return updated[None], moment_one[None], moment_two[None]
 

time: 123 us -> 128 us (1.041)
  other arithmetic: 2.82 us -> 7.89 us
  starting transfers between devices: 25.9 us -> 23.8 us
  local copies, waits for them, and re-layouts: 6.3 us -> 7.69 us
    reduce_sum x0 -> x1, other arithmetic: none -> 5.11 us  [local(): jnp.sum(jnp.square(decoder.astype(jnp.float32)), axis=1) + 1e-06]
    ppermute x12, starting transfers between devices: 13.5 us -> 9.27 us  [_pair_swap(): return lax.ppermute(value, axis, [(i, i ^ mask) for i in range(size)])]
    ppermute x12, waiting for transfers between devices: 39.8 us -> 43.8 us  [_pair_swap(): return lax.ppermute(value, axis, [(i, i ^ mask) for i in range(size)])]
    ppermute x7, waiting for transfers between devices: 6.9 us -> 4.18 us  [_direct_gather(): lax.ppermute(value, axis, [(i, (i + k) % size) for i in range(size)])]
    ppermute x7, starting transfers between devices: 12.3 us -> 14.5 us  [_direct_gather(): lax.ppermute(value, axis, [(i, (i + k) % size) for i in range(size)])]
    sqrt x0 -> x1, local copies, waits for them, and re-layouts: none -> 1.38 us  [local(): jnp.sqrt(jnp.sum(jnp.square(decoder.astype(jnp.float32)), axis=1) + 1e-06)]
  transfers between devices with their start and end apart: 20 -> 20, of which waited for: 12 -> 12; matrix products, arithmetic and copies ran while one was open for 3% -> 8% of each run, Pallas kernels for 0% -> 0%
where the time goes in v8:
time: 128 us
  waiting for transfers between devices  49.7 us (39%)
  Pallas kernels  28.6 us (22%)
  starting transfers between devices  23.8 us (19%)
  matrix products  8.83 us (7%)
  other arithmetic  7.89 us (6%)
  local copies, waits for them, and re-layouts  7.69 us (6%)
  between operations  1.34 us (1%)
    ppermute x12, waiting for transfers between devices, _pair_swap(): return lax.ppermute(value, axis, [(i, i ^ mask) for i in range(size)])  43.8 us
    pallas_call x1, Pallas kernels, tail(): pl.pallas_call(_tail_kernel, grid=(n_lat // tile,), in_specs=[pl.BlockSpe...  28.6 us
    ppermute x7, starting transfers between devices, _direct_gather(): lax.ppermute(value, axis, [(i, (i + k) % size) for i in range(size)])  14.5 us
    ppermute x12, starting transfers between devices, _pair_swap(): return lax.ppermute(value, axis, [(i, i ^ mask) for i in range(size)])  9.27 us
    dot_general x1, matrix products, local(): lax.dot_general(weight_in, centered, (((1,), (1,)), ((), ())), preferred_...  6.48 us
    reduce_sum x1, other arithmetic, local(): jnp.sum(jnp.square(decoder.astype(jnp.float32)), axis=1) + 1e-06  5.11 us
    ppermute x7, waiting for transfers between devices, _direct_gather(): lax.ppermute(value, axis, [(i, (i + k) % size) for i in range(size)])  4.18 us
  transfers between devices with their start and end apart: 20, of which 12 were waited for; matrix products, arithmetic and copies ran while one was open for 8% of the time, Pallas kernels for 0%

profile of v8, /device:TPU:0, one launch (start us, length us, event | category | flops | bytes accessed | tf_op | source)
XLA Modules:
  0.0 127.9 jit_solution(12920128006212300500)
XLA Ops:
  0.6 5.0 %collective-permute-start.4 = (bf16[128,256]{1,0:T(8,128)(2,1)}, bf16[128,256]{1,0:T(8,128)(2,1)S(1)}, u32[]{:S(2)}, u32[]{:S(2)}) collective-permute-start(bf16[128,256]{1,0:T(8,128)(2,1)} %param.11), channel_id=1, source_target_pairs={{0,10},{2,12},{4,14},{6,0},{8,2},{10,4},{12,6},{14,8},{1,11},{3,13... | collective-permute-start | bytes 196616 | tf_op jit(solution)/shard_map/ppermute | solution.py:105
  6.0 1.7 %collective-permute-start.2 = (bf16[128,256]{1,0:T(8,128)(2,1)}, bf16[128,256]{1,0:T(8,128)(2,1)S(1)}, u32[]{:S(2)}, u32[]{:S(2)}) collective-permute-start(bf16[128,256]{1,0:T(8,128)(2,1)} %param.11), channel_id=1, source_target_pairs={{0,6},{2,8},{4,10},{6,12},{8,14},{10,0},{12,2},{14,4},{1,7},{3,9},... | collective-permute-start | bytes 196616 | tf_op jit(solution)/shard_map/ppermute | solution.py:105
  7.6 2.5 %collective-permute-start.1 = (bf16[128,256]{1,0:T(8,128)(2,1)}, bf16[128,256]{1,0:T(8,128)(2,1)S(1)}, u32[]{:S(2)}, u32[]{:S(2)}) collective-permute-start(bf16[128,256]{1,0:T(8,128)(2,1)} %param.11), channel_id=1, source_target_pairs={{0,4},{2,6},{4,8},{6,10},{8,12},{10,14},{12,0},{14,2},{1,5},{3,7},... | collective-permute-start | bytes 196616 | tf_op jit(solution)/shard_map/ppermute | solution.py:105
  10.1 1.5 %collective-permute-start = (bf16[128,256]{1,0:T(8,128)(2,1)}, bf16[128,256]{1,0:T(8,128)(2,1)S(1)}, u32[]{:S(2)}, u32[]{:S(2)}) collective-permute-start(bf16[128,256]{1,0:T(8,128)(2,1)} %param.11), channel_id=1, source_target_pairs={{0,2},{2,4},{4,6},{6,8},{8,10},{10,12},{12,14},{14,0},{1,3},{3,5},... | collective-permute-start | bytes 196616 | tf_op jit(solution)/shard_map/ppermute | solution.py:105
  13.9 5.1 %multiply_reduce_fusion = f32[2048]{0:T(1024)S(1)} fusion(bf16[1,2048,2048]{2,1,0:T(8,128)(2,1)} %param.16), kind=kLoop, calls=%fused_computation.4 | loop fusion | flops 12580864 | bytes 8396800 | tf_op jit(solution)/shard_map/reduce_sum | solution.py:212
  20.4 3.3 %collective-permute-start.6 = (bf16[128,256]{1,0:T(8,128)(2,1)S(1)}, bf16[128,256]{1,0:T(8,128)(2,1)S(1)}, u32[]{:S(2)}, u32[]{:S(2)}) collective-permute-start(bf16[128,256]{1,0:T(8,128)(2,1)S(1)} %copy-done.2), channel_id=1, source_target_pairs={{0,14},{2,0},{4,2},{6,4},{8,6},{10,8},{12,10},{14,12},{1,15},{3,1}... | collective-permute-start | bytes 196616 | tf_op jit(solution)/shard_map/ppermute | solution.py:105
  24.1 4.2 %collective-permute-done.5 = bf16[128,256]{1,0:T(8,128)(2,1)S(1)} collective-permute-done((bf16[128,256]{1,0:T(8,128)(2,1)S(1)}, bf16[128,256]{1,0:T(8,128)(2,1)S(1)}, u32[]{:S(2)}, u32[]{:S(2)}) %collective-permute-start.5) | collective-permute-done | bytes 65568 | tf_op jit(solution)/shard_map/ppermute | solution.py:105
  29.2 1.8 %collective-permute-done.7 = bf16[128,2048]{1,0:T(8,128)(2,1)S(1)} collective-permute-done((bf16[128,2048]{1,0:T(8,128)(2,1)S(1)}, bf16[128,2048]{1,0:T(8,128)(2,1)S(1)}, u32[]{:S(2)}, u32[]{:S(2)}) %collective-permute-start.7) | collective-permute-done | bytes 524320 | tf_op jit(solution)/shard_map/ppermute | solution.py:175
  33.2 6.5 %fusion.pre_ref = f32[2048,256]{1,0:T(8,128)S(1)} fusion(bf16[256,2048]{1,0:T(8,128)(2,1)S(1)} %get-tuple-element.9.cen_ref, f32[2048]{0:T(1024)S(1)} %bitcast.105, bf16[1,2048,2048]{2,1,0:T(8,128)(2,1)} %param.14), kind=kOutput, calls=%fused_computation.6 | convolution fusion | flops 2148007936 | bytes 11542528 | tf_op jit(solution)/shard_map/dot_general | solution.py:188
  39.8 2.3 %fusion.1 = f32[256,2048]{1,0:T(8,128)S(1)} fusion(f32[2048,256]{1,0:T(8,128)S(1)} %fusion.pre_ref, bf16[1,2048,2048]{2,1,0:T(8,128)(2,1)S(1)} %bitcast.85), kind=kOutput, calls=%fused_computation.9 | convolution fusion | flops 2148532224 | bytes 12582912 | tf_op jit(solution)/shard_map/dot_general | solution.py:194
  42.7 13.7 %collective-permute-done.14 = f32[128,1024]{1,0:T(8,128)S(1)} collective-permute-done((f32[128,1024]{1,0:T(8,128)S(1)}, f32[128,1024]{1,0:T(8,128)S(1)}, u32[]{:S(2)}, u32[]{:S(2)}) %collective-permute-start.14) | collective-permute-done | bytes 524320 | tf_op jit(solution)/shard_map/ppermute | solution.py:68
  56.8 1.7 %collective-permute-start.9 = (f32[128,512]{1,0:T(8,128)S(1)}, f32[128,512]{1,0:T(8,128)S(1)}, u32[]{:S(2)}, u32[]{:S(2)}) collective-permute-start(f32[128,512]{1,0:T(8,128)S(1)} %constant_dynamic-slice_fusion.8), channel_id=1, source_target_pairs={{0,4},{2,6},{4,0},{6,2},{8,12},{10,14},{12,8},{14,10},{1,5},{3,7},... | collective-permute-start | bytes 786440 | tf_op jit(solution)/shard_map/ppermute | solution.py:68
  58.5 5.7 %collective-permute-done.15 = f32[128,512]{1,0:T(8,128)S(1)} collective-permute-done((f32[128,512]{1,0:T(8,128)S(1)}, f32[128,512]{1,0:T(8,128)S(1)}, u32[]{:S(2)}, u32[]{:S(2)}) %collective-permute-start.15) | collective-permute-done | bytes 262176 | tf_op jit(solution)/shard_map/ppermute | solution.py:68
  64.2 1.5 %collective-permute-start.16 = (f32[128,256]{1,0:T(8,128)S(1)}, f32[128,256]{1,0:T(8,128)S(1)}, u32[]{:S(2)}, u32[]{:S(2)}) collective-permute-start(f32[128,256]{1,0:T(8,128)S(1)} %constant_dynamic-slice_fusion.1), channel_id=1, source_target_pairs={{0,8},{2,10},{4,12},{6,14},{8,0},{10,2},{12,4},{14,6},{1,9},{3,11}... | collective-permute-start | bytes 393224 | tf_op jit(solution)/shard_map/ppermute | solution.py:68
  65.7 1.6 %collective-permute-start.10 = (f32[128,256]{1,0:T(8,128)S(1)}, f32[128,256]{1,0:T(8,128)S(1)}, u32[]{:S(2)}, u32[]{:S(2)}) collective-permute-start(f32[128,256]{1,0:T(8,128)S(1)} %constant_dynamic-slice_fusion.7), channel_id=1, source_target_pairs={{0,8},{2,10},{4,12},{6,14},{8,0},{10,2},{12,4},{14,6},{1,9},{3,11}... | collective-permute-start | bytes 393224 | tf_op jit(solution)/shard_map/ppermute | solution.py:68
  67.3 8.0 %collective-permute-done.16 = f32[128,256]{1,0:T(8,128)S(1)} collective-permute-done((f32[128,256]{1,0:T(8,128)S(1)}, f32[128,256]{1,0:T(8,128)S(1)}, u32[]{:S(2)}, u32[]{:S(2)}) %collective-permute-start.16) | collective-permute-done | bytes 131104 | tf_op jit(solution)/shard_map/ppermute | solution.py:68
  75.5 1.9 %collective-permute-done.10 = f32[128,256]{1,0:T(8,128)S(1)} collective-permute-done((f32[128,256]{1,0:T(8,128)S(1)}, f32[128,256]{1,0:T(8,128)S(1)}, u32[]{:S(2)}, u32[]{:S(2)}) %collective-permute-start.10) | collective-permute-done | bytes 131104 | tf_op jit(solution)/shard_map/ppermute | solution.py:68
  78.5 2.5 %collective-permute-done.17 = bf16[128,256]{1,0:T(8,128)(2,1)S(1)} collective-permute-done((bf16[128,256]{1,0:T(8,128)(2,1)S(1)}, bf16[128,256]{1,0:T(8,128)(2,1)S(1)}, u32[]{:S(2)}, u32[]{:S(2)}) %collective-permute-start.17) | collective-permute-done | bytes 65568 | tf_op jit(solution)/shard_map/ppermute | solution.py:68
  81.0 1.7 %collective-permute-start.18 = (bf16[2,128,256]{2,1,0:T(8,128)(2,1)S(1)}, bf16[2,128,256]{2,1,0:T(8,128)(2,1)S(1)}, u32[]{:S(2)}, u32[]{:S(2)}) collective-permute-start(bf16[2,128,256]{2,1,0:T(8,128)(2,1)S(1)} %pad_maximum_fusion.4), channel_id=1, source_target_pairs={{0,2},{2,0},{4,6},{6,4},{8,10},{10,8},{12,14},{14,12},{1,3},{3,1},... | collective-permute-start | bytes 393224 | tf_op jit(solution)/shard_map/ppermute | solution.py:68
  83.7 2.3 %collective-permute-done.18 = bf16[2,128,256]{2,1,0:T(8,128)(2,1)S(1)} collective-permute-done((bf16[2,128,256]{2,1,0:T(8,128)(2,1)S(1)}, bf16[2,128,256]{2,1,0:T(8,128)(2,1)S(1)}, u32[]{:S(2)}, u32[]{:S(2)}) %collective-permute-start.18) | collective-permute-done | bytes 131104 | tf_op jit(solution)/shard_map/ppermute | solution.py:68
  86.5 3.5 %collective-permute-done.12 = bf16[2,128,256]{2,1,0:T(8,128)(2,1)S(1)} collective-permute-done((bf16[2,128,256]{2,1,0:T(8,128)(2,1)S(1)}, bf16[2,128,256]{2,1,0:T(8,128)(2,1)S(1)}, u32[]{:S(2)}, u32[]{:S(2)}) %collective-permute-start.12) | collective-permute-done | bytes 131104 | tf_op jit(solution)/shard_map/ppermute | solution.py:68
  90.8 2.1 %collective-permute-done.19 = bf16[2,2,128,256]{3,2,1,0:T(8,128)(2,1)S(1)} collective-permute-done((bf16[2,2,128,256]{3,2,1,0:T(8,128)(2,1)S(1)}, bf16[2,2,128,256]{3,2,1,0:T(8,128)(2,1)S(1)}, u32[]{:S(2)}, u32[]{:S(2)}) %collective-permute-start.19) | collective-permute-done | bytes 262176 | tf_op jit(solution)/shard_map/ppermute | solution.py:68
  93.1 3.4 %collective-permute-done.13 = bf16[2,2,128,256]{3,2,1,0:T(8,128)(2,1)S(1)} collective-permute-done((bf16[2,2,128,256]{3,2,1,0:T(8,128)(2,1)S(1)}, bf16[2,2,128,256]{3,2,1,0:T(8,128)(2,1)S(1)}, u32[]{:S(2)}, u32[]{:S(2)}) %collective-permute-start.13) | collective-permute-done | bytes 262176 | tf_op jit(solution)/shard_map/ppermute | solution.py:68
  99.2 28.6 %shard_map.130 = (bf16[2048,2048]{1,0:T(8,128)(2,1)}, bf16[2048,2048]{1,0:T(8,128)(2,1)}, bf16[2048,2048]{1,0:T(8,128)(2,1)}) custom-call(f32[2048,256]{1,0:T(8,128)} %copy-done, f32[2048,1]{1,0:T(8,128)} %copy.21.norm_ref, bf16[2048,256]{1,0:T(8,128)(2,1)} %bitcast.89, bf16[256,2048]{1,0:T(8,128)(2,1)} %copy-done.1, bf16[2048,2048]{1,0:T(8,128)(2,1)} %bitcast.83, ...), custom_call_target="tpu_custom_call" | custom-call | tf_op jit(solution)/shard_map/pallas_call | solution.py:48
  (99 shorter events, 14.6 us)
Async XLA Ops:
  0.6 23.4 %collective-permute-start.4 = (bf16[128,256]{1,0:T(8,128)(2,1)}, bf16[128,256]{1,0:T(8,128)(2,1)S(1)}, u32[]{:S(2)}, u32[]{:S(2)}) collective-permute-start(bf16[128,256]{1,0:T(8,128)(2,1)} %param.11), channel_id=1, source_target_pairs={{0,10},{2,12},{4,14},{6,0},{8,2},{10,4},{12,6},{14,8},{1,11},{3,13... | collective-permute-start | bytes 196616 | tf_op jit(solution)/shard_map/ppermute | solution.py:105
  5.6 18.4 %collective-permute-start.3 = (bf16[128,256]{1,0:T(8,128)(2,1)}, bf16[128,256]{1,0:T(8,128)(2,1)S(1)}, u32[]{:S(2)}, u32[]{:S(2)}) collective-permute-start(bf16[128,256]{1,0:T(8,128)(2,1)} %param.11), channel_id=1, source_target_pairs={{0,8},{2,10},{4,12},{6,14},{8,0},{10,2},{12,4},{14,6},{1,9},{3,11}... | collective-permute-start | bytes 196616 | tf_op jit(solution)/shard_map/ppermute | solution.py:105
  6.0 18.0 %collective-permute-start.2 = (bf16[128,256]{1,0:T(8,128)(2,1)}, bf16[128,256]{1,0:T(8,128)(2,1)S(1)}, u32[]{:S(2)}, u32[]{:S(2)}) collective-permute-start(bf16[128,256]{1,0:T(8,128)(2,1)} %param.11), channel_id=1, source_target_pairs={{0,6},{2,8},{4,10},{6,12},{8,14},{10,0},{12,2},{14,4},{1,7},{3,9},... | collective-permute-start | bytes 196616 | tf_op jit(solution)/shard_map/ppermute | solution.py:105
  7.6 16.1 %collective-permute-start.1 = (bf16[128,256]{1,0:T(8,128)(2,1)}, bf16[128,256]{1,0:T(8,128)(2,1)S(1)}, u32[]{:S(2)}, u32[]{:S(2)}) collective-permute-start(bf16[128,256]{1,0:T(8,128)(2,1)} %param.11), channel_id=1, source_target_pairs={{0,4},{2,6},{4,8},{6,10},{8,12},{10,14},{12,0},{14,2},{1,5},{3,7},... | collective-permute-start | bytes 196616 | tf_op jit(solution)/shard_map/ppermute | solution.py:105
  10.1 10.3 %collective-permute-start = (bf16[128,256]{1,0:T(8,128)(2,1)}, bf16[128,256]{1,0:T(8,128)(2,1)S(1)}, u32[]{:S(2)}, u32[]{:S(2)}) collective-permute-start(bf16[128,256]{1,0:T(8,128)(2,1)} %param.11), channel_id=1, source_target_pairs={{0,2},{2,4},{4,6},{6,8},{8,10},{10,12},{12,14},{14,0},{1,3},{3,5},... | collective-permute-start | bytes 196616 | tf_op jit(solution)/shard_map/ppermute | solution.py:105
  20.4 8.7 %copy-start.3 = (f32[1,2048]{1,0:T(1,128)S(1)}, f32[1,2048]{1,0:T(1,128)}, u32[]{:S(2)}) copy-start(f32[1,2048]{1,0:T(1,128)} %param.17) | copy-start | bytes 24580
  20.4 8.8 %copy-start.5 = (s32[8]{0:T(128)S(1)}, s32[8]{0:T(128)}, u32[]{:S(2)}) copy-start(s32[8]{0:T(128)} %constant.98) | copy-start | bytes 100
  20.4 8.8 %copy-start.6 = (s32[8]{0:T(128)S(1)}, s32[8]{0:T(128)}, u32[]{:S(2)}) copy-start(s32[8]{0:T(128)} %constant.97) | copy-start | bytes 100
  20.4 8.8 %copy-start.4 = (s32[1,256]{1,0:T(1,128)S(1)}, s32[1,256]{1,0:T(1,128)}, u32[]{:S(2)}) copy-start(s32[1,256]{1,0:T(1,128)} %param.12) | copy-start | bytes 3076
  20.4 7.8 %collective-permute-start.6 = (bf16[128,256]{1,0:T(8,128)(2,1)S(1)}, bf16[128,256]{1,0:T(8,128)(2,1)S(1)}, u32[]{:S(2)}, u32[]{:S(2)}) collective-permute-start(bf16[128,256]{1,0:T(8,128)(2,1)S(1)} %copy-done.2), channel_id=1, source_target_pairs={{0,14},{2,0},{4,2},{6,4},{8,6},{10,8},{12,10},{14,12},{1,15},{3,1}... | collective-permute-start | bytes 196616 | tf_op jit(solution)/shard_map/ppermute | solution.py:105
  23.7 4.5 %collective-permute-start.5 = (bf16[128,256]{1,0:T(8,128)(2,1)S(1)}, bf16[128,256]{1,0:T(8,128)(2,1)S(1)}, u32[]{:S(2)}, u32[]{:S(2)}) collective-permute-start(bf16[128,256]{1,0:T(8,128)(2,1)S(1)} %copy-done.2), channel_id=1, source_target_pairs={{0,12},{2,14},{4,0},{6,2},{8,4},{10,6},{12,8},{14,10},{1,13},{3,15... | collective-permute-start | bytes 196616 | tf_op jit(solution)/shard_map/ppermute | solution.py:105
  29.0 2.0 %collective-permute-start.7 = (bf16[128,2048]{1,0:T(8,128)(2,1)S(1)}, bf16[128,2048]{1,0:T(8,128)(2,1)S(1)}, u32[]{:S(2)}, u32[]{:S(2)}) collective-permute-start(bf16[128,2048]{1,0:T(8,128)(2,1)S(1)} %bitcast.90), channel_id=1, source_target_pairs={{0,1},{1,0},{2,3},{3,2},{4,5},{5,4},{6,7},{7,6},{8,9},{9,8},{10,11... | collective-permute-start | bytes 1572872 | tf_op jit(solution)/shard_map/ppermute | solution.py:175
  42.4 14.0 %collective-permute-start.14 = (f32[128,1024]{1,0:T(8,128)S(1)}, f32[128,1024]{1,0:T(8,128)S(1)}, u32[]{:S(2)}, u32[]{:S(2)}) collective-permute-start(f32[128,1024]{1,0:T(8,128)S(1)} %constant_dynamic-slice_fusion.3), channel_id=1, source_target_pairs={{0,4},{2,6},{4,0},{6,2},{8,12},{10,14},{12,8},{14,10},{1,5},{3,7},... | collective-permute-start | bytes 1572872 | tf_op jit(solution)/shard_map/ppermute | solution.py:68
  42.5 14.1 %collective-permute-start.8 = (f32[128,1024]{1,0:T(8,128)S(1)}, f32[128,1024]{1,0:T(8,128)S(1)}, u32[]{:S(2)}, u32[]{:S(2)}) collective-permute-start(f32[128,1024]{1,0:T(8,128)S(1)} %constant_dynamic-slice_fusion.9), channel_id=1, source_target_pairs={{0,2},{2,0},{4,6},{6,4},{8,10},{10,8},{12,14},{14,12},{1,3},{3,1},... | collective-permute-start | bytes 1572872 | tf_op jit(solution)/shard_map/ppermute | solution.py:68
  56.5 7.6 %collective-permute-start.15 = (f32[128,512]{1,0:T(8,128)S(1)}, f32[128,512]{1,0:T(8,128)S(1)}, u32[]{:S(2)}, u32[]{:S(2)}) collective-permute-start(f32[128,512]{1,0:T(8,128)S(1)} %constant_dynamic-slice_fusion.2), channel_id=1, source_target_pairs={{0,2},{2,0},{4,6},{6,4},{8,10},{10,8},{12,14},{14,12},{1,3},{3,1},... | collective-permute-start | bytes 786440 | tf_op jit(solution)/shard_map/ppermute | solution.py:68
  56.8 8.9 %collective-permute-start.9 = (f32[128,512]{1,0:T(8,128)S(1)}, f32[128,512]{1,0:T(8,128)S(1)}, u32[]{:S(2)}, u32[]{:S(2)}) collective-permute-start(f32[128,512]{1,0:T(8,128)S(1)} %constant_dynamic-slice_fusion.8), channel_id=1, source_target_pairs={{0,4},{2,6},{4,0},{6,2},{8,12},{10,14},{12,8},{14,10},{1,5},{3,7},... | collective-permute-start | bytes 786440 | tf_op jit(solution)/shard_map/ppermute | solution.py:68
  64.2 11.1 %collective-permute-start.16 = (f32[128,256]{1,0:T(8,128)S(1)}, f32[128,256]{1,0:T(8,128)S(1)}, u32[]{:S(2)}, u32[]{:S(2)}) collective-permute-start(f32[128,256]{1,0:T(8,128)S(1)} %constant_dynamic-slice_fusion.1), channel_id=1, source_target_pairs={{0,8},{2,10},{4,12},{6,14},{8,0},{10,2},{12,4},{14,6},{1,9},{3,11}... | collective-permute-start | bytes 393224 | tf_op jit(solution)/shard_map/ppermute | solution.py:68
  65.7 11.7 %collective-permute-start.10 = (f32[128,256]{1,0:T(8,128)S(1)}, f32[128,256]{1,0:T(8,128)S(1)}, u32[]{:S(2)}, u32[]{:S(2)}) collective-permute-start(f32[128,256]{1,0:T(8,128)S(1)} %constant_dynamic-slice_fusion.7), channel_id=1, source_target_pairs={{0,8},{2,10},{4,12},{6,14},{8,0},{10,2},{12,4},{14,6},{1,9},{3,11}... | collective-permute-start | bytes 393224 | tf_op jit(solution)/shard_map/ppermute | solution.py:68
  75.4 5.6 %collective-permute-start.17 = (bf16[128,256]{1,0:T(8,128)(2,1)S(1)}, bf16[128,256]{1,0:T(8,128)(2,1)S(1)}, u32[]{:S(2)}, u32[]{:S(2)}) collective-permute-start(bf16[128,256]{1,0:T(8,128)(2,1)S(1)} %multiply_convert_fusion), channel_id=1, source_target_pairs={{0,8},{2,10},{4,12},{6,14},{8,0},{10,2},{12,4},{14,6},{1,9},{3,11}... | collective-permute-start | bytes 196616 | tf_op jit(solution)/shard_map/ppermute | solution.py:68
  77.4 6.0 %collective-permute-start.11 = (bf16[128,256]{1,0:T(8,128)(2,1)S(1)}, bf16[128,256]{1,0:T(8,128)(2,1)S(1)}, u32[]{:S(2)}, u32[]{:S(2)}) collective-permute-start(bf16[128,256]{1,0:T(8,128)(2,1)S(1)} %multiply_convert_fusion.1), channel_id=1, source_target_pairs={{0,8},{2,10},{4,12},{6,14},{8,0},{10,2},{12,4},{14,6},{1,9},{3,11}... | collective-permute-start | bytes 196616 | tf_op jit(solution)/shard_map/ppermute | solution.py:68
  81.0 5.0 %collective-permute-start.18 = (bf16[2,128,256]{2,1,0:T(8,128)(2,1)S(1)}, bf16[2,128,256]{2,1,0:T(8,128)(2,1)S(1)}, u32[]{:S(2)}, u32[]{:S(2)}) collective-permute-start(bf16[2,128,256]{2,1,0:T(8,128)(2,1)S(1)} %pad_maximum_fusion.4), channel_id=1, source_target_pairs={{0,2},{2,0},{4,6},{6,4},{8,10},{10,8},{12,14},{14,12},{1,3},{3,1},... | collective-permute-start | bytes 393224 | tf_op jit(solution)/shard_map/ppermute | solution.py:68
  83.5 6.5 %collective-permute-start.12 = (bf16[2,128,256]{2,1,0:T(8,128)(2,1)S(1)}, bf16[2,128,256]{2,1,0:T(8,128)(2,1)S(1)}, u32[]{:S(2)}, u32[]{:S(2)}) collective-permute-start(bf16[2,128,256]{2,1,0:T(8,128)(2,1)S(1)} %pad_maximum_fusion.3), channel_id=1, source_target_pairs={{0,4},{2,6},{4,0},{6,2},{8,12},{10,14},{12,8},{14,10},{1,5},{3,7},... | collective-permute-start | bytes 393224 | tf_op jit(solution)/shard_map/ppermute | solution.py:68
  86.1 6.8 %collective-permute-start.19 = (bf16[2,2,128,256]{3,2,1,0:T(8,128)(2,1)S(1)}, bf16[2,2,128,256]{3,2,1,0:T(8,128)(2,1)S(1)}, u32[]{:S(2)}, u32[]{:S(2)}) collective-permute-start(bf16[2,2,128,256]{3,2,1,0:T(8,128)(2,1)S(1)} %pad_maximum_fusion.2), channel_id=1, source_target_pairs={{0,4},{2,6},{4,0},{6,2},{8,12},{10,14},{12,8},{14,10},{1,5},{3,7},... | collective-permute-start | bytes 786440 | tf_op jit(solution)/shard_map/ppermute | solution.py:68
  90.0 6.4 %collective-permute-start.13 = (bf16[2,2,128,256]{3,2,1,0:T(8,128)(2,1)S(1)}, bf16[2,2,128,256]{3,2,1,0:T(8,128)(2,1)S(1)}, u32[]{:S(2)}, u32[]{:S(2)}) collective-permute-start(bf16[2,2,128,256]{3,2,1,0:T(8,128)(2,1)S(1)} %pad_maximum_fusion.1), channel_id=1, source_target_pairs={{0,2},{2,0},{4,6},{6,4},{8,10},{10,8},{12,14},{14,12},{1,3},{3,1},... | collective-permute-start | bytes 786440 | tf_op jit(solution)/shard_map/ppermute | solution.py:68
  (6 other events, 30.1 us)

commit v9 on v7

--- a/solution.py
+++ b/solution.py
@@ -15,7 +15,9 @@
 decay_rate = 0.1
 
 
-def _tail_kernel(pre_ref, err_ref, cen_ref, dec_ref, enc_ref, m1_ref, m2_ref, w_out, m1_out, m2_out):
+def _tail_kernel(
+    pre_ref, err_ref, cen_ref, dec_ref, enc_ref, m1_ref, m2_ref, w_out, m1_out, m2_out
+):
     dec = dec_ref[...]
     dec32 = dec.astype(jnp.float32)
     row_norm = jnp.sqrt(jnp.sum(dec32 * dec32, axis=1, keepdims=True) + 1e-06)
@@ -27,11 +29,13 @@
     grad = jnp.dot(d_pre, cen_ref[...], preferred_element_type=jnp.float32)
     moment_one = beta_one * m1_ref[...].astype(jnp.float32) + (1.0 - beta_one) * grad
     moment_two = beta_two * m2_ref[...].astype(jnp.float32) + (1.0 - beta_two) * grad * grad
-    direction = (moment_one * (1.0 / corr_one)) / (
-        jnp.sqrt(moment_two * (1.0 / corr_two)) + adam_eps
+    direction = moment_one / (
+        jnp.sqrt(moment_two * (corr_one * corr_one / corr_two)) + corr_one * adam_eps
     )
     old = enc_ref[...].astype(jnp.float32)
-    w_out[...] = (old - rate_step * (direction + decay_rate * old)).astype(jnp.bfloat16)
+    w_out[...] = (old * (1.0 - rate_step * decay_rate) - rate_step * direction).astype(
+        jnp.bfloat16
+    )
     m1_out[...] = moment_one.astype(jnp.bfloat16)
     m2_out[...] = moment_two.astype(jnp.bfloat16)
 
@@ -164,10 +168,8 @@
 ):
     lat_size = LAT_SIZE[0]
     first, second = _orders(lat_size)
-    if lat_size <= 8:
-        act_blocks = _direct_gather(activations, "lat", lat_size)
-    else:
-        act_blocks = _doubling_gather(activations, "lat", lat_size, first[::-1])
+    copies = jnp.broadcast_to(activations[None], (lat_size,) + activations.shape)
+    act_blocks = lax.all_to_all(copies, "lat", 0, 0, tiled=True)
     half_rows = jnp.transpose(act_blocks, (1, 0, 2)).reshape(activations.shape[0], -1)
     other_rows = lax.ppermute(half_rows, "seed", [(0, 1), (1, 0)])
     seed_first = lax.axis_index("seed") == 0

time: 123 us -> 123 us (level)
  waiting for transfers between devices: 48.5 us -> 59.1 us
  starting transfers between devices: 25.9 us -> 16.3 us
    all_to_all x0 -> x1, waiting for transfers between devices: none -> 13.1 us  [local(): act_blocks = lax.all_to_all(copies, 'lat', 0, 0, tiled=True)]
    ppermute x7 -> x0, starting transfers between devices: 12.3 us -> none  [_direct_gather(): lax.ppermute(value, axis, [(i, (i + k) % size) for i in range(size)])]
    all_to_all x0 -> x1, starting transfers between devices: none -> 7.25 us  [local(): act_blocks = lax.all_to_all(copies, 'lat', 0, 0, tiled=True)]
    ppermute x7 -> x0, waiting for transfers between devices: 6.9 us -> none  [_direct_gather(): lax.ppermute(value, axis, [(i, (i + k) % size) for i in range(size)])]
    ppermute x12, waiting for transfers between devices: 39.8 us -> 44.2 us  [_pair_swap(): return lax.ppermute(value, axis, [(i, i ^ mask) for i in range(size)])]
    ppermute x12, starting transfers between devices: 13.5 us -> 8.98 us  [_pair_swap(): return lax.ppermute(value, axis, [(i, i ^ mask) for i in range(size)])]
    broadcast_in_dim x0 -> x1, local copies, waits for them, and re-layouts: none -> 1.68 us  [local(): jnp.broadcast_to(activations[None], (lat_size,) + activations.shape)]
  transfers between devices with their start and end apart: 20 -> 14, of which waited for: 12 -> 13; matrix products, arithmetic and copies ran while one was open for 3% -> 2% of each run, Pallas kernels for 0% -> 0%
where the time goes in v9:
time: 123 us
  waiting for transfers between devices  59.1 us (48%)
  Pallas kernels  28.6 us (23%)
  starting transfers between devices  16.3 us (13%)
  matrix products  8.83 us (7%)
  local copies, waits for them, and re-layouts  6.49 us (5%)
  other arithmetic  2.62 us (2%)
    ppermute x12, waiting for transfers between devices, _pair_swap(): return lax.ppermute(value, axis, [(i, i ^ mask) for i in range(size)])  44.2 us
    pallas_call x1, Pallas kernels, tail(): pl.pallas_call(_tail_kernel, grid=(n_lat // tile,), in_specs=[pl.BlockSpe...  28.6 us
    all_to_all x1, waiting for transfers between devices, local(): act_blocks = lax.all_to_all(copies, 'lat', 0, 0, tiled=True)  13.1 us
    ppermute x12, starting transfers between devices, _pair_swap(): return lax.ppermute(value, axis, [(i, i ^ mask) for i in range(size)])  8.98 us
    all_to_all x1, starting transfers between devices, local(): act_blocks = lax.all_to_all(copies, 'lat', 0, 0, tiled=True)  7.25 us
    dot_general x1, matrix products, local(): lax.dot_general(weight_in, centered, (((1,), (1,)), ((), ())), preferred_...  6.48 us
  transfers between devices with their start and end apart: 14, of which 13 were waited for; matrix products, arithmetic and copies ran while one was open for 2% of the time, Pallas kernels for 0%

profile of v9, /device:TPU:0, one launch (start us, length us, event | category | flops | bytes accessed | tf_op | source)
XLA Modules:
  0.0 123.1 jit_solution(4939435453544729522)
XLA Ops:
  0.7 1.7 %broadcast_in_dim.36 = bf16[8,128,256]{2,1,0:T(8,128)(2,1)} broadcast(bf16[128,256]{1,0:T(8,128)(2,1)} %param.11), dimensions={1,2} | broadcast | bytes 589824 | tf_op jit(solution)/shard_map/broadcast_in_dim | solution.py:171
  2.4 7.3 %all-to-all-start = ((bf16[8,128,256]{2,1,0:T(8,128)(2,1)}), bf16[8,128,256]{2,1,0:T(8,128)(2,1)S(1)}, u32[]{:S(2)}, u32[]{:S(2)}) async-start(bf16[8,128,256]{2,1,0:T(8,128)(2,1)} %broadcast_in_dim.36), calls=%async_computation | async-start | bytes 1048576 | tf_op jit(solution)/shard_map/all_to_all | solution.py:172
  11.0 13.1 %all-to-all-done = bf16[8,128,256]{2,1,0:T(8,128)(2,1)S(1)} async-done(((bf16[8,128,256]{2,1,0:T(8,128)(2,1)}), bf16[8,128,256]{2,1,0:T(8,128)(2,1)S(1)}, u32[]{:S(2)}, u32[]{:S(2)}) %all-to-all-start) | async-done | bytes 524320 | tf_op jit(solution)/shard_map/all_to_all | solution.py:172
  24.3 1.8 %collective-permute-done = bf16[128,2048]{1,0:T(8,128)(2,1)S(1)} collective-permute-done((bf16[128,2048]{1,0:T(8,128)(2,1)S(1)}, bf16[128,2048]{1,0:T(8,128)(2,1)S(1)}, u32[]{:S(2)}, u32[]{:S(2)}) %collective-permute-start) | collective-permute-done | bytes 524320 | tf_op jit(solution)/shard_map/ppermute | solution.py:174
  26.3 1.4 %gather_fusion = bf16[256,2048]{1,0:T(8,128)(2,1)S(1)} fusion(bf16[256,2048]{1,0:T(8,128)(2,1)S(1)} %pad_maximum_fusion, s32[1024]{0:T(1024)S(1)} %pad_clamp_fusion.2), kind=kCustom, calls=%fused_computation | custom fusion | bytes 2098176 | tf_op jit(solution)/shard_map/jit(_take)/gather | solution.py:181
  28.4 6.5 %fusion.pre_ref = f32[2048,256]{1,0:T(8,128)S(1)} fusion(bf16[256,2048]{1,0:T(8,128)(2,1)S(1)} %get-tuple-element.9.cen_ref, f32[2048]{0:T(1024)S(1)} %bitcast.84, bf16[1,2048,2048]{2,1,0:T(8,128)(2,1)} %param.14), kind=kOutput, calls=%fused_computation.4 | convolution fusion | flops 2148007936 | bytes 11542528 | tf_op jit(solution)/shard_map/dot_general | solution.py:187
  34.9 2.3 %fusion.1 = f32[256,2048]{1,0:T(8,128)S(1)} fusion(f32[2048,256]{1,0:T(8,128)S(1)} %fusion.pre_ref, bf16[1,2048,2048]{2,1,0:T(8,128)(2,1)S(1)} %bitcast.64), kind=kOutput, calls=%fused_computation.7 | convolution fusion | flops 2148532224 | bytes 12582912 | tf_op jit(solution)/shard_map/dot_general | solution.py:193
  39.3 12.3 %collective-permute-done.7 = f32[128,1024]{1,0:T(8,128)S(1)} collective-permute-done((f32[128,1024]{1,0:T(8,128)S(1)}, f32[128,1024]{1,0:T(8,128)S(1)}, u32[]{:S(2)}, u32[]{:S(2)}) %collective-permute-start.7) | collective-permute-done | bytes 524320 | tf_op jit(solution)/shard_map/ppermute | solution.py:69
  51.7 1.5 %collective-permute-start.8 = (f32[128,512]{1,0:T(8,128)S(1)}, f32[128,512]{1,0:T(8,128)S(1)}, u32[]{:S(2)}, u32[]{:S(2)}) collective-permute-start(f32[128,512]{1,0:T(8,128)S(1)} %constant_dynamic-slice_fusion.1), channel_id=1, source_target_pairs={{0,2},{2,0},{4,6},{6,4},{8,10},{10,8},{12,14},{14,12},{1,3},{3,1},... | collective-permute-start | bytes 786440 | tf_op jit(solution)/shard_map/ppermute | solution.py:69
  53.7 5.6 %collective-permute-done.8 = f32[128,512]{1,0:T(8,128)S(1)} collective-permute-done((f32[128,512]{1,0:T(8,128)S(1)}, f32[128,512]{1,0:T(8,128)S(1)}, u32[]{:S(2)}, u32[]{:S(2)}) %collective-permute-start.8) | collective-permute-done | bytes 262176 | tf_op jit(solution)/shard_map/ppermute | solution.py:69
  59.7 0.9 collective-permute-done.2
  60.7 1.8 %collective-permute-start.3 = (f32[128,256]{1,0:T(8,128)S(1)}, f32[128,256]{1,0:T(8,128)S(1)}, u32[]{:S(2)}, u32[]{:S(2)}) collective-permute-start(f32[128,256]{1,0:T(8,128)S(1)} %constant_dynamic-slice_fusion.7), channel_id=1, source_target_pairs={{0,8},{2,10},{4,12},{6,14},{8,0},{10,2},{12,4},{14,6},{1,9},{3,11}... | collective-permute-start | bytes 393224 | tf_op jit(solution)/shard_map/ppermute | solution.py:69
  62.5 7.5 %collective-permute-done.9 = f32[128,256]{1,0:T(8,128)S(1)} collective-permute-done((f32[128,256]{1,0:T(8,128)S(1)}, f32[128,256]{1,0:T(8,128)S(1)}, u32[]{:S(2)}, u32[]{:S(2)}) %collective-permute-start.9) | collective-permute-done | bytes 131104 | tf_op jit(solution)/shard_map/ppermute | solution.py:69
  70.1 3.1 %collective-permute-done.3 = f32[128,256]{1,0:T(8,128)S(1)} collective-permute-done((f32[128,256]{1,0:T(8,128)S(1)}, f32[128,256]{1,0:T(8,128)S(1)}, u32[]{:S(2)}, u32[]{:S(2)}) %collective-permute-start.3) | collective-permute-done | bytes 131104 | tf_op jit(solution)/shard_map/ppermute | solution.py:69
  73.4 2.6 %collective-permute-done.10 = bf16[128,256]{1,0:T(8,128)(2,1)S(1)} collective-permute-done((bf16[128,256]{1,0:T(8,128)(2,1)S(1)}, bf16[128,256]{1,0:T(8,128)(2,1)S(1)}, u32[]{:S(2)}, u32[]{:S(2)}) %collective-permute-start.10) | collective-permute-done | bytes 65568 | tf_op jit(solution)/shard_map/ppermute | solution.py:69
  76.1 1.5 %collective-permute-start.11 = (bf16[2,128,256]{2,1,0:T(8,128)(2,1)S(1)}, bf16[2,128,256]{2,1,0:T(8,128)(2,1)S(1)}, u32[]{:S(2)}, u32[]{:S(2)}) collective-permute-start(bf16[2,128,256]{2,1,0:T(8,128)(2,1)S(1)} %pad_maximum_fusion.4), channel_id=1, source_target_pairs={{0,2},{2,0},{4,6},{6,4},{8,10},{10,8},{12,14},{14,12},{1,3},{3,1},... | collective-permute-start | bytes 393224 | tf_op jit(solution)/shard_map/ppermute | solution.py:69
  77.6 1.1 collective-permute-done.4
  78.8 2.3 %collective-permute-done.11 = bf16[2,128,256]{2,1,0:T(8,128)(2,1)S(1)} collective-permute-done((bf16[2,128,256]{2,1,0:T(8,128)(2,1)S(1)}, bf16[2,128,256]{2,1,0:T(8,128)(2,1)S(1)}, u32[]{:S(2)}, u32[]{:S(2)}) %collective-permute-start.11) | collective-permute-done | bytes 131104 | tf_op jit(solution)/shard_map/ppermute | solution.py:69
  81.2 4.0 %collective-permute-done.5 = bf16[2,128,256]{2,1,0:T(8,128)(2,1)S(1)} collective-permute-done((bf16[2,128,256]{2,1,0:T(8,128)(2,1)S(1)}, bf16[2,128,256]{2,1,0:T(8,128)(2,1)S(1)}, u32[]{:S(2)}, u32[]{:S(2)}) %collective-permute-start.5) | collective-permute-done | bytes 131104 | tf_op jit(solution)/shard_map/ppermute | solution.py:69
  85.3 1.5 %collective-permute-start.6 = (bf16[2,2,128,256]{3,2,1,0:T(8,128)(2,1)S(1)}, bf16[2,2,128,256]{3,2,1,0:T(8,128)(2,1)S(1)}, u32[]{:S(2)}, u32[]{:S(2)}) collective-permute-start(bf16[2,2,128,256]{3,2,1,0:T(8,128)(2,1)S(1)} %pad_maximum_fusion.1), channel_id=1, source_target_pairs={{0,2},{2,0},{4,6},{6,4},{8,10},{10,8},{12,14},{14,12},{1,3},{3,1},... | collective-permute-start | bytes 786440 | tf_op jit(solution)/shard_map/ppermute | solution.py:69
  86.8 2.6 %collective-permute-done.12 = bf16[2,2,128,256]{3,2,1,0:T(8,128)(2,1)S(1)} collective-permute-done((bf16[2,2,128,256]{3,2,1,0:T(8,128)(2,1)S(1)}, bf16[2,2,128,256]{3,2,1,0:T(8,128)(2,1)S(1)}, u32[]{:S(2)}, u32[]{:S(2)}) %collective-permute-start.12) | collective-permute-done | bytes 262176 | tf_op jit(solution)/shard_map/ppermute | solution.py:69
  89.6 2.2 %collective-permute-done.6 = bf16[2,2,128,256]{3,2,1,0:T(8,128)(2,1)S(1)} collective-permute-done((bf16[2,2,128,256]{3,2,1,0:T(8,128)(2,1)S(1)}, bf16[2,2,128,256]{3,2,1,0:T(8,128)(2,1)S(1)}, u32[]{:S(2)}, u32[]{:S(2)}) %collective-permute-start.6) | collective-permute-done | bytes 262176 | tf_op jit(solution)/shard_map/ppermute | solution.py:69
  93.1 1.3 %copy.23 = bf16[256,8,256]{0,2,1:T(8,128)(2,1)} copy(bf16[256,8,256]{2,0,1:T(8,128)(2,1)S(1)} %maximum_bitcast_fusion) | data formatting | bytes 2097152 | tf_op jit(solution)/shard_map/transpose | solution.py:210
  94.5 28.6 %shard_map.130 = (bf16[2048,2048]{1,0:T(8,128)(2,1)}, bf16[2048,2048]{1,0:T(8,128)(2,1)}, bf16[2048,2048]{1,0:T(8,128)(2,1)}) custom-call(f32[2048,256]{1,0:T(8,128)} %copy-done, bf16[2048,256]{1,0:T(8,128)(2,1)} %bitcast.68, bf16[256,2048]{1,0:T(8,128)(2,1)} %copy-done.1, bf16[2048,2048]{1,0:T(8,128)(2,1)} %bitcast.62, bf16[2048,2048]{1,0:T(8,128)(2,1)} %bitcast.65, ...), custom_call_target="tpu_custom_call" | custom-call | tf_op jit(solution)/shard_map/pallas_call | solution.py:50
  (71 shorter events, 7.5 us)
Async XLA Ops:
  0.6 23.6 %copy-start.5 = (s32[8]{0:T(128)S(1)}, s32[8]{0:T(128)}, u32[]{:S(2)}) copy-start(s32[8]{0:T(128)} %constant.67) | copy-start | bytes 100
  0.6 23.6 %copy-start.4 = (s32[8]{0:T(128)S(1)}, s32[8]{0:T(128)}, u32[]{:S(2)}) copy-start(s32[8]{0:T(128)} %constant.68) | copy-start | bytes 100
  0.7 23.7 %copy-start.3 = (s32[1,256]{1,0:T(1,128)S(1)}, s32[1,256]{1,0:T(1,128)}, u32[]{:S(2)}) copy-start(s32[1,256]{1,0:T(1,128)} %param.12) | copy-start | bytes 3076
  0.7 23.6 %copy-start.2 = (f32[1,2048]{1,0:T(1,128)S(1)}, f32[1,2048]{1,0:T(1,128)}, u32[]{:S(2)}) copy-start(f32[1,2048]{1,0:T(1,128)} %param.17) | copy-start | bytes 24580
  2.4 21.7 %all-to-all-start = ((bf16[8,128,256]{2,1,0:T(8,128)(2,1)}), bf16[8,128,256]{2,1,0:T(8,128)(2,1)S(1)}, u32[]{:S(2)}, u32[]{:S(2)}) async-start(bf16[8,128,256]{2,1,0:T(8,128)(2,1)} %broadcast_in_dim.36), calls=%async_computation | async-start | bytes 1048576 | tf_op jit(solution)/shard_map/all_to_all | solution.py:172
  24.2 2.0 %collective-permute-start = (bf16[128,2048]{1,0:T(8,128)(2,1)S(1)}, bf16[128,2048]{1,0:T(8,128)(2,1)S(1)}, u32[]{:S(2)}, u32[]{:S(2)}) collective-permute-start(bf16[128,2048]{1,0:T(8,128)(2,1)S(1)} %bitcast.69), channel_id=1, source_target_pairs={{0,1},{1,0},{2,3},{3,2},{4,5},{5,4},{6,7},{7,6},{8,9},{9,8},{10,11... | collective-permute-start | bytes 1572872 | tf_op jit(solution)/shard_map/ppermute | solution.py:174
  27.7 0.7 copy-start.6
  27.7 7.2 %slice-start = ((s8[8388608]{0:T(1024)(128)(4,1)}), s8[4194304]{0:T(1024)(128)(4,1)S(1)}, s32[]{:S(2)}) async-start(s8[8388608]{0:T(1024)(128)(4,1)} %bitcast.63), calls=%async_computation.1 | async-start | bytes 8388608
  28.0 6.8 %copy-start.1 = (bf16[256,2048]{1,0:T(8,128)(2,1)}, bf16[256,2048]{1,0:T(8,128)(2,1)S(1)}, u32[]{:S(2)}) copy-start(bf16[256,2048]{1,0:T(8,128)(2,1)S(1)} %get-tuple-element.9.cen_ref) | copy-start | bytes 3145732
  28.4 6.5 %slice-start.1 = ((s8[8388608]{0:T(1024)(128)(4,1)}), s8[4194304]{0:T(1024)(128)(4,1)S(1)}, s32[]{:S(2)}) async-start(s8[8388608]{0:T(1024)(128)(4,1)} %bitcast.63), calls=%async_computation.2 | async-start | bytes 8388608
  34.9 2.4 %copy-start = (f32[2048,256]{1,0:T(8,128)}, f32[2048,256]{1,0:T(8,128)S(1)}, u32[]{:S(2)}) copy-start(f32[2048,256]{1,0:T(8,128)S(1)} %fusion.pre_ref) | copy-start | bytes 6291460
  37.5 14.0 %collective-permute-start.7 = (f32[128,1024]{1,0:T(8,128)S(1)}, f32[128,1024]{1,0:T(8,128)S(1)}, u32[]{:S(2)}, u32[]{:S(2)}) collective-permute-start(f32[128,1024]{1,0:T(8,128)S(1)} %constant_dynamic-slice_fusion.2), channel_id=1, source_target_pairs={{0,4},{2,6},{4,0},{6,2},{8,12},{10,14},{12,8},{14,10},{1,5},{3,7},... | collective-permute-start | bytes 1572872 | tf_op jit(solution)/shard_map/ppermute | solution.py:69
  38.4 14.8 %collective-permute-start.1 = (f32[128,1024]{1,0:T(8,128)S(1)}, f32[128,1024]{1,0:T(8,128)S(1)}, u32[]{:S(2)}, u32[]{:S(2)}) collective-permute-start(f32[128,1024]{1,0:T(8,128)S(1)} %constant_dynamic-slice_fusion.9), channel_id=1, source_target_pairs={{0,2},{2,0},{4,6},{6,4},{8,10},{10,8},{12,14},{14,12},{1,3},{3,1},... | collective-permute-start | bytes 1572872 | tf_op jit(solution)/shard_map/ppermute | solution.py:69
  51.7 7.6 %collective-permute-start.8 = (f32[128,512]{1,0:T(8,128)S(1)}, f32[128,512]{1,0:T(8,128)S(1)}, u32[]{:S(2)}, u32[]{:S(2)}) collective-permute-start(f32[128,512]{1,0:T(8,128)S(1)} %constant_dynamic-slice_fusion.1), channel_id=1, source_target_pairs={{0,2},{2,0},{4,6},{6,4},{8,10},{10,8},{12,14},{14,12},{1,3},{3,1},... | collective-permute-start | bytes 786440 | tf_op jit(solution)/shard_map/ppermute | solution.py:69
  53.3 7.3 %collective-permute-start.2 = (f32[128,512]{1,0:T(8,128)S(1)}, f32[128,512]{1,0:T(8,128)S(1)}, u32[]{:S(2)}, u32[]{:S(2)}) collective-permute-start(f32[128,512]{1,0:T(8,128)S(1)} %constant_dynamic-slice_fusion.8), channel_id=1, source_target_pairs={{0,4},{2,6},{4,0},{6,2},{8,12},{10,14},{12,8},{14,10},{1,5},{3,7},... | collective-permute-start | bytes 786440 | tf_op jit(solution)/shard_map/ppermute | solution.py:69
  59.3 10.7 %collective-permute-start.9 = (f32[128,256]{1,0:T(8,128)S(1)}, f32[128,256]{1,0:T(8,128)S(1)}, u32[]{:S(2)}, u32[]{:S(2)}) collective-permute-start(f32[128,256]{1,0:T(8,128)S(1)} %constant_dynamic-slice_fusion), channel_id=1, source_target_pairs={{0,8},{2,10},{4,12},{6,14},{8,0},{10,2},{12,4},{14,6},{1,9},{3,11}... | collective-permute-start | bytes 393224 | tf_op jit(solution)/shard_map/ppermute | solution.py:69
  60.7 12.6 %collective-permute-start.3 = (f32[128,256]{1,0:T(8,128)S(1)}, f32[128,256]{1,0:T(8,128)S(1)}, u32[]{:S(2)}, u32[]{:S(2)}) collective-permute-start(f32[128,256]{1,0:T(8,128)S(1)} %constant_dynamic-slice_fusion.7), channel_id=1, source_target_pairs={{0,8},{2,10},{4,12},{6,14},{8,0},{10,2},{12,4},{14,6},{1,9},{3,11}... | collective-permute-start | bytes 393224 | tf_op jit(solution)/shard_map/ppermute | solution.py:69
  70.1 6.0 %collective-permute-start.10 = (bf16[128,256]{1,0:T(8,128)(2,1)S(1)}, bf16[128,256]{1,0:T(8,128)(2,1)S(1)}, u32[]{:S(2)}, u32[]{:S(2)}) collective-permute-start(bf16[128,256]{1,0:T(8,128)(2,1)S(1)} %multiply_convert_fusion), channel_id=1, source_target_pairs={{0,8},{2,10},{4,12},{6,14},{8,0},{10,2},{12,4},{14,6},{1,9},{3,11}... | collective-permute-start | bytes 196616 | tf_op jit(solution)/shard_map/ppermute | solution.py:69
  73.3 5.4 %collective-permute-start.4 = (bf16[128,256]{1,0:T(8,128)(2,1)S(1)}, bf16[128,256]{1,0:T(8,128)(2,1)S(1)}, u32[]{:S(2)}, u32[]{:S(2)}) collective-permute-start(bf16[128,256]{1,0:T(8,128)(2,1)S(1)} %multiply_convert_fusion.1), channel_id=1, source_target_pairs={{0,8},{2,10},{4,12},{6,14},{8,0},{10,2},{12,4},{14,6},{1,9},{3,11}... | collective-permute-start | bytes 196616 | tf_op jit(solution)/shard_map/ppermute | solution.py:69
  76.1 5.0 %collective-permute-start.11 = (bf16[2,128,256]{2,1,0:T(8,128)(2,1)S(1)}, bf16[2,128,256]{2,1,0:T(8,128)(2,1)S(1)}, u32[]{:S(2)}, u32[]{:S(2)}) collective-permute-start(bf16[2,128,256]{2,1,0:T(8,128)(2,1)S(1)} %pad_maximum_fusion.4), channel_id=1, source_target_pairs={{0,2},{2,0},{4,6},{6,4},{8,10},{10,8},{12,14},{14,12},{1,3},{3,1},... | collective-permute-start | bytes 393224 | tf_op jit(solution)/shard_map/ppermute | solution.py:69
  78.8 6.5 %collective-permute-start.5 = (bf16[2,128,256]{2,1,0:T(8,128)(2,1)S(1)}, bf16[2,128,256]{2,1,0:T(8,128)(2,1)S(1)}, u32[]{:S(2)}, u32[]{:S(2)}) collective-permute-start(bf16[2,128,256]{2,1,0:T(8,128)(2,1)S(1)} %pad_maximum_fusion.3), channel_id=1, source_target_pairs={{0,4},{2,6},{4,0},{6,2},{8,12},{10,14},{12,8},{14,10},{1,5},{3,7},... | collective-permute-start | bytes 393224 | tf_op jit(solution)/shard_map/ppermute | solution.py:69
  81.2 8.3 %collective-permute-start.12 = (bf16[2,2,128,256]{3,2,1,0:T(8,128)(2,1)S(1)}, bf16[2,2,128,256]{3,2,1,0:T(8,128)(2,1)S(1)}, u32[]{:S(2)}, u32[]{:S(2)}) collective-permute-start(bf16[2,2,128,256]{3,2,1,0:T(8,128)(2,1)S(1)} %pad_maximum_fusion.2), channel_id=1, source_target_pairs={{0,4},{2,6},{4,0},{6,2},{8,12},{10,14},{12,8},{14,10},{1,5},{3,7},... | collective-permute-start | bytes 786440 | tf_op jit(solution)/shard_map/ppermute | solution.py:69
  85.3 6.4 %collective-permute-start.6 = (bf16[2,2,128,256]{3,2,1,0:T(8,128)(2,1)S(1)}, bf16[2,2,128,256]{3,2,1,0:T(8,128)(2,1)S(1)}, u32[]{:S(2)}, u32[]{:S(2)}) collective-permute-start(bf16[2,2,128,256]{3,2,1,0:T(8,128)(2,1)S(1)} %pad_maximum_fusion.1), channel_id=1, source_target_pairs={{0,2},{2,0},{4,6},{6,4},{8,10},{10,8},{12,14},{14,12},{1,3},{3,1},... | collective-permute-start | bytes 786440 | tf_op jit(solution)/shard_map/ppermute | solution.py:69

commit v10 on v9

--- a/solution.py
+++ b/solution.py
@@ -193,9 +193,11 @@
     partial_sum = lax.dot_general(
         latent_t, decoder, (((0,), (0,)), ((), ())), preferred_element_type=jnp.float32
     )
-    half = partial_sum.shape[0] // 2
+    chunk = partial_sum.shape[0] // 4
     error_parts = []
-    for rows, order in ((slice(0, half), first), (slice(half, None), second)):
+    for part in range(4):
+        rows = slice(part * chunk, (part + 1) * chunk)
+        order = (first, second)[part % 2]
         total, block = _halving_cols(partial_sum[rows], "lat", lat_size, order)
         start = block * width
         sample_cols = lax.dynamic_slice_in_dim(sample[rows], start, width, axis=1)

time: 123 us -> 121 us (0.984)
  waiting for transfers between devices: 59.1 us -> 38.6 us
  starting transfers between devices: 16.3 us -> 33.5 us
    ppermute x12 -> x24, waiting for transfers between devices: 44.2 us -> 23.7 us  [_pair_swap(): return lax.ppermute(value, axis, [(i, i ^ mask) for i in range(size)])]
    ppermute x12 -> x24, starting transfers between devices: 8.98 us -> 26.2 us  [_pair_swap(): return lax.ppermute(value, axis, [(i, i ^ mask) for i in range(size)])]
  transfers between devices with their start and end apart: 14 -> 26, of which waited for: 13 -> 16; matrix products, arithmetic and copies ran while one was open for 2% -> 3% of each run, Pallas kernels for 0% -> 0%
where the time goes in v10:
time: 121 us
  waiting for transfers between devices  38.6 us (32%)
  starting transfers between devices  33.5 us (28%)
  Pallas kernels  28.7 us (24%)
  matrix products  8.83 us (7%)
  local copies, waits for them, and re-layouts  7.6 us (6%)
  other arithmetic  2.66 us (2%)
  between operations  1.24 us (1%)
    pallas_call x1, Pallas kernels, tail(): pl.pallas_call(_tail_kernel, grid=(n_lat // tile,), in_specs=[pl.BlockSpe...  28.7 us
    ppermute x24, starting transfers between devices, _pair_swap(): return lax.ppermute(value, axis, [(i, i ^ mask) for i in range(size)])  26.2 us
    ppermute x24, waiting for transfers between devices, _pair_swap(): return lax.ppermute(value, axis, [(i, i ^ mask) for i in range(size)])  23.7 us
    all_to_all x1, waiting for transfers between devices, local(): act_blocks = lax.all_to_all(copies, 'lat', 0, 0, tiled=True)  13.1 us
    all_to_all x1, starting transfers between devices, local(): act_blocks = lax.all_to_all(copies, 'lat', 0, 0, tiled=True)  7.25 us
    dot_general x1, matrix products, local(): lax.dot_general(weight_in, centered, (((1,), (1,)), ((), ())), preferred_...  6.49 us
  transfers between devices with their start and end apart: 26, of which 16 were waited for; matrix products, arithmetic and copies ran while one was open for 3% of the time, Pallas kernels for 0%

profile of v10, /device:TPU:0, one launch (start us, length us, event | category | flops | bytes accessed | tf_op | source)
XLA Modules:
  0.0 121.2 jit_solution(18117292661838847689)
XLA Ops:
  0.7 1.7 %broadcast_in_dim.46 = bf16[8,128,256]{2,1,0:T(8,128)(2,1)} broadcast(bf16[128,256]{1,0:T(8,128)(2,1)} %param.13), dimensions={1,2} | broadcast | bytes 589824 | tf_op jit(solution)/shard_map/broadcast_in_dim | solution.py:171
  2.4 7.3 %all-to-all-start = ((bf16[8,128,256]{2,1,0:T(8,128)(2,1)}), bf16[8,128,256]{2,1,0:T(8,128)(2,1)S(1)}, u32[]{:S(2)}, u32[]{:S(2)}) async-start(bf16[8,128,256]{2,1,0:T(8,128)(2,1)} %broadcast_in_dim.46), calls=%async_computation | async-start | bytes 1048576 | tf_op jit(solution)/shard_map/all_to_all | solution.py:172
  11.0 13.1 %all-to-all-done = bf16[8,128,256]{2,1,0:T(8,128)(2,1)S(1)} async-done(((bf16[8,128,256]{2,1,0:T(8,128)(2,1)}), bf16[8,128,256]{2,1,0:T(8,128)(2,1)S(1)}, u32[]{:S(2)}, u32[]{:S(2)}) %all-to-all-start) | async-done | bytes 524320 | tf_op jit(solution)/shard_map/all_to_all | solution.py:172
  24.3 1.8 %collective-permute-done = bf16[128,2048]{1,0:T(8,128)(2,1)S(1)} collective-permute-done((bf16[128,2048]{1,0:T(8,128)(2,1)S(1)}, bf16[128,2048]{1,0:T(8,128)(2,1)S(1)}, u32[]{:S(2)}, u32[]{:S(2)}) %collective-permute-start) | collective-permute-done | bytes 524320 | tf_op jit(solution)/shard_map/ppermute | solution.py:174
  26.3 1.4 %gather_fusion = bf16[256,2048]{1,0:T(8,128)(2,1)S(1)} fusion(bf16[256,2048]{1,0:T(8,128)(2,1)S(1)} %pad_maximum_fusion, s32[1024]{0:T(1024)S(1)} %pad_clamp_fusion.2), kind=kCustom, calls=%fused_computation | custom fusion | bytes 2098176 | tf_op jit(solution)/shard_map/jit(_take)/gather | solution.py:181
  28.4 6.5 %fusion.pre_ref = f32[2048,256]{1,0:T(8,128)S(1)} fusion(bf16[256,2048]{1,0:T(8,128)(2,1)S(1)} %get-tuple-element.9.cen_ref, f32[2048]{0:T(1024)S(1)} %bitcast.116, bf16[1,2048,2048]{2,1,0:T(8,128)(2,1)} %param.16), kind=kOutput, calls=%fused_computation.6 | convolution fusion | flops 2148007936 | bytes 11542528 | tf_op jit(solution)/shard_map/dot_general | solution.py:187
  34.9 2.3 %fusion.1 = f32[256,2048]{1,0:T(8,128)S(1)} fusion(f32[2048,256]{1,0:T(8,128)S(1)} %fusion.pre_ref, bf16[1,2048,2048]{2,1,0:T(8,128)(2,1)S(1)} %bitcast.94), kind=kOutput, calls=%fused_computation.9 | convolution fusion | flops 2148532224 | bytes 12582912 | tf_op jit(solution)/shard_map/dot_general | solution.py:193
  39.7 1.5 %collective-permute-start.13 = (f32[64,1024]{1,0:T(8,128)S(1)}, f32[64,1024]{1,0:T(8,128)S(1)}, u32[]{:S(2)}, u32[]{:S(2)}) collective-permute-start(f32[64,1024]{1,0:T(8,128)S(1)} %constant_dynamic-slice_fusion.3), channel_id=1, source_target_pairs={{0,2},{2,0},{4,6},{6,4},{8,10},{10,8},{12,14},{14,12},{1,3},{3,1},... | collective-permute-start | bytes 786440 | tf_op jit(solution)/shard_map/ppermute | solution.py:69
  41.8 5.0 %collective-permute-done.7 = f32[64,1024]{1,0:T(8,128)S(1)} collective-permute-done((f32[64,1024]{1,0:T(8,128)S(1)}, f32[64,1024]{1,0:T(8,128)S(1)}, u32[]{:S(2)}, u32[]{:S(2)}) %collective-permute-start.7) | collective-permute-done | bytes 262176 | tf_op jit(solution)/shard_map/ppermute | solution.py:69
  46.9 1.5 %collective-permute-start.8 = (f32[64,512]{1,0:T(8,128)S(1)}, f32[64,512]{1,0:T(8,128)S(1)}, u32[]{:S(2)}, u32[]{:S(2)}) collective-permute-start(f32[64,512]{1,0:T(8,128)S(1)} %constant_dynamic-slice_fusion.8), channel_id=1, source_target_pairs={{0,2},{2,0},{4,6},{6,4},{8,10},{10,8},{12,14},{14,12},{1,3},{3,1},... | collective-permute-start | bytes 393224 | tf_op jit(solution)/shard_map/ppermute | solution.py:69
  48.4 3.2 %collective-permute-done.19 = f32[64,1024]{1,0:T(8,128)S(1)} collective-permute-done((f32[64,1024]{1,0:T(8,128)S(1)}, f32[64,1024]{1,0:T(8,128)S(1)}, u32[]{:S(2)}, u32[]{:S(2)}) %collective-permute-start.19) | collective-permute-done | bytes 262176 | tf_op jit(solution)/shard_map/ppermute | solution.py:69
  51.7 1.5 %collective-permute-start.20 = (f32[64,512]{1,0:T(8,128)S(1)}, f32[64,512]{1,0:T(8,128)S(1)}, u32[]{:S(2)}, u32[]{:S(2)}) collective-permute-start(f32[64,512]{1,0:T(8,128)S(1)} %constant_dynamic-slice_fusion.5), channel_id=1, source_target_pairs={{0,2},{2,0},{4,6},{6,4},{8,10},{10,8},{12,14},{14,12},{1,3},{3,1},... | collective-permute-start | bytes 393224 | tf_op jit(solution)/shard_map/ppermute | solution.py:69
  55.5 1.8 %collective-permute-done.8 = f32[64,512]{1,0:T(8,128)S(1)} collective-permute-done((f32[64,512]{1,0:T(8,128)S(1)}, f32[64,512]{1,0:T(8,128)S(1)}, u32[]{:S(2)}, u32[]{:S(2)}) %collective-permute-start.8) | collective-permute-done | bytes 131104 | tf_op jit(solution)/shard_map/ppermute | solution.py:69
  58.8 1.7 %collective-permute-start.21 = (f32[64,256]{1,0:T(8,128)S(1)}, f32[64,256]{1,0:T(8,128)S(1)}, u32[]{:S(2)}, u32[]{:S(2)}) collective-permute-start(f32[64,256]{1,0:T(8,128)S(1)} %constant_dynamic-slice_fusion.10), channel_id=1, source_target_pairs={{0,8},{2,10},{4,12},{6,14},{8,0},{10,2},{12,4},{14,6},{1,9},{3,11}... | collective-permute-start | bytes 196616 | tf_op jit(solution)/shard_map/ppermute | solution.py:69
  61.9 1.7 %collective-permute-start.3 = (f32[64,256]{1,0:T(8,128)S(1)}, f32[64,256]{1,0:T(8,128)S(1)}, u32[]{:S(2)}, u32[]{:S(2)}) collective-permute-start(f32[64,256]{1,0:T(8,128)S(1)} %constant_dynamic-slice_fusion.13), channel_id=1, source_target_pairs={{0,8},{2,10},{4,12},{6,14},{8,0},{10,2},{12,4},{14,6},{1,9},{3,11}... | collective-permute-start | bytes 196616 | tf_op jit(solution)/shard_map/ppermute | solution.py:69
  63.6 4.8 %collective-permute-done.9 = f32[64,256]{1,0:T(8,128)S(1)} collective-permute-done((f32[64,256]{1,0:T(8,128)S(1)}, f32[64,256]{1,0:T(8,128)S(1)}, u32[]{:S(2)}, u32[]{:S(2)}) %collective-permute-start.9) | collective-permute-done | bytes 65568 | tf_op jit(solution)/shard_map/ppermute | solution.py:69
  68.4 1.4 %collective-permute-done.21 = f32[64,256]{1,0:T(8,128)S(1)} collective-permute-done((f32[64,256]{1,0:T(8,128)S(1)}, f32[64,256]{1,0:T(8,128)S(1)}, u32[]{:S(2)}, u32[]{:S(2)}) %collective-permute-start.21) | collective-permute-done | bytes 65568 | tf_op jit(solution)/shard_map/ppermute | solution.py:69
  70.0 2.9 %collective-permute-start.22 = (bf16[64,256]{1,0:T(8,128)(2,1)S(1)}, bf16[64,256]{1,0:T(8,128)(2,1)S(1)}, u32[]{:S(2)}, u32[]{:S(2)}) collective-permute-start(bf16[64,256]{1,0:T(8,128)(2,1)S(1)} %get-tuple-element.52), channel_id=1, source_target_pairs={{0,8},{2,10},{4,12},{6,14},{8,0},{10,2},{12,4},{14,6},{1,9},{3,11}... | collective-permute-start | bytes 98312 | tf_op jit(solution)/shard_map/ppermute | solution.py:69
  73.1 2.9 %collective-permute-start.16 = (bf16[64,256]{1,0:T(8,128)(2,1)S(1)}, bf16[64,256]{1,0:T(8,128)(2,1)S(1)}, u32[]{:S(2)}, u32[]{:S(2)}) collective-permute-start(bf16[64,256]{1,0:T(8,128)(2,1)S(1)} %get-tuple-element.50), channel_id=1, source_target_pairs={{0,8},{2,10},{4,12},{6,14},{8,0},{10,2},{12,4},{14,6},{1,9},{3,11}... | collective-permute-start | bytes 98312 | tf_op jit(solution)/shard_map/ppermute | solution.py:69
  78.5 2.1 %collective-permute-start.17 = (bf16[2,64,256]{2,1,0:T(8,128)(2,1)S(1)}, bf16[2,64,256]{2,1,0:T(8,128)(2,1)S(1)}, u32[]{:S(2)}, u32[]{:S(2)}) collective-permute-start(bf16[2,64,256]{2,1,0:T(8,128)(2,1)S(1)} %pad_maximum_fusion.7), channel_id=1, source_target_pairs={{0,4},{2,6},{4,0},{6,2},{8,12},{10,14},{12,8},{14,10},{1,5},{3,7},... | collective-permute-start | bytes 196616 | tf_op jit(solution)/shard_map/ppermute | solution.py:69
  80.7 1.8 %collective-permute-done.23 = bf16[2,64,256]{2,1,0:T(8,128)(2,1)S(1)} collective-permute-done((bf16[2,64,256]{2,1,0:T(8,128)(2,1)S(1)}, bf16[2,64,256]{2,1,0:T(8,128)(2,1)S(1)}, u32[]{:S(2)}, u32[]{:S(2)}) %collective-permute-start.23) | collective-permute-done | bytes 65568 | tf_op jit(solution)/shard_map/ppermute | solution.py:69
  83.3 1.5 %collective-permute-start.6 = (bf16[2,2,64,256]{3,2,1,0:T(8,128)(2,1)S(1)}, bf16[2,2,64,256]{3,2,1,0:T(8,128)(2,1)S(1)}, u32[]{:S(2)}, u32[]{:S(2)}) collective-permute-start(bf16[2,2,64,256]{3,2,1,0:T(8,128)(2,1)S(1)} %pad_maximum_fusion.1), channel_id=1, source_target_pairs={{0,2},{2,0},{4,6},{6,4},{8,10},{10,8},{12,14},{14,12},{1,3},{3,1},... | collective-permute-start | bytes 393224 | tf_op jit(solution)/shard_map/ppermute | solution.py:69
  85.7 1.9 %collective-permute-done.24 = bf16[2,2,64,256]{3,2,1,0:T(8,128)(2,1)S(1)} collective-permute-done((bf16[2,2,64,256]{3,2,1,0:T(8,128)(2,1)S(1)}, bf16[2,2,64,256]{3,2,1,0:T(8,128)(2,1)S(1)}, u32[]{:S(2)}, u32[]{:S(2)}) %collective-permute-start.24) | collective-permute-done | bytes 131104 | tf_op jit(solution)/shard_map/ppermute | solution.py:69
  92.5 28.7 %shard_map.148 = (bf16[2048,2048]{1,0:T(8,128)(2,1)}, bf16[2048,2048]{1,0:T(8,128)(2,1)}, bf16[2048,2048]{1,0:T(8,128)(2,1)}) custom-call(f32[2048,256]{1,0:T(8,128)} %copy-done, bf16[2048,256]{1,0:T(8,128)(2,1)} %bitcast.98, bf16[256,2048]{1,0:T(8,128)(2,1)} %copy-done.1, bf16[2048,2048]{1,0:T(8,128)(2,1)} %bitcast.92, bf16[2048,2048]{1,0:T(8,128)(2,1)} %bitcast.95, ...), custom_call_target="tpu_custom_call" | custom-call | tf_op jit(solution)/shard_map/pallas_call | solution.py:50
  (121 shorter events, 20.0 us)
Async XLA Ops:
  2.4 21.7 %all-to-all-start = ((bf16[8,128,256]{2,1,0:T(8,128)(2,1)}), bf16[8,128,256]{2,1,0:T(8,128)(2,1)S(1)}, u32[]{:S(2)}, u32[]{:S(2)}) async-start(bf16[8,128,256]{2,1,0:T(8,128)(2,1)} %broadcast_in_dim.46), calls=%async_computation | async-start | bytes 1048576 | tf_op jit(solution)/shard_map/all_to_all | solution.py:172
  37.6 9.2 %collective-permute-start.7 = (f32[64,1024]{1,0:T(8,128)S(1)}, f32[64,1024]{1,0:T(8,128)S(1)}, u32[]{:S(2)}, u32[]{:S(2)}) collective-permute-start(f32[64,1024]{1,0:T(8,128)S(1)} %constant_dynamic-slice_fusion.9), channel_id=1, source_target_pairs={{0,4},{2,6},{4,0},{6,2},{8,12},{10,14},{12,8},{14,10},{1,5},{3,7},... | collective-permute-start | bytes 786440 | tf_op jit(solution)/shard_map/ppermute | solution.py:69
  38.4 13.2 %collective-permute-start.19 = (f32[64,1024]{1,0:T(8,128)S(1)}, f32[64,1024]{1,0:T(8,128)S(1)}, u32[]{:S(2)}, u32[]{:S(2)}) collective-permute-start(f32[64,1024]{1,0:T(8,128)S(1)} %constant_dynamic-slice_fusion), channel_id=1, source_target_pairs={{0,4},{2,6},{4,0},{6,2},{8,12},{10,14},{12,8},{14,10},{1,5},{3,7},... | collective-permute-start | bytes 786440 | tf_op jit(solution)/shard_map/ppermute | solution.py:69
  39.7 13.5 %collective-permute-start.13 = (f32[64,1024]{1,0:T(8,128)S(1)}, f32[64,1024]{1,0:T(8,128)S(1)}, u32[]{:S(2)}, u32[]{:S(2)}) collective-permute-start(f32[64,1024]{1,0:T(8,128)S(1)} %constant_dynamic-slice_fusion.3), channel_id=1, source_target_pairs={{0,2},{2,0},{4,6},{6,4},{8,10},{10,8},{12,14},{14,12},{1,3},{3,1},... | collective-permute-start | bytes 786440 | tf_op jit(solution)/shard_map/ppermute | solution.py:69
  41.2 13.4 %collective-permute-start.1 = (f32[64,1024]{1,0:T(8,128)S(1)}, f32[64,1024]{1,0:T(8,128)S(1)}, u32[]{:S(2)}, u32[]{:S(2)}) collective-permute-start(f32[64,1024]{1,0:T(8,128)S(1)} %constant_dynamic-slice_fusion.15), channel_id=1, source_target_pairs={{0,2},{2,0},{4,6},{6,4},{8,10},{10,8},{12,14},{14,12},{1,3},{3,1},... | collective-permute-start | bytes 786440 | tf_op jit(solution)/shard_map/ppermute | solution.py:69
  46.9 10.4 %collective-permute-start.8 = (f32[64,512]{1,0:T(8,128)S(1)}, f32[64,512]{1,0:T(8,128)S(1)}, u32[]{:S(2)}, u32[]{:S(2)}) collective-permute-start(f32[64,512]{1,0:T(8,128)S(1)} %constant_dynamic-slice_fusion.8), channel_id=1, source_target_pairs={{0,2},{2,0},{4,6},{6,4},{8,10},{10,8},{12,14},{14,12},{1,3},{3,1},... | collective-permute-start | bytes 393224 | tf_op jit(solution)/shard_map/ppermute | solution.py:69
  51.7 7.0 %collective-permute-start.20 = (f32[64,512]{1,0:T(8,128)S(1)}, f32[64,512]{1,0:T(8,128)S(1)}, u32[]{:S(2)}, u32[]{:S(2)}) collective-permute-start(f32[64,512]{1,0:T(8,128)S(1)} %constant_dynamic-slice_fusion.5), channel_id=1, source_target_pairs={{0,2},{2,0},{4,6},{6,4},{8,10},{10,8},{12,14},{14,12},{1,3},{3,1},... | collective-permute-start | bytes 393224 | tf_op jit(solution)/shard_map/ppermute | solution.py:69
  53.3 7.2 %collective-permute-start.14 = (f32[64,512]{1,0:T(8,128)S(1)}, f32[64,512]{1,0:T(8,128)S(1)}, u32[]{:S(2)}, u32[]{:S(2)}) collective-permute-start(f32[64,512]{1,0:T(8,128)S(1)} %constant_dynamic-slice_fusion.2), channel_id=1, source_target_pairs={{0,4},{2,6},{4,0},{6,2},{8,12},{10,14},{12,8},{14,10},{1,5},{3,7},... | collective-permute-start | bytes 393224 | tf_op jit(solution)/shard_map/ppermute | solution.py:69
  54.6 7.3 %collective-permute-start.2 = (f32[64,512]{1,0:T(8,128)S(1)}, f32[64,512]{1,0:T(8,128)S(1)}, u32[]{:S(2)}, u32[]{:S(2)}) collective-permute-start(f32[64,512]{1,0:T(8,128)S(1)} %constant_dynamic-slice_fusion.14), channel_id=1, source_target_pairs={{0,4},{2,6},{4,0},{6,2},{8,12},{10,14},{12,8},{14,10},{1,5},{3,7},... | collective-permute-start | bytes 393224 | tf_op jit(solution)/shard_map/ppermute | solution.py:69
  57.4 11.1 %collective-permute-start.9 = (f32[64,256]{1,0:T(8,128)S(1)}, f32[64,256]{1,0:T(8,128)S(1)}, u32[]{:S(2)}, u32[]{:S(2)}) collective-permute-start(f32[64,256]{1,0:T(8,128)S(1)} %constant_dynamic-slice_fusion.7), channel_id=1, source_target_pairs={{0,8},{2,10},{4,12},{6,14},{8,0},{10,2},{12,4},{14,6},{1,9},{3,11}... | collective-permute-start | bytes 196616 | tf_op jit(solution)/shard_map/ppermute | solution.py:69
  58.8 11.1 %collective-permute-start.21 = (f32[64,256]{1,0:T(8,128)S(1)}, f32[64,256]{1,0:T(8,128)S(1)}, u32[]{:S(2)}, u32[]{:S(2)}) collective-permute-start(f32[64,256]{1,0:T(8,128)S(1)} %constant_dynamic-slice_fusion.10), channel_id=1, source_target_pairs={{0,8},{2,10},{4,12},{6,14},{8,0},{10,2},{12,4},{14,6},{1,9},{3,11}... | collective-permute-start | bytes 196616 | tf_op jit(solution)/shard_map/ppermute | solution.py:69
  60.5 12.4 %collective-permute-start.15 = (f32[64,256]{1,0:T(8,128)S(1)}, f32[64,256]{1,0:T(8,128)S(1)}, u32[]{:S(2)}, u32[]{:S(2)}) collective-permute-start(f32[64,256]{1,0:T(8,128)S(1)} %constant_dynamic-slice_fusion.1), channel_id=1, source_target_pairs={{0,8},{2,10},{4,12},{6,14},{8,0},{10,2},{12,4},{14,6},{1,9},{3,11}... | collective-permute-start | bytes 196616 | tf_op jit(solution)/shard_map/ppermute | solution.py:69
  61.9 11.0 %collective-permute-start.3 = (f32[64,256]{1,0:T(8,128)S(1)}, f32[64,256]{1,0:T(8,128)S(1)}, u32[]{:S(2)}, u32[]{:S(2)}) collective-permute-start(f32[64,256]{1,0:T(8,128)S(1)} %constant_dynamic-slice_fusion.13), channel_id=1, source_target_pairs={{0,8},{2,10},{4,12},{6,14},{8,0},{10,2},{12,4},{14,6},{1,9},{3,11}... | collective-permute-start | bytes 196616 | tf_op jit(solution)/shard_map/ppermute | solution.py:69
  69.9 6.3 %collective-permute-start.10 = (bf16[64,256]{1,0:T(8,128)(2,1)S(1)}, bf16[64,256]{1,0:T(8,128)(2,1)S(1)}, u32[]{:S(2)}, u32[]{:S(2)}) collective-permute-start(bf16[64,256]{1,0:T(8,128)(2,1)S(1)} %get-tuple-element.51), channel_id=1, source_target_pairs={{0,8},{2,10},{4,12},{6,14},{8,0},{10,2},{12,4},{14,6},{1,9},{3,11}... | collective-permute-start | bytes 98312 | tf_op jit(solution)/shard_map/ppermute | solution.py:69
  70.0 7.6 %collective-permute-start.22 = (bf16[64,256]{1,0:T(8,128)(2,1)S(1)}, bf16[64,256]{1,0:T(8,128)(2,1)S(1)}, u32[]{:S(2)}, u32[]{:S(2)}) collective-permute-start(bf16[64,256]{1,0:T(8,128)(2,1)S(1)} %get-tuple-element.52), channel_id=1, source_target_pairs={{0,8},{2,10},{4,12},{6,14},{8,0},{10,2},{12,4},{14,6},{1,9},{3,11}... | collective-permute-start | bytes 98312 | tf_op jit(solution)/shard_map/ppermute | solution.py:69
  72.9 5.4 %collective-permute-start.4 = (bf16[64,256]{1,0:T(8,128)(2,1)S(1)}, bf16[64,256]{1,0:T(8,128)(2,1)S(1)}, u32[]{:S(2)}, u32[]{:S(2)}) collective-permute-start(bf16[64,256]{1,0:T(8,128)(2,1)S(1)} %get-tuple-element.49), channel_id=1, source_target_pairs={{0,8},{2,10},{4,12},{6,14},{8,0},{10,2},{12,4},{14,6},{1,9},{3,11}... | collective-permute-start | bytes 98312 | tf_op jit(solution)/shard_map/ppermute | solution.py:69
  73.1 5.4 %collective-permute-start.16 = (bf16[64,256]{1,0:T(8,128)(2,1)S(1)}, bf16[64,256]{1,0:T(8,128)(2,1)S(1)}, u32[]{:S(2)}, u32[]{:S(2)}) collective-permute-start(bf16[64,256]{1,0:T(8,128)(2,1)S(1)} %get-tuple-element.50), channel_id=1, source_target_pairs={{0,8},{2,10},{4,12},{6,14},{8,0},{10,2},{12,4},{14,6},{1,9},{3,11}... | collective-permute-start | bytes 98312 | tf_op jit(solution)/shard_map/ppermute | solution.py:69
  77.6 5.0 %collective-permute-start.23 = (bf16[2,64,256]{2,1,0:T(8,128)(2,1)S(1)}, bf16[2,64,256]{2,1,0:T(8,128)(2,1)S(1)}, u32[]{:S(2)}, u32[]{:S(2)}) collective-permute-start(bf16[2,64,256]{2,1,0:T(8,128)(2,1)S(1)} %pad_maximum_fusion.8), channel_id=1, source_target_pairs={{0,2},{2,0},{4,6},{6,4},{8,10},{10,8},{12,14},{14,12},{1,3},{3,1},... | collective-permute-start | bytes 196616 | tf_op jit(solution)/shard_map/ppermute | solution.py:69
  78.4 4.8 %collective-permute-start.5 = (bf16[2,64,256]{2,1,0:T(8,128)(2,1)S(1)}, bf16[2,64,256]{2,1,0:T(8,128)(2,1)S(1)}, u32[]{:S(2)}, u32[]{:S(2)}) collective-permute-start(bf16[2,64,256]{2,1,0:T(8,128)(2,1)S(1)} %pad_maximum_fusion.5), channel_id=1, source_target_pairs={{0,4},{2,6},{4,0},{6,2},{8,12},{10,14},{12,8},{14,10},{1,5},{3,7},... | collective-permute-start | bytes 196616 | tf_op jit(solution)/shard_map/ppermute | solution.py:69
  78.5 6.2 %collective-permute-start.17 = (bf16[2,64,256]{2,1,0:T(8,128)(2,1)S(1)}, bf16[2,64,256]{2,1,0:T(8,128)(2,1)S(1)}, u32[]{:S(2)}, u32[]{:S(2)}) collective-permute-start(bf16[2,64,256]{2,1,0:T(8,128)(2,1)S(1)} %pad_maximum_fusion.7), channel_id=1, source_target_pairs={{0,4},{2,6},{4,0},{6,2},{8,12},{10,14},{12,8},{14,10},{1,5},{3,7},... | collective-permute-start | bytes 196616 | tf_op jit(solution)/shard_map/ppermute | solution.py:69
  80.7 5.0 %collective-permute-start.12 = (bf16[2,2,64,256]{3,2,1,0:T(8,128)(2,1)S(1)}, bf16[2,2,64,256]{3,2,1,0:T(8,128)(2,1)S(1)}, u32[]{:S(2)}, u32[]{:S(2)}) collective-permute-start(bf16[2,2,64,256]{3,2,1,0:T(8,128)(2,1)S(1)} %pad_maximum_fusion.2), channel_id=1, source_target_pairs={{0,4},{2,6},{4,0},{6,2},{8,12},{10,14},{12,8},{14,10},{1,5},{3,7},... | collective-permute-start | bytes 393224 | tf_op jit(solution)/shard_map/ppermute | solution.py:69
  82.6 5.0 %collective-permute-start.24 = (bf16[2,2,64,256]{3,2,1,0:T(8,128)(2,1)S(1)}, bf16[2,2,64,256]{3,2,1,0:T(8,128)(2,1)S(1)}, u32[]{:S(2)}, u32[]{:S(2)}) collective-permute-start(bf16[2,2,64,256]{3,2,1,0:T(8,128)(2,1)S(1)} %pad_maximum_fusion.4), channel_id=1, source_target_pairs={{0,4},{2,6},{4,0},{6,2},{8,12},{10,14},{12,8},{14,10},{1,5},{3,7},... | collective-permute-start | bytes 393224 | tf_op jit(solution)/shard_map/ppermute | solution.py:69
  83.3 5.0 %collective-permute-start.6 = (bf16[2,2,64,256]{3,2,1,0:T(8,128)(2,1)S(1)}, bf16[2,2,64,256]{3,2,1,0:T(8,128)(2,1)S(1)}, u32[]{:S(2)}, u32[]{:S(2)}) collective-permute-start(bf16[2,2,64,256]{3,2,1,0:T(8,128)(2,1)S(1)} %pad_maximum_fusion.1), channel_id=1, source_target_pairs={{0,2},{2,0},{4,6},{6,4},{8,10},{10,8},{12,14},{14,12},{1,3},{3,1},... | collective-permute-start | bytes 393224 | tf_op jit(solution)/shard_map/ppermute | solution.py:69
  84.8 5.0 %collective-permute-start.18 = (bf16[2,2,64,256]{3,2,1,0:T(8,128)(2,1)S(1)}, bf16[2,2,64,256]{3,2,1,0:T(8,128)(2,1)S(1)}, u32[]{:S(2)}, u32[]{:S(2)}) collective-permute-start(bf16[2,2,64,256]{3,2,1,0:T(8,128)(2,1)S(1)} %pad_maximum_fusion.3), channel_id=1, source_target_pairs={{0,2},{2,0},{4,6},{6,4},{8,10},{10,8},{12,14},{14,12},{1,3},{3,1},... | collective-permute-start | bytes 393224 | tf_op jit(solution)/shard_map/ppermute | solution.py:69
  (11 other events, 124.5 us)

commit v11 on v10

--- a/solution.py
+++ b/solution.py
@@ -197,7 +197,7 @@
     error_parts = []
     for part in range(4):
         rows = slice(part * chunk, (part + 1) * chunk)
-        order = (first, second)[part % 2]
+        order = (first, second, first, first)[part]
         total, block = _halving_cols(partial_sum[rows], "lat", lat_size, order)
         start = block * width
         sample_cols = lax.dynamic_slice_in_dim(sample[rows], start, width, axis=1)

time: 121 us -> 124 us (1.025)
  waiting for transfers between devices: 38.6 us -> 40.8 us
    ppermute x24, waiting for transfers between devices: 23.7 us -> 25.9 us  [_pair_swap(): return lax.ppermute(value, axis, [(i, i ^ mask) for i in range(size)])]
  transfers between devices with their start and end apart: 26 -> 26, of which waited for: 16 -> 15; matrix products, arithmetic and copies ran while one was open for 3% -> 3% of each run, Pallas kernels for 0% -> 0%
where the time goes in v11:
time: 124 us
  waiting for transfers between devices  40.8 us (33%)
  starting transfers between devices  34.3 us (28%)
  Pallas kernels  28.7 us (23%)
  matrix products  8.83 us (7%)
  local copies, waits for them, and re-layouts  7.61 us (6%)
  other arithmetic  2.66 us (2%)
  between operations  1.25 us (1%)
    pallas_call x1, Pallas kernels, tail(): pl.pallas_call(_tail_kernel, grid=(n_lat // tile,), in_specs=[pl.BlockSpe...  28.7 us
    ppermute x24, starting transfers between devices, _pair_swap(): return lax.ppermute(value, axis, [(i, i ^ mask) for i in range(size)])  27 us
    ppermute x24, waiting for transfers between devices, _pair_swap(): return lax.ppermute(value, axis, [(i, i ^ mask) for i in range(size)])  25.9 us
    all_to_all x1, waiting for transfers between devices, local(): act_blocks = lax.all_to_all(copies, 'lat', 0, 0, tiled=True)  13.1 us
    all_to_all x1, starting transfers between devices, local(): act_blocks = lax.all_to_all(copies, 'lat', 0, 0, tiled=True)  7.25 us
    dot_general x1, matrix products, local(): lax.dot_general(weight_in, centered, (((1,), (1,)), ((), ())), preferred_...  6.49 us
  transfers between devices with their start and end apart: 26, of which 15 were waited for; matrix products, arithmetic and copies ran while one was open for 3% of the time, Pallas kernels for 0%

profile of v11, /device:TPU:0, one launch (start us, length us, event | category | flops | bytes accessed | tf_op | source)
XLA Modules:
  0.0 124.1 jit_solution(15792823234524000051)
XLA Ops:
  0.7 1.7 %broadcast_in_dim.46 = bf16[8,128,256]{2,1,0:T(8,128)(2,1)} broadcast(bf16[128,256]{1,0:T(8,128)(2,1)} %param.13), dimensions={1,2} | broadcast | bytes 589824 | tf_op jit(solution)/shard_map/broadcast_in_dim | solution.py:171
  2.4 7.3 %all-to-all-start = ((bf16[8,128,256]{2,1,0:T(8,128)(2,1)}), bf16[8,128,256]{2,1,0:T(8,128)(2,1)S(1)}, u32[]{:S(2)}, u32[]{:S(2)}) async-start(bf16[8,128,256]{2,1,0:T(8,128)(2,1)} %broadcast_in_dim.46), calls=%async_computation | async-start | bytes 1048576 | tf_op jit(solution)/shard_map/all_to_all | solution.py:172
  11.0 13.1 %all-to-all-done = bf16[8,128,256]{2,1,0:T(8,128)(2,1)S(1)} async-done(((bf16[8,128,256]{2,1,0:T(8,128)(2,1)}), bf16[8,128,256]{2,1,0:T(8,128)(2,1)S(1)}, u32[]{:S(2)}, u32[]{:S(2)}) %all-to-all-start) | async-done | bytes 524320 | tf_op jit(solution)/shard_map/all_to_all | solution.py:172
  24.3 1.8 %collective-permute-done = bf16[128,2048]{1,0:T(8,128)(2,1)S(1)} collective-permute-done((bf16[128,2048]{1,0:T(8,128)(2,1)S(1)}, bf16[128,2048]{1,0:T(8,128)(2,1)S(1)}, u32[]{:S(2)}, u32[]{:S(2)}) %collective-permute-start) | collective-permute-done | bytes 524320 | tf_op jit(solution)/shard_map/ppermute | solution.py:174
  26.3 1.4 %gather_fusion = bf16[256,2048]{1,0:T(8,128)(2,1)S(1)} fusion(bf16[256,2048]{1,0:T(8,128)(2,1)S(1)} %pad_maximum_fusion, s32[1024]{0:T(1024)S(1)} %pad_clamp_fusion.2), kind=kCustom, calls=%fused_computation | custom fusion | bytes 2098176 | tf_op jit(solution)/shard_map/jit(_take)/gather | solution.py:181
  28.4 6.5 %fusion.pre_ref = f32[2048,256]{1,0:T(8,128)S(1)} fusion(bf16[256,2048]{1,0:T(8,128)(2,1)S(1)} %get-tuple-element.9.cen_ref, f32[2048]{0:T(1024)S(1)} %bitcast.116, bf16[1,2048,2048]{2,1,0:T(8,128)(2,1)} %param.16), kind=kOutput, calls=%fused_computation.6 | convolution fusion | flops 2148007936 | bytes 11542528 | tf_op jit(solution)/shard_map/dot_general | solution.py:187
  34.9 2.3 %fusion.1 = f32[256,2048]{1,0:T(8,128)S(1)} fusion(f32[2048,256]{1,0:T(8,128)S(1)} %fusion.pre_ref, bf16[1,2048,2048]{2,1,0:T(8,128)(2,1)S(1)} %bitcast.94), kind=kOutput, calls=%fused_computation.9 | convolution fusion | flops 2148532224 | bytes 12582912 | tf_op jit(solution)/shard_map/dot_general | solution.py:193
  37.6 1.5 %collective-permute-start.13 = (f32[64,1024]{1,0:T(8,128)S(1)}, f32[64,1024]{1,0:T(8,128)S(1)}, u32[]{:S(2)}, u32[]{:S(2)}) collective-permute-start(f32[64,1024]{1,0:T(8,128)S(1)} %constant_dynamic-slice_fusion.3), channel_id=1, source_target_pairs={{0,2},{2,0},{4,6},{6,4},{8,10},{10,8},{12,14},{14,12},{1,3},{3,1},... | collective-permute-start | bytes 786440 | tf_op jit(solution)/shard_map/ppermute | solution.py:69
  39.7 1.5 %collective-permute-start.1 = (f32[64,1024]{1,0:T(8,128)S(1)}, f32[64,1024]{1,0:T(8,128)S(1)}, u32[]{:S(2)}, u32[]{:S(2)}) collective-permute-start(f32[64,1024]{1,0:T(8,128)S(1)} %constant_dynamic-slice_fusion.15), channel_id=1, source_target_pairs={{0,2},{2,0},{4,6},{6,4},{8,10},{10,8},{12,14},{14,12},{1,3},{3,1},... | collective-permute-start | bytes 786440 | tf_op jit(solution)/shard_map/ppermute | solution.py:69
  41.3 5.5 %collective-permute-done.13 = f32[64,1024]{1,0:T(8,128)S(1)} collective-permute-done((f32[64,1024]{1,0:T(8,128)S(1)}, f32[64,1024]{1,0:T(8,128)S(1)}, u32[]{:S(2)}, u32[]{:S(2)}) %collective-permute-start.13) | collective-permute-done | bytes 262176 | tf_op jit(solution)/shard_map/ppermute | solution.py:69
  47.7 4.7 %collective-permute-done.19 = f32[64,1024]{1,0:T(8,128)S(1)} collective-permute-done((f32[64,1024]{1,0:T(8,128)S(1)}, f32[64,1024]{1,0:T(8,128)S(1)}, u32[]{:S(2)}, u32[]{:S(2)}) %collective-permute-start.19) | collective-permute-done | bytes 262176 | tf_op jit(solution)/shard_map/ppermute | solution.py:69
  53.3 3.9 %collective-permute-done.1 = f32[64,1024]{1,0:T(8,128)S(1)} collective-permute-done((f32[64,1024]{1,0:T(8,128)S(1)}, f32[64,1024]{1,0:T(8,128)S(1)}, u32[]{:S(2)}, u32[]{:S(2)}) %collective-permute-start.1) | collective-permute-done | bytes 262176 | tf_op jit(solution)/shard_map/ppermute | solution.py:69
  59.0 2.1 %collective-permute-start.15 = (f32[64,256]{1,0:T(8,128)S(1)}, f32[64,256]{1,0:T(8,128)S(1)}, u32[]{:S(2)}, u32[]{:S(2)}) collective-permute-start(f32[64,256]{1,0:T(8,128)S(1)} %constant_dynamic-slice_fusion.1), channel_id=1, source_target_pairs={{0,8},{2,10},{4,12},{6,14},{8,0},{10,2},{12,4},{14,6},{1,9},{3,11}... | collective-permute-start | bytes 196616 | tf_op jit(solution)/shard_map/ppermute | solution.py:69
  64.3 1.9 %collective-permute-start.9 = (f32[64,256]{1,0:T(8,128)S(1)}, f32[64,256]{1,0:T(8,128)S(1)}, u32[]{:S(2)}, u32[]{:S(2)}) collective-permute-start(f32[64,256]{1,0:T(8,128)S(1)} %constant_dynamic-slice_fusion.7), channel_id=1, source_target_pairs={{0,8},{2,10},{4,12},{6,14},{8,0},{10,2},{12,4},{14,6},{1,9},{3,11}... | collective-permute-start | bytes 196616 | tf_op jit(solution)/shard_map/ppermute | solution.py:69
  66.2 3.6 %collective-permute-done.15 = f32[64,256]{1,0:T(8,128)S(1)} collective-permute-done((f32[64,256]{1,0:T(8,128)S(1)}, f32[64,256]{1,0:T(8,128)S(1)}, u32[]{:S(2)}, u32[]{:S(2)}) %collective-permute-start.15) | collective-permute-done | bytes 65568 | tf_op jit(solution)/shard_map/ppermute | solution.py:69
  69.8 1.4 %collective-permute-done.21 = f32[64,256]{1,0:T(8,128)S(1)} collective-permute-done((f32[64,256]{1,0:T(8,128)S(1)}, f32[64,256]{1,0:T(8,128)S(1)}, u32[]{:S(2)}, u32[]{:S(2)}) %collective-permute-start.21) | collective-permute-done | bytes 65568 | tf_op jit(solution)/shard_map/ppermute | solution.py:69
  71.2 1.4 %collective-permute-done.3 = f32[64,256]{1,0:T(8,128)S(1)} collective-permute-done((f32[64,256]{1,0:T(8,128)S(1)}, f32[64,256]{1,0:T(8,128)S(1)}, u32[]{:S(2)}, u32[]{:S(2)}) %collective-permute-start.3) | collective-permute-done | bytes 65568 | tf_op jit(solution)/shard_map/ppermute | solution.py:69
  72.7 2.9 %collective-permute-start.22 = (bf16[64,256]{1,0:T(8,128)(2,1)S(1)}, bf16[64,256]{1,0:T(8,128)(2,1)S(1)}, u32[]{:S(2)}, u32[]{:S(2)}) collective-permute-start(bf16[64,256]{1,0:T(8,128)(2,1)S(1)} %get-tuple-element.50), channel_id=1, source_target_pairs={{0,8},{2,10},{4,12},{6,14},{8,0},{10,2},{12,4},{14,6},{1,9},{3,11}... | collective-permute-start | bytes 98312 | tf_op jit(solution)/shard_map/ppermute | solution.py:69
  75.7 2.9 %collective-permute-start.10 = (bf16[64,256]{1,0:T(8,128)(2,1)S(1)}, bf16[64,256]{1,0:T(8,128)(2,1)S(1)}, u32[]{:S(2)}, u32[]{:S(2)}) collective-permute-start(bf16[64,256]{1,0:T(8,128)(2,1)S(1)} %multiply_convert_fusion.2), channel_id=1, source_target_pairs={{0,8},{2,10},{4,12},{6,14},{8,0},{10,2},{12,4},{14,6},{1,9},{3,11}... | collective-permute-start | bytes 98312 | tf_op jit(solution)/shard_map/ppermute | solution.py:69
  78.9 2.0 %collective-permute-start.23 = (bf16[2,64,256]{2,1,0:T(8,128)(2,1)S(1)}, bf16[2,64,256]{2,1,0:T(8,128)(2,1)S(1)}, u32[]{:S(2)}, u32[]{:S(2)}) collective-permute-start(bf16[2,64,256]{2,1,0:T(8,128)(2,1)S(1)} %pad_maximum_fusion.8), channel_id=1, source_target_pairs={{0,4},{2,6},{4,0},{6,2},{8,12},{10,14},{12,8},{14,10},{1,5},{3,7},... | collective-permute-start | bytes 196616 | tf_op jit(solution)/shard_map/ppermute | solution.py:69
  83.8 1.5 %collective-permute-start.24 = (bf16[2,2,64,256]{3,2,1,0:T(8,128)(2,1)S(1)}, bf16[2,2,64,256]{3,2,1,0:T(8,128)(2,1)S(1)}, u32[]{:S(2)}, u32[]{:S(2)}) collective-permute-start(bf16[2,2,64,256]{3,2,1,0:T(8,128)(2,1)S(1)} %pad_maximum_fusion.4), channel_id=1, source_target_pairs={{0,2},{2,0},{4,6},{6,4},{8,10},{10,8},{12,14},{14,12},{1,3},{3,1},... | collective-permute-start | bytes 393224 | tf_op jit(solution)/shard_map/ppermute | solution.py:69
  86.2 2.0 %collective-permute-start.12 = (bf16[2,2,64,256]{3,2,1,0:T(8,128)(2,1)S(1)}, bf16[2,2,64,256]{3,2,1,0:T(8,128)(2,1)S(1)}, u32[]{:S(2)}, u32[]{:S(2)}) collective-permute-start(bf16[2,2,64,256]{3,2,1,0:T(8,128)(2,1)S(1)} %pad_maximum_fusion.2), channel_id=1, source_target_pairs={{0,4},{2,6},{4,0},{6,2},{8,12},{10,14},{12,8},{14,10},{1,5},{3,7},... | collective-permute-start | bytes 393224 | tf_op jit(solution)/shard_map/ppermute | solution.py:69
  88.7 1.4 %collective-permute-done.24 = bf16[2,2,64,256]{3,2,1,0:T(8,128)(2,1)S(1)} collective-permute-done((bf16[2,2,64,256]{3,2,1,0:T(8,128)(2,1)S(1)}, bf16[2,2,64,256]{3,2,1,0:T(8,128)(2,1)S(1)}, u32[]{:S(2)}, u32[]{:S(2)}) %collective-permute-start.24) | collective-permute-done | bytes 131104 | tf_op jit(solution)/shard_map/ppermute | solution.py:69
  95.4 28.7 %shard_map.148 = (bf16[2048,2048]{1,0:T(8,128)(2,1)}, bf16[2048,2048]{1,0:T(8,128)(2,1)}, bf16[2048,2048]{1,0:T(8,128)(2,1)}) custom-call(f32[2048,256]{1,0:T(8,128)} %copy-done, bf16[2048,256]{1,0:T(8,128)(2,1)} %bitcast.98, bf16[256,2048]{1,0:T(8,128)(2,1)} %copy-done.1, bf16[2048,2048]{1,0:T(8,128)(2,1)} %bitcast.92, bf16[2048,2048]{1,0:T(8,128)(2,1)} %bitcast.95, ...), custom_call_target="tpu_custom_call" | custom-call | tf_op jit(solution)/shard_map/pallas_call | solution.py:50
  (121 shorter events, 19.9 us)
Async XLA Ops:
  2.4 21.7 %all-to-all-start = ((bf16[8,128,256]{2,1,0:T(8,128)(2,1)}), bf16[8,128,256]{2,1,0:T(8,128)(2,1)S(1)}, u32[]{:S(2)}, u32[]{:S(2)}) async-start(bf16[8,128,256]{2,1,0:T(8,128)(2,1)} %broadcast_in_dim.46), calls=%async_computation | async-start | bytes 1048576 | tf_op jit(solution)/shard_map/all_to_all | solution.py:172
  37.6 9.2 %collective-permute-start.13 = (f32[64,1024]{1,0:T(8,128)S(1)}, f32[64,1024]{1,0:T(8,128)S(1)}, u32[]{:S(2)}, u32[]{:S(2)}) collective-permute-start(f32[64,1024]{1,0:T(8,128)S(1)} %constant_dynamic-slice_fusion.3), channel_id=1, source_target_pairs={{0,2},{2,0},{4,6},{6,4},{8,10},{10,8},{12,14},{14,12},{1,3},{3,1},... | collective-permute-start | bytes 786440 | tf_op jit(solution)/shard_map/ppermute | solution.py:69
  39.1 13.3 %collective-permute-start.19 = (f32[64,1024]{1,0:T(8,128)S(1)}, f32[64,1024]{1,0:T(8,128)S(1)}, u32[]{:S(2)}, u32[]{:S(2)}) collective-permute-start(f32[64,1024]{1,0:T(8,128)S(1)} %constant_dynamic-slice_fusion), channel_id=1, source_target_pairs={{0,2},{2,0},{4,6},{6,4},{8,10},{10,8},{12,14},{14,12},{1,3},{3,1},... | collective-permute-start | bytes 786440 | tf_op jit(solution)/shard_map/ppermute | solution.py:69
  39.7 17.6 %collective-permute-start.1 = (f32[64,1024]{1,0:T(8,128)S(1)}, f32[64,1024]{1,0:T(8,128)S(1)}, u32[]{:S(2)}, u32[]{:S(2)}) collective-permute-start(f32[64,1024]{1,0:T(8,128)S(1)} %constant_dynamic-slice_fusion.15), channel_id=1, source_target_pairs={{0,2},{2,0},{4,6},{6,4},{8,10},{10,8},{12,14},{14,12},{1,3},{3,1},... | collective-permute-start | bytes 786440 | tf_op jit(solution)/shard_map/ppermute | solution.py:69
  41.2 17.0 %collective-permute-start.7 = (f32[64,1024]{1,0:T(8,128)S(1)}, f32[64,1024]{1,0:T(8,128)S(1)}, u32[]{:S(2)}, u32[]{:S(2)}) collective-permute-start(f32[64,1024]{1,0:T(8,128)S(1)} %constant_dynamic-slice_fusion.9), channel_id=1, source_target_pairs={{0,4},{2,6},{4,0},{6,2},{8,12},{10,14},{12,8},{14,10},{1,5},{3,7},... | collective-permute-start | bytes 786440 | tf_op jit(solution)/shard_map/ppermute | solution.py:69
  46.9 12.1 %collective-permute-start.14 = (f32[64,512]{1,0:T(8,128)S(1)}, f32[64,512]{1,0:T(8,128)S(1)}, u32[]{:S(2)}, u32[]{:S(2)}) collective-permute-start(f32[64,512]{1,0:T(8,128)S(1)} %constant_dynamic-slice_fusion.2), channel_id=1, source_target_pairs={{0,4},{2,6},{4,0},{6,2},{8,12},{10,14},{12,8},{14,10},{1,5},{3,7},... | collective-permute-start | bytes 393224 | tf_op jit(solution)/shard_map/ppermute | solution.py:69
  52.5 8.6 %collective-permute-start.20 = (f32[64,512]{1,0:T(8,128)S(1)}, f32[64,512]{1,0:T(8,128)S(1)}, u32[]{:S(2)}, u32[]{:S(2)}) collective-permute-start(f32[64,512]{1,0:T(8,128)S(1)} %constant_dynamic-slice_fusion.5), channel_id=1, source_target_pairs={{0,4},{2,6},{4,0},{6,2},{8,12},{10,14},{12,8},{14,10},{1,5},{3,7},... | collective-permute-start | bytes 393224 | tf_op jit(solution)/shard_map/ppermute | solution.py:69
  57.3 5.7 %collective-permute-start.2 = (f32[64,512]{1,0:T(8,128)S(1)}, f32[64,512]{1,0:T(8,128)S(1)}, u32[]{:S(2)}, u32[]{:S(2)}) collective-permute-start(f32[64,512]{1,0:T(8,128)S(1)} %constant_dynamic-slice_fusion.14), channel_id=1, source_target_pairs={{0,4},{2,6},{4,0},{6,2},{8,12},{10,14},{12,8},{14,10},{1,5},{3,7},... | collective-permute-start | bytes 393224 | tf_op jit(solution)/shard_map/ppermute | solution.py:69
  58.2 6.1 %collective-permute-start.8 = (f32[64,512]{1,0:T(8,128)S(1)}, f32[64,512]{1,0:T(8,128)S(1)}, u32[]{:S(2)}, u32[]{:S(2)}) collective-permute-start(f32[64,512]{1,0:T(8,128)S(1)} %constant_dynamic-slice_fusion.8), channel_id=1, source_target_pairs={{0,2},{2,0},{4,6},{6,4},{8,10},{10,8},{12,14},{14,12},{1,3},{3,1},... | collective-permute-start | bytes 393224 | tf_op jit(solution)/shard_map/ppermute | solution.py:69
  59.0 10.8 %collective-permute-start.15 = (f32[64,256]{1,0:T(8,128)S(1)}, f32[64,256]{1,0:T(8,128)S(1)}, u32[]{:S(2)}, u32[]{:S(2)}) collective-permute-start(f32[64,256]{1,0:T(8,128)S(1)} %constant_dynamic-slice_fusion.1), channel_id=1, source_target_pairs={{0,8},{2,10},{4,12},{6,14},{8,0},{10,2},{12,4},{14,6},{1,9},{3,11}... | collective-permute-start | bytes 196616 | tf_op jit(solution)/shard_map/ppermute | solution.py:69
  61.1 10.1 %collective-permute-start.21 = (f32[64,256]{1,0:T(8,128)S(1)}, f32[64,256]{1,0:T(8,128)S(1)}, u32[]{:S(2)}, u32[]{:S(2)}) collective-permute-start(f32[64,256]{1,0:T(8,128)S(1)} %constant_dynamic-slice_fusion.10), channel_id=1, source_target_pairs={{0,8},{2,10},{4,12},{6,14},{8,0},{10,2},{12,4},{14,6},{1,9},{3,11}... | collective-permute-start | bytes 196616 | tf_op jit(solution)/shard_map/ppermute | solution.py:69
  63.1 9.5 %collective-permute-start.3 = (f32[64,256]{1,0:T(8,128)S(1)}, f32[64,256]{1,0:T(8,128)S(1)}, u32[]{:S(2)}, u32[]{:S(2)}) collective-permute-start(f32[64,256]{1,0:T(8,128)S(1)} %constant_dynamic-slice_fusion.13), channel_id=1, source_target_pairs={{0,8},{2,10},{4,12},{6,14},{8,0},{10,2},{12,4},{14,6},{1,9},{3,11}... | collective-permute-start | bytes 196616 | tf_op jit(solution)/shard_map/ppermute | solution.py:69
  64.3 11.4 %collective-permute-start.9 = (f32[64,256]{1,0:T(8,128)S(1)}, f32[64,256]{1,0:T(8,128)S(1)}, u32[]{:S(2)}, u32[]{:S(2)}) collective-permute-start(f32[64,256]{1,0:T(8,128)S(1)} %constant_dynamic-slice_fusion.7), channel_id=1, source_target_pairs={{0,8},{2,10},{4,12},{6,14},{8,0},{10,2},{12,4},{14,6},{1,9},{3,11}... | collective-permute-start | bytes 196616 | tf_op jit(solution)/shard_map/ppermute | solution.py:69
  72.6 6.0 %collective-permute-start.4 = (bf16[64,256]{1,0:T(8,128)(2,1)S(1)}, bf16[64,256]{1,0:T(8,128)(2,1)S(1)}, u32[]{:S(2)}, u32[]{:S(2)}) collective-permute-start(bf16[64,256]{1,0:T(8,128)(2,1)S(1)} %get-tuple-element.49), channel_id=1, source_target_pairs={{0,8},{2,10},{4,12},{6,14},{8,0},{10,2},{12,4},{14,6},{1,9},{3,11}... | collective-permute-start | bytes 98312 | tf_op jit(solution)/shard_map/ppermute | solution.py:69
  72.7 6.1 %collective-permute-start.22 = (bf16[64,256]{1,0:T(8,128)(2,1)S(1)}, bf16[64,256]{1,0:T(8,128)(2,1)S(1)}, u32[]{:S(2)}, u32[]{:S(2)}) collective-permute-start(bf16[64,256]{1,0:T(8,128)(2,1)S(1)} %get-tuple-element.50), channel_id=1, source_target_pairs={{0,8},{2,10},{4,12},{6,14},{8,0},{10,2},{12,4},{14,6},{1,9},{3,11}... | collective-permute-start | bytes 98312 | tf_op jit(solution)/shard_map/ppermute | solution.py:69
  75.6 5.2 %collective-permute-start.16 = (bf16[64,256]{1,0:T(8,128)(2,1)S(1)}, bf16[64,256]{1,0:T(8,128)(2,1)S(1)}, u32[]{:S(2)}, u32[]{:S(2)}) collective-permute-start(bf16[64,256]{1,0:T(8,128)(2,1)S(1)} %get-tuple-element.51), channel_id=1, source_target_pairs={{0,8},{2,10},{4,12},{6,14},{8,0},{10,2},{12,4},{14,6},{1,9},{3,11}... | collective-permute-start | bytes 98312 | tf_op jit(solution)/shard_map/ppermute | solution.py:69
  75.7 5.3 %collective-permute-start.10 = (bf16[64,256]{1,0:T(8,128)(2,1)S(1)}, bf16[64,256]{1,0:T(8,128)(2,1)S(1)}, u32[]{:S(2)}, u32[]{:S(2)}) collective-permute-start(bf16[64,256]{1,0:T(8,128)(2,1)S(1)} %multiply_convert_fusion.2), channel_id=1, source_target_pairs={{0,8},{2,10},{4,12},{6,14},{8,0},{10,2},{12,4},{14,6},{1,9},{3,11}... | collective-permute-start | bytes 98312 | tf_op jit(solution)/shard_map/ppermute | solution.py:69
  78.9 4.9 %collective-permute-start.23 = (bf16[2,64,256]{2,1,0:T(8,128)(2,1)S(1)}, bf16[2,64,256]{2,1,0:T(8,128)(2,1)S(1)}, u32[]{:S(2)}, u32[]{:S(2)}) collective-permute-start(bf16[2,64,256]{2,1,0:T(8,128)(2,1)S(1)} %pad_maximum_fusion.8), channel_id=1, source_target_pairs={{0,4},{2,6},{4,0},{6,2},{8,12},{10,14},{12,8},{14,10},{1,5},{3,7},... | collective-permute-start | bytes 196616 | tf_op jit(solution)/shard_map/ppermute | solution.py:69
  80.9 4.4 %collective-permute-start.17 = (bf16[2,64,256]{2,1,0:T(8,128)(2,1)S(1)}, bf16[2,64,256]{2,1,0:T(8,128)(2,1)S(1)}, u32[]{:S(2)}, u32[]{:S(2)}) collective-permute-start(bf16[2,64,256]{2,1,0:T(8,128)(2,1)S(1)} %pad_maximum_fusion.7), channel_id=1, source_target_pairs={{0,4},{2,6},{4,0},{6,2},{8,12},{10,14},{12,8},{14,10},{1,5},{3,7},... | collective-permute-start | bytes 196616 | tf_op jit(solution)/shard_map/ppermute | solution.py:69
  81.1 5.1 %collective-permute-start.11 = (bf16[2,64,256]{2,1,0:T(8,128)(2,1)S(1)}, bf16[2,64,256]{2,1,0:T(8,128)(2,1)S(1)}, u32[]{:S(2)}, u32[]{:S(2)}) collective-permute-start(bf16[2,64,256]{2,1,0:T(8,128)(2,1)S(1)} %pad_maximum_fusion.6), channel_id=1, source_target_pairs={{0,2},{2,0},{4,6},{6,4},{8,10},{10,8},{12,14},{14,12},{1,3},{3,1},... | collective-permute-start | bytes 196616 | tf_op jit(solution)/shard_map/ppermute | solution.py:69
  83.1 5.6 %collective-permute-start.6 = (bf16[2,2,64,256]{3,2,1,0:T(8,128)(2,1)S(1)}, bf16[2,2,64,256]{3,2,1,0:T(8,128)(2,1)S(1)}, u32[]{:S(2)}, u32[]{:S(2)}) collective-permute-start(bf16[2,2,64,256]{3,2,1,0:T(8,128)(2,1)S(1)} %pad_maximum_fusion.1), channel_id=1, source_target_pairs={{0,2},{2,0},{4,6},{6,4},{8,10},{10,8},{12,14},{14,12},{1,3},{3,1},... | collective-permute-start | bytes 393224 | tf_op jit(solution)/shard_map/ppermute | solution.py:69
  83.8 6.3 %collective-permute-start.24 = (bf16[2,2,64,256]{3,2,1,0:T(8,128)(2,1)S(1)}, bf16[2,2,64,256]{3,2,1,0:T(8,128)(2,1)S(1)}, u32[]{:S(2)}, u32[]{:S(2)}) collective-permute-start(bf16[2,2,64,256]{3,2,1,0:T(8,128)(2,1)S(1)} %pad_maximum_fusion.4), channel_id=1, source_target_pairs={{0,2},{2,0},{4,6},{6,4},{8,10},{10,8},{12,14},{14,12},{1,3},{3,1},... | collective-permute-start | bytes 393224 | tf_op jit(solution)/shard_map/ppermute | solution.py:69
  85.3 6.2 %collective-permute-start.18 = (bf16[2,2,64,256]{3,2,1,0:T(8,128)(2,1)S(1)}, bf16[2,2,64,256]{3,2,1,0:T(8,128)(2,1)S(1)}, u32[]{:S(2)}, u32[]{:S(2)}) collective-permute-start(bf16[2,2,64,256]{3,2,1,0:T(8,128)(2,1)S(1)} %pad_maximum_fusion.3), channel_id=1, source_target_pairs={{0,2},{2,0},{4,6},{6,4},{8,10},{10,8},{12,14},{14,12},{1,3},{3,1},... | collective-permute-start | bytes 393224 | tf_op jit(solution)/shard_map/ppermute | solution.py:69
  86.2 7.1 %collective-permute-start.12 = (bf16[2,2,64,256]{3,2,1,0:T(8,128)(2,1)S(1)}, bf16[2,2,64,256]{3,2,1,0:T(8,128)(2,1)S(1)}, u32[]{:S(2)}, u32[]{:S(2)}) collective-permute-start(bf16[2,2,64,256]{3,2,1,0:T(8,128)(2,1)S(1)} %pad_maximum_fusion.2), channel_id=1, source_target_pairs={{0,4},{2,6},{4,0},{6,2},{8,12},{10,14},{12,8},{14,10},{1,5},{3,7},... | collective-permute-start | bytes 393224 | tf_op jit(solution)/shard_map/ppermute | solution.py:69
  (11 other events, 124.4 us)

commit v12 on v10

--- a/solution.py
+++ b/solution.py
@@ -193,9 +193,9 @@
     partial_sum = lax.dot_general(
         latent_t, decoder, (((0,), (0,)), ((), ())), preferred_element_type=jnp.float32
     )
-    chunk = partial_sum.shape[0] // 4
+    chunk = partial_sum.shape[0] // 8
     error_parts = []
-    for part in range(4):
+    for part in range(8):
         rows = slice(part * chunk, (part + 1) * chunk)
         order = (first, second)[part % 2]
         total, block = _halving_cols(partial_sum[rows], "lat", lat_size, order)

time: 121 us -> 144 us (1.19)
  starting transfers between devices: 33.5 us -> 64.9 us
  waiting for transfers between devices: 38.6 us -> 26.9 us
  local copies, waits for them, and re-layouts: 7.6 us -> 9.93 us
    ppermute x24 -> x48, starting transfers between devices: 26.2 us -> 57.6 us  [_pair_swap(): return lax.ppermute(value, axis, [(i, i ^ mask) for i in range(size)])]
    ppermute x24 -> x48, waiting for transfers between devices: 23.7 us -> 12 us  [_pair_swap(): return lax.ppermute(value, axis, [(i, i ^ mask) for i in range(size)])]
    gather x4 -> x8, local copies, waits for them, and re-layouts: 2.25 us -> 4.44 us  [local(): error_parts.append(stacked[jnp.array(_block_owners(lat_size, order))])]
  transfers between devices with their start and end apart: 26 -> 50, of which waited for: 16 -> 13; matrix products, arithmetic and copies ran while one was open for 3% -> 4% of each run, Pallas kernels for 0% -> 0%
where the time goes in v12:
time: 144 us
  starting transfers between devices  64.9 us (45%)
  Pallas kernels  28.7 us (20%)
  waiting for transfers between devices  26.9 us (19%)
  local copies, waits for them, and re-layouts  9.93 us (7%)
  matrix products  8.65 us (6%)
  other arithmetic  2.71 us (2%)
  between operations  1.78 us (1%)
    ppermute x48, starting transfers between devices, _pair_swap(): return lax.ppermute(value, axis, [(i, i ^ mask) for i in range(size)])  57.6 us
    pallas_call x1, Pallas kernels, tail(): pl.pallas_call(_tail_kernel, grid=(n_lat // tile,), in_specs=[pl.BlockSpe...  28.7 us
    all_to_all x1, waiting for transfers between devices, local(): act_blocks = lax.all_to_all(copies, 'lat', 0, 0, tiled=True)  13.1 us
    ppermute x48, waiting for transfers between devices, _pair_swap(): return lax.ppermute(value, axis, [(i, i ^ mask) for i in range(size)])  12 us
    all_to_all x1, starting transfers between devices, local(): act_blocks = lax.all_to_all(copies, 'lat', 0, 0, tiled=True)  7.25 us
    dot_general x1, matrix products, local(): lax.dot_general(weight_in, centered, (((1,), (1,)), ((), ())), preferred_...  6.3 us
    gather x8, local copies, waits for them, and re-layouts, local(): error_parts.append(stacked[jnp.array(_block_owners(lat_size, order))])  4.44 us
  transfers between devices with their start and end apart: 50, of which 13 were waited for; matrix products, arithmetic and copies ran while one was open for 4% of the time, Pallas kernels for 0%

profile of v12, /device:TPU:0, one launch (start us, length us, event | category | flops | bytes accessed | tf_op | source)
XLA Modules:
  0.0 143.6 jit_solution(15395479358574791232)
XLA Ops:
  0.7 1.7 %broadcast_in_dim.35 = bf16[8,128,256]{2,1,0:T(8,128)(2,1)} broadcast(bf16[128,256]{1,0:T(8,128)(2,1)} %param.17), dimensions={1,2} | broadcast | bytes 589824 | tf_op jit(solution)/shard_map/broadcast_in_dim | solution.py:171
  2.4 7.3 %all-to-all-start = ((bf16[8,128,256]{2,1,0:T(8,128)(2,1)}), bf16[8,128,256]{2,1,0:T(8,128)(2,1)S(1)}, u32[]{:S(2)}, u32[]{:S(2)}) async-start(bf16[8,128,256]{2,1,0:T(8,128)(2,1)} %broadcast_in_dim.35), calls=%async_computation | async-start | bytes 1048576 | tf_op jit(solution)/shard_map/all_to_all | solution.py:172
  11.0 13.1 %all-to-all-done = bf16[8,128,256]{2,1,0:T(8,128)(2,1)S(1)} async-done(((bf16[8,128,256]{2,1,0:T(8,128)(2,1)}), bf16[8,128,256]{2,1,0:T(8,128)(2,1)S(1)}, u32[]{:S(2)}, u32[]{:S(2)}) %all-to-all-start) | async-done | bytes 524320 | tf_op jit(solution)/shard_map/all_to_all | solution.py:172
  24.3 1.8 %collective-permute-done = bf16[128,2048]{1,0:T(8,128)(2,1)S(1)} collective-permute-done((bf16[128,2048]{1,0:T(8,128)(2,1)S(1)}, bf16[128,2048]{1,0:T(8,128)(2,1)S(1)}, u32[]{:S(2)}, u32[]{:S(2)}) %collective-permute-start) | collective-permute-done | bytes 524320 | tf_op jit(solution)/shard_map/ppermute | solution.py:174
  28.4 6.3 %fusion.pre_ref = f32[2048,256]{1,0:T(8,128)S(1)} fusion(bf16[256,2048]{1,0:T(8,128)(2,1)S(1)} %get-tuple-element.9.cen_ref, f32[2048]{0:T(1024)S(1)} %bitcast.180, bf16[1,2048,2048]{2,1,0:T(8,128)(2,1)} %param.20), kind=kOutput, calls=%fused_computation.10 | convolution fusion | flops 2148007936 | bytes 11542528 | tf_op jit(solution)/shard_map/dot_general | solution.py:187
  34.7 2.3 %fusion.1 = f32[256,2048]{1,0:T(8,128)S(1)} fusion(f32[2048,256]{1,0:T(8,128)S(1)} %fusion.pre_ref, bf16[1,2048,2048]{2,1,0:T(8,128)(2,1)S(1)} %bitcast.153), kind=kOutput, calls=%fused_computation.13 | convolution fusion | flops 2148532224 | bytes 12582912 | tf_op jit(solution)/shard_map/dot_general | solution.py:193
  37.4 1.5 %collective-permute-start.1 = (f32[32,1024]{1,0:T(8,128)S(1)}, f32[32,1024]{1,0:T(8,128)S(1)}, u32[]{:S(2)}, u32[]{:S(2)}) collective-permute-start(f32[32,1024]{1,0:T(8,128)S(1)} %constant_dynamic-slice_fusion.27), channel_id=1, source_target_pairs={{0,2},{2,0},{4,6},{6,4},{8,10},{10,8},{12,14},{14,12},{1,3},{3,1},... | collective-permute-start | bytes 393224 | tf_op jit(solution)/shard_map/ppermute | solution.py:69
  44.6 2.0 %collective-permute-done.13 = f32[32,1024]{1,0:T(8,128)S(1)} collective-permute-done((f32[32,1024]{1,0:T(8,128)S(1)}, f32[32,1024]{1,0:T(8,128)S(1)}, u32[]{:S(2)}, u32[]{:S(2)}) %collective-permute-start.13) | collective-permute-done | bytes 131104 | tf_op jit(solution)/shard_map/ppermute | solution.py:69
  48.8 1.5 %collective-permute-start.2 = (f32[32,512]{1,0:T(8,128)S(1)}, f32[32,512]{1,0:T(8,128)S(1)}, u32[]{:S(2)}, u32[]{:S(2)}) collective-permute-start(f32[32,512]{1,0:T(8,128)S(1)} %constant_dynamic-slice_fusion.26), channel_id=1, source_target_pairs={{0,4},{2,6},{4,0},{6,2},{8,12},{10,14},{12,8},{14,10},{1,5},{3,7},... | collective-permute-start | bytes 196616 | tf_op jit(solution)/shard_map/ppermute | solution.py:69
  51.3 1.8 %collective-permute-start.8 = (f32[32,512]{1,0:T(8,128)S(1)}, f32[32,512]{1,0:T(8,128)S(1)}, u32[]{:S(2)}, u32[]{:S(2)}) collective-permute-start(f32[32,512]{1,0:T(8,128)S(1)} %constant_dynamic-slice_fusion.19), channel_id=1, source_target_pairs={{0,2},{2,0},{4,6},{6,4},{8,10},{10,8},{12,14},{14,12},{1,3},{3,1},... | collective-permute-start | bytes 196616 | tf_op jit(solution)/shard_map/ppermute | solution.py:69
  60.3 1.7 %collective-permute-start.15 = (f32[32,256]{1,0:T(8,128)S(1)}, f32[32,256]{1,0:T(8,128)S(1)}, u32[]{:S(2)}, u32[]{:S(2)}) collective-permute-start(f32[32,256]{1,0:T(8,128)S(1)} %constant_dynamic-slice_fusion.13), channel_id=1, source_target_pairs={{0,8},{2,10},{4,12},{6,14},{8,0},{10,2},{12,4},{14,6},{1,9},{3,11}... | collective-permute-start | bytes 98312 | tf_op jit(solution)/shard_map/ppermute | solution.py:69
  63.4 1.7 %collective-permute-start.27 = (f32[32,256]{1,0:T(8,128)S(1)}, f32[32,256]{1,0:T(8,128)S(1)}, u32[]{:S(2)}, u32[]{:S(2)}) collective-permute-start(f32[32,256]{1,0:T(8,128)S(1)} %constant_dynamic-slice_fusion.6), channel_id=1, source_target_pairs={{0,8},{2,10},{4,12},{6,14},{8,0},{10,2},{12,4},{14,6},{1,9},{3,11}... | collective-permute-start | bytes 98312 | tf_op jit(solution)/shard_map/ppermute | solution.py:69
  66.6 1.7 %collective-permute-start.21 = (f32[32,256]{1,0:T(8,128)S(1)}, f32[32,256]{1,0:T(8,128)S(1)}, u32[]{:S(2)}, u32[]{:S(2)}) collective-permute-start(f32[32,256]{1,0:T(8,128)S(1)} %constant_dynamic-slice_fusion.10), channel_id=1, source_target_pairs={{0,8},{2,10},{4,12},{6,14},{8,0},{10,2},{12,4},{14,6},{1,9},{3,11}... | collective-permute-start | bytes 98312 | tf_op jit(solution)/shard_map/ppermute | solution.py:69
  71.3 1.5 %collective-permute-start.40 = (bf16[32,256]{1,0:T(8,128)(2,1)S(1)}, bf16[32,256]{1,0:T(8,128)(2,1)S(1)}, u32[]{:S(2)}, u32[]{:S(2)}) collective-permute-start(bf16[32,256]{1,0:T(8,128)(2,1)S(1)} %get-tuple-element.85), channel_id=1, source_target_pairs={{0,8},{2,10},{4,12},{6,14},{8,0},{10,2},{12,4},{14,6},{1,9},{3,11}... | collective-permute-start | bytes 49160 | tf_op jit(solution)/shard_map/ppermute | solution.py:69
  77.2 1.5 %collective-permute-start.46 = (bf16[32,256]{1,0:T(8,128)(2,1)S(1)}, bf16[32,256]{1,0:T(8,128)(2,1)S(1)}, u32[]{:S(2)}, u32[]{:S(2)}) collective-permute-start(bf16[32,256]{1,0:T(8,128)(2,1)S(1)} %get-tuple-element.81), channel_id=1, source_target_pairs={{0,8},{2,10},{4,12},{6,14},{8,0},{10,2},{12,4},{14,6},{1,9},{3,11}... | collective-permute-start | bytes 49160 | tf_op jit(solution)/shard_map/ppermute | solution.py:69
  78.8 1.6 %collective-permute-done.4 = bf16[32,256]{1,0:T(8,128)(2,1)S(1)} collective-permute-done((bf16[32,256]{1,0:T(8,128)(2,1)S(1)}, bf16[32,256]{1,0:T(8,128)(2,1)S(1)}, u32[]{:S(2)}, u32[]{:S(2)}) %collective-permute-start.4) | collective-permute-done | bytes 16416 | tf_op jit(solution)/shard_map/ppermute | solution.py:69
  81.9 1.5 %collective-permute-start.22 = (bf16[32,256]{1,0:T(8,128)(2,1)S(1)}, bf16[32,256]{1,0:T(8,128)(2,1)S(1)}, u32[]{:S(2)}, u32[]{:S(2)}) collective-permute-start(bf16[32,256]{1,0:T(8,128)(2,1)S(1)} %get-tuple-element.83), channel_id=1, source_target_pairs={{0,8},{2,10},{4,12},{6,14},{8,0},{10,2},{12,4},{14,6},{1,9},{3,11}... | collective-permute-start | bytes 49160 | tf_op jit(solution)/shard_map/ppermute | solution.py:69
  83.4 1.5 %collective-permute-start.10 = (bf16[32,256]{1,0:T(8,128)(2,1)S(1)}, bf16[32,256]{1,0:T(8,128)(2,1)S(1)}, u32[]{:S(2)}, u32[]{:S(2)}) collective-permute-start(bf16[32,256]{1,0:T(8,128)(2,1)S(1)} %get-tuple-element.84), channel_id=1, source_target_pairs={{0,8},{2,10},{4,12},{6,14},{8,0},{10,2},{12,4},{14,6},{1,9},{3,11}... | collective-permute-start | bytes 49160 | tf_op jit(solution)/shard_map/ppermute | solution.py:69
  85.0 1.7 %collective-permute-start.41 = (bf16[2,32,256]{2,1,0:T(8,128)(2,1)S(1)}, bf16[2,32,256]{2,1,0:T(8,128)(2,1)S(1)}, u32[]{:S(2)}, u32[]{:S(2)}) collective-permute-start(bf16[2,32,256]{2,1,0:T(8,128)(2,1)S(1)} %pad_maximum_fusion.15), channel_id=1, source_target_pairs={{0,4},{2,6},{4,0},{6,2},{8,12},{10,14},{12,8},{14,10},{1,5},{3,7},... | collective-permute-start | bytes 98312 | tf_op jit(solution)/shard_map/ppermute | solution.py:69
  88.6 1.7 %collective-permute-start.17 = (bf16[2,32,256]{2,1,0:T(8,128)(2,1)S(1)}, bf16[2,32,256]{2,1,0:T(8,128)(2,1)S(1)}, u32[]{:S(2)}, u32[]{:S(2)}) collective-permute-start(bf16[2,32,256]{2,1,0:T(8,128)(2,1)S(1)} %pad_maximum_fusion.11), channel_id=1, source_target_pairs={{0,4},{2,6},{4,0},{6,2},{8,12},{10,14},{12,8},{14,10},{1,5},{3,7},... | collective-permute-start | bytes 98312 | tf_op jit(solution)/shard_map/ppermute | solution.py:69
  90.8 1.7 %collective-permute-start.47 = (bf16[2,32,256]{2,1,0:T(8,128)(2,1)S(1)}, bf16[2,32,256]{2,1,0:T(8,128)(2,1)S(1)}, u32[]{:S(2)}, u32[]{:S(2)}) collective-permute-start(bf16[2,32,256]{2,1,0:T(8,128)(2,1)S(1)} %pad_maximum_fusion.16), channel_id=1, source_target_pairs={{0,2},{2,0},{4,6},{6,4},{8,10},{10,8},{12,14},{14,12},{1,3},{3,1},... | collective-permute-start | bytes 98312 | tf_op jit(solution)/shard_map/ppermute | solution.py:69
  92.5 1.8 %collective-permute-done.5 = bf16[2,32,256]{2,1,0:T(8,128)(2,1)S(1)} collective-permute-done((bf16[2,32,256]{2,1,0:T(8,128)(2,1)S(1)}, bf16[2,32,256]{2,1,0:T(8,128)(2,1)S(1)}, u32[]{:S(2)}, u32[]{:S(2)}) %collective-permute-start.5) | collective-permute-done | bytes 32800 | tf_op jit(solution)/shard_map/ppermute | solution.py:69
  98.7 1.8 %collective-permute-done.11 = bf16[2,32,256]{2,1,0:T(8,128)(2,1)S(1)} collective-permute-done((bf16[2,32,256]{2,1,0:T(8,128)(2,1)S(1)}, bf16[2,32,256]{2,1,0:T(8,128)(2,1)S(1)}, u32[]{:S(2)}, u32[]{:S(2)}) %collective-permute-start.11) | collective-permute-done | bytes 32800 | tf_op jit(solution)/shard_map/ppermute | solution.py:69
  114.8 28.7 %shard_map.184 = (bf16[2048,2048]{1,0:T(8,128)(2,1)}, bf16[2048,2048]{1,0:T(8,128)(2,1)}, bf16[2048,2048]{1,0:T(8,128)(2,1)}) custom-call(f32[2048,256]{1,0:T(8,128)} %copy-done, bf16[2048,256]{1,0:T(8,128)(2,1)} %bitcast.157, bf16[256,2048]{1,0:T(8,128)(2,1)} %copy-done.1, bf16[2048,2048]{1,0:T(8,128)(2,1)} %bitcast.151, bf16[2048,2048]{1,0:T(8,128)(2,1)} %bitcast.154, ...), custom_call_target="tpu_custom_call" | custom-call | tf_op jit(solution)/shard_map/pallas_call | solution.py:50
  (227 shorter events, 52.2 us)
Async XLA Ops:
  2.4 21.7 %all-to-all-start = ((bf16[8,128,256]{2,1,0:T(8,128)(2,1)}), bf16[8,128,256]{2,1,0:T(8,128)(2,1)S(1)}, u32[]{:S(2)}, u32[]{:S(2)}) async-start(bf16[8,128,256]{2,1,0:T(8,128)(2,1)} %broadcast_in_dim.35), calls=%async_computation | async-start | bytes 1048576 | tf_op jit(solution)/shard_map/all_to_all | solution.py:172
  39.0 7.7 %collective-permute-start.13 = (f32[32,1024]{1,0:T(8,128)S(1)}, f32[32,1024]{1,0:T(8,128)S(1)}, u32[]{:S(2)}, u32[]{:S(2)}) collective-permute-start(f32[32,1024]{1,0:T(8,128)S(1)} %constant_dynamic-slice_fusion.15), channel_id=1, source_target_pairs={{0,2},{2,0},{4,6},{6,4},{8,10},{10,8},{12,14},{14,12},{1,3},{3,1},... | collective-permute-start | bytes 393224 | tf_op jit(solution)/shard_map/ppermute | solution.py:69
  39.6 8.5 %collective-permute-start.7 = (f32[32,1024]{1,0:T(8,128)S(1)}, f32[32,1024]{1,0:T(8,128)S(1)}, u32[]{:S(2)}, u32[]{:S(2)}) collective-permute-start(f32[32,1024]{1,0:T(8,128)S(1)} %constant_dynamic-slice_fusion.20), channel_id=1, source_target_pairs={{0,4},{2,6},{4,0},{6,2},{8,12},{10,14},{12,8},{14,10},{1,5},{3,7},... | collective-permute-start | bytes 393224 | tf_op jit(solution)/shard_map/ppermute | solution.py:69
  40.4 8.4 %collective-permute-start.19 = (f32[32,1024]{1,0:T(8,128)S(1)}, f32[32,1024]{1,0:T(8,128)S(1)}, u32[]{:S(2)}, u32[]{:S(2)}) collective-permute-start(f32[32,1024]{1,0:T(8,128)S(1)} %constant_dynamic-slice_fusion.12), channel_id=1, source_target_pairs={{0,4},{2,6},{4,0},{6,2},{8,12},{10,14},{12,8},{14,10},{1,5},{3,7},... | collective-permute-start | bytes 393224 | tf_op jit(solution)/shard_map/ppermute | solution.py:69
  41.6 8.8 %collective-permute-start.25 = (f32[32,1024]{1,0:T(8,128)S(1)}, f32[32,1024]{1,0:T(8,128)S(1)}, u32[]{:S(2)}, u32[]{:S(2)}) collective-permute-start(f32[32,1024]{1,0:T(8,128)S(1)} %constant_dynamic-slice_fusion.8), channel_id=1, source_target_pairs={{0,2},{2,0},{4,6},{6,4},{8,10},{10,8},{12,14},{14,12},{1,3},{3,1},... | collective-permute-start | bytes 393224 | tf_op jit(solution)/shard_map/ppermute | solution.py:69
  43.9 7.5 %collective-permute-start.31 = (f32[32,1024]{1,0:T(8,128)S(1)}, f32[32,1024]{1,0:T(8,128)S(1)}, u32[]{:S(2)}, u32[]{:S(2)}) collective-permute-start(f32[32,1024]{1,0:T(8,128)S(1)} %constant_dynamic-slice_fusion.5), channel_id=1, source_target_pairs={{0,4},{2,6},{4,0},{6,2},{8,12},{10,14},{12,8},{14,10},{1,5},{3,7},... | collective-permute-start | bytes 393224 | tf_op jit(solution)/shard_map/ppermute | solution.py:69
  48.8 7.0 %collective-permute-start.2 = (f32[32,512]{1,0:T(8,128)S(1)}, f32[32,512]{1,0:T(8,128)S(1)}, u32[]{:S(2)}, u32[]{:S(2)}) collective-permute-start(f32[32,512]{1,0:T(8,128)S(1)} %constant_dynamic-slice_fusion.26), channel_id=1, source_target_pairs={{0,4},{2,6},{4,0},{6,2},{8,12},{10,14},{12,8},{14,10},{1,5},{3,7},... | collective-permute-start | bytes 196616 | tf_op jit(solution)/shard_map/ppermute | solution.py:69
  58.9 7.7 %collective-permute-start.3 = (f32[32,256]{1,0:T(8,128)S(1)}, f32[32,256]{1,0:T(8,128)S(1)}, u32[]{:S(2)}, u32[]{:S(2)}) collective-permute-start(f32[32,256]{1,0:T(8,128)S(1)} %constant_dynamic-slice_fusion.25), channel_id=1, source_target_pairs={{0,8},{2,10},{4,12},{6,14},{8,0},{10,2},{12,4},{14,6},{1,9},{3,11}... | collective-permute-start | bytes 98312 | tf_op jit(solution)/shard_map/ppermute | solution.py:69
  60.3 8.0 %collective-permute-start.15 = (f32[32,256]{1,0:T(8,128)S(1)}, f32[32,256]{1,0:T(8,128)S(1)}, u32[]{:S(2)}, u32[]{:S(2)}) collective-permute-start(f32[32,256]{1,0:T(8,128)S(1)} %constant_dynamic-slice_fusion.13), channel_id=1, source_target_pairs={{0,8},{2,10},{4,12},{6,14},{8,0},{10,2},{12,4},{14,6},{1,9},{3,11}... | collective-permute-start | bytes 98312 | tf_op jit(solution)/shard_map/ppermute | solution.py:69
  62.0 10.8 %collective-permute-start.9 = (f32[32,256]{1,0:T(8,128)S(1)}, f32[32,256]{1,0:T(8,128)S(1)}, u32[]{:S(2)}, u32[]{:S(2)}) collective-permute-start(f32[32,256]{1,0:T(8,128)S(1)} %constant_dynamic-slice_fusion.18), channel_id=1, source_target_pairs={{0,8},{2,10},{4,12},{6,14},{8,0},{10,2},{12,4},{14,6},{1,9},{3,11}... | collective-permute-start | bytes 98312 | tf_op jit(solution)/shard_map/ppermute | solution.py:69
  66.6 7.7 %collective-permute-start.21 = (f32[32,256]{1,0:T(8,128)S(1)}, f32[32,256]{1,0:T(8,128)S(1)}, u32[]{:S(2)}, u32[]{:S(2)}) collective-permute-start(f32[32,256]{1,0:T(8,128)S(1)} %constant_dynamic-slice_fusion.10), channel_id=1, source_target_pairs={{0,8},{2,10},{4,12},{6,14},{8,0},{10,2},{12,4},{14,6},{1,9},{3,11}... | collective-permute-start | bytes 98312 | tf_op jit(solution)/shard_map/ppermute | solution.py:69
  68.3 7.5 %collective-permute-start.33 = (f32[32,256]{1,0:T(8,128)S(1)}, f32[32,256]{1,0:T(8,128)S(1)}, u32[]{:S(2)}, u32[]{:S(2)}) collective-permute-start(f32[32,256]{1,0:T(8,128)S(1)} %constant_dynamic-slice_fusion.3), channel_id=1, source_target_pairs={{0,8},{2,10},{4,12},{6,14},{8,0},{10,2},{12,4},{14,6},{1,9},{3,11}... | collective-permute-start | bytes 98312 | tf_op jit(solution)/shard_map/ppermute | solution.py:69
  69.8 7.4 %collective-permute-start.45 = (f32[32,256]{1,0:T(8,128)S(1)}, f32[32,256]{1,0:T(8,128)S(1)}, u32[]{:S(2)}, u32[]{:S(2)}) collective-permute-start(f32[32,256]{1,0:T(8,128)S(1)} %constant_dynamic-slice_fusion.21), channel_id=1, source_target_pairs={{0,8},{2,10},{4,12},{6,14},{8,0},{10,2},{12,4},{14,6},{1,9},{3,11}... | collective-permute-start | bytes 98312 | tf_op jit(solution)/shard_map/ppermute | solution.py:69
  71.3 12.2 %collective-permute-start.40 = (bf16[32,256]{1,0:T(8,128)(2,1)S(1)}, bf16[32,256]{1,0:T(8,128)(2,1)S(1)}, u32[]{:S(2)}, u32[]{:S(2)}) collective-permute-start(bf16[32,256]{1,0:T(8,128)(2,1)S(1)} %get-tuple-element.85), channel_id=1, source_target_pairs={{0,8},{2,10},{4,12},{6,14},{8,0},{10,2},{12,4},{14,6},{1,9},{3,11}... | collective-permute-start | bytes 49160 | tf_op jit(solution)/shard_map/ppermute | solution.py:69
  72.8 12.2 %collective-permute-start.28 = (bf16[32,256]{1,0:T(8,128)(2,1)S(1)}, bf16[32,256]{1,0:T(8,128)(2,1)S(1)}, u32[]{:S(2)}, u32[]{:S(2)}) collective-permute-start(bf16[32,256]{1,0:T(8,128)(2,1)S(1)} %get-tuple-element.86), channel_id=1, source_target_pairs={{0,8},{2,10},{4,12},{6,14},{8,0},{10,2},{12,4},{14,6},{1,9},{3,11}... | collective-permute-start | bytes 49160 | tf_op jit(solution)/shard_map/ppermute | solution.py:69
  74.3 7.6 %collective-permute-start.16 = (bf16[32,256]{1,0:T(8,128)(2,1)S(1)}, bf16[32,256]{1,0:T(8,128)(2,1)S(1)}, u32[]{:S(2)}, u32[]{:S(2)}) collective-permute-start(bf16[32,256]{1,0:T(8,128)(2,1)S(1)} %get-tuple-element.87), channel_id=1, source_target_pairs={{0,8},{2,10},{4,12},{6,14},{8,0},{10,2},{12,4},{14,6},{1,9},{3,11}... | collective-permute-start | bytes 49160 | tf_op jit(solution)/shard_map/ppermute | solution.py:69
  77.2 13.0 %collective-permute-start.46 = (bf16[32,256]{1,0:T(8,128)(2,1)S(1)}, bf16[32,256]{1,0:T(8,128)(2,1)S(1)}, u32[]{:S(2)}, u32[]{:S(2)}) collective-permute-start(bf16[32,256]{1,0:T(8,128)(2,1)S(1)} %get-tuple-element.81), channel_id=1, source_target_pairs={{0,8},{2,10},{4,12},{6,14},{8,0},{10,2},{12,4},{14,6},{1,9},{3,11}... | collective-permute-start | bytes 49160 | tf_op jit(solution)/shard_map/ppermute | solution.py:69
  80.4 10.4 %collective-permute-start.34 = (bf16[32,256]{1,0:T(8,128)(2,1)S(1)}, bf16[32,256]{1,0:T(8,128)(2,1)S(1)}, u32[]{:S(2)}, u32[]{:S(2)}) collective-permute-start(bf16[32,256]{1,0:T(8,128)(2,1)S(1)} %get-tuple-element.82), channel_id=1, source_target_pairs={{0,8},{2,10},{4,12},{6,14},{8,0},{10,2},{12,4},{14,6},{1,9},{3,11}... | collective-permute-start | bytes 49160 | tf_op jit(solution)/shard_map/ppermute | solution.py:69
  85.0 11.4 %collective-permute-start.41 = (bf16[2,32,256]{2,1,0:T(8,128)(2,1)S(1)}, bf16[2,32,256]{2,1,0:T(8,128)(2,1)S(1)}, u32[]{:S(2)}, u32[]{:S(2)}) collective-permute-start(bf16[2,32,256]{2,1,0:T(8,128)(2,1)S(1)} %pad_maximum_fusion.15), channel_id=1, source_target_pairs={{0,4},{2,6},{4,0},{6,2},{8,12},{10,14},{12,8},{14,10},{1,5},{3,7},... | collective-permute-start | bytes 98312 | tf_op jit(solution)/shard_map/ppermute | solution.py:69
  88.1 9.6 %collective-permute-start.29 = (bf16[2,32,256]{2,1,0:T(8,128)(2,1)S(1)}, bf16[2,32,256]{2,1,0:T(8,128)(2,1)S(1)}, u32[]{:S(2)}, u32[]{:S(2)}) collective-permute-start(bf16[2,32,256]{2,1,0:T(8,128)(2,1)S(1)} %pad_maximum_fusion.13), channel_id=1, source_target_pairs={{0,4},{2,6},{4,0},{6,2},{8,12},{10,14},{12,8},{14,10},{1,5},{3,7},... | collective-permute-start | bytes 98312 | tf_op jit(solution)/shard_map/ppermute | solution.py:69
  90.8 11.8 %collective-permute-start.47 = (bf16[2,32,256]{2,1,0:T(8,128)(2,1)S(1)}, bf16[2,32,256]{2,1,0:T(8,128)(2,1)S(1)}, u32[]{:S(2)}, u32[]{:S(2)}) collective-permute-start(bf16[2,32,256]{2,1,0:T(8,128)(2,1)S(1)} %pad_maximum_fusion.16), channel_id=1, source_target_pairs={{0,2},{2,0},{4,6},{6,4},{8,10},{10,8},{12,14},{14,12},{1,3},{3,1},... | collective-permute-start | bytes 98312 | tf_op jit(solution)/shard_map/ppermute | solution.py:69
  94.3 9.7 %collective-permute-start.35 = (bf16[2,32,256]{2,1,0:T(8,128)(2,1)S(1)}, bf16[2,32,256]{2,1,0:T(8,128)(2,1)S(1)}, u32[]{:S(2)}, u32[]{:S(2)}) collective-permute-start(bf16[2,32,256]{2,1,0:T(8,128)(2,1)S(1)} %pad_maximum_fusion.14), channel_id=1, source_target_pairs={{0,2},{2,0},{4,6},{6,4},{8,10},{10,8},{12,14},{14,12},{1,3},{3,1},... | collective-permute-start | bytes 98312 | tf_op jit(solution)/shard_map/ppermute | solution.py:69
  97.8 7.0 %collective-permute-start.42 = (bf16[2,2,32,256]{3,2,1,0:T(8,128)(2,1)S(1)}, bf16[2,2,32,256]{3,2,1,0:T(8,128)(2,1)S(1)}, u32[]{:S(2)}, u32[]{:S(2)}) collective-permute-start(bf16[2,2,32,256]{3,2,1,0:T(8,128)(2,1)S(1)} %pad_maximum_fusion.7), channel_id=1, source_target_pairs={{0,2},{2,0},{4,6},{6,4},{8,10},{10,8},{12,14},{14,12},{1,3},{3,1},... | collective-permute-start | bytes 196616 | tf_op jit(solution)/shard_map/ppermute | solution.py:69
  102.6 7.6 %collective-permute-start.6 = (bf16[2,2,32,256]{3,2,1,0:T(8,128)(2,1)S(1)}, bf16[2,2,32,256]{3,2,1,0:T(8,128)(2,1)S(1)}, u32[]{:S(2)}, u32[]{:S(2)}) collective-permute-start(bf16[2,2,32,256]{3,2,1,0:T(8,128)(2,1)S(1)} %pad_maximum_fusion.1), channel_id=1, source_target_pairs={{0,2},{2,0},{4,6},{6,4},{8,10},{10,8},{12,14},{14,12},{1,3},{3,1},... | collective-permute-start | bytes 196616 | tf_op jit(solution)/shard_map/ppermute | solution.py:69
  (35 other events, 268.1 us)

commit v13 on v10

--- a/solution.py
+++ b/solution.py
@@ -29,9 +29,8 @@
     grad = jnp.dot(d_pre, cen_ref[...], preferred_element_type=jnp.float32)
     moment_one = beta_one * m1_ref[...].astype(jnp.float32) + (1.0 - beta_one) * grad
     moment_two = beta_two * m2_ref[...].astype(jnp.float32) + (1.0 - beta_two) * grad * grad
-    direction = moment_one / (
-        jnp.sqrt(moment_two * (corr_one * corr_one / corr_two)) + corr_one * adam_eps
-    )
+    scaled_two = moment_two * (corr_one * corr_one / corr_two)
+    direction = moment_one / (scaled_two * lax.rsqrt(scaled_two) + corr_one * adam_eps)
     old = enc_ref[...].astype(jnp.float32)
     w_out[...] = (old * (1.0 - rate_step * decay_rate) - rate_step * direction).astype(
         jnp.bfloat16

time: 121 us -> 121 us (level)
  no operation moved by 1% of the time
where the time goes in v13:
time: 121 us
  waiting for transfers between devices  38.6 us (32%)
  starting transfers between devices  33.6 us (28%)
  Pallas kernels  28.1 us (23%)
  matrix products  8.83 us (7%)
  local copies, waits for them, and re-layouts  7.6 us (6%)
  other arithmetic  2.66 us (2%)
  between operations  1.24 us (1%)
    pallas_call x1, Pallas kernels, tail(): pl.pallas_call(_tail_kernel, grid=(n_lat // tile,), in_specs=[pl.BlockSpe...  28.1 us
    ppermute x24, starting transfers between devices, _pair_swap(): return lax.ppermute(value, axis, [(i, i ^ mask) for i in range(size)])  26.2 us
    ppermute x24, waiting for transfers between devices, _pair_swap(): return lax.ppermute(value, axis, [(i, i ^ mask) for i in range(size)])  23.7 us
    all_to_all x1, waiting for transfers between devices, local(): act_blocks = lax.all_to_all(copies, 'lat', 0, 0, tiled=True)  13.1 us
    all_to_all x1, starting transfers between devices, local(): act_blocks = lax.all_to_all(copies, 'lat', 0, 0, tiled=True)  7.25 us
    dot_general x1, matrix products, local(): lax.dot_general(weight_in, centered, (((1,), (1,)), ((), ())), preferred_...  6.48 us
  transfers between devices with their start and end apart: 26, of which 16 were waited for; matrix products, arithmetic and copies ran while one was open for 3% of the time, Pallas kernels for 0%

profile of v13, /device:TPU:0, one launch (start us, length us, event | category | flops | bytes accessed | tf_op | source)
XLA Modules:
  0.0 120.5 jit_solution(5770225099930983746)
XLA Ops:
  0.7 1.7 %broadcast_in_dim.46 = bf16[8,128,256]{2,1,0:T(8,128)(2,1)} broadcast(bf16[128,256]{1,0:T(8,128)(2,1)} %param.13), dimensions={1,2} | broadcast | bytes 589824 | tf_op jit(solution)/shard_map/broadcast_in_dim | solution.py:170
  2.4 7.3 %all-to-all-start = ((bf16[8,128,256]{2,1,0:T(8,128)(2,1)}), bf16[8,128,256]{2,1,0:T(8,128)(2,1)S(1)}, u32[]{:S(2)}, u32[]{:S(2)}) async-start(bf16[8,128,256]{2,1,0:T(8,128)(2,1)} %broadcast_in_dim.46), calls=%async_computation | async-start | bytes 1048576 | tf_op jit(solution)/shard_map/all_to_all | solution.py:171
  11.0 13.1 %all-to-all-done = bf16[8,128,256]{2,1,0:T(8,128)(2,1)S(1)} async-done(((bf16[8,128,256]{2,1,0:T(8,128)(2,1)}), bf16[8,128,256]{2,1,0:T(8,128)(2,1)S(1)}, u32[]{:S(2)}, u32[]{:S(2)}) %all-to-all-start) | async-done | bytes 524320 | tf_op jit(solution)/shard_map/all_to_all | solution.py:171
  24.3 1.8 %collective-permute-done = bf16[128,2048]{1,0:T(8,128)(2,1)S(1)} collective-permute-done((bf16[128,2048]{1,0:T(8,128)(2,1)S(1)}, bf16[128,2048]{1,0:T(8,128)(2,1)S(1)}, u32[]{:S(2)}, u32[]{:S(2)}) %collective-permute-start) | collective-permute-done | bytes 524320 | tf_op jit(solution)/shard_map/ppermute | solution.py:173
  26.3 1.4 %gather_fusion = bf16[256,2048]{1,0:T(8,128)(2,1)S(1)} fusion(bf16[256,2048]{1,0:T(8,128)(2,1)S(1)} %pad_maximum_fusion, s32[1024]{0:T(1024)S(1)} %pad_clamp_fusion.2), kind=kCustom, calls=%fused_computation | custom fusion | bytes 2098176 | tf_op jit(solution)/shard_map/jit(_take)/gather | solution.py:180
  28.4 6.5 %fusion.pre_ref = f32[2048,256]{1,0:T(8,128)S(1)} fusion(bf16[256,2048]{1,0:T(8,128)(2,1)S(1)} %get-tuple-element.9.cen_ref, f32[2048]{0:T(1024)S(1)} %bitcast.116, bf16[1,2048,2048]{2,1,0:T(8,128)(2,1)} %param.16), kind=kOutput, calls=%fused_computation.6 | convolution fusion | flops 2148007936 | bytes 11542528 | tf_op jit(solution)/shard_map/dot_general | solution.py:186
  34.9 2.3 %fusion.1 = f32[256,2048]{1,0:T(8,128)S(1)} fusion(f32[2048,256]{1,0:T(8,128)S(1)} %fusion.pre_ref, bf16[1,2048,2048]{2,1,0:T(8,128)(2,1)S(1)} %bitcast.94), kind=kOutput, calls=%fused_computation.9 | convolution fusion | flops 2148532224 | bytes 12582912 | tf_op jit(solution)/shard_map/dot_general | solution.py:192
  39.7 1.5 %collective-permute-start.13 = (f32[64,1024]{1,0:T(8,128)S(1)}, f32[64,1024]{1,0:T(8,128)S(1)}, u32[]{:S(2)}, u32[]{:S(2)}) collective-permute-start(f32[64,1024]{1,0:T(8,128)S(1)} %constant_dynamic-slice_fusion.3), channel_id=1, source_target_pairs={{0,2},{2,0},{4,6},{6,4},{8,10},{10,8},{12,14},{14,12},{1,3},{3,1},... | collective-permute-start | bytes 786440 | tf_op jit(solution)/shard_map/ppermute | solution.py:68
  41.8 5.0 %collective-permute-done.7 = f32[64,1024]{1,0:T(8,128)S(1)} collective-permute-done((f32[64,1024]{1,0:T(8,128)S(1)}, f32[64,1024]{1,0:T(8,128)S(1)}, u32[]{:S(2)}, u32[]{:S(2)}) %collective-permute-start.7) | collective-permute-done | bytes 262176 | tf_op jit(solution)/shard_map/ppermute | solution.py:68
  46.9 1.5 %collective-permute-start.8 = (f32[64,512]{1,0:T(8,128)S(1)}, f32[64,512]{1,0:T(8,128)S(1)}, u32[]{:S(2)}, u32[]{:S(2)}) collective-permute-start(f32[64,512]{1,0:T(8,128)S(1)} %constant_dynamic-slice_fusion.8), channel_id=1, source_target_pairs={{0,2},{2,0},{4,6},{6,4},{8,10},{10,8},{12,14},{14,12},{1,3},{3,1},... | collective-permute-start | bytes 393224 | tf_op jit(solution)/shard_map/ppermute | solution.py:68
  48.4 3.2 %collective-permute-done.19 = f32[64,1024]{1,0:T(8,128)S(1)} collective-permute-done((f32[64,1024]{1,0:T(8,128)S(1)}, f32[64,1024]{1,0:T(8,128)S(1)}, u32[]{:S(2)}, u32[]{:S(2)}) %collective-permute-start.19) | collective-permute-done | bytes 262176 | tf_op jit(solution)/shard_map/ppermute | solution.py:68
  51.7 1.5 %collective-permute-start.20 = (f32[64,512]{1,0:T(8,128)S(1)}, f32[64,512]{1,0:T(8,128)S(1)}, u32[]{:S(2)}, u32[]{:S(2)}) collective-permute-start(f32[64,512]{1,0:T(8,128)S(1)} %constant_dynamic-slice_fusion.5), channel_id=1, source_target_pairs={{0,2},{2,0},{4,6},{6,4},{8,10},{10,8},{12,14},{14,12},{1,3},{3,1},... | collective-permute-start | bytes 393224 | tf_op jit(solution)/shard_map/ppermute | solution.py:68
  55.5 1.8 %collective-permute-done.8 = f32[64,512]{1,0:T(8,128)S(1)} collective-permute-done((f32[64,512]{1,0:T(8,128)S(1)}, f32[64,512]{1,0:T(8,128)S(1)}, u32[]{:S(2)}, u32[]{:S(2)}) %collective-permute-start.8) | collective-permute-done | bytes 131104 | tf_op jit(solution)/shard_map/ppermute | solution.py:68
  58.8 1.7 %collective-permute-start.21 = (f32[64,256]{1,0:T(8,128)S(1)}, f32[64,256]{1,0:T(8,128)S(1)}, u32[]{:S(2)}, u32[]{:S(2)}) collective-permute-start(f32[64,256]{1,0:T(8,128)S(1)} %constant_dynamic-slice_fusion.10), channel_id=1, source_target_pairs={{0,8},{2,10},{4,12},{6,14},{8,0},{10,2},{12,4},{14,6},{1,9},{3,11}... | collective-permute-start | bytes 196616 | tf_op jit(solution)/shard_map/ppermute | solution.py:68
  61.9 1.7 %collective-permute-start.3 = (f32[64,256]{1,0:T(8,128)S(1)}, f32[64,256]{1,0:T(8,128)S(1)}, u32[]{:S(2)}, u32[]{:S(2)}) collective-permute-start(f32[64,256]{1,0:T(8,128)S(1)} %constant_dynamic-slice_fusion.13), channel_id=1, source_target_pairs={{0,8},{2,10},{4,12},{6,14},{8,0},{10,2},{12,4},{14,6},{1,9},{3,11}... | collective-permute-start | bytes 196616 | tf_op jit(solution)/shard_map/ppermute | solution.py:68
  63.6 4.8 %collective-permute-done.9 = f32[64,256]{1,0:T(8,128)S(1)} collective-permute-done((f32[64,256]{1,0:T(8,128)S(1)}, f32[64,256]{1,0:T(8,128)S(1)}, u32[]{:S(2)}, u32[]{:S(2)}) %collective-permute-start.9) | collective-permute-done | bytes 65568 | tf_op jit(solution)/shard_map/ppermute | solution.py:68
  68.4 1.4 %collective-permute-done.21 = f32[64,256]{1,0:T(8,128)S(1)} collective-permute-done((f32[64,256]{1,0:T(8,128)S(1)}, f32[64,256]{1,0:T(8,128)S(1)}, u32[]{:S(2)}, u32[]{:S(2)}) %collective-permute-start.21) | collective-permute-done | bytes 65568 | tf_op jit(solution)/shard_map/ppermute | solution.py:68
  70.0 2.9 %collective-permute-start.22 = (bf16[64,256]{1,0:T(8,128)(2,1)S(1)}, bf16[64,256]{1,0:T(8,128)(2,1)S(1)}, u32[]{:S(2)}, u32[]{:S(2)}) collective-permute-start(bf16[64,256]{1,0:T(8,128)(2,1)S(1)} %get-tuple-element.52), channel_id=1, source_target_pairs={{0,8},{2,10},{4,12},{6,14},{8,0},{10,2},{12,4},{14,6},{1,9},{3,11}... | collective-permute-start | bytes 98312 | tf_op jit(solution)/shard_map/ppermute | solution.py:68
  73.1 2.9 %collective-permute-start.16 = (bf16[64,256]{1,0:T(8,128)(2,1)S(1)}, bf16[64,256]{1,0:T(8,128)(2,1)S(1)}, u32[]{:S(2)}, u32[]{:S(2)}) collective-permute-start(bf16[64,256]{1,0:T(8,128)(2,1)S(1)} %get-tuple-element.50), channel_id=1, source_target_pairs={{0,8},{2,10},{4,12},{6,14},{8,0},{10,2},{12,4},{14,6},{1,9},{3,11}... | collective-permute-start | bytes 98312 | tf_op jit(solution)/shard_map/ppermute | solution.py:68
  78.5 2.1 %collective-permute-start.17 = (bf16[2,64,256]{2,1,0:T(8,128)(2,1)S(1)}, bf16[2,64,256]{2,1,0:T(8,128)(2,1)S(1)}, u32[]{:S(2)}, u32[]{:S(2)}) collective-permute-start(bf16[2,64,256]{2,1,0:T(8,128)(2,1)S(1)} %pad_maximum_fusion.7), channel_id=1, source_target_pairs={{0,4},{2,6},{4,0},{6,2},{8,12},{10,14},{12,8},{14,10},{1,5},{3,7},... | collective-permute-start | bytes 196616 | tf_op jit(solution)/shard_map/ppermute | solution.py:68
  80.7 1.8 %collective-permute-done.23 = bf16[2,64,256]{2,1,0:T(8,128)(2,1)S(1)} collective-permute-done((bf16[2,64,256]{2,1,0:T(8,128)(2,1)S(1)}, bf16[2,64,256]{2,1,0:T(8,128)(2,1)S(1)}, u32[]{:S(2)}, u32[]{:S(2)}) %collective-permute-start.23) | collective-permute-done | bytes 65568 | tf_op jit(solution)/shard_map/ppermute | solution.py:68
  83.3 1.5 %collective-permute-start.6 = (bf16[2,2,64,256]{3,2,1,0:T(8,128)(2,1)S(1)}, bf16[2,2,64,256]{3,2,1,0:T(8,128)(2,1)S(1)}, u32[]{:S(2)}, u32[]{:S(2)}) collective-permute-start(bf16[2,2,64,256]{3,2,1,0:T(8,128)(2,1)S(1)} %pad_maximum_fusion.1), channel_id=1, source_target_pairs={{0,2},{2,0},{4,6},{6,4},{8,10},{10,8},{12,14},{14,12},{1,3},{3,1},... | collective-permute-start | bytes 393224 | tf_op jit(solution)/shard_map/ppermute | solution.py:68
  85.7 1.9 %collective-permute-done.24 = bf16[2,2,64,256]{3,2,1,0:T(8,128)(2,1)S(1)} collective-permute-done((bf16[2,2,64,256]{3,2,1,0:T(8,128)(2,1)S(1)}, bf16[2,2,64,256]{3,2,1,0:T(8,128)(2,1)S(1)}, u32[]{:S(2)}, u32[]{:S(2)}) %collective-permute-start.24) | collective-permute-done | bytes 131104 | tf_op jit(solution)/shard_map/ppermute | solution.py:68
  92.5 28.1 %shard_map.148 = (bf16[2048,2048]{1,0:T(8,128)(2,1)}, bf16[2048,2048]{1,0:T(8,128)(2,1)}, bf16[2048,2048]{1,0:T(8,128)(2,1)}) custom-call(f32[2048,256]{1,0:T(8,128)} %copy-done, bf16[2048,256]{1,0:T(8,128)(2,1)} %bitcast.98, bf16[256,2048]{1,0:T(8,128)(2,1)} %copy-done.1, bf16[2048,2048]{1,0:T(8,128)(2,1)} %bitcast.92, bf16[2048,2048]{1,0:T(8,128)(2,1)} %bitcast.95, ...), custom_call_target="tpu_custom_call" | custom-call | tf_op jit(solution)/shard_map/pallas_call | solution.py:49
  (121 shorter events, 20.0 us)
Async XLA Ops:
  2.4 21.7 %all-to-all-start = ((bf16[8,128,256]{2,1,0:T(8,128)(2,1)}), bf16[8,128,256]{2,1,0:T(8,128)(2,1)S(1)}, u32[]{:S(2)}, u32[]{:S(2)}) async-start(bf16[8,128,256]{2,1,0:T(8,128)(2,1)} %broadcast_in_dim.46), calls=%async_computation | async-start | bytes 1048576 | tf_op jit(solution)/shard_map/all_to_all | solution.py:171
  37.6 9.2 %collective-permute-start.7 = (f32[64,1024]{1,0:T(8,128)S(1)}, f32[64,1024]{1,0:T(8,128)S(1)}, u32[]{:S(2)}, u32[]{:S(2)}) collective-permute-start(f32[64,1024]{1,0:T(8,128)S(1)} %constant_dynamic-slice_fusion.9), channel_id=1, source_target_pairs={{0,4},{2,6},{4,0},{6,2},{8,12},{10,14},{12,8},{14,10},{1,5},{3,7},... | collective-permute-start | bytes 786440 | tf_op jit(solution)/shard_map/ppermute | solution.py:68
  38.4 13.2 %collective-permute-start.19 = (f32[64,1024]{1,0:T(8,128)S(1)}, f32[64,1024]{1,0:T(8,128)S(1)}, u32[]{:S(2)}, u32[]{:S(2)}) collective-permute-start(f32[64,1024]{1,0:T(8,128)S(1)} %constant_dynamic-slice_fusion), channel_id=1, source_target_pairs={{0,4},{2,6},{4,0},{6,2},{8,12},{10,14},{12,8},{14,10},{1,5},{3,7},... | collective-permute-start | bytes 786440 | tf_op jit(solution)/shard_map/ppermute | solution.py:68
  39.7 13.5 %collective-permute-start.13 = (f32[64,1024]{1,0:T(8,128)S(1)}, f32[64,1024]{1,0:T(8,128)S(1)}, u32[]{:S(2)}, u32[]{:S(2)}) collective-permute-start(f32[64,1024]{1,0:T(8,128)S(1)} %constant_dynamic-slice_fusion.3), channel_id=1, source_target_pairs={{0,2},{2,0},{4,6},{6,4},{8,10},{10,8},{12,14},{14,12},{1,3},{3,1},... | collective-permute-start | bytes 786440 | tf_op jit(solution)/shard_map/ppermute | solution.py:68
  41.2 13.4 %collective-permute-start.1 = (f32[64,1024]{1,0:T(8,128)S(1)}, f32[64,1024]{1,0:T(8,128)S(1)}, u32[]{:S(2)}, u32[]{:S(2)}) collective-permute-start(f32[64,1024]{1,0:T(8,128)S(1)} %constant_dynamic-slice_fusion.15), channel_id=1, source_target_pairs={{0,2},{2,0},{4,6},{6,4},{8,10},{10,8},{12,14},{14,12},{1,3},{3,1},... | collective-permute-start | bytes 786440 | tf_op jit(solution)/shard_map/ppermute | solution.py:68
  46.9 10.4 %collective-permute-start.8 = (f32[64,512]{1,0:T(8,128)S(1)}, f32[64,512]{1,0:T(8,128)S(1)}, u32[]{:S(2)}, u32[]{:S(2)}) collective-permute-start(f32[64,512]{1,0:T(8,128)S(1)} %constant_dynamic-slice_fusion.8), channel_id=1, source_target_pairs={{0,2},{2,0},{4,6},{6,4},{8,10},{10,8},{12,14},{14,12},{1,3},{3,1},... | collective-permute-start | bytes 393224 | tf_op jit(solution)/shard_map/ppermute | solution.py:68
  51.7 7.0 %collective-permute-start.20 = (f32[64,512]{1,0:T(8,128)S(1)}, f32[64,512]{1,0:T(8,128)S(1)}, u32[]{:S(2)}, u32[]{:S(2)}) collective-permute-start(f32[64,512]{1,0:T(8,128)S(1)} %constant_dynamic-slice_fusion.5), channel_id=1, source_target_pairs={{0,2},{2,0},{4,6},{6,4},{8,10},{10,8},{12,14},{14,12},{1,3},{3,1},... | collective-permute-start | bytes 393224 | tf_op jit(solution)/shard_map/ppermute | solution.py:68
  53.3 7.2 %collective-permute-start.14 = (f32[64,512]{1,0:T(8,128)S(1)}, f32[64,512]{1,0:T(8,128)S(1)}, u32[]{:S(2)}, u32[]{:S(2)}) collective-permute-start(f32[64,512]{1,0:T(8,128)S(1)} %constant_dynamic-slice_fusion.2), channel_id=1, source_target_pairs={{0,4},{2,6},{4,0},{6,2},{8,12},{10,14},{12,8},{14,10},{1,5},{3,7},... | collective-permute-start | bytes 393224 | tf_op jit(solution)/shard_map/ppermute | solution.py:68
  54.6 7.3 %collective-permute-start.2 = (f32[64,512]{1,0:T(8,128)S(1)}, f32[64,512]{1,0:T(8,128)S(1)}, u32[]{:S(2)}, u32[]{:S(2)}) collective-permute-start(f32[64,512]{1,0:T(8,128)S(1)} %constant_dynamic-slice_fusion.14), channel_id=1, source_target_pairs={{0,4},{2,6},{4,0},{6,2},{8,12},{10,14},{12,8},{14,10},{1,5},{3,7},... | collective-permute-start | bytes 393224 | tf_op jit(solution)/shard_map/ppermute | solution.py:68
  57.4 11.1 %collective-permute-start.9 = (f32[64,256]{1,0:T(8,128)S(1)}, f32[64,256]{1,0:T(8,128)S(1)}, u32[]{:S(2)}, u32[]{:S(2)}) collective-permute-start(f32[64,256]{1,0:T(8,128)S(1)} %constant_dynamic-slice_fusion.7), channel_id=1, source_target_pairs={{0,8},{2,10},{4,12},{6,14},{8,0},{10,2},{12,4},{14,6},{1,9},{3,11}... | collective-permute-start | bytes 196616 | tf_op jit(solution)/shard_map/ppermute | solution.py:68
  58.8 11.1 %collective-permute-start.21 = (f32[64,256]{1,0:T(8,128)S(1)}, f32[64,256]{1,0:T(8,128)S(1)}, u32[]{:S(2)}, u32[]{:S(2)}) collective-permute-start(f32[64,256]{1,0:T(8,128)S(1)} %constant_dynamic-slice_fusion.10), channel_id=1, source_target_pairs={{0,8},{2,10},{4,12},{6,14},{8,0},{10,2},{12,4},{14,6},{1,9},{3,11}... | collective-permute-start | bytes 196616 | tf_op jit(solution)/shard_map/ppermute | solution.py:68
  60.5 12.4 %collective-permute-start.15 = (f32[64,256]{1,0:T(8,128)S(1)}, f32[64,256]{1,0:T(8,128)S(1)}, u32[]{:S(2)}, u32[]{:S(2)}) collective-permute-start(f32[64,256]{1,0:T(8,128)S(1)} %constant_dynamic-slice_fusion.1), channel_id=1, source_target_pairs={{0,8},{2,10},{4,12},{6,14},{8,0},{10,2},{12,4},{14,6},{1,9},{3,11}... | collective-permute-start | bytes 196616 | tf_op jit(solution)/shard_map/ppermute | solution.py:68
  61.9 11.0 %collective-permute-start.3 = (f32[64,256]{1,0:T(8,128)S(1)}, f32[64,256]{1,0:T(8,128)S(1)}, u32[]{:S(2)}, u32[]{:S(2)}) collective-permute-start(f32[64,256]{1,0:T(8,128)S(1)} %constant_dynamic-slice_fusion.13), channel_id=1, source_target_pairs={{0,8},{2,10},{4,12},{6,14},{8,0},{10,2},{12,4},{14,6},{1,9},{3,11}... | collective-permute-start | bytes 196616 | tf_op jit(solution)/shard_map/ppermute | solution.py:68
  69.9 6.3 %collective-permute-start.10 = (bf16[64,256]{1,0:T(8,128)(2,1)S(1)}, bf16[64,256]{1,0:T(8,128)(2,1)S(1)}, u32[]{:S(2)}, u32[]{:S(2)}) collective-permute-start(bf16[64,256]{1,0:T(8,128)(2,1)S(1)} %get-tuple-element.51), channel_id=1, source_target_pairs={{0,8},{2,10},{4,12},{6,14},{8,0},{10,2},{12,4},{14,6},{1,9},{3,11}... | collective-permute-start | bytes 98312 | tf_op jit(solution)/shard_map/ppermute | solution.py:68
  70.0 7.6 %collective-permute-start.22 = (bf16[64,256]{1,0:T(8,128)(2,1)S(1)}, bf16[64,256]{1,0:T(8,128)(2,1)S(1)}, u32[]{:S(2)}, u32[]{:S(2)}) collective-permute-start(bf16[64,256]{1,0:T(8,128)(2,1)S(1)} %get-tuple-element.52), channel_id=1, source_target_pairs={{0,8},{2,10},{4,12},{6,14},{8,0},{10,2},{12,4},{14,6},{1,9},{3,11}... | collective-permute-start | bytes 98312 | tf_op jit(solution)/shard_map/ppermute | solution.py:68
  73.0 5.4 %collective-permute-start.4 = (bf16[64,256]{1,0:T(8,128)(2,1)S(1)}, bf16[64,256]{1,0:T(8,128)(2,1)S(1)}, u32[]{:S(2)}, u32[]{:S(2)}) collective-permute-start(bf16[64,256]{1,0:T(8,128)(2,1)S(1)} %get-tuple-element.49), channel_id=1, source_target_pairs={{0,8},{2,10},{4,12},{6,14},{8,0},{10,2},{12,4},{14,6},{1,9},{3,11}... | collective-permute-start | bytes 98312 | tf_op jit(solution)/shard_map/ppermute | solution.py:68
  73.1 5.4 %collective-permute-start.16 = (bf16[64,256]{1,0:T(8,128)(2,1)S(1)}, bf16[64,256]{1,0:T(8,128)(2,1)S(1)}, u32[]{:S(2)}, u32[]{:S(2)}) collective-permute-start(bf16[64,256]{1,0:T(8,128)(2,1)S(1)} %get-tuple-element.50), channel_id=1, source_target_pairs={{0,8},{2,10},{4,12},{6,14},{8,0},{10,2},{12,4},{14,6},{1,9},{3,11}... | collective-permute-start | bytes 98312 | tf_op jit(solution)/shard_map/ppermute | solution.py:68
  77.6 5.0 %collective-permute-start.23 = (bf16[2,64,256]{2,1,0:T(8,128)(2,1)S(1)}, bf16[2,64,256]{2,1,0:T(8,128)(2,1)S(1)}, u32[]{:S(2)}, u32[]{:S(2)}) collective-permute-start(bf16[2,64,256]{2,1,0:T(8,128)(2,1)S(1)} %pad_maximum_fusion.8), channel_id=1, source_target_pairs={{0,2},{2,0},{4,6},{6,4},{8,10},{10,8},{12,14},{14,12},{1,3},{3,1},... | collective-permute-start | bytes 196616 | tf_op jit(solution)/shard_map/ppermute | solution.py:68
  78.4 4.9 %collective-permute-start.5 = (bf16[2,64,256]{2,1,0:T(8,128)(2,1)S(1)}, bf16[2,64,256]{2,1,0:T(8,128)(2,1)S(1)}, u32[]{:S(2)}, u32[]{:S(2)}) collective-permute-start(bf16[2,64,256]{2,1,0:T(8,128)(2,1)S(1)} %pad_maximum_fusion.5), channel_id=1, source_target_pairs={{0,4},{2,6},{4,0},{6,2},{8,12},{10,14},{12,8},{14,10},{1,5},{3,7},... | collective-permute-start | bytes 196616 | tf_op jit(solution)/shard_map/ppermute | solution.py:68
  78.5 6.2 %collective-permute-start.17 = (bf16[2,64,256]{2,1,0:T(8,128)(2,1)S(1)}, bf16[2,64,256]{2,1,0:T(8,128)(2,1)S(1)}, u32[]{:S(2)}, u32[]{:S(2)}) collective-permute-start(bf16[2,64,256]{2,1,0:T(8,128)(2,1)S(1)} %pad_maximum_fusion.7), channel_id=1, source_target_pairs={{0,4},{2,6},{4,0},{6,2},{8,12},{10,14},{12,8},{14,10},{1,5},{3,7},... | collective-permute-start | bytes 196616 | tf_op jit(solution)/shard_map/ppermute | solution.py:68
  80.7 5.0 %collective-permute-start.12 = (bf16[2,2,64,256]{3,2,1,0:T(8,128)(2,1)S(1)}, bf16[2,2,64,256]{3,2,1,0:T(8,128)(2,1)S(1)}, u32[]{:S(2)}, u32[]{:S(2)}) collective-permute-start(bf16[2,2,64,256]{3,2,1,0:T(8,128)(2,1)S(1)} %pad_maximum_fusion.2), channel_id=1, source_target_pairs={{0,4},{2,6},{4,0},{6,2},{8,12},{10,14},{12,8},{14,10},{1,5},{3,7},... | collective-permute-start | bytes 393224 | tf_op jit(solution)/shard_map/ppermute | solution.py:68
  82.6 5.0 %collective-permute-start.24 = (bf16[2,2,64,256]{3,2,1,0:T(8,128)(2,1)S(1)}, bf16[2,2,64,256]{3,2,1,0:T(8,128)(2,1)S(1)}, u32[]{:S(2)}, u32[]{:S(2)}) collective-permute-start(bf16[2,2,64,256]{3,2,1,0:T(8,128)(2,1)S(1)} %pad_maximum_fusion.4), channel_id=1, source_target_pairs={{0,4},{2,6},{4,0},{6,2},{8,12},{10,14},{12,8},{14,10},{1,5},{3,7},... | collective-permute-start | bytes 393224 | tf_op jit(solution)/shard_map/ppermute | solution.py:68
  83.3 5.0 %collective-permute-start.6 = (bf16[2,2,64,256]{3,2,1,0:T(8,128)(2,1)S(1)}, bf16[2,2,64,256]{3,2,1,0:T(8,128)(2,1)S(1)}, u32[]{:S(2)}, u32[]{:S(2)}) collective-permute-start(bf16[2,2,64,256]{3,2,1,0:T(8,128)(2,1)S(1)} %pad_maximum_fusion.1), channel_id=1, source_target_pairs={{0,2},{2,0},{4,6},{6,4},{8,10},{10,8},{12,14},{14,12},{1,3},{3,1},... | collective-permute-start | bytes 393224 | tf_op jit(solution)/shard_map/ppermute | solution.py:68
  84.8 5.0 %collective-permute-start.18 = (bf16[2,2,64,256]{3,2,1,0:T(8,128)(2,1)S(1)}, bf16[2,2,64,256]{3,2,1,0:T(8,128)(2,1)S(1)}, u32[]{:S(2)}, u32[]{:S(2)}) collective-permute-start(bf16[2,2,64,256]{3,2,1,0:T(8,128)(2,1)S(1)} %pad_maximum_fusion.3), channel_id=1, source_target_pairs={{0,2},{2,0},{4,6},{6,4},{8,10},{10,8},{12,14},{14,12},{1,3},{3,1},... | collective-permute-start | bytes 393224 | tf_op jit(solution)/shard_map/ppermute | solution.py:68
  (11 other events, 124.5 us)

commit v14 on v13

--- a/solution.py
+++ b/solution.py
@@ -41,6 +41,8 @@
 
 def tail(pre_t, error, centered, decoder, weight_in, first, second, tile=256):
     n_lat, width = decoder.shape
+    if n_lat % tile:
+        tile = n_lat
     tokens = error.shape[0]
     error_t = error.T
     row_block = pl.BlockSpec((tile, width), lambda i: (i, 0))

time: 121 us -> 121 us (level)
  no operation moved by 1% of the time
where the time goes in v14:
time: 121 us
  waiting for transfers between devices  38.6 us (32%)
  starting transfers between devices  33.6 us (28%)
  Pallas kernels  28.1 us (23%)
  matrix products  8.83 us (7%)
  local copies, waits for them, and re-layouts  7.6 us (6%)
  other arithmetic  2.66 us (2%)
  between operations  1.24 us (1%)
    pallas_call x1, Pallas kernels, tail(): pl.pallas_call(_tail_kernel, grid=(n_lat // tile,), in_specs=[pl.BlockSpe...  28.1 us
    ppermute x24, starting transfers between devices, _pair_swap(): return lax.ppermute(value, axis, [(i, i ^ mask) for i in range(size)])  26.2 us
    ppermute x24, waiting for transfers between devices, _pair_swap(): return lax.ppermute(value, axis, [(i, i ^ mask) for i in range(size)])  23.7 us
    all_to_all x1, waiting for transfers between devices, local(): act_blocks = lax.all_to_all(copies, 'lat', 0, 0, tiled=True)  13.1 us
    all_to_all x1, starting transfers between devices, local(): act_blocks = lax.all_to_all(copies, 'lat', 0, 0, tiled=True)  7.25 us
    dot_general x1, matrix products, local(): lax.dot_general(weight_in, centered, (((1,), (1,)), ((), ())), preferred_...  6.48 us
  transfers between devices with their start and end apart: 26, of which 16 were waited for; matrix products, arithmetic and copies ran while one was open for 3% of the time, Pallas kernels for 0%

profile of v14, /device:TPU:0, one launch (start us, length us, event | category | flops | bytes accessed | tf_op | source)
XLA Modules:
  0.0 120.5 jit_solution(5770225099930983746)
XLA Ops:
  0.7 1.7 %broadcast_in_dim.46 = bf16[8,128,256]{2,1,0:T(8,128)(2,1)} broadcast(bf16[128,256]{1,0:T(8,128)(2,1)} %param.13), dimensions={1,2} | broadcast | bytes 589824 | tf_op jit(solution)/shard_map/broadcast_in_dim | solution.py:172
  2.4 7.3 %all-to-all-start = ((bf16[8,128,256]{2,1,0:T(8,128)(2,1)}), bf16[8,128,256]{2,1,0:T(8,128)(2,1)S(1)}, u32[]{:S(2)}, u32[]{:S(2)}) async-start(bf16[8,128,256]{2,1,0:T(8,128)(2,1)} %broadcast_in_dim.46), calls=%async_computation | async-start | bytes 1048576 | tf_op jit(solution)/shard_map/all_to_all | solution.py:173
  11.0 13.1 %all-to-all-done = bf16[8,128,256]{2,1,0:T(8,128)(2,1)S(1)} async-done(((bf16[8,128,256]{2,1,0:T(8,128)(2,1)}), bf16[8,128,256]{2,1,0:T(8,128)(2,1)S(1)}, u32[]{:S(2)}, u32[]{:S(2)}) %all-to-all-start) | async-done | bytes 524320 | tf_op jit(solution)/shard_map/all_to_all | solution.py:173
  24.3 1.8 %collective-permute-done = bf16[128,2048]{1,0:T(8,128)(2,1)S(1)} collective-permute-done((bf16[128,2048]{1,0:T(8,128)(2,1)S(1)}, bf16[128,2048]{1,0:T(8,128)(2,1)S(1)}, u32[]{:S(2)}, u32[]{:S(2)}) %collective-permute-start) | collective-permute-done | bytes 524320 | tf_op jit(solution)/shard_map/ppermute | solution.py:175
  26.3 1.4 %gather_fusion = bf16[256,2048]{1,0:T(8,128)(2,1)S(1)} fusion(bf16[256,2048]{1,0:T(8,128)(2,1)S(1)} %pad_maximum_fusion, s32[1024]{0:T(1024)S(1)} %pad_clamp_fusion.2), kind=kCustom, calls=%fused_computation | custom fusion | bytes 2098176 | tf_op jit(solution)/shard_map/jit(_take)/gather | solution.py:182
  28.4 6.5 %fusion.pre_ref = f32[2048,256]{1,0:T(8,128)S(1)} fusion(bf16[256,2048]{1,0:T(8,128)(2,1)S(1)} %get-tuple-element.9.cen_ref, f32[2048]{0:T(1024)S(1)} %bitcast.116, bf16[1,2048,2048]{2,1,0:T(8,128)(2,1)} %param.16), kind=kOutput, calls=%fused_computation.6 | convolution fusion | flops 2148007936 | bytes 11542528 | tf_op jit(solution)/shard_map/dot_general | solution.py:188
  34.9 2.3 %fusion.1 = f32[256,2048]{1,0:T(8,128)S(1)} fusion(f32[2048,256]{1,0:T(8,128)S(1)} %fusion.pre_ref, bf16[1,2048,2048]{2,1,0:T(8,128)(2,1)S(1)} %bitcast.94), kind=kOutput, calls=%fused_computation.9 | convolution fusion | flops 2148532224 | bytes 12582912 | tf_op jit(solution)/shard_map/dot_general | solution.py:194
  39.7 1.5 %collective-permute-start.13 = (f32[64,1024]{1,0:T(8,128)S(1)}, f32[64,1024]{1,0:T(8,128)S(1)}, u32[]{:S(2)}, u32[]{:S(2)}) collective-permute-start(f32[64,1024]{1,0:T(8,128)S(1)} %constant_dynamic-slice_fusion.3), channel_id=1, source_target_pairs={{0,2},{2,0},{4,6},{6,4},{8,10},{10,8},{12,14},{14,12},{1,3},{3,1},... | collective-permute-start | bytes 786440 | tf_op jit(solution)/shard_map/ppermute | solution.py:70
  41.8 5.0 %collective-permute-done.7 = f32[64,1024]{1,0:T(8,128)S(1)} collective-permute-done((f32[64,1024]{1,0:T(8,128)S(1)}, f32[64,1024]{1,0:T(8,128)S(1)}, u32[]{:S(2)}, u32[]{:S(2)}) %collective-permute-start.7) | collective-permute-done | bytes 262176 | tf_op jit(solution)/shard_map/ppermute | solution.py:70
  46.9 1.5 %collective-permute-start.8 = (f32[64,512]{1,0:T(8,128)S(1)}, f32[64,512]{1,0:T(8,128)S(1)}, u32[]{:S(2)}, u32[]{:S(2)}) collective-permute-start(f32[64,512]{1,0:T(8,128)S(1)} %constant_dynamic-slice_fusion.8), channel_id=1, source_target_pairs={{0,2},{2,0},{4,6},{6,4},{8,10},{10,8},{12,14},{14,12},{1,3},{3,1},... | collective-permute-start | bytes 393224 | tf_op jit(solution)/shard_map/ppermute | solution.py:70
  48.4 3.2 %collective-permute-done.19 = f32[64,1024]{1,0:T(8,128)S(1)} collective-permute-done((f32[64,1024]{1,0:T(8,128)S(1)}, f32[64,1024]{1,0:T(8,128)S(1)}, u32[]{:S(2)}, u32[]{:S(2)}) %collective-permute-start.19) | collective-permute-done | bytes 262176 | tf_op jit(solution)/shard_map/ppermute | solution.py:70
  51.7 1.5 %collective-permute-start.20 = (f32[64,512]{1,0:T(8,128)S(1)}, f32[64,512]{1,0:T(8,128)S(1)}, u32[]{:S(2)}, u32[]{:S(2)}) collective-permute-start(f32[64,512]{1,0:T(8,128)S(1)} %constant_dynamic-slice_fusion.5), channel_id=1, source_target_pairs={{0,2},{2,0},{4,6},{6,4},{8,10},{10,8},{12,14},{14,12},{1,3},{3,1},... | collective-permute-start | bytes 393224 | tf_op jit(solution)/shard_map/ppermute | solution.py:70
  55.5 1.8 %collective-permute-done.8 = f32[64,512]{1,0:T(8,128)S(1)} collective-permute-done((f32[64,512]{1,0:T(8,128)S(1)}, f32[64,512]{1,0:T(8,128)S(1)}, u32[]{:S(2)}, u32[]{:S(2)}) %collective-permute-start.8) | collective-permute-done | bytes 131104 | tf_op jit(solution)/shard_map/ppermute | solution.py:70
  58.8 1.7 %collective-permute-start.21 = (f32[64,256]{1,0:T(8,128)S(1)}, f32[64,256]{1,0:T(8,128)S(1)}, u32[]{:S(2)}, u32[]{:S(2)}) collective-permute-start(f32[64,256]{1,0:T(8,128)S(1)} %constant_dynamic-slice_fusion.10), channel_id=1, source_target_pairs={{0,8},{2,10},{4,12},{6,14},{8,0},{10,2},{12,4},{14,6},{1,9},{3,11}... | collective-permute-start | bytes 196616 | tf_op jit(solution)/shard_map/ppermute | solution.py:70
  61.9 1.7 %collective-permute-start.3 = (f32[64,256]{1,0:T(8,128)S(1)}, f32[64,256]{1,0:T(8,128)S(1)}, u32[]{:S(2)}, u32[]{:S(2)}) collective-permute-start(f32[64,256]{1,0:T(8,128)S(1)} %constant_dynamic-slice_fusion.13), channel_id=1, source_target_pairs={{0,8},{2,10},{4,12},{6,14},{8,0},{10,2},{12,4},{14,6},{1,9},{3,11}... | collective-permute-start | bytes 196616 | tf_op jit(solution)/shard_map/ppermute | solution.py:70
  63.6 4.8 %collective-permute-done.9 = f32[64,256]{1,0:T(8,128)S(1)} collective-permute-done((f32[64,256]{1,0:T(8,128)S(1)}, f32[64,256]{1,0:T(8,128)S(1)}, u32[]{:S(2)}, u32[]{:S(2)}) %collective-permute-start.9) | collective-permute-done | bytes 65568 | tf_op jit(solution)/shard_map/ppermute | solution.py:70
  68.4 1.4 %collective-permute-done.21 = f32[64,256]{1,0:T(8,128)S(1)} collective-permute-done((f32[64,256]{1,0:T(8,128)S(1)}, f32[64,256]{1,0:T(8,128)S(1)}, u32[]{:S(2)}, u32[]{:S(2)}) %collective-permute-start.21) | collective-permute-done | bytes 65568 | tf_op jit(solution)/shard_map/ppermute | solution.py:70
  70.0 2.9 %collective-permute-start.22 = (bf16[64,256]{1,0:T(8,128)(2,1)S(1)}, bf16[64,256]{1,0:T(8,128)(2,1)S(1)}, u32[]{:S(2)}, u32[]{:S(2)}) collective-permute-start(bf16[64,256]{1,0:T(8,128)(2,1)S(1)} %get-tuple-element.52), channel_id=1, source_target_pairs={{0,8},{2,10},{4,12},{6,14},{8,0},{10,2},{12,4},{14,6},{1,9},{3,11}... | collective-permute-start | bytes 98312 | tf_op jit(solution)/shard_map/ppermute | solution.py:70
  73.1 2.9 %collective-permute-start.16 = (bf16[64,256]{1,0:T(8,128)(2,1)S(1)}, bf16[64,256]{1,0:T(8,128)(2,1)S(1)}, u32[]{:S(2)}, u32[]{:S(2)}) collective-permute-start(bf16[64,256]{1,0:T(8,128)(2,1)S(1)} %get-tuple-element.50), channel_id=1, source_target_pairs={{0,8},{2,10},{4,12},{6,14},{8,0},{10,2},{12,4},{14,6},{1,9},{3,11}... | collective-permute-start | bytes 98312 | tf_op jit(solution)/shard_map/ppermute | solution.py:70
  78.5 2.1 %collective-permute-start.17 = (bf16[2,64,256]{2,1,0:T(8,128)(2,1)S(1)}, bf16[2,64,256]{2,1,0:T(8,128)(2,1)S(1)}, u32[]{:S(2)}, u32[]{:S(2)}) collective-permute-start(bf16[2,64,256]{2,1,0:T(8,128)(2,1)S(1)} %pad_maximum_fusion.7), channel_id=1, source_target_pairs={{0,4},{2,6},{4,0},{6,2},{8,12},{10,14},{12,8},{14,10},{1,5},{3,7},... | collective-permute-start | bytes 196616 | tf_op jit(solution)/shard_map/ppermute | solution.py:70
  80.7 1.8 %collective-permute-done.23 = bf16[2,64,256]{2,1,0:T(8,128)(2,1)S(1)} collective-permute-done((bf16[2,64,256]{2,1,0:T(8,128)(2,1)S(1)}, bf16[2,64,256]{2,1,0:T(8,128)(2,1)S(1)}, u32[]{:S(2)}, u32[]{:S(2)}) %collective-permute-start.23) | collective-permute-done | bytes 65568 | tf_op jit(solution)/shard_map/ppermute | solution.py:70
  83.3 1.5 %collective-permute-start.6 = (bf16[2,2,64,256]{3,2,1,0:T(8,128)(2,1)S(1)}, bf16[2,2,64,256]{3,2,1,0:T(8,128)(2,1)S(1)}, u32[]{:S(2)}, u32[]{:S(2)}) collective-permute-start(bf16[2,2,64,256]{3,2,1,0:T(8,128)(2,1)S(1)} %pad_maximum_fusion.1), channel_id=1, source_target_pairs={{0,2},{2,0},{4,6},{6,4},{8,10},{10,8},{12,14},{14,12},{1,3},{3,1},... | collective-permute-start | bytes 393224 | tf_op jit(solution)/shard_map/ppermute | solution.py:70
  85.7 1.9 %collective-permute-done.24 = bf16[2,2,64,256]{3,2,1,0:T(8,128)(2,1)S(1)} collective-permute-done((bf16[2,2,64,256]{3,2,1,0:T(8,128)(2,1)S(1)}, bf16[2,2,64,256]{3,2,1,0:T(8,128)(2,1)S(1)}, u32[]{:S(2)}, u32[]{:S(2)}) %collective-permute-start.24) | collective-permute-done | bytes 131104 | tf_op jit(solution)/shard_map/ppermute | solution.py:70
  92.5 28.1 %shard_map.148 = (bf16[2048,2048]{1,0:T(8,128)(2,1)}, bf16[2048,2048]{1,0:T(8,128)(2,1)}, bf16[2048,2048]{1,0:T(8,128)(2,1)}) custom-call(f32[2048,256]{1,0:T(8,128)} %copy-done, bf16[2048,256]{1,0:T(8,128)(2,1)} %bitcast.98, bf16[256,2048]{1,0:T(8,128)(2,1)} %copy-done.1, bf16[2048,2048]{1,0:T(8,128)(2,1)} %bitcast.92, bf16[2048,2048]{1,0:T(8,128)(2,1)} %bitcast.95, ...), custom_call_target="tpu_custom_call" | custom-call | tf_op jit(solution)/shard_map/pallas_call | solution.py:51
  (121 shorter events, 20.0 us)
Async XLA Ops:
  2.4 21.7 %all-to-all-start = ((bf16[8,128,256]{2,1,0:T(8,128)(2,1)}), bf16[8,128,256]{2,1,0:T(8,128)(2,1)S(1)}, u32[]{:S(2)}, u32[]{:S(2)}) async-start(bf16[8,128,256]{2,1,0:T(8,128)(2,1)} %broadcast_in_dim.46), calls=%async_computation | async-start | bytes 1048576 | tf_op jit(solution)/shard_map/all_to_all | solution.py:173
  37.6 9.2 %collective-permute-start.7 = (f32[64,1024]{1,0:T(8,128)S(1)}, f32[64,1024]{1,0:T(8,128)S(1)}, u32[]{:S(2)}, u32[]{:S(2)}) collective-permute-start(f32[64,1024]{1,0:T(8,128)S(1)} %constant_dynamic-slice_fusion.9), channel_id=1, source_target_pairs={{0,4},{2,6},{4,0},{6,2},{8,12},{10,14},{12,8},{14,10},{1,5},{3,7},... | collective-permute-start | bytes 786440 | tf_op jit(solution)/shard_map/ppermute | solution.py:70
  38.4 13.2 %collective-permute-start.19 = (f32[64,1024]{1,0:T(8,128)S(1)}, f32[64,1024]{1,0:T(8,128)S(1)}, u32[]{:S(2)}, u32[]{:S(2)}) collective-permute-start(f32[64,1024]{1,0:T(8,128)S(1)} %constant_dynamic-slice_fusion), channel_id=1, source_target_pairs={{0,4},{2,6},{4,0},{6,2},{8,12},{10,14},{12,8},{14,10},{1,5},{3,7},... | collective-permute-start | bytes 786440 | tf_op jit(solution)/shard_map/ppermute | solution.py:70
  39.7 13.5 %collective-permute-start.13 = (f32[64,1024]{1,0:T(8,128)S(1)}, f32[64,1024]{1,0:T(8,128)S(1)}, u32[]{:S(2)}, u32[]{:S(2)}) collective-permute-start(f32[64,1024]{1,0:T(8,128)S(1)} %constant_dynamic-slice_fusion.3), channel_id=1, source_target_pairs={{0,2},{2,0},{4,6},{6,4},{8,10},{10,8},{12,14},{14,12},{1,3},{3,1},... | collective-permute-start | bytes 786440 | tf_op jit(solution)/shard_map/ppermute | solution.py:70
  41.2 13.4 %collective-permute-start.1 = (f32[64,1024]{1,0:T(8,128)S(1)}, f32[64,1024]{1,0:T(8,128)S(1)}, u32[]{:S(2)}, u32[]{:S(2)}) collective-permute-start(f32[64,1024]{1,0:T(8,128)S(1)} %constant_dynamic-slice_fusion.15), channel_id=1, source_target_pairs={{0,2},{2,0},{4,6},{6,4},{8,10},{10,8},{12,14},{14,12},{1,3},{3,1},... | collective-permute-start | bytes 786440 | tf_op jit(solution)/shard_map/ppermute | solution.py:70
  46.9 10.4 %collective-permute-start.8 = (f32[64,512]{1,0:T(8,128)S(1)}, f32[64,512]{1,0:T(8,128)S(1)}, u32[]{:S(2)}, u32[]{:S(2)}) collective-permute-start(f32[64,512]{1,0:T(8,128)S(1)} %constant_dynamic-slice_fusion.8), channel_id=1, source_target_pairs={{0,2},{2,0},{4,6},{6,4},{8,10},{10,8},{12,14},{14,12},{1,3},{3,1},... | collective-permute-start | bytes 393224 | tf_op jit(solution)/shard_map/ppermute | solution.py:70
  51.7 7.0 %collective-permute-start.20 = (f32[64,512]{1,0:T(8,128)S(1)}, f32[64,512]{1,0:T(8,128)S(1)}, u32[]{:S(2)}, u32[]{:S(2)}) collective-permute-start(f32[64,512]{1,0:T(8,128)S(1)} %constant_dynamic-slice_fusion.5), channel_id=1, source_target_pairs={{0,2},{2,0},{4,6},{6,4},{8,10},{10,8},{12,14},{14,12},{1,3},{3,1},... | collective-permute-start | bytes 393224 | tf_op jit(solution)/shard_map/ppermute | solution.py:70
  53.3 7.2 %collective-permute-start.14 = (f32[64,512]{1,0:T(8,128)S(1)}, f32[64,512]{1,0:T(8,128)S(1)}, u32[]{:S(2)}, u32[]{:S(2)}) collective-permute-start(f32[64,512]{1,0:T(8,128)S(1)} %constant_dynamic-slice_fusion.2), channel_id=1, source_target_pairs={{0,4},{2,6},{4,0},{6,2},{8,12},{10,14},{12,8},{14,10},{1,5},{3,7},... | collective-permute-start | bytes 393224 | tf_op jit(solution)/shard_map/ppermute | solution.py:70
  54.6 7.3 %collective-permute-start.2 = (f32[64,512]{1,0:T(8,128)S(1)}, f32[64,512]{1,0:T(8,128)S(1)}, u32[]{:S(2)}, u32[]{:S(2)}) collective-permute-start(f32[64,512]{1,0:T(8,128)S(1)} %constant_dynamic-slice_fusion.14), channel_id=1, source_target_pairs={{0,4},{2,6},{4,0},{6,2},{8,12},{10,14},{12,8},{14,10},{1,5},{3,7},... | collective-permute-start | bytes 393224 | tf_op jit(solution)/shard_map/ppermute | solution.py:70
  57.4 11.1 %collective-permute-start.9 = (f32[64,256]{1,0:T(8,128)S(1)}, f32[64,256]{1,0:T(8,128)S(1)}, u32[]{:S(2)}, u32[]{:S(2)}) collective-permute-start(f32[64,256]{1,0:T(8,128)S(1)} %constant_dynamic-slice_fusion.7), channel_id=1, source_target_pairs={{0,8},{2,10},{4,12},{6,14},{8,0},{10,2},{12,4},{14,6},{1,9},{3,11}... | collective-permute-start | bytes 196616 | tf_op jit(solution)/shard_map/ppermute | solution.py:70
  58.8 11.1 %collective-permute-start.21 = (f32[64,256]{1,0:T(8,128)S(1)}, f32[64,256]{1,0:T(8,128)S(1)}, u32[]{:S(2)}, u32[]{:S(2)}) collective-permute-start(f32[64,256]{1,0:T(8,128)S(1)} %constant_dynamic-slice_fusion.10), channel_id=1, source_target_pairs={{0,8},{2,10},{4,12},{6,14},{8,0},{10,2},{12,4},{14,6},{1,9},{3,11}... | collective-permute-start | bytes 196616 | tf_op jit(solution)/shard_map/ppermute | solution.py:70
  60.5 12.4 %collective-permute-start.15 = (f32[64,256]{1,0:T(8,128)S(1)}, f32[64,256]{1,0:T(8,128)S(1)}, u32[]{:S(2)}, u32[]{:S(2)}) collective-permute-start(f32[64,256]{1,0:T(8,128)S(1)} %constant_dynamic-slice_fusion.1), channel_id=1, source_target_pairs={{0,8},{2,10},{4,12},{6,14},{8,0},{10,2},{12,4},{14,6},{1,9},{3,11}... | collective-permute-start | bytes 196616 | tf_op jit(solution)/shard_map/ppermute | solution.py:70
  61.9 11.0 %collective-permute-start.3 = (f32[64,256]{1,0:T(8,128)S(1)}, f32[64,256]{1,0:T(8,128)S(1)}, u32[]{:S(2)}, u32[]{:S(2)}) collective-permute-start(f32[64,256]{1,0:T(8,128)S(1)} %constant_dynamic-slice_fusion.13), channel_id=1, source_target_pairs={{0,8},{2,10},{4,12},{6,14},{8,0},{10,2},{12,4},{14,6},{1,9},{3,11}... | collective-permute-start | bytes 196616 | tf_op jit(solution)/shard_map/ppermute | solution.py:70
  69.9 6.3 %collective-permute-start.10 = (bf16[64,256]{1,0:T(8,128)(2,1)S(1)}, bf16[64,256]{1,0:T(8,128)(2,1)S(1)}, u32[]{:S(2)}, u32[]{:S(2)}) collective-permute-start(bf16[64,256]{1,0:T(8,128)(2,1)S(1)} %get-tuple-element.51), channel_id=1, source_target_pairs={{0,8},{2,10},{4,12},{6,14},{8,0},{10,2},{12,4},{14,6},{1,9},{3,11}... | collective-permute-start | bytes 98312 | tf_op jit(solution)/shard_map/ppermute | solution.py:70
  70.0 7.6 %collective-permute-start.22 = (bf16[64,256]{1,0:T(8,128)(2,1)S(1)}, bf16[64,256]{1,0:T(8,128)(2,1)S(1)}, u32[]{:S(2)}, u32[]{:S(2)}) collective-permute-start(bf16[64,256]{1,0:T(8,128)(2,1)S(1)} %get-tuple-element.52), channel_id=1, source_target_pairs={{0,8},{2,10},{4,12},{6,14},{8,0},{10,2},{12,4},{14,6},{1,9},{3,11}... | collective-permute-start | bytes 98312 | tf_op jit(solution)/shard_map/ppermute | solution.py:70
  73.0 5.4 %collective-permute-start.4 = (bf16[64,256]{1,0:T(8,128)(2,1)S(1)}, bf16[64,256]{1,0:T(8,128)(2,1)S(1)}, u32[]{:S(2)}, u32[]{:S(2)}) collective-permute-start(bf16[64,256]{1,0:T(8,128)(2,1)S(1)} %get-tuple-element.49), channel_id=1, source_target_pairs={{0,8},{2,10},{4,12},{6,14},{8,0},{10,2},{12,4},{14,6},{1,9},{3,11}... | collective-permute-start | bytes 98312 | tf_op jit(solution)/shard_map/ppermute | solution.py:70
  73.1 5.4 %collective-permute-start.16 = (bf16[64,256]{1,0:T(8,128)(2,1)S(1)}, bf16[64,256]{1,0:T(8,128)(2,1)S(1)}, u32[]{:S(2)}, u32[]{:S(2)}) collective-permute-start(bf16[64,256]{1,0:T(8,128)(2,1)S(1)} %get-tuple-element.50), channel_id=1, source_target_pairs={{0,8},{2,10},{4,12},{6,14},{8,0},{10,2},{12,4},{14,6},{1,9},{3,11}... | collective-permute-start | bytes 98312 | tf_op jit(solution)/shard_map/ppermute | solution.py:70
  77.6 5.0 %collective-permute-start.23 = (bf16[2,64,256]{2,1,0:T(8,128)(2,1)S(1)}, bf16[2,64,256]{2,1,0:T(8,128)(2,1)S(1)}, u32[]{:S(2)}, u32[]{:S(2)}) collective-permute-start(bf16[2,64,256]{2,1,0:T(8,128)(2,1)S(1)} %pad_maximum_fusion.8), channel_id=1, source_target_pairs={{0,2},{2,0},{4,6},{6,4},{8,10},{10,8},{12,14},{14,12},{1,3},{3,1},... | collective-permute-start | bytes 196616 | tf_op jit(solution)/shard_map/ppermute | solution.py:70
  78.4 4.9 %collective-permute-start.5 = (bf16[2,64,256]{2,1,0:T(8,128)(2,1)S(1)}, bf16[2,64,256]{2,1,0:T(8,128)(2,1)S(1)}, u32[]{:S(2)}, u32[]{:S(2)}) collective-permute-start(bf16[2,64,256]{2,1,0:T(8,128)(2,1)S(1)} %pad_maximum_fusion.5), channel_id=1, source_target_pairs={{0,4},{2,6},{4,0},{6,2},{8,12},{10,14},{12,8},{14,10},{1,5},{3,7},... | collective-permute-start | bytes 196616 | tf_op jit(solution)/shard_map/ppermute | solution.py:70
  78.5 6.2 %collective-permute-start.17 = (bf16[2,64,256]{2,1,0:T(8,128)(2,1)S(1)}, bf16[2,64,256]{2,1,0:T(8,128)(2,1)S(1)}, u32[]{:S(2)}, u32[]{:S(2)}) collective-permute-start(bf16[2,64,256]{2,1,0:T(8,128)(2,1)S(1)} %pad_maximum_fusion.7), channel_id=1, source_target_pairs={{0,4},{2,6},{4,0},{6,2},{8,12},{10,14},{12,8},{14,10},{1,5},{3,7},... | collective-permute-start | bytes 196616 | tf_op jit(solution)/shard_map/ppermute | solution.py:70
  80.7 5.0 %collective-permute-start.12 = (bf16[2,2,64,256]{3,2,1,0:T(8,128)(2,1)S(1)}, bf16[2,2,64,256]{3,2,1,0:T(8,128)(2,1)S(1)}, u32[]{:S(2)}, u32[]{:S(2)}) collective-permute-start(bf16[2,2,64,256]{3,2,1,0:T(8,128)(2,1)S(1)} %pad_maximum_fusion.2), channel_id=1, source_target_pairs={{0,4},{2,6},{4,0},{6,2},{8,12},{10,14},{12,8},{14,10},{1,5},{3,7},... | collective-permute-start | bytes 393224 | tf_op jit(solution)/shard_map/ppermute | solution.py:70
  82.6 5.0 %collective-permute-start.24 = (bf16[2,2,64,256]{3,2,1,0:T(8,128)(2,1)S(1)}, bf16[2,2,64,256]{3,2,1,0:T(8,128)(2,1)S(1)}, u32[]{:S(2)}, u32[]{:S(2)}) collective-permute-start(bf16[2,2,64,256]{3,2,1,0:T(8,128)(2,1)S(1)} %pad_maximum_fusion.4), channel_id=1, source_target_pairs={{0,4},{2,6},{4,0},{6,2},{8,12},{10,14},{12,8},{14,10},{1,5},{3,7},... | collective-permute-start | bytes 393224 | tf_op jit(solution)/shard_map/ppermute | solution.py:70
  83.3 5.0 %collective-permute-start.6 = (bf16[2,2,64,256]{3,2,1,0:T(8,128)(2,1)S(1)}, bf16[2,2,64,256]{3,2,1,0:T(8,128)(2,1)S(1)}, u32[]{:S(2)}, u32[]{:S(2)}) collective-permute-start(bf16[2,2,64,256]{3,2,1,0:T(8,128)(2,1)S(1)} %pad_maximum_fusion.1), channel_id=1, source_target_pairs={{0,2},{2,0},{4,6},{6,4},{8,10},{10,8},{12,14},{14,12},{1,3},{3,1},... | collective-permute-start | bytes 393224 | tf_op jit(solution)/shard_map/ppermute | solution.py:70
  84.8 5.0 %collective-permute-start.18 = (bf16[2,2,64,256]{3,2,1,0:T(8,128)(2,1)S(1)}, bf16[2,2,64,256]{3,2,1,0:T(8,128)(2,1)S(1)}, u32[]{:S(2)}, u32[]{:S(2)}) collective-permute-start(bf16[2,2,64,256]{3,2,1,0:T(8,128)(2,1)S(1)} %pad_maximum_fusion.3), channel_id=1, source_target_pairs={{0,2},{2,0},{4,6},{6,4},{8,10},{10,8},{12,14},{14,12},{1,3},{3,1},... | collective-permute-start | bytes 393224 | tf_op jit(solution)/shard_map/ppermute | solution.py:70
  (11 other events, 124.5 us)

commit v15 on v14

--- a/solution.py
+++ b/solution.py
@@ -39,7 +39,7 @@
     m2_out[...] = moment_two.astype(jnp.bfloat16)
 
 
-def tail(pre_t, error, centered, decoder, weight_in, first, second, tile=256):
+def tail(pre_t, error, centered, decoder, weight_in, first, second, tile=512):
     n_lat, width = decoder.shape
     if n_lat % tile:
         tile = n_lat

time: 121 us -> 121 us (level)
  no operation moved by 1% of the time
where the time goes in v15:
time: 121 us; the launch traced here: 120 us
  waiting for transfers between devices  38.6 us (32%)
  starting transfers between devices  33.5 us (28%)
  Pallas kernels  28 us (23%)
  matrix products  8.83 us (7%)
  local copies, waits for them, and re-layouts  7.6 us (6%)
  other arithmetic  2.66 us (2%)
  between operations  1.24 us (1%)
    pallas_call x1, Pallas kernels, tail(): pl.pallas_call(_tail_kernel, grid=(n_lat // tile,), in_specs=[pl.BlockSpe...  28 us
    ppermute x24, starting transfers between devices, _pair_swap(): return lax.ppermute(value, axis, [(i, i ^ mask) for i in range(size)])  26.2 us
    ppermute x24, waiting for transfers between devices, _pair_swap(): return lax.ppermute(value, axis, [(i, i ^ mask) for i in range(size)])  23.7 us
    all_to_all x1, waiting for transfers between devices, local(): act_blocks = lax.all_to_all(copies, 'lat', 0, 0, tiled=True)  13.1 us
    all_to_all x1, starting transfers between devices, local(): act_blocks = lax.all_to_all(copies, 'lat', 0, 0, tiled=True)  7.25 us
    dot_general x1, matrix products, local(): lax.dot_general(weight_in, centered, (((1,), (1,)), ((), ())), preferred_...  6.49 us
  transfers between devices with their start and end apart: 26, of which 16 were waited for; matrix products, arithmetic and copies ran while one was open for 3% of the time, Pallas kernels for 0%

profile of v15, /device:TPU:0, one launch (start us, length us, event | category | flops | bytes accessed | tf_op | source)
XLA Modules:
  0.0 120.5 jit_solution(9577203183106921622)
XLA Ops:
  0.7 1.7 %broadcast_in_dim.46 = bf16[8,128,256]{2,1,0:T(8,128)(2,1)} broadcast(bf16[128,256]{1,0:T(8,128)(2,1)} %param.13), dimensions={1,2} | broadcast | bytes 589824 | tf_op jit(solution)/shard_map/broadcast_in_dim | solution.py:172
  2.4 7.3 %all-to-all-start = ((bf16[8,128,256]{2,1,0:T(8,128)(2,1)}), bf16[8,128,256]{2,1,0:T(8,128)(2,1)S(1)}, u32[]{:S(2)}, u32[]{:S(2)}) async-start(bf16[8,128,256]{2,1,0:T(8,128)(2,1)} %broadcast_in_dim.46), calls=%async_computation | async-start | bytes 1048576 | tf_op jit(solution)/shard_map/all_to_all | solution.py:173
  11.0 13.1 %all-to-all-done = bf16[8,128,256]{2,1,0:T(8,128)(2,1)S(1)} async-done(((bf16[8,128,256]{2,1,0:T(8,128)(2,1)}), bf16[8,128,256]{2,1,0:T(8,128)(2,1)S(1)}, u32[]{:S(2)}, u32[]{:S(2)}) %all-to-all-start) | async-done | bytes 524320 | tf_op jit(solution)/shard_map/all_to_all | solution.py:173
  24.3 1.8 %collective-permute-done = bf16[128,2048]{1,0:T(8,128)(2,1)S(1)} collective-permute-done((bf16[128,2048]{1,0:T(8,128)(2,1)S(1)}, bf16[128,2048]{1,0:T(8,128)(2,1)S(1)}, u32[]{:S(2)}, u32[]{:S(2)}) %collective-permute-start) | collective-permute-done | bytes 524320 | tf_op jit(solution)/shard_map/ppermute | solution.py:175
  26.3 1.4 %gather_fusion = bf16[256,2048]{1,0:T(8,128)(2,1)S(1)} fusion(bf16[256,2048]{1,0:T(8,128)(2,1)S(1)} %pad_maximum_fusion, s32[1024]{0:T(1024)S(1)} %pad_clamp_fusion.2), kind=kCustom, calls=%fused_computation | custom fusion | bytes 2098176 | tf_op jit(solution)/shard_map/jit(_take)/gather | solution.py:182
  28.4 6.5 %fusion.pre_ref = f32[2048,256]{1,0:T(8,128)S(1)} fusion(bf16[256,2048]{1,0:T(8,128)(2,1)S(1)} %get-tuple-element.9.cen_ref, f32[2048]{0:T(1024)S(1)} %bitcast.116, bf16[1,2048,2048]{2,1,0:T(8,128)(2,1)} %param.16), kind=kOutput, calls=%fused_computation.6 | convolution fusion | flops 2148007936 | bytes 11542528 | tf_op jit(solution)/shard_map/dot_general | solution.py:188
  34.9 2.3 %fusion.1 = f32[256,2048]{1,0:T(8,128)S(1)} fusion(f32[2048,256]{1,0:T(8,128)S(1)} %fusion.pre_ref, bf16[1,2048,2048]{2,1,0:T(8,128)(2,1)S(1)} %bitcast.94), kind=kOutput, calls=%fused_computation.9 | convolution fusion | flops 2148532224 | bytes 12582912 | tf_op jit(solution)/shard_map/dot_general | solution.py:194
  39.7 1.5 %collective-permute-start.13 = (f32[64,1024]{1,0:T(8,128)S(1)}, f32[64,1024]{1,0:T(8,128)S(1)}, u32[]{:S(2)}, u32[]{:S(2)}) collective-permute-start(f32[64,1024]{1,0:T(8,128)S(1)} %constant_dynamic-slice_fusion.3), channel_id=1, source_target_pairs={{0,2},{2,0},{4,6},{6,4},{8,10},{10,8},{12,14},{14,12},{1,3},{3,1},... | collective-permute-start | bytes 786440 | tf_op jit(solution)/shard_map/ppermute | solution.py:70
  41.8 5.0 %collective-permute-done.7 = f32[64,1024]{1,0:T(8,128)S(1)} collective-permute-done((f32[64,1024]{1,0:T(8,128)S(1)}, f32[64,1024]{1,0:T(8,128)S(1)}, u32[]{:S(2)}, u32[]{:S(2)}) %collective-permute-start.7) | collective-permute-done | bytes 262176 | tf_op jit(solution)/shard_map/ppermute | solution.py:70
  46.9 1.5 %collective-permute-start.8 = (f32[64,512]{1,0:T(8,128)S(1)}, f32[64,512]{1,0:T(8,128)S(1)}, u32[]{:S(2)}, u32[]{:S(2)}) collective-permute-start(f32[64,512]{1,0:T(8,128)S(1)} %constant_dynamic-slice_fusion.8), channel_id=1, source_target_pairs={{0,2},{2,0},{4,6},{6,4},{8,10},{10,8},{12,14},{14,12},{1,3},{3,1},... | collective-permute-start | bytes 393224 | tf_op jit(solution)/shard_map/ppermute | solution.py:70
  48.4 3.2 %collective-permute-done.19 = f32[64,1024]{1,0:T(8,128)S(1)} collective-permute-done((f32[64,1024]{1,0:T(8,128)S(1)}, f32[64,1024]{1,0:T(8,128)S(1)}, u32[]{:S(2)}, u32[]{:S(2)}) %collective-permute-start.19) | collective-permute-done | bytes 262176 | tf_op jit(solution)/shard_map/ppermute | solution.py:70
  51.7 1.5 %collective-permute-start.20 = (f32[64,512]{1,0:T(8,128)S(1)}, f32[64,512]{1,0:T(8,128)S(1)}, u32[]{:S(2)}, u32[]{:S(2)}) collective-permute-start(f32[64,512]{1,0:T(8,128)S(1)} %constant_dynamic-slice_fusion.5), channel_id=1, source_target_pairs={{0,2},{2,0},{4,6},{6,4},{8,10},{10,8},{12,14},{14,12},{1,3},{3,1},... | collective-permute-start | bytes 393224 | tf_op jit(solution)/shard_map/ppermute | solution.py:70
  55.5 1.8 %collective-permute-done.8 = f32[64,512]{1,0:T(8,128)S(1)} collective-permute-done((f32[64,512]{1,0:T(8,128)S(1)}, f32[64,512]{1,0:T(8,128)S(1)}, u32[]{:S(2)}, u32[]{:S(2)}) %collective-permute-start.8) | collective-permute-done | bytes 131104 | tf_op jit(solution)/shard_map/ppermute | solution.py:70
  58.8 1.7 %collective-permute-start.21 = (f32[64,256]{1,0:T(8,128)S(1)}, f32[64,256]{1,0:T(8,128)S(1)}, u32[]{:S(2)}, u32[]{:S(2)}) collective-permute-start(f32[64,256]{1,0:T(8,128)S(1)} %constant_dynamic-slice_fusion.10), channel_id=1, source_target_pairs={{0,8},{2,10},{4,12},{6,14},{8,0},{10,2},{12,4},{14,6},{1,9},{3,11}... | collective-permute-start | bytes 196616 | tf_op jit(solution)/shard_map/ppermute | solution.py:70
  61.9 1.7 %collective-permute-start.3 = (f32[64,256]{1,0:T(8,128)S(1)}, f32[64,256]{1,0:T(8,128)S(1)}, u32[]{:S(2)}, u32[]{:S(2)}) collective-permute-start(f32[64,256]{1,0:T(8,128)S(1)} %constant_dynamic-slice_fusion.13), channel_id=1, source_target_pairs={{0,8},{2,10},{4,12},{6,14},{8,0},{10,2},{12,4},{14,6},{1,9},{3,11}... | collective-permute-start | bytes 196616 | tf_op jit(solution)/shard_map/ppermute | solution.py:70
  63.6 4.8 %collective-permute-done.9 = f32[64,256]{1,0:T(8,128)S(1)} collective-permute-done((f32[64,256]{1,0:T(8,128)S(1)}, f32[64,256]{1,0:T(8,128)S(1)}, u32[]{:S(2)}, u32[]{:S(2)}) %collective-permute-start.9) | collective-permute-done | bytes 65568 | tf_op jit(solution)/shard_map/ppermute | solution.py:70
  68.4 1.4 %collective-permute-done.21 = f32[64,256]{1,0:T(8,128)S(1)} collective-permute-done((f32[64,256]{1,0:T(8,128)S(1)}, f32[64,256]{1,0:T(8,128)S(1)}, u32[]{:S(2)}, u32[]{:S(2)}) %collective-permute-start.21) | collective-permute-done | bytes 65568 | tf_op jit(solution)/shard_map/ppermute | solution.py:70
  70.0 2.9 %collective-permute-start.22 = (bf16[64,256]{1,0:T(8,128)(2,1)S(1)}, bf16[64,256]{1,0:T(8,128)(2,1)S(1)}, u32[]{:S(2)}, u32[]{:S(2)}) collective-permute-start(bf16[64,256]{1,0:T(8,128)(2,1)S(1)} %get-tuple-element.52), channel_id=1, source_target_pairs={{0,8},{2,10},{4,12},{6,14},{8,0},{10,2},{12,4},{14,6},{1,9},{3,11}... | collective-permute-start | bytes 98312 | tf_op jit(solution)/shard_map/ppermute | solution.py:70
  73.1 2.9 %collective-permute-start.16 = (bf16[64,256]{1,0:T(8,128)(2,1)S(1)}, bf16[64,256]{1,0:T(8,128)(2,1)S(1)}, u32[]{:S(2)}, u32[]{:S(2)}) collective-permute-start(bf16[64,256]{1,0:T(8,128)(2,1)S(1)} %get-tuple-element.50), channel_id=1, source_target_pairs={{0,8},{2,10},{4,12},{6,14},{8,0},{10,2},{12,4},{14,6},{1,9},{3,11}... | collective-permute-start | bytes 98312 | tf_op jit(solution)/shard_map/ppermute | solution.py:70
  78.5 2.1 %collective-permute-start.17 = (bf16[2,64,256]{2,1,0:T(8,128)(2,1)S(1)}, bf16[2,64,256]{2,1,0:T(8,128)(2,1)S(1)}, u32[]{:S(2)}, u32[]{:S(2)}) collective-permute-start(bf16[2,64,256]{2,1,0:T(8,128)(2,1)S(1)} %pad_maximum_fusion.7), channel_id=1, source_target_pairs={{0,4},{2,6},{4,0},{6,2},{8,12},{10,14},{12,8},{14,10},{1,5},{3,7},... | collective-permute-start | bytes 196616 | tf_op jit(solution)/shard_map/ppermute | solution.py:70
  80.7 1.8 %collective-permute-done.23 = bf16[2,64,256]{2,1,0:T(8,128)(2,1)S(1)} collective-permute-done((bf16[2,64,256]{2,1,0:T(8,128)(2,1)S(1)}, bf16[2,64,256]{2,1,0:T(8,128)(2,1)S(1)}, u32[]{:S(2)}, u32[]{:S(2)}) %collective-permute-start.23) | collective-permute-done | bytes 65568 | tf_op jit(solution)/shard_map/ppermute | solution.py:70
  83.3 1.5 %collective-permute-start.6 = (bf16[2,2,64,256]{3,2,1,0:T(8,128)(2,1)S(1)}, bf16[2,2,64,256]{3,2,1,0:T(8,128)(2,1)S(1)}, u32[]{:S(2)}, u32[]{:S(2)}) collective-permute-start(bf16[2,2,64,256]{3,2,1,0:T(8,128)(2,1)S(1)} %pad_maximum_fusion.1), channel_id=1, source_target_pairs={{0,2},{2,0},{4,6},{6,4},{8,10},{10,8},{12,14},{14,12},{1,3},{3,1},... | collective-permute-start | bytes 393224 | tf_op jit(solution)/shard_map/ppermute | solution.py:70
  85.7 1.9 %collective-permute-done.24 = bf16[2,2,64,256]{3,2,1,0:T(8,128)(2,1)S(1)} collective-permute-done((bf16[2,2,64,256]{3,2,1,0:T(8,128)(2,1)S(1)}, bf16[2,2,64,256]{3,2,1,0:T(8,128)(2,1)S(1)}, u32[]{:S(2)}, u32[]{:S(2)}) %collective-permute-start.24) | collective-permute-done | bytes 131104 | tf_op jit(solution)/shard_map/ppermute | solution.py:70
  92.5 28.0 %shard_map.148 = (bf16[2048,2048]{1,0:T(8,128)(2,1)}, bf16[2048,2048]{1,0:T(8,128)(2,1)}, bf16[2048,2048]{1,0:T(8,128)(2,1)}) custom-call(f32[2048,256]{1,0:T(8,128)} %copy-done, bf16[2048,256]{1,0:T(8,128)(2,1)} %bitcast.98, bf16[256,2048]{1,0:T(8,128)(2,1)} %copy-done.1, bf16[2048,2048]{1,0:T(8,128)(2,1)} %bitcast.92, bf16[2048,2048]{1,0:T(8,128)(2,1)} %bitcast.95, ...), custom_call_target="tpu_custom_call" | custom-call | tf_op jit(solution)/shard_map/pallas_call | solution.py:51
  (121 shorter events, 20.0 us)
Async XLA Ops:
  2.4 21.7 %all-to-all-start = ((bf16[8,128,256]{2,1,0:T(8,128)(2,1)}), bf16[8,128,256]{2,1,0:T(8,128)(2,1)S(1)}, u32[]{:S(2)}, u32[]{:S(2)}) async-start(bf16[8,128,256]{2,1,0:T(8,128)(2,1)} %broadcast_in_dim.46), calls=%async_computation | async-start | bytes 1048576 | tf_op jit(solution)/shard_map/all_to_all | solution.py:173
  37.6 9.2 %collective-permute-start.7 = (f32[64,1024]{1,0:T(8,128)S(1)}, f32[64,1024]{1,0:T(8,128)S(1)}, u32[]{:S(2)}, u32[]{:S(2)}) collective-permute-start(f32[64,1024]{1,0:T(8,128)S(1)} %constant_dynamic-slice_fusion.9), channel_id=1, source_target_pairs={{0,4},{2,6},{4,0},{6,2},{8,12},{10,14},{12,8},{14,10},{1,5},{3,7},... | collective-permute-start | bytes 786440 | tf_op jit(solution)/shard_map/ppermute | solution.py:70
  38.4 13.2 %collective-permute-start.19 = (f32[64,1024]{1,0:T(8,128)S(1)}, f32[64,1024]{1,0:T(8,128)S(1)}, u32[]{:S(2)}, u32[]{:S(2)}) collective-permute-start(f32[64,1024]{1,0:T(8,128)S(1)} %constant_dynamic-slice_fusion), channel_id=1, source_target_pairs={{0,4},{2,6},{4,0},{6,2},{8,12},{10,14},{12,8},{14,10},{1,5},{3,7},... | collective-permute-start | bytes 786440 | tf_op jit(solution)/shard_map/ppermute | solution.py:70
  39.7 13.5 %collective-permute-start.13 = (f32[64,1024]{1,0:T(8,128)S(1)}, f32[64,1024]{1,0:T(8,128)S(1)}, u32[]{:S(2)}, u32[]{:S(2)}) collective-permute-start(f32[64,1024]{1,0:T(8,128)S(1)} %constant_dynamic-slice_fusion.3), channel_id=1, source_target_pairs={{0,2},{2,0},{4,6},{6,4},{8,10},{10,8},{12,14},{14,12},{1,3},{3,1},... | collective-permute-start | bytes 786440 | tf_op jit(solution)/shard_map/ppermute | solution.py:70
  41.2 13.4 %collective-permute-start.1 = (f32[64,1024]{1,0:T(8,128)S(1)}, f32[64,1024]{1,0:T(8,128)S(1)}, u32[]{:S(2)}, u32[]{:S(2)}) collective-permute-start(f32[64,1024]{1,0:T(8,128)S(1)} %constant_dynamic-slice_fusion.15), channel_id=1, source_target_pairs={{0,2},{2,0},{4,6},{6,4},{8,10},{10,8},{12,14},{14,12},{1,3},{3,1},... | collective-permute-start | bytes 786440 | tf_op jit(solution)/shard_map/ppermute | solution.py:70
  46.9 10.4 %collective-permute-start.8 = (f32[64,512]{1,0:T(8,128)S(1)}, f32[64,512]{1,0:T(8,128)S(1)}, u32[]{:S(2)}, u32[]{:S(2)}) collective-permute-start(f32[64,512]{1,0:T(8,128)S(1)} %constant_dynamic-slice_fusion.8), channel_id=1, source_target_pairs={{0,2},{2,0},{4,6},{6,4},{8,10},{10,8},{12,14},{14,12},{1,3},{3,1},... | collective-permute-start | bytes 393224 | tf_op jit(solution)/shard_map/ppermute | solution.py:70
  51.7 7.0 %collective-permute-start.20 = (f32[64,512]{1,0:T(8,128)S(1)}, f32[64,512]{1,0:T(8,128)S(1)}, u32[]{:S(2)}, u32[]{:S(2)}) collective-permute-start(f32[64,512]{1,0:T(8,128)S(1)} %constant_dynamic-slice_fusion.5), channel_id=1, source_target_pairs={{0,2},{2,0},{4,6},{6,4},{8,10},{10,8},{12,14},{14,12},{1,3},{3,1},... | collective-permute-start | bytes 393224 | tf_op jit(solution)/shard_map/ppermute | solution.py:70
  53.3 7.2 %collective-permute-start.14 = (f32[64,512]{1,0:T(8,128)S(1)}, f32[64,512]{1,0:T(8,128)S(1)}, u32[]{:S(2)}, u32[]{:S(2)}) collective-permute-start(f32[64,512]{1,0:T(8,128)S(1)} %constant_dynamic-slice_fusion.2), channel_id=1, source_target_pairs={{0,4},{2,6},{4,0},{6,2},{8,12},{10,14},{12,8},{14,10},{1,5},{3,7},... | collective-permute-start | bytes 393224 | tf_op jit(solution)/shard_map/ppermute | solution.py:70
  54.6 7.3 %collective-permute-start.2 = (f32[64,512]{1,0:T(8,128)S(1)}, f32[64,512]{1,0:T(8,128)S(1)}, u32[]{:S(2)}, u32[]{:S(2)}) collective-permute-start(f32[64,512]{1,0:T(8,128)S(1)} %constant_dynamic-slice_fusion.14), channel_id=1, source_target_pairs={{0,4},{2,6},{4,0},{6,2},{8,12},{10,14},{12,8},{14,10},{1,5},{3,7},... | collective-permute-start | bytes 393224 | tf_op jit(solution)/shard_map/ppermute | solution.py:70
  57.4 11.1 %collective-permute-start.9 = (f32[64,256]{1,0:T(8,128)S(1)}, f32[64,256]{1,0:T(8,128)S(1)}, u32[]{:S(2)}, u32[]{:S(2)}) collective-permute-start(f32[64,256]{1,0:T(8,128)S(1)} %constant_dynamic-slice_fusion.7), channel_id=1, source_target_pairs={{0,8},{2,10},{4,12},{6,14},{8,0},{10,2},{12,4},{14,6},{1,9},{3,11}... | collective-permute-start | bytes 196616 | tf_op jit(solution)/shard_map/ppermute | solution.py:70
  58.8 11.1 %collective-permute-start.21 = (f32[64,256]{1,0:T(8,128)S(1)}, f32[64,256]{1,0:T(8,128)S(1)}, u32[]{:S(2)}, u32[]{:S(2)}) collective-permute-start(f32[64,256]{1,0:T(8,128)S(1)} %constant_dynamic-slice_fusion.10), channel_id=1, source_target_pairs={{0,8},{2,10},{4,12},{6,14},{8,0},{10,2},{12,4},{14,6},{1,9},{3,11}... | collective-permute-start | bytes 196616 | tf_op jit(solution)/shard_map/ppermute | solution.py:70
  60.5 12.4 %collective-permute-start.15 = (f32[64,256]{1,0:T(8,128)S(1)}, f32[64,256]{1,0:T(8,128)S(1)}, u32[]{:S(2)}, u32[]{:S(2)}) collective-permute-start(f32[64,256]{1,0:T(8,128)S(1)} %constant_dynamic-slice_fusion.1), channel_id=1, source_target_pairs={{0,8},{2,10},{4,12},{6,14},{8,0},{10,2},{12,4},{14,6},{1,9},{3,11}... | collective-permute-start | bytes 196616 | tf_op jit(solution)/shard_map/ppermute | solution.py:70
  61.9 11.0 %collective-permute-start.3 = (f32[64,256]{1,0:T(8,128)S(1)}, f32[64,256]{1,0:T(8,128)S(1)}, u32[]{:S(2)}, u32[]{:S(2)}) collective-permute-start(f32[64,256]{1,0:T(8,128)S(1)} %constant_dynamic-slice_fusion.13), channel_id=1, source_target_pairs={{0,8},{2,10},{4,12},{6,14},{8,0},{10,2},{12,4},{14,6},{1,9},{3,11}... | collective-permute-start | bytes 196616 | tf_op jit(solution)/shard_map/ppermute | solution.py:70
  69.9 6.3 %collective-permute-start.10 = (bf16[64,256]{1,0:T(8,128)(2,1)S(1)}, bf16[64,256]{1,0:T(8,128)(2,1)S(1)}, u32[]{:S(2)}, u32[]{:S(2)}) collective-permute-start(bf16[64,256]{1,0:T(8,128)(2,1)S(1)} %get-tuple-element.51), channel_id=1, source_target_pairs={{0,8},{2,10},{4,12},{6,14},{8,0},{10,2},{12,4},{14,6},{1,9},{3,11}... | collective-permute-start | bytes 98312 | tf_op jit(solution)/shard_map/ppermute | solution.py:70
  70.0 7.6 %collective-permute-start.22 = (bf16[64,256]{1,0:T(8,128)(2,1)S(1)}, bf16[64,256]{1,0:T(8,128)(2,1)S(1)}, u32[]{:S(2)}, u32[]{:S(2)}) collective-permute-start(bf16[64,256]{1,0:T(8,128)(2,1)S(1)} %get-tuple-element.52), channel_id=1, source_target_pairs={{0,8},{2,10},{4,12},{6,14},{8,0},{10,2},{12,4},{14,6},{1,9},{3,11}... | collective-permute-start | bytes 98312 | tf_op jit(solution)/shard_map/ppermute | solution.py:70
  72.9 5.4 %collective-permute-start.4 = (bf16[64,256]{1,0:T(8,128)(2,1)S(1)}, bf16[64,256]{1,0:T(8,128)(2,1)S(1)}, u32[]{:S(2)}, u32[]{:S(2)}) collective-permute-start(bf16[64,256]{1,0:T(8,128)(2,1)S(1)} %get-tuple-element.49), channel_id=1, source_target_pairs={{0,8},{2,10},{4,12},{6,14},{8,0},{10,2},{12,4},{14,6},{1,9},{3,11}... | collective-permute-start | bytes 98312 | tf_op jit(solution)/shard_map/ppermute | solution.py:70
  73.1 5.4 %collective-permute-start.16 = (bf16[64,256]{1,0:T(8,128)(2,1)S(1)}, bf16[64,256]{1,0:T(8,128)(2,1)S(1)}, u32[]{:S(2)}, u32[]{:S(2)}) collective-permute-start(bf16[64,256]{1,0:T(8,128)(2,1)S(1)} %get-tuple-element.50), channel_id=1, source_target_pairs={{0,8},{2,10},{4,12},{6,14},{8,0},{10,2},{12,4},{14,6},{1,9},{3,11}... | collective-permute-start | bytes 98312 | tf_op jit(solution)/shard_map/ppermute | solution.py:70
  77.6 5.0 %collective-permute-start.23 = (bf16[2,64,256]{2,1,0:T(8,128)(2,1)S(1)}, bf16[2,64,256]{2,1,0:T(8,128)(2,1)S(1)}, u32[]{:S(2)}, u32[]{:S(2)}) collective-permute-start(bf16[2,64,256]{2,1,0:T(8,128)(2,1)S(1)} %pad_maximum_fusion.8), channel_id=1, source_target_pairs={{0,2},{2,0},{4,6},{6,4},{8,10},{10,8},{12,14},{14,12},{1,3},{3,1},... | collective-permute-start | bytes 196616 | tf_op jit(solution)/shard_map/ppermute | solution.py:70
  78.4 4.8 %collective-permute-start.5 = (bf16[2,64,256]{2,1,0:T(8,128)(2,1)S(1)}, bf16[2,64,256]{2,1,0:T(8,128)(2,1)S(1)}, u32[]{:S(2)}, u32[]{:S(2)}) collective-permute-start(bf16[2,64,256]{2,1,0:T(8,128)(2,1)S(1)} %pad_maximum_fusion.5), channel_id=1, source_target_pairs={{0,4},{2,6},{4,0},{6,2},{8,12},{10,14},{12,8},{14,10},{1,5},{3,7},... | collective-permute-start | bytes 196616 | tf_op jit(solution)/shard_map/ppermute | solution.py:70
  78.5 6.2 %collective-permute-start.17 = (bf16[2,64,256]{2,1,0:T(8,128)(2,1)S(1)}, bf16[2,64,256]{2,1,0:T(8,128)(2,1)S(1)}, u32[]{:S(2)}, u32[]{:S(2)}) collective-permute-start(bf16[2,64,256]{2,1,0:T(8,128)(2,1)S(1)} %pad_maximum_fusion.7), channel_id=1, source_target_pairs={{0,4},{2,6},{4,0},{6,2},{8,12},{10,14},{12,8},{14,10},{1,5},{3,7},... | collective-permute-start | bytes 196616 | tf_op jit(solution)/shard_map/ppermute | solution.py:70
  80.7 5.0 %collective-permute-start.12 = (bf16[2,2,64,256]{3,2,1,0:T(8,128)(2,1)S(1)}, bf16[2,2,64,256]{3,2,1,0:T(8,128)(2,1)S(1)}, u32[]{:S(2)}, u32[]{:S(2)}) collective-permute-start(bf16[2,2,64,256]{3,2,1,0:T(8,128)(2,1)S(1)} %pad_maximum_fusion.2), channel_id=1, source_target_pairs={{0,4},{2,6},{4,0},{6,2},{8,12},{10,14},{12,8},{14,10},{1,5},{3,7},... | collective-permute-start | bytes 393224 | tf_op jit(solution)/shard_map/ppermute | solution.py:70
  82.6 5.0 %collective-permute-start.24 = (bf16[2,2,64,256]{3,2,1,0:T(8,128)(2,1)S(1)}, bf16[2,2,64,256]{3,2,1,0:T(8,128)(2,1)S(1)}, u32[]{:S(2)}, u32[]{:S(2)}) collective-permute-start(bf16[2,2,64,256]{3,2,1,0:T(8,128)(2,1)S(1)} %pad_maximum_fusion.4), channel_id=1, source_target_pairs={{0,4},{2,6},{4,0},{6,2},{8,12},{10,14},{12,8},{14,10},{1,5},{3,7},... | collective-permute-start | bytes 393224 | tf_op jit(solution)/shard_map/ppermute | solution.py:70
  83.3 5.0 %collective-permute-start.6 = (bf16[2,2,64,256]{3,2,1,0:T(8,128)(2,1)S(1)}, bf16[2,2,64,256]{3,2,1,0:T(8,128)(2,1)S(1)}, u32[]{:S(2)}, u32[]{:S(2)}) collective-permute-start(bf16[2,2,64,256]{3,2,1,0:T(8,128)(2,1)S(1)} %pad_maximum_fusion.1), channel_id=1, source_target_pairs={{0,2},{2,0},{4,6},{6,4},{8,10},{10,8},{12,14},{14,12},{1,3},{3,1},... | collective-permute-start | bytes 393224 | tf_op jit(solution)/shard_map/ppermute | solution.py:70
  84.8 5.0 %collective-permute-start.18 = (bf16[2,2,64,256]{3,2,1,0:T(8,128)(2,1)S(1)}, bf16[2,2,64,256]{3,2,1,0:T(8,128)(2,1)S(1)}, u32[]{:S(2)}, u32[]{:S(2)}) collective-permute-start(bf16[2,2,64,256]{3,2,1,0:T(8,128)(2,1)S(1)} %pad_maximum_fusion.3), channel_id=1, source_target_pairs={{0,2},{2,0},{4,6},{6,4},{8,10},{10,8},{12,14},{14,12},{1,3},{3,1},... | collective-permute-start | bytes 393224 | tf_op jit(solution)/shard_map/ppermute | solution.py:70
  (11 other events, 124.5 us)

commit v16 on v15

--- a/solution.py
+++ b/solution.py
@@ -207,9 +207,19 @@
         error_cols = (
             (total + bias_cols - sample_cols.astype(jnp.float32)) * keep_cols_f
         ).astype(jnp.bfloat16)
-        stacked = _doubling_gather(error_cols, "lat", lat_size, order[::-1])
-        error_parts.append(stacked[jnp.array(_block_owners(lat_size, order))])
-    error_blocks = jnp.concatenate(error_parts, axis=1)
+        error_parts.append(error_cols)
+    gathered_parts = []
+    for group, order in enumerate((first, second)):
+        joined = jnp.concatenate(error_parts[group::2], axis=0)
+        stacked = _doubling_gather(joined, "lat", lat_size, order[::-1])
+        gathered_parts.append(stacked[jnp.array(_block_owners(lat_size, order))])
+    error_blocks = jnp.concatenate(
+        [
+            gathered_parts[part % 2][:, (part // 2) * chunk : (part // 2 + 1) * chunk]
+            for part in range(4)
+        ],
+        axis=1,
+    )
     error = jnp.transpose(error_blocks, (1, 0, 2)).reshape(error_blocks.shape[1], -1)
     updated, moment_one, moment_two = tail(
         pre_t, error, centered, decoder, weight_in, first_moment[0], second_moment[0]

time: 121 us -> 122 us (level)
  waiting for transfers between devices: 38.6 us -> 45.5 us
  starting transfers between devices: 33.5 us -> 28 us
    ppermute x24 -> x18, waiting for transfers between devices: 23.7 us -> 31.3 us  [_pair_swap(): return lax.ppermute(value, axis, [(i, i ^ mask) for i in range(size)])]
    ppermute x24 -> x18, starting transfers between devices: 26.2 us -> 20.6 us  [_pair_swap(): return lax.ppermute(value, axis, [(i, i ^ mask) for i in range(size)])]
  transfers between devices with their start and end apart: 26 -> 20, of which waited for: 16 -> 17; matrix products, arithmetic and copies ran while one was open for 3% -> 3% of each run, Pallas kernels for 0% -> 0%
where the time goes in v16:
time: 122 us; the launch traced here: 121 us
  waiting for transfers between devices  45.5 us (37%)
  starting transfers between devices  28 us (23%)
  Pallas kernels  28 us (23%)
  matrix products  8.83 us (7%)
  local copies, waits for them, and re-layouts  7.32 us (6%)
  other arithmetic  2.64 us (2%)
    ppermute x18, waiting for transfers between devices, _pair_swap(): return lax.ppermute(value, axis, [(i, i ^ mask) for i in range(size)])  31.3 us
    pallas_call x1, Pallas kernels, tail(): pl.pallas_call(_tail_kernel, grid=(n_lat // tile,), in_specs=[pl.BlockSpe...  28 us
    ppermute x18, starting transfers between devices, _pair_swap(): return lax.ppermute(value, axis, [(i, i ^ mask) for i in range(size)])  20.6 us
    all_to_all x1, waiting for transfers between devices, local(): act_blocks = lax.all_to_all(copies, 'lat', 0, 0, tiled=True)  12.3 us
    all_to_all x1, starting transfers between devices, local(): act_blocks = lax.all_to_all(copies, 'lat', 0, 0, tiled=True)  7.25 us
    dot_general x1, matrix products, local(): lax.dot_general(weight_in, centered, (((1,), (1,)), ((), ())), preferred_...  6.48 us
  transfers between devices with their start and end apart: 20, of which 17 were waited for; matrix products, arithmetic and copies ran while one was open for 3% of the time, Pallas kernels for 0%

profile of v16, /device:TPU:0, one launch (start us, length us, event | category | flops | bytes accessed | tf_op | source)
XLA Modules:
  0.0 121.4 jit_solution(1489602305659394291)
XLA Ops:
  0.7 1.7 %broadcast_in_dim.40 = bf16[8,128,256]{2,1,0:T(8,128)(2,1)} broadcast(bf16[128,256]{1,0:T(8,128)(2,1)} %param.11), dimensions={1,2} | broadcast | bytes 589824 | tf_op jit(solution)/shard_map/broadcast_in_dim | solution.py:172
  2.3 7.3 %all-to-all-start = ((bf16[8,128,256]{2,1,0:T(8,128)(2,1)}), bf16[8,128,256]{2,1,0:T(8,128)(2,1)S(1)}, u32[]{:S(2)}, u32[]{:S(2)}) async-start(bf16[8,128,256]{2,1,0:T(8,128)(2,1)} %broadcast_in_dim.40), calls=%async_computation | async-start | bytes 1048576 | tf_op jit(solution)/shard_map/all_to_all | solution.py:173
  11.7 12.3 %all-to-all-done = bf16[8,128,256]{2,1,0:T(8,128)(2,1)S(1)} async-done(((bf16[8,128,256]{2,1,0:T(8,128)(2,1)}), bf16[8,128,256]{2,1,0:T(8,128)(2,1)S(1)}, u32[]{:S(2)}, u32[]{:S(2)}) %all-to-all-start) | async-done | bytes 524320 | tf_op jit(solution)/shard_map/all_to_all | solution.py:173
  24.3 1.8 %collective-permute-done = bf16[128,2048]{1,0:T(8,128)(2,1)S(1)} collective-permute-done((bf16[128,2048]{1,0:T(8,128)(2,1)S(1)}, bf16[128,2048]{1,0:T(8,128)(2,1)S(1)}, u32[]{:S(2)}, u32[]{:S(2)}) %collective-permute-start) | collective-permute-done | bytes 524320 | tf_op jit(solution)/shard_map/ppermute | solution.py:175
  28.3 6.5 %fusion.pre_ref = f32[2048,256]{1,0:T(8,128)S(1)} fusion(bf16[256,2048]{1,0:T(8,128)(2,1)S(1)} %get-tuple-element.9.cen_ref, f32[2048]{0:T(1024)S(1)} %bitcast.84, bf16[1,2048,2048]{2,1,0:T(8,128)(2,1)} %param.14), kind=kOutput, calls=%fused_computation.4 | convolution fusion | flops 2148007936 | bytes 11542528 | tf_op jit(solution)/shard_map/dot_general | solution.py:188
  34.9 2.3 %fusion.1 = f32[256,2048]{1,0:T(8,128)S(1)} fusion(f32[2048,256]{1,0:T(8,128)S(1)} %fusion.pre_ref, bf16[1,2048,2048]{2,1,0:T(8,128)(2,1)S(1)} %bitcast.64), kind=kOutput, calls=%fused_computation.7 | convolution fusion | flops 2148532224 | bytes 12582912 | tf_op jit(solution)/shard_map/dot_general | solution.py:194
  39.7 1.5 %collective-permute-start.4 = (f32[64,1024]{1,0:T(8,128)S(1)}, f32[64,1024]{1,0:T(8,128)S(1)}, u32[]{:S(2)}, u32[]{:S(2)}) collective-permute-start(f32[64,1024]{1,0:T(8,128)S(1)} %constant_dynamic-slice_fusion.10), channel_id=1, source_target_pairs={{0,2},{2,0},{4,6},{6,4},{8,10},{10,8},{12,14},{14,12},{1,3},{3,1},... | collective-permute-start | bytes 786440 | tf_op jit(solution)/shard_map/ppermute | solution.py:70
  41.9 4.8 %collective-permute-done.10 = f32[64,1024]{1,0:T(8,128)S(1)} collective-permute-done((f32[64,1024]{1,0:T(8,128)S(1)}, f32[64,1024]{1,0:T(8,128)S(1)}, u32[]{:S(2)}, u32[]{:S(2)}) %collective-permute-start.10) | collective-permute-done | bytes 262176 | tf_op jit(solution)/shard_map/ppermute | solution.py:70
  46.8 1.5 %collective-permute-start.11 = (f32[64,512]{1,0:T(8,128)S(1)}, f32[64,512]{1,0:T(8,128)S(1)}, u32[]{:S(2)}, u32[]{:S(2)}) collective-permute-start(f32[64,512]{1,0:T(8,128)S(1)} %constant_dynamic-slice_fusion.4), channel_id=1, source_target_pairs={{0,2},{2,0},{4,6},{6,4},{8,10},{10,8},{12,14},{14,12},{1,3},{3,1},... | collective-permute-start | bytes 393224 | tf_op jit(solution)/shard_map/ppermute | solution.py:70
  48.3 3.2 %collective-permute-done.13 = f32[64,1024]{1,0:T(8,128)S(1)} collective-permute-done((f32[64,1024]{1,0:T(8,128)S(1)}, f32[64,1024]{1,0:T(8,128)S(1)}, u32[]{:S(2)}, u32[]{:S(2)}) %collective-permute-start.13) | collective-permute-done | bytes 262176 | tf_op jit(solution)/shard_map/ppermute | solution.py:70
  51.6 1.5 %collective-permute-start.14 = (f32[64,512]{1,0:T(8,128)S(1)}, f32[64,512]{1,0:T(8,128)S(1)}, u32[]{:S(2)}, u32[]{:S(2)}) collective-permute-start(f32[64,512]{1,0:T(8,128)S(1)} %constant_dynamic-slice_fusion.7), channel_id=1, source_target_pairs={{0,2},{2,0},{4,6},{6,4},{8,10},{10,8},{12,14},{14,12},{1,3},{3,1},... | collective-permute-start | bytes 393224 | tf_op jit(solution)/shard_map/ppermute | solution.py:70
  55.5 1.9 %collective-permute-done.11 = f32[64,512]{1,0:T(8,128)S(1)} collective-permute-done((f32[64,512]{1,0:T(8,128)S(1)}, f32[64,512]{1,0:T(8,128)S(1)}, u32[]{:S(2)}, u32[]{:S(2)}) %collective-permute-start.11) | collective-permute-done | bytes 131104 | tf_op jit(solution)/shard_map/ppermute | solution.py:70
  58.8 1.7 %collective-permute-start.15 = (f32[64,256]{1,0:T(8,128)S(1)}, f32[64,256]{1,0:T(8,128)S(1)}, u32[]{:S(2)}, u32[]{:S(2)}) collective-permute-start(f32[64,256]{1,0:T(8,128)S(1)} %constant_dynamic-slice_fusion.6), channel_id=1, source_target_pairs={{0,8},{2,10},{4,12},{6,14},{8,0},{10,2},{12,4},{14,6},{1,9},{3,11}... | collective-permute-start | bytes 196616 | tf_op jit(solution)/shard_map/ppermute | solution.py:70
  62.0 1.7 %collective-permute-start.3 = (f32[64,256]{1,0:T(8,128)S(1)}, f32[64,256]{1,0:T(8,128)S(1)}, u32[]{:S(2)}, u32[]{:S(2)}) collective-permute-start(f32[64,256]{1,0:T(8,128)S(1)} %constant_dynamic-slice_fusion.13), channel_id=1, source_target_pairs={{0,8},{2,10},{4,12},{6,14},{8,0},{10,2},{12,4},{14,6},{1,9},{3,11}... | collective-permute-start | bytes 196616 | tf_op jit(solution)/shard_map/ppermute | solution.py:70
  63.7 3.9 %collective-permute-done.12 = f32[64,256]{1,0:T(8,128)S(1)} collective-permute-done((f32[64,256]{1,0:T(8,128)S(1)}, f32[64,256]{1,0:T(8,128)S(1)}, u32[]{:S(2)}, u32[]{:S(2)}) %collective-permute-start.12) | collective-permute-done | bytes 65568 | tf_op jit(solution)/shard_map/ppermute | solution.py:70
  67.7 1.4 %collective-permute-done.15 = f32[64,256]{1,0:T(8,128)S(1)} collective-permute-done((f32[64,256]{1,0:T(8,128)S(1)}, f32[64,256]{1,0:T(8,128)S(1)}, u32[]{:S(2)}, u32[]{:S(2)}) %collective-permute-start.15) | collective-permute-done | bytes 65568 | tf_op jit(solution)/shard_map/ppermute | solution.py:70
  71.1 2.9 %collective-permute-start.16 = (bf16[128,256]{1,0:T(8,128)(2,1)S(1)}, bf16[128,256]{1,0:T(8,128)(2,1)S(1)}, u32[]{:S(2)}, u32[]{:S(2)}) collective-permute-start(bf16[128,256]{1,0:T(8,128)(2,1)S(1)} %pad_maximum_fusion.6), channel_id=1, source_target_pairs={{0,8},{2,10},{4,12},{6,14},{8,0},{10,2},{12,4},{14,6},{1,9},{3,11}... | collective-permute-start | bytes 196616 | tf_op jit(solution)/shard_map/ppermute | solution.py:70
  74.0 3.0 %collective-permute-done.7 = bf16[128,256]{1,0:T(8,128)(2,1)S(1)} collective-permute-done((bf16[128,256]{1,0:T(8,128)(2,1)S(1)}, bf16[128,256]{1,0:T(8,128)(2,1)S(1)}, u32[]{:S(2)}, u32[]{:S(2)}) %collective-permute-start.7) | collective-permute-done | bytes 65568 | tf_op jit(solution)/shard_map/ppermute | solution.py:70
  77.1 1.4 %collective-permute-done.16 = bf16[128,256]{1,0:T(8,128)(2,1)S(1)} collective-permute-done((bf16[128,256]{1,0:T(8,128)(2,1)S(1)}, bf16[128,256]{1,0:T(8,128)(2,1)S(1)}, u32[]{:S(2)}, u32[]{:S(2)}) %collective-permute-start.16) | collective-permute-done | bytes 65568 | tf_op jit(solution)/shard_map/ppermute | solution.py:70
  78.6 1.7 %collective-permute-start.17 = (bf16[2,128,256]{2,1,0:T(8,128)(2,1)S(1)}, bf16[2,128,256]{2,1,0:T(8,128)(2,1)S(1)}, u32[]{:S(2)}, u32[]{:S(2)}) collective-permute-start(bf16[2,128,256]{2,1,0:T(8,128)(2,1)S(1)} %pad_maximum_fusion.4), channel_id=1, source_target_pairs={{0,2},{2,0},{4,6},{6,4},{8,10},{10,8},{12,14},{14,12},{1,3},{3,1},... | collective-permute-start | bytes 393224 | tf_op jit(solution)/shard_map/ppermute | solution.py:70
  80.3 1.8 %collective-permute-done.8 = bf16[2,128,256]{2,1,0:T(8,128)(2,1)S(1)} collective-permute-done((bf16[2,128,256]{2,1,0:T(8,128)(2,1)S(1)}, bf16[2,128,256]{2,1,0:T(8,128)(2,1)S(1)}, u32[]{:S(2)}, u32[]{:S(2)}) %collective-permute-start.8) | collective-permute-done | bytes 131104 | tf_op jit(solution)/shard_map/ppermute | solution.py:70
  82.1 1.6 %collective-permute-start.9 = (bf16[2,2,128,256]{3,2,1,0:T(8,128)(2,1)S(1)}, bf16[2,2,128,256]{3,2,1,0:T(8,128)(2,1)S(1)}, u32[]{:S(2)}, u32[]{:S(2)}) collective-permute-start(bf16[2,2,128,256]{3,2,1,0:T(8,128)(2,1)S(1)} %pad_maximum_fusion.1), channel_id=1, source_target_pairs={{0,2},{2,0},{4,6},{6,4},{8,10},{10,8},{12,14},{14,12},{1,3},{3,1},... | collective-permute-start | bytes 786440 | tf_op jit(solution)/shard_map/ppermute | solution.py:70
  85.6 3.7 %collective-permute-done.9 = bf16[2,2,128,256]{3,2,1,0:T(8,128)(2,1)S(1)} collective-permute-done((bf16[2,2,128,256]{3,2,1,0:T(8,128)(2,1)S(1)}, bf16[2,2,128,256]{3,2,1,0:T(8,128)(2,1)S(1)}, u32[]{:S(2)}, u32[]{:S(2)}) %collective-permute-start.9) | collective-permute-done | bytes 262176 | tf_op jit(solution)/shard_map/ppermute | solution.py:70
  93.4 28.0 %shard_map.130 = (bf16[2048,2048]{1,0:T(8,128)(2,1)}, bf16[2048,2048]{1,0:T(8,128)(2,1)}, bf16[2048,2048]{1,0:T(8,128)(2,1)}) custom-call(f32[2048,256]{1,0:T(8,128)} %copy-done, bf16[2048,256]{1,0:T(8,128)(2,1)} %bitcast.68, bf16[256,2048]{1,0:T(8,128)(2,1)} %copy-done.1, bf16[2048,2048]{1,0:T(8,128)(2,1)} %bitcast.62, bf16[2048,2048]{1,0:T(8,128)(2,1)} %bitcast.65, ...), custom_call_target="tpu_custom_call" | custom-call | tf_op jit(solution)/shard_map/pallas_call | solution.py:51
  (97 shorter events, 21.0 us)
Async XLA Ops:
  0.6 23.6 %copy-start.5 = (s32[8]{0:T(128)S(1)}, s32[8]{0:T(128)}, u32[]{:S(2)}) copy-start(s32[8]{0:T(128)} %constant.67) | copy-start | bytes 100
  0.6 23.6 %copy-start.4 = (s32[8]{0:T(128)S(1)}, s32[8]{0:T(128)}, u32[]{:S(2)}) copy-start(s32[8]{0:T(128)} %constant.68) | copy-start | bytes 100
  0.7 23.6 %copy-start.3 = (s32[1,256]{1,0:T(1,128)S(1)}, s32[1,256]{1,0:T(1,128)}, u32[]{:S(2)}) copy-start(s32[1,256]{1,0:T(1,128)} %param.12) | copy-start | bytes 3076
  2.3 21.7 %all-to-all-start = ((bf16[8,128,256]{2,1,0:T(8,128)(2,1)}), bf16[8,128,256]{2,1,0:T(8,128)(2,1)S(1)}, u32[]{:S(2)}, u32[]{:S(2)}) async-start(bf16[8,128,256]{2,1,0:T(8,128)(2,1)} %broadcast_in_dim.40), calls=%async_computation | async-start | bytes 1048576 | tf_op jit(solution)/shard_map/all_to_all | solution.py:173
  24.1 2.0 %collective-permute-start = (bf16[128,2048]{1,0:T(8,128)(2,1)S(1)}, bf16[128,2048]{1,0:T(8,128)(2,1)S(1)}, u32[]{:S(2)}, u32[]{:S(2)}) collective-permute-start(bf16[128,2048]{1,0:T(8,128)(2,1)S(1)} %bitcast.69), channel_id=1, source_target_pairs={{0,1},{1,0},{2,3},{3,2},{4,5},{5,4},{6,7},{7,6},{8,9},{9,8},{10,11... | collective-permute-start | bytes 1572872 | tf_op jit(solution)/shard_map/ppermute | solution.py:175
  27.7 7.2 %slice-start = ((s8[8388608]{0:T(1024)(128)(4,1)}), s8[4194304]{0:T(1024)(128)(4,1)S(1)}, s32[]{:S(2)}) async-start(s8[8388608]{0:T(1024)(128)(4,1)} %bitcast.63), calls=%async_computation.1 | async-start | bytes 8388608
  37.5 9.2 %collective-permute-start.10 = (f32[64,1024]{1,0:T(8,128)S(1)}, f32[64,1024]{1,0:T(8,128)S(1)}, u32[]{:S(2)}, u32[]{:S(2)}) collective-permute-start(f32[64,1024]{1,0:T(8,128)S(1)} %constant_dynamic-slice_fusion.5), channel_id=1, source_target_pairs={{0,4},{2,6},{4,0},{6,2},{8,12},{10,14},{12,8},{14,10},{1,5},{3,7},... | collective-permute-start | bytes 786440 | tf_op jit(solution)/shard_map/ppermute | solution.py:70
  38.3 13.2 %collective-permute-start.13 = (f32[64,1024]{1,0:T(8,128)S(1)}, f32[64,1024]{1,0:T(8,128)S(1)}, u32[]{:S(2)}, u32[]{:S(2)}) collective-permute-start(f32[64,1024]{1,0:T(8,128)S(1)} %constant_dynamic-slice_fusion), channel_id=1, source_target_pairs={{0,4},{2,6},{4,0},{6,2},{8,12},{10,14},{12,8},{14,10},{1,5},{3,7},... | collective-permute-start | bytes 786440 | tf_op jit(solution)/shard_map/ppermute | solution.py:70
  39.7 13.4 %collective-permute-start.4 = (f32[64,1024]{1,0:T(8,128)S(1)}, f32[64,1024]{1,0:T(8,128)S(1)}, u32[]{:S(2)}, u32[]{:S(2)}) collective-permute-start(f32[64,1024]{1,0:T(8,128)S(1)} %constant_dynamic-slice_fusion.10), channel_id=1, source_target_pairs={{0,2},{2,0},{4,6},{6,4},{8,10},{10,8},{12,14},{14,12},{1,3},{3,1},... | collective-permute-start | bytes 786440 | tf_op jit(solution)/shard_map/ppermute | solution.py:70
  41.2 13.4 %collective-permute-start.1 = (f32[64,1024]{1,0:T(8,128)S(1)}, f32[64,1024]{1,0:T(8,128)S(1)}, u32[]{:S(2)}, u32[]{:S(2)}) collective-permute-start(f32[64,1024]{1,0:T(8,128)S(1)} %constant_dynamic-slice_fusion.15), channel_id=1, source_target_pairs={{0,2},{2,0},{4,6},{6,4},{8,10},{10,8},{12,14},{14,12},{1,3},{3,1},... | collective-permute-start | bytes 786440 | tf_op jit(solution)/shard_map/ppermute | solution.py:70
  46.8 10.6 %collective-permute-start.11 = (f32[64,512]{1,0:T(8,128)S(1)}, f32[64,512]{1,0:T(8,128)S(1)}, u32[]{:S(2)}, u32[]{:S(2)}) collective-permute-start(f32[64,512]{1,0:T(8,128)S(1)} %constant_dynamic-slice_fusion.4), channel_id=1, source_target_pairs={{0,2},{2,0},{4,6},{6,4},{8,10},{10,8},{12,14},{14,12},{1,3},{3,1},... | collective-permute-start | bytes 393224 | tf_op jit(solution)/shard_map/ppermute | solution.py:70
  51.6 7.2 %collective-permute-start.14 = (f32[64,512]{1,0:T(8,128)S(1)}, f32[64,512]{1,0:T(8,128)S(1)}, u32[]{:S(2)}, u32[]{:S(2)}) collective-permute-start(f32[64,512]{1,0:T(8,128)S(1)} %constant_dynamic-slice_fusion.7), channel_id=1, source_target_pairs={{0,2},{2,0},{4,6},{6,4},{8,10},{10,8},{12,14},{14,12},{1,3},{3,1},... | collective-permute-start | bytes 393224 | tf_op jit(solution)/shard_map/ppermute | solution.py:70
  53.2 7.3 %collective-permute-start.5 = (f32[64,512]{1,0:T(8,128)S(1)}, f32[64,512]{1,0:T(8,128)S(1)}, u32[]{:S(2)}, u32[]{:S(2)}) collective-permute-start(f32[64,512]{1,0:T(8,128)S(1)} %constant_dynamic-slice_fusion.9), channel_id=1, source_target_pairs={{0,4},{2,6},{4,0},{6,2},{8,12},{10,14},{12,8},{14,10},{1,5},{3,7},... | collective-permute-start | bytes 393224 | tf_op jit(solution)/shard_map/ppermute | solution.py:70
  54.7 7.3 %collective-permute-start.2 = (f32[64,512]{1,0:T(8,128)S(1)}, f32[64,512]{1,0:T(8,128)S(1)}, u32[]{:S(2)}, u32[]{:S(2)}) collective-permute-start(f32[64,512]{1,0:T(8,128)S(1)} %constant_dynamic-slice_fusion.14), channel_id=1, source_target_pairs={{0,4},{2,6},{4,0},{6,2},{8,12},{10,14},{12,8},{14,10},{1,5},{3,7},... | collective-permute-start | bytes 393224 | tf_op jit(solution)/shard_map/ppermute | solution.py:70
  57.4 10.3 %collective-permute-start.12 = (f32[64,256]{1,0:T(8,128)S(1)}, f32[64,256]{1,0:T(8,128)S(1)}, u32[]{:S(2)}, u32[]{:S(2)}) collective-permute-start(f32[64,256]{1,0:T(8,128)S(1)} %constant_dynamic-slice_fusion.3), channel_id=1, source_target_pairs={{0,8},{2,10},{4,12},{6,14},{8,0},{10,2},{12,4},{14,6},{1,9},{3,11}... | collective-permute-start | bytes 196616 | tf_op jit(solution)/shard_map/ppermute | solution.py:70
  58.8 10.3 %collective-permute-start.15 = (f32[64,256]{1,0:T(8,128)S(1)}, f32[64,256]{1,0:T(8,128)S(1)}, u32[]{:S(2)}, u32[]{:S(2)}) collective-permute-start(f32[64,256]{1,0:T(8,128)S(1)} %constant_dynamic-slice_fusion.6), channel_id=1, source_target_pairs={{0,8},{2,10},{4,12},{6,14},{8,0},{10,2},{12,4},{14,6},{1,9},{3,11}... | collective-permute-start | bytes 196616 | tf_op jit(solution)/shard_map/ppermute | solution.py:70
  60.6 9.6 %collective-permute-start.6 = (f32[64,256]{1,0:T(8,128)S(1)}, f32[64,256]{1,0:T(8,128)S(1)}, u32[]{:S(2)}, u32[]{:S(2)}) collective-permute-start(f32[64,256]{1,0:T(8,128)S(1)} %constant_dynamic-slice_fusion.8), channel_id=1, source_target_pairs={{0,8},{2,10},{4,12},{6,14},{8,0},{10,2},{12,4},{14,6},{1,9},{3,11}... | collective-permute-start | bytes 196616 | tf_op jit(solution)/shard_map/ppermute | solution.py:70
  62.0 8.9 %collective-permute-start.3 = (f32[64,256]{1,0:T(8,128)S(1)}, f32[64,256]{1,0:T(8,128)S(1)}, u32[]{:S(2)}, u32[]{:S(2)}) collective-permute-start(f32[64,256]{1,0:T(8,128)S(1)} %constant_dynamic-slice_fusion.13), channel_id=1, source_target_pairs={{0,8},{2,10},{4,12},{6,14},{8,0},{10,2},{12,4},{14,6},{1,9},{3,11}... | collective-permute-start | bytes 196616 | tf_op jit(solution)/shard_map/ppermute | solution.py:70
  71.0 6.0 %collective-permute-start.7 = (bf16[128,256]{1,0:T(8,128)(2,1)S(1)}, bf16[128,256]{1,0:T(8,128)(2,1)S(1)}, u32[]{:S(2)}, u32[]{:S(2)}) collective-permute-start(bf16[128,256]{1,0:T(8,128)(2,1)S(1)} %pad_maximum_fusion.5), channel_id=1, source_target_pairs={{0,8},{2,10},{4,12},{6,14},{8,0},{10,2},{12,4},{14,6},{1,9},{3,11}... | collective-permute-start | bytes 196616 | tf_op jit(solution)/shard_map/ppermute | solution.py:70
  71.1 7.5 %collective-permute-start.16 = (bf16[128,256]{1,0:T(8,128)(2,1)S(1)}, bf16[128,256]{1,0:T(8,128)(2,1)S(1)}, u32[]{:S(2)}, u32[]{:S(2)}) collective-permute-start(bf16[128,256]{1,0:T(8,128)(2,1)S(1)} %pad_maximum_fusion.6), channel_id=1, source_target_pairs={{0,8},{2,10},{4,12},{6,14},{8,0},{10,2},{12,4},{14,6},{1,9},{3,11}... | collective-permute-start | bytes 196616 | tf_op jit(solution)/shard_map/ppermute | solution.py:70
  77.0 5.0 %collective-permute-start.8 = (bf16[2,128,256]{2,1,0:T(8,128)(2,1)S(1)}, bf16[2,128,256]{2,1,0:T(8,128)(2,1)S(1)}, u32[]{:S(2)}, u32[]{:S(2)}) collective-permute-start(bf16[2,128,256]{2,1,0:T(8,128)(2,1)S(1)} %pad_maximum_fusion.3), channel_id=1, source_target_pairs={{0,4},{2,6},{4,0},{6,2},{8,12},{10,14},{12,8},{14,10},{1,5},{3,7},... | collective-permute-start | bytes 393224 | tf_op jit(solution)/shard_map/ppermute | solution.py:70
  78.6 6.1 %collective-permute-start.17 = (bf16[2,128,256]{2,1,0:T(8,128)(2,1)S(1)}, bf16[2,128,256]{2,1,0:T(8,128)(2,1)S(1)}, u32[]{:S(2)}, u32[]{:S(2)}) collective-permute-start(bf16[2,128,256]{2,1,0:T(8,128)(2,1)S(1)} %pad_maximum_fusion.4), channel_id=1, source_target_pairs={{0,2},{2,0},{4,6},{6,4},{8,10},{10,8},{12,14},{14,12},{1,3},{3,1},... | collective-permute-start | bytes 393224 | tf_op jit(solution)/shard_map/ppermute | solution.py:70
  82.1 7.1 %collective-permute-start.9 = (bf16[2,2,128,256]{3,2,1,0:T(8,128)(2,1)S(1)}, bf16[2,2,128,256]{3,2,1,0:T(8,128)(2,1)S(1)}, u32[]{:S(2)}, u32[]{:S(2)}) collective-permute-start(bf16[2,2,128,256]{3,2,1,0:T(8,128)(2,1)S(1)} %pad_maximum_fusion.1), channel_id=1, source_target_pairs={{0,2},{2,0},{4,6},{6,4},{8,10},{10,8},{12,14},{14,12},{1,3},{3,1},... | collective-permute-start | bytes 786440 | tf_op jit(solution)/shard_map/ppermute | solution.py:70
  84.8 6.4 %collective-permute-start.18 = (bf16[2,2,128,256]{3,2,1,0:T(8,128)(2,1)S(1)}, bf16[2,2,128,256]{3,2,1,0:T(8,128)(2,1)S(1)}, u32[]{:S(2)}, u32[]{:S(2)}) collective-permute-start(bf16[2,2,128,256]{3,2,1,0:T(8,128)(2,1)S(1)} %pad_maximum_fusion.2), channel_id=1, source_target_pairs={{0,4},{2,6},{4,0},{6,2},{8,12},{10,14},{12,8},{14,10},{1,5},{3,7},... | collective-permute-start | bytes 786440 | tf_op jit(solution)/shard_map/ppermute | solution.py:70
  (5 other events, 17.8 us)

commit v17 on v15

--- a/solution.py
+++ b/solution.py
@@ -24,7 +24,7 @@
     back_t = jnp.dot(dec, err_ref[...], preferred_element_type=jnp.float32)
     tokens = err_ref.shape[1]
     d_pre = (
-        jnp.where(pre_ref[...] > 0, 2.0 * back_t + sparsity * row_norm, 0.0) / tokens
+        jnp.where(pre_ref[...].astype(jnp.float32) > 0, 2.0 * back_t + sparsity * row_norm, 0.0) / tokens
     ).astype(jnp.bfloat16)
     grad = jnp.dot(d_pre, cen_ref[...], preferred_element_type=jnp.float32)
     moment_one = beta_one * m1_ref[...].astype(jnp.float32) + (1.0 - beta_one) * grad
@@ -212,7 +212,7 @@
     error_blocks = jnp.concatenate(error_parts, axis=1)
     error = jnp.transpose(error_blocks, (1, 0, 2)).reshape(error_blocks.shape[1], -1)
     updated, moment_one, moment_two = tail(
-        pre_t, error, centered, decoder, weight_in, first_moment[0], second_moment[0]
+        latent_t, error, centered, decoder, weight_in, first_moment[0], second_moment[0]
     )
     return updated[None], moment_one[None], moment_two[None]
 

time: 121 us -> 120 us (level)
  no operation moved by 1% of the time
where the time goes in v17:
time: 120 us
  waiting for transfers between devices  38.6 us (32%)
  starting transfers between devices  33.5 us (28%)
  Pallas kernels  27.7 us (23%)
  matrix products  8.84 us (7%)
  local copies, waits for them, and re-layouts  7.57 us (6%)
  other arithmetic  2.66 us (2%)
  between operations  1.24 us (1%)
    pallas_call x1, Pallas kernels, tail(): pl.pallas_call(_tail_kernel, grid=(n_lat // tile,), in_specs=[pl.BlockSpe...  27.7 us
    ppermute x24, starting transfers between devices, _pair_swap(): return lax.ppermute(value, axis, [(i, i ^ mask) for i in range(size)])  26.2 us
    ppermute x24, waiting for transfers between devices, _pair_swap(): return lax.ppermute(value, axis, [(i, i ^ mask) for i in range(size)])  23.7 us
    all_to_all x1, waiting for transfers between devices, local(): act_blocks = lax.all_to_all(copies, 'lat', 0, 0, tiled=True)  13.1 us
    all_to_all x1, starting transfers between devices, local(): act_blocks = lax.all_to_all(copies, 'lat', 0, 0, tiled=True)  7.25 us
    dot_general x1, matrix products, local(): lax.dot_general(weight_in, centered, (((1,), (1,)), ((), ())), preferred_...  6.5 us
  transfers between devices with their start and end apart: 26, of which 16 were waited for; matrix products, arithmetic and copies ran while one was open for 3% of the time, Pallas kernels for 0%

profile of v17, /device:TPU:0, one launch (start us, length us, event | category | flops | bytes accessed | tf_op | source)
XLA Modules:
  0.0 120.1 jit_solution(6925805645984097201)
XLA Ops:
  0.7 1.7 %broadcast_in_dim.46 = bf16[8,128,256]{2,1,0:T(8,128)(2,1)} broadcast(bf16[128,256]{1,0:T(8,128)(2,1)} %param.13), dimensions={1,2} | broadcast | bytes 589824 | tf_op jit(solution)/shard_map/broadcast_in_dim | solution.py:172
  2.4 7.3 %all-to-all-start = ((bf16[8,128,256]{2,1,0:T(8,128)(2,1)}), bf16[8,128,256]{2,1,0:T(8,128)(2,1)S(1)}, u32[]{:S(2)}, u32[]{:S(2)}) async-start(bf16[8,128,256]{2,1,0:T(8,128)(2,1)} %broadcast_in_dim.46), calls=%async_computation | async-start | bytes 1048576 | tf_op jit(solution)/shard_map/all_to_all | solution.py:173
  11.0 13.1 %all-to-all-done = bf16[8,128,256]{2,1,0:T(8,128)(2,1)S(1)} async-done(((bf16[8,128,256]{2,1,0:T(8,128)(2,1)}), bf16[8,128,256]{2,1,0:T(8,128)(2,1)S(1)}, u32[]{:S(2)}, u32[]{:S(2)}) %all-to-all-start) | async-done | bytes 524320 | tf_op jit(solution)/shard_map/all_to_all | solution.py:173
  24.3 1.8 %collective-permute-done = bf16[128,2048]{1,0:T(8,128)(2,1)S(1)} collective-permute-done((bf16[128,2048]{1,0:T(8,128)(2,1)S(1)}, bf16[128,2048]{1,0:T(8,128)(2,1)S(1)}, u32[]{:S(2)}, u32[]{:S(2)}) %collective-permute-start) | collective-permute-done | bytes 524320 | tf_op jit(solution)/shard_map/ppermute | solution.py:175
  26.3 1.4 %gather_fusion = bf16[256,2048]{1,0:T(8,128)(2,1)S(1)} fusion(bf16[256,2048]{1,0:T(8,128)(2,1)S(1)} %pad_maximum_fusion, s32[1024]{0:T(1024)S(1)} %pad_clamp_fusion.2), kind=kCustom, calls=%fused_computation | custom fusion | bytes 2098176 | tf_op jit(solution)/shard_map/jit(_take)/gather | solution.py:182
  28.4 6.5 %fusion.1 = bf16[256,2048]{0,1:T(8,128)(2,1)S(1)} fusion(bf16[256,2048]{1,0:T(8,128)(2,1)S(1)} %get-tuple-element.9.cen_ref, f32[2048]{0:T(1024)S(1)} %bitcast.117, bf16[1,2048,2048]{2,1,0:T(8,128)(2,1)} %param.16), kind=kOutput, calls=%fused_computation.7 | convolution fusion | flops 2149056512 | bytes 10493952 | tf_op jit(solution)/shard_map/dot_general | solution.py:188
  34.9 2.3 %fusion.2 = f32[256,2048]{1,0:T(8,128)S(1)} fusion(bf16[256,2048]{0,1:T(8,128)(2,1)S(1)} %fusion.1, bf16[1,2048,2048]{2,1,0:T(8,128)(2,1)S(1)} %bitcast.94), kind=kOutput, calls=%fused_computation.84 | convolution fusion | flops 2147483648 | bytes 11534336 | tf_op jit(solution)/shard_map/dot_general | solution.py:194
  39.6 1.5 %collective-permute-start.13 = (f32[64,1024]{1,0:T(8,128)S(1)}, f32[64,1024]{1,0:T(8,128)S(1)}, u32[]{:S(2)}, u32[]{:S(2)}) collective-permute-start(f32[64,1024]{1,0:T(8,128)S(1)} %constant_dynamic-slice_fusion.3), channel_id=1, source_target_pairs={{0,2},{2,0},{4,6},{6,4},{8,10},{10,8},{12,14},{14,12},{1,3},{3,1},... | collective-permute-start | bytes 786440 | tf_op jit(solution)/shard_map/ppermute | solution.py:70
  41.8 5.0 %collective-permute-done.7 = f32[64,1024]{1,0:T(8,128)S(1)} collective-permute-done((f32[64,1024]{1,0:T(8,128)S(1)}, f32[64,1024]{1,0:T(8,128)S(1)}, u32[]{:S(2)}, u32[]{:S(2)}) %collective-permute-start.7) | collective-permute-done | bytes 262176 | tf_op jit(solution)/shard_map/ppermute | solution.py:70
  46.8 1.5 %collective-permute-start.8 = (f32[64,512]{1,0:T(8,128)S(1)}, f32[64,512]{1,0:T(8,128)S(1)}, u32[]{:S(2)}, u32[]{:S(2)}) collective-permute-start(f32[64,512]{1,0:T(8,128)S(1)} %constant_dynamic-slice_fusion.8), channel_id=1, source_target_pairs={{0,2},{2,0},{4,6},{6,4},{8,10},{10,8},{12,14},{14,12},{1,3},{3,1},... | collective-permute-start | bytes 393224 | tf_op jit(solution)/shard_map/ppermute | solution.py:70
  48.4 3.2 %collective-permute-done.19 = f32[64,1024]{1,0:T(8,128)S(1)} collective-permute-done((f32[64,1024]{1,0:T(8,128)S(1)}, f32[64,1024]{1,0:T(8,128)S(1)}, u32[]{:S(2)}, u32[]{:S(2)}) %collective-permute-start.19) | collective-permute-done | bytes 262176 | tf_op jit(solution)/shard_map/ppermute | solution.py:70
  51.6 1.5 %collective-permute-start.20 = (f32[64,512]{1,0:T(8,128)S(1)}, f32[64,512]{1,0:T(8,128)S(1)}, u32[]{:S(2)}, u32[]{:S(2)}) collective-permute-start(f32[64,512]{1,0:T(8,128)S(1)} %constant_dynamic-slice_fusion.5), channel_id=1, source_target_pairs={{0,2},{2,0},{4,6},{6,4},{8,10},{10,8},{12,14},{14,12},{1,3},{3,1},... | collective-permute-start | bytes 393224 | tf_op jit(solution)/shard_map/ppermute | solution.py:70
  55.5 1.8 %collective-permute-done.8 = f32[64,512]{1,0:T(8,128)S(1)} collective-permute-done((f32[64,512]{1,0:T(8,128)S(1)}, f32[64,512]{1,0:T(8,128)S(1)}, u32[]{:S(2)}, u32[]{:S(2)}) %collective-permute-start.8) | collective-permute-done | bytes 131104 | tf_op jit(solution)/shard_map/ppermute | solution.py:70
  58.7 1.7 %collective-permute-start.21 = (f32[64,256]{1,0:T(8,128)S(1)}, f32[64,256]{1,0:T(8,128)S(1)}, u32[]{:S(2)}, u32[]{:S(2)}) collective-permute-start(f32[64,256]{1,0:T(8,128)S(1)} %constant_dynamic-slice_fusion.10), channel_id=1, source_target_pairs={{0,8},{2,10},{4,12},{6,14},{8,0},{10,2},{12,4},{14,6},{1,9},{3,11}... | collective-permute-start | bytes 196616 | tf_op jit(solution)/shard_map/ppermute | solution.py:70
  61.9 1.7 %collective-permute-start.3 = (f32[64,256]{1,0:T(8,128)S(1)}, f32[64,256]{1,0:T(8,128)S(1)}, u32[]{:S(2)}, u32[]{:S(2)}) collective-permute-start(f32[64,256]{1,0:T(8,128)S(1)} %constant_dynamic-slice_fusion.13), channel_id=1, source_target_pairs={{0,8},{2,10},{4,12},{6,14},{8,0},{10,2},{12,4},{14,6},{1,9},{3,11}... | collective-permute-start | bytes 196616 | tf_op jit(solution)/shard_map/ppermute | solution.py:70
  63.6 4.8 %collective-permute-done.9 = f32[64,256]{1,0:T(8,128)S(1)} collective-permute-done((f32[64,256]{1,0:T(8,128)S(1)}, f32[64,256]{1,0:T(8,128)S(1)}, u32[]{:S(2)}, u32[]{:S(2)}) %collective-permute-start.9) | collective-permute-done | bytes 65568 | tf_op jit(solution)/shard_map/ppermute | solution.py:70
  68.4 1.4 %collective-permute-done.21 = f32[64,256]{1,0:T(8,128)S(1)} collective-permute-done((f32[64,256]{1,0:T(8,128)S(1)}, f32[64,256]{1,0:T(8,128)S(1)}, u32[]{:S(2)}, u32[]{:S(2)}) %collective-permute-start.21) | collective-permute-done | bytes 65568 | tf_op jit(solution)/shard_map/ppermute | solution.py:70
  69.9 2.9 %collective-permute-start.22 = (bf16[64,256]{1,0:T(8,128)(2,1)S(1)}, bf16[64,256]{1,0:T(8,128)(2,1)S(1)}, u32[]{:S(2)}, u32[]{:S(2)}) collective-permute-start(bf16[64,256]{1,0:T(8,128)(2,1)S(1)} %get-tuple-element.52), channel_id=1, source_target_pairs={{0,8},{2,10},{4,12},{6,14},{8,0},{10,2},{12,4},{14,6},{1,9},{3,11}... | collective-permute-start | bytes 98312 | tf_op jit(solution)/shard_map/ppermute | solution.py:70
  73.0 2.8 %collective-permute-start.16 = (bf16[64,256]{1,0:T(8,128)(2,1)S(1)}, bf16[64,256]{1,0:T(8,128)(2,1)S(1)}, u32[]{:S(2)}, u32[]{:S(2)}) collective-permute-start(bf16[64,256]{1,0:T(8,128)(2,1)S(1)} %get-tuple-element.50), channel_id=1, source_target_pairs={{0,8},{2,10},{4,12},{6,14},{8,0},{10,2},{12,4},{14,6},{1,9},{3,11}... | collective-permute-start | bytes 98312 | tf_op jit(solution)/shard_map/ppermute | solution.py:70
  78.5 2.1 %collective-permute-start.17 = (bf16[2,64,256]{2,1,0:T(8,128)(2,1)S(1)}, bf16[2,64,256]{2,1,0:T(8,128)(2,1)S(1)}, u32[]{:S(2)}, u32[]{:S(2)}) collective-permute-start(bf16[2,64,256]{2,1,0:T(8,128)(2,1)S(1)} %pad_maximum_fusion.7), channel_id=1, source_target_pairs={{0,4},{2,6},{4,0},{6,2},{8,12},{10,14},{12,8},{14,10},{1,5},{3,7},... | collective-permute-start | bytes 196616 | tf_op jit(solution)/shard_map/ppermute | solution.py:70
  80.7 1.8 %collective-permute-done.23 = bf16[2,64,256]{2,1,0:T(8,128)(2,1)S(1)} collective-permute-done((bf16[2,64,256]{2,1,0:T(8,128)(2,1)S(1)}, bf16[2,64,256]{2,1,0:T(8,128)(2,1)S(1)}, u32[]{:S(2)}, u32[]{:S(2)}) %collective-permute-start.23) | collective-permute-done | bytes 65568 | tf_op jit(solution)/shard_map/ppermute | solution.py:70
  83.2 1.5 %collective-permute-start.6 = (bf16[2,2,64,256]{3,2,1,0:T(8,128)(2,1)S(1)}, bf16[2,2,64,256]{3,2,1,0:T(8,128)(2,1)S(1)}, u32[]{:S(2)}, u32[]{:S(2)}) collective-permute-start(bf16[2,2,64,256]{3,2,1,0:T(8,128)(2,1)S(1)} %pad_maximum_fusion.1), channel_id=1, source_target_pairs={{0,2},{2,0},{4,6},{6,4},{8,10},{10,8},{12,14},{14,12},{1,3},{3,1},... | collective-permute-start | bytes 393224 | tf_op jit(solution)/shard_map/ppermute | solution.py:70
  85.7 1.9 %collective-permute-done.24 = bf16[2,2,64,256]{3,2,1,0:T(8,128)(2,1)S(1)} collective-permute-done((bf16[2,2,64,256]{3,2,1,0:T(8,128)(2,1)S(1)}, bf16[2,2,64,256]{3,2,1,0:T(8,128)(2,1)S(1)}, u32[]{:S(2)}, u32[]{:S(2)}) %collective-permute-start.24) | collective-permute-done | bytes 131104 | tf_op jit(solution)/shard_map/ppermute | solution.py:70
  92.4 27.7 %shard_map.148 = (bf16[2048,2048]{1,0:T(8,128)(2,1)}, bf16[2048,2048]{1,0:T(8,128)(2,1)}, bf16[2048,2048]{1,0:T(8,128)(2,1)}) custom-call(bf16[2048,256]{1,0:T(8,128)(2,1)} %bitcast.98, bf16[2048,256]{1,0:T(8,128)(2,1)} %bitcast.99, bf16[256,2048]{1,0:T(8,128)(2,1)} %copy-done.1, bf16[2048,2048]{1,0:T(8,128)(2,1)} %bitcast.92, bf16[2048,2048]{1,0:T(8,128)(2,1)} %bitcast.95, ...), custom_call_target="tpu_custom_call" | custom-call | tf_op jit(solution)/shard_map/pallas_call | solution.py:51
  (121 shorter events, 20.0 us)
Async XLA Ops:
  2.4 21.7 %all-to-all-start = ((bf16[8,128,256]{2,1,0:T(8,128)(2,1)}), bf16[8,128,256]{2,1,0:T(8,128)(2,1)S(1)}, u32[]{:S(2)}, u32[]{:S(2)}) async-start(bf16[8,128,256]{2,1,0:T(8,128)(2,1)} %broadcast_in_dim.46), calls=%async_computation | async-start | bytes 1048576 | tf_op jit(solution)/shard_map/all_to_all | solution.py:173
  37.6 9.2 %collective-permute-start.7 = (f32[64,1024]{1,0:T(8,128)S(1)}, f32[64,1024]{1,0:T(8,128)S(1)}, u32[]{:S(2)}, u32[]{:S(2)}) collective-permute-start(f32[64,1024]{1,0:T(8,128)S(1)} %constant_dynamic-slice_fusion.9), channel_id=1, source_target_pairs={{0,4},{2,6},{4,0},{6,2},{8,12},{10,14},{12,8},{14,10},{1,5},{3,7},... | collective-permute-start | bytes 786440 | tf_op jit(solution)/shard_map/ppermute | solution.py:70
  38.4 13.2 %collective-permute-start.19 = (f32[64,1024]{1,0:T(8,128)S(1)}, f32[64,1024]{1,0:T(8,128)S(1)}, u32[]{:S(2)}, u32[]{:S(2)}) collective-permute-start(f32[64,1024]{1,0:T(8,128)S(1)} %constant_dynamic-slice_fusion), channel_id=1, source_target_pairs={{0,4},{2,6},{4,0},{6,2},{8,12},{10,14},{12,8},{14,10},{1,5},{3,7},... | collective-permute-start | bytes 786440 | tf_op jit(solution)/shard_map/ppermute | solution.py:70
  39.6 13.5 %collective-permute-start.13 = (f32[64,1024]{1,0:T(8,128)S(1)}, f32[64,1024]{1,0:T(8,128)S(1)}, u32[]{:S(2)}, u32[]{:S(2)}) collective-permute-start(f32[64,1024]{1,0:T(8,128)S(1)} %constant_dynamic-slice_fusion.3), channel_id=1, source_target_pairs={{0,2},{2,0},{4,6},{6,4},{8,10},{10,8},{12,14},{14,12},{1,3},{3,1},... | collective-permute-start | bytes 786440 | tf_op jit(solution)/shard_map/ppermute | solution.py:70
  41.1 13.4 %collective-permute-start.1 = (f32[64,1024]{1,0:T(8,128)S(1)}, f32[64,1024]{1,0:T(8,128)S(1)}, u32[]{:S(2)}, u32[]{:S(2)}) collective-permute-start(f32[64,1024]{1,0:T(8,128)S(1)} %constant_dynamic-slice_fusion.15), channel_id=1, source_target_pairs={{0,2},{2,0},{4,6},{6,4},{8,10},{10,8},{12,14},{14,12},{1,3},{3,1},... | collective-permute-start | bytes 786440 | tf_op jit(solution)/shard_map/ppermute | solution.py:70
  46.8 10.4 %collective-permute-start.8 = (f32[64,512]{1,0:T(8,128)S(1)}, f32[64,512]{1,0:T(8,128)S(1)}, u32[]{:S(2)}, u32[]{:S(2)}) collective-permute-start(f32[64,512]{1,0:T(8,128)S(1)} %constant_dynamic-slice_fusion.8), channel_id=1, source_target_pairs={{0,2},{2,0},{4,6},{6,4},{8,10},{10,8},{12,14},{14,12},{1,3},{3,1},... | collective-permute-start | bytes 393224 | tf_op jit(solution)/shard_map/ppermute | solution.py:70
  51.6 7.0 %collective-permute-start.20 = (f32[64,512]{1,0:T(8,128)S(1)}, f32[64,512]{1,0:T(8,128)S(1)}, u32[]{:S(2)}, u32[]{:S(2)}) collective-permute-start(f32[64,512]{1,0:T(8,128)S(1)} %constant_dynamic-slice_fusion.5), channel_id=1, source_target_pairs={{0,2},{2,0},{4,6},{6,4},{8,10},{10,8},{12,14},{14,12},{1,3},{3,1},... | collective-permute-start | bytes 393224 | tf_op jit(solution)/shard_map/ppermute | solution.py:70
  53.2 7.2 %collective-permute-start.14 = (f32[64,512]{1,0:T(8,128)S(1)}, f32[64,512]{1,0:T(8,128)S(1)}, u32[]{:S(2)}, u32[]{:S(2)}) collective-permute-start(f32[64,512]{1,0:T(8,128)S(1)} %constant_dynamic-slice_fusion.2), channel_id=1, source_target_pairs={{0,4},{2,6},{4,0},{6,2},{8,12},{10,14},{12,8},{14,10},{1,5},{3,7},... | collective-permute-start | bytes 393224 | tf_op jit(solution)/shard_map/ppermute | solution.py:70
  54.6 7.3 %collective-permute-start.2 = (f32[64,512]{1,0:T(8,128)S(1)}, f32[64,512]{1,0:T(8,128)S(1)}, u32[]{:S(2)}, u32[]{:S(2)}) collective-permute-start(f32[64,512]{1,0:T(8,128)S(1)} %constant_dynamic-slice_fusion.14), channel_id=1, source_target_pairs={{0,4},{2,6},{4,0},{6,2},{8,12},{10,14},{12,8},{14,10},{1,5},{3,7},... | collective-permute-start | bytes 393224 | tf_op jit(solution)/shard_map/ppermute | solution.py:70
  57.3 11.1 %collective-permute-start.9 = (f32[64,256]{1,0:T(8,128)S(1)}, f32[64,256]{1,0:T(8,128)S(1)}, u32[]{:S(2)}, u32[]{:S(2)}) collective-permute-start(f32[64,256]{1,0:T(8,128)S(1)} %constant_dynamic-slice_fusion.7), channel_id=1, source_target_pairs={{0,8},{2,10},{4,12},{6,14},{8,0},{10,2},{12,4},{14,6},{1,9},{3,11}... | collective-permute-start | bytes 196616 | tf_op jit(solution)/shard_map/ppermute | solution.py:70
  58.7 11.1 %collective-permute-start.21 = (f32[64,256]{1,0:T(8,128)S(1)}, f32[64,256]{1,0:T(8,128)S(1)}, u32[]{:S(2)}, u32[]{:S(2)}) collective-permute-start(f32[64,256]{1,0:T(8,128)S(1)} %constant_dynamic-slice_fusion.10), channel_id=1, source_target_pairs={{0,8},{2,10},{4,12},{6,14},{8,0},{10,2},{12,4},{14,6},{1,9},{3,11}... | collective-permute-start | bytes 196616 | tf_op jit(solution)/shard_map/ppermute | solution.py:70
  60.5 12.4 %collective-permute-start.15 = (f32[64,256]{1,0:T(8,128)S(1)}, f32[64,256]{1,0:T(8,128)S(1)}, u32[]{:S(2)}, u32[]{:S(2)}) collective-permute-start(f32[64,256]{1,0:T(8,128)S(1)} %constant_dynamic-slice_fusion.1), channel_id=1, source_target_pairs={{0,8},{2,10},{4,12},{6,14},{8,0},{10,2},{12,4},{14,6},{1,9},{3,11}... | collective-permute-start | bytes 196616 | tf_op jit(solution)/shard_map/ppermute | solution.py:70
  61.9 11.0 %collective-permute-start.3 = (f32[64,256]{1,0:T(8,128)S(1)}, f32[64,256]{1,0:T(8,128)S(1)}, u32[]{:S(2)}, u32[]{:S(2)}) collective-permute-start(f32[64,256]{1,0:T(8,128)S(1)} %constant_dynamic-slice_fusion.13), channel_id=1, source_target_pairs={{0,8},{2,10},{4,12},{6,14},{8,0},{10,2},{12,4},{14,6},{1,9},{3,11}... | collective-permute-start | bytes 196616 | tf_op jit(solution)/shard_map/ppermute | solution.py:70
  69.8 6.3 %collective-permute-start.10 = (bf16[64,256]{1,0:T(8,128)(2,1)S(1)}, bf16[64,256]{1,0:T(8,128)(2,1)S(1)}, u32[]{:S(2)}, u32[]{:S(2)}) collective-permute-start(bf16[64,256]{1,0:T(8,128)(2,1)S(1)} %get-tuple-element.51), channel_id=1, source_target_pairs={{0,8},{2,10},{4,12},{6,14},{8,0},{10,2},{12,4},{14,6},{1,9},{3,11}... | collective-permute-start | bytes 98312 | tf_op jit(solution)/shard_map/ppermute | solution.py:70
  69.9 7.5 %collective-permute-start.22 = (bf16[64,256]{1,0:T(8,128)(2,1)S(1)}, bf16[64,256]{1,0:T(8,128)(2,1)S(1)}, u32[]{:S(2)}, u32[]{:S(2)}) collective-permute-start(bf16[64,256]{1,0:T(8,128)(2,1)S(1)} %get-tuple-element.52), channel_id=1, source_target_pairs={{0,8},{2,10},{4,12},{6,14},{8,0},{10,2},{12,4},{14,6},{1,9},{3,11}... | collective-permute-start | bytes 98312 | tf_op jit(solution)/shard_map/ppermute | solution.py:70
  72.9 5.5 %collective-permute-start.4 = (bf16[64,256]{1,0:T(8,128)(2,1)S(1)}, bf16[64,256]{1,0:T(8,128)(2,1)S(1)}, u32[]{:S(2)}, u32[]{:S(2)}) collective-permute-start(bf16[64,256]{1,0:T(8,128)(2,1)S(1)} %get-tuple-element.49), channel_id=1, source_target_pairs={{0,8},{2,10},{4,12},{6,14},{8,0},{10,2},{12,4},{14,6},{1,9},{3,11}... | collective-permute-start | bytes 98312 | tf_op jit(solution)/shard_map/ppermute | solution.py:70
  73.0 5.4 %collective-permute-start.16 = (bf16[64,256]{1,0:T(8,128)(2,1)S(1)}, bf16[64,256]{1,0:T(8,128)(2,1)S(1)}, u32[]{:S(2)}, u32[]{:S(2)}) collective-permute-start(bf16[64,256]{1,0:T(8,128)(2,1)S(1)} %get-tuple-element.50), channel_id=1, source_target_pairs={{0,8},{2,10},{4,12},{6,14},{8,0},{10,2},{12,4},{14,6},{1,9},{3,11}... | collective-permute-start | bytes 98312 | tf_op jit(solution)/shard_map/ppermute | solution.py:70
  77.5 5.0 %collective-permute-start.23 = (bf16[2,64,256]{2,1,0:T(8,128)(2,1)S(1)}, bf16[2,64,256]{2,1,0:T(8,128)(2,1)S(1)}, u32[]{:S(2)}, u32[]{:S(2)}) collective-permute-start(bf16[2,64,256]{2,1,0:T(8,128)(2,1)S(1)} %pad_maximum_fusion.8), channel_id=1, source_target_pairs={{0,2},{2,0},{4,6},{6,4},{8,10},{10,8},{12,14},{14,12},{1,3},{3,1},... | collective-permute-start | bytes 196616 | tf_op jit(solution)/shard_map/ppermute | solution.py:70
  78.4 4.8 %collective-permute-start.5 = (bf16[2,64,256]{2,1,0:T(8,128)(2,1)S(1)}, bf16[2,64,256]{2,1,0:T(8,128)(2,1)S(1)}, u32[]{:S(2)}, u32[]{:S(2)}) collective-permute-start(bf16[2,64,256]{2,1,0:T(8,128)(2,1)S(1)} %pad_maximum_fusion.5), channel_id=1, source_target_pairs={{0,4},{2,6},{4,0},{6,2},{8,12},{10,14},{12,8},{14,10},{1,5},{3,7},... | collective-permute-start | bytes 196616 | tf_op jit(solution)/shard_map/ppermute | solution.py:70
  78.5 6.2 %collective-permute-start.17 = (bf16[2,64,256]{2,1,0:T(8,128)(2,1)S(1)}, bf16[2,64,256]{2,1,0:T(8,128)(2,1)S(1)}, u32[]{:S(2)}, u32[]{:S(2)}) collective-permute-start(bf16[2,64,256]{2,1,0:T(8,128)(2,1)S(1)} %pad_maximum_fusion.7), channel_id=1, source_target_pairs={{0,4},{2,6},{4,0},{6,2},{8,12},{10,14},{12,8},{14,10},{1,5},{3,7},... | collective-permute-start | bytes 196616 | tf_op jit(solution)/shard_map/ppermute | solution.py:70
  80.6 5.0 %collective-permute-start.12 = (bf16[2,2,64,256]{3,2,1,0:T(8,128)(2,1)S(1)}, bf16[2,2,64,256]{3,2,1,0:T(8,128)(2,1)S(1)}, u32[]{:S(2)}, u32[]{:S(2)}) collective-permute-start(bf16[2,2,64,256]{3,2,1,0:T(8,128)(2,1)S(1)} %pad_maximum_fusion.2), channel_id=1, source_target_pairs={{0,4},{2,6},{4,0},{6,2},{8,12},{10,14},{12,8},{14,10},{1,5},{3,7},... | collective-permute-start | bytes 393224 | tf_op jit(solution)/shard_map/ppermute | solution.py:70
  82.5 5.0 %collective-permute-start.24 = (bf16[2,2,64,256]{3,2,1,0:T(8,128)(2,1)S(1)}, bf16[2,2,64,256]{3,2,1,0:T(8,128)(2,1)S(1)}, u32[]{:S(2)}, u32[]{:S(2)}) collective-permute-start(bf16[2,2,64,256]{3,2,1,0:T(8,128)(2,1)S(1)} %pad_maximum_fusion.4), channel_id=1, source_target_pairs={{0,4},{2,6},{4,0},{6,2},{8,12},{10,14},{12,8},{14,10},{1,5},{3,7},... | collective-permute-start | bytes 393224 | tf_op jit(solution)/shard_map/ppermute | solution.py:70
  83.2 5.0 %collective-permute-start.6 = (bf16[2,2,64,256]{3,2,1,0:T(8,128)(2,1)S(1)}, bf16[2,2,64,256]{3,2,1,0:T(8,128)(2,1)S(1)}, u32[]{:S(2)}, u32[]{:S(2)}) collective-permute-start(bf16[2,2,64,256]{3,2,1,0:T(8,128)(2,1)S(1)} %pad_maximum_fusion.1), channel_id=1, source_target_pairs={{0,2},{2,0},{4,6},{6,4},{8,10},{10,8},{12,14},{14,12},{1,3},{3,1},... | collective-permute-start | bytes 393224 | tf_op jit(solution)/shard_map/ppermute | solution.py:70
  84.8 5.0 %collective-permute-start.18 = (bf16[2,2,64,256]{3,2,1,0:T(8,128)(2,1)S(1)}, bf16[2,2,64,256]{3,2,1,0:T(8,128)(2,1)S(1)}, u32[]{:S(2)}, u32[]{:S(2)}) collective-permute-start(bf16[2,2,64,256]{3,2,1,0:T(8,128)(2,1)S(1)} %pad_maximum_fusion.3), channel_id=1, source_target_pairs={{0,2},{2,0},{4,6},{6,4},{8,10},{10,8},{12,14},{14,12},{1,3},{3,1},... | collective-permute-start | bytes 393224 | tf_op jit(solution)/shard_map/ppermute | solution.py:70
  (11 other events, 124.5 us)

commit v18 on v17

--- a/solution.py
+++ b/solution.py
@@ -39,7 +39,7 @@
     m2_out[...] = moment_two.astype(jnp.bfloat16)
 
 
-def tail(pre_t, error, centered, decoder, weight_in, first, second, tile=512):
+def tail(pre_t, error, centered, decoder, weight_in, first, second, tile=128):
     n_lat, width = decoder.shape
     if n_lat % tile:
         tile = n_lat

time: 120 us -> 124 us (1.033); the launches traced: 120 us -> 123 us
  Pallas kernels: 27.7 us -> 30.4 us
    pallas_call x1, Pallas kernels: 27.7 us -> 30.4 us  [tail(): pl.pallas_call(_tail_kernel, grid=(n_lat // tile,), in_specs=[pl.BlockSpe...]
where the time goes in v18:
time: 124 us; the launch traced here: 123 us
  waiting for transfers between devices  38.5 us (31%)
  starting transfers between devices  33.6 us (27%)
  Pallas kernels  30.4 us (25%)
  matrix products  8.84 us (7%)
  local copies, waits for them, and re-layouts  7.57 us (6%)
  other arithmetic  2.66 us (2%)
  between operations  1.24 us (1%)
    pallas_call x1, Pallas kernels, tail(): pl.pallas_call(_tail_kernel, grid=(n_lat // tile,), in_specs=[pl.BlockSpe...  30.4 us
    ppermute x24, starting transfers between devices, _pair_swap(): return lax.ppermute(value, axis, [(i, i ^ mask) for i in range(size)])  26.3 us
    ppermute x24, waiting for transfers between devices, _pair_swap(): return lax.ppermute(value, axis, [(i, i ^ mask) for i in range(size)])  23.6 us
    all_to_all x1, waiting for transfers between devices, local(): act_blocks = lax.all_to_all(copies, 'lat', 0, 0, tiled=True)  13.1 us
    all_to_all x1, starting transfers between devices, local(): act_blocks = lax.all_to_all(copies, 'lat', 0, 0, tiled=True)  7.25 us
    dot_general x1, matrix products, local(): lax.dot_general(weight_in, centered, (((1,), (1,)), ((), ())), preferred_...  6.5 us
  transfers between devices with their start and end apart: 26, of which 16 were waited for; matrix products, arithmetic and copies ran while one was open for 3% of the time, Pallas kernels for 0%

profile of v18, /device:TPU:0, one launch (start us, length us, event | category | flops | bytes accessed | tf_op | source)
XLA Modules:
  0.0 122.9 jit_solution(12299138892891205320)
XLA Ops:
  0.7 1.7 %broadcast_in_dim.46 = bf16[8,128,256]{2,1,0:T(8,128)(2,1)} broadcast(bf16[128,256]{1,0:T(8,128)(2,1)} %param.13), dimensions={1,2} | broadcast | bytes 589824 | tf_op jit(solution)/shard_map/broadcast_in_dim | solution.py:172
  2.4 7.3 %all-to-all-start = ((bf16[8,128,256]{2,1,0:T(8,128)(2,1)}), bf16[8,128,256]{2,1,0:T(8,128)(2,1)S(1)}, u32[]{:S(2)}, u32[]{:S(2)}) async-start(bf16[8,128,256]{2,1,0:T(8,128)(2,1)} %broadcast_in_dim.46), calls=%async_computation | async-start | bytes 1048576 | tf_op jit(solution)/shard_map/all_to_all | solution.py:173
  11.0 13.1 %all-to-all-done = bf16[8,128,256]{2,1,0:T(8,128)(2,1)S(1)} async-done(((bf16[8,128,256]{2,1,0:T(8,128)(2,1)}), bf16[8,128,256]{2,1,0:T(8,128)(2,1)S(1)}, u32[]{:S(2)}, u32[]{:S(2)}) %all-to-all-start) | async-done | bytes 524320 | tf_op jit(solution)/shard_map/all_to_all | solution.py:173
  24.3 1.8 %collective-permute-done = bf16[128,2048]{1,0:T(8,128)(2,1)S(1)} collective-permute-done((bf16[128,2048]{1,0:T(8,128)(2,1)S(1)}, bf16[128,2048]{1,0:T(8,128)(2,1)S(1)}, u32[]{:S(2)}, u32[]{:S(2)}) %collective-permute-start) | collective-permute-done | bytes 524320 | tf_op jit(solution)/shard_map/ppermute | solution.py:175
  26.3 1.4 %gather_fusion = bf16[256,2048]{1,0:T(8,128)(2,1)S(1)} fusion(bf16[256,2048]{1,0:T(8,128)(2,1)S(1)} %pad_maximum_fusion, s32[1024]{0:T(1024)S(1)} %pad_clamp_fusion.2), kind=kCustom, calls=%fused_computation | custom fusion | bytes 2098176 | tf_op jit(solution)/shard_map/jit(_take)/gather | solution.py:182
  28.4 6.5 %fusion.1 = bf16[256,2048]{0,1:T(8,128)(2,1)S(1)} fusion(bf16[256,2048]{1,0:T(8,128)(2,1)S(1)} %get-tuple-element.9.cen_ref, f32[2048]{0:T(1024)S(1)} %bitcast.117, bf16[1,2048,2048]{2,1,0:T(8,128)(2,1)} %param.16), kind=kOutput, calls=%fused_computation.7 | convolution fusion | flops 2149056512 | bytes 10493952 | tf_op jit(solution)/shard_map/dot_general | solution.py:188
  34.9 2.3 %fusion.2 = f32[256,2048]{1,0:T(8,128)S(1)} fusion(bf16[256,2048]{0,1:T(8,128)(2,1)S(1)} %fusion.1, bf16[1,2048,2048]{2,1,0:T(8,128)(2,1)S(1)} %bitcast.94), kind=kOutput, calls=%fused_computation.84 | convolution fusion | flops 2147483648 | bytes 11534336 | tf_op jit(solution)/shard_map/dot_general | solution.py:194
  39.6 1.5 %collective-permute-start.13 = (f32[64,1024]{1,0:T(8,128)S(1)}, f32[64,1024]{1,0:T(8,128)S(1)}, u32[]{:S(2)}, u32[]{:S(2)}) collective-permute-start(f32[64,1024]{1,0:T(8,128)S(1)} %constant_dynamic-slice_fusion.3), channel_id=1, source_target_pairs={{0,2},{2,0},{4,6},{6,4},{8,10},{10,8},{12,14},{14,12},{1,3},{3,1},... | collective-permute-start | bytes 786440 | tf_op jit(solution)/shard_map/ppermute | solution.py:70
  41.8 5.0 %collective-permute-done.7 = f32[64,1024]{1,0:T(8,128)S(1)} collective-permute-done((f32[64,1024]{1,0:T(8,128)S(1)}, f32[64,1024]{1,0:T(8,128)S(1)}, u32[]{:S(2)}, u32[]{:S(2)}) %collective-permute-start.7) | collective-permute-done | bytes 262176 | tf_op jit(solution)/shard_map/ppermute | solution.py:70
  46.8 1.5 %collective-permute-start.8 = (f32[64,512]{1,0:T(8,128)S(1)}, f32[64,512]{1,0:T(8,128)S(1)}, u32[]{:S(2)}, u32[]{:S(2)}) collective-permute-start(f32[64,512]{1,0:T(8,128)S(1)} %constant_dynamic-slice_fusion.8), channel_id=1, source_target_pairs={{0,2},{2,0},{4,6},{6,4},{8,10},{10,8},{12,14},{14,12},{1,3},{3,1},... | collective-permute-start | bytes 393224 | tf_op jit(solution)/shard_map/ppermute | solution.py:70
  48.4 3.2 %collective-permute-done.19 = f32[64,1024]{1,0:T(8,128)S(1)} collective-permute-done((f32[64,1024]{1,0:T(8,128)S(1)}, f32[64,1024]{1,0:T(8,128)S(1)}, u32[]{:S(2)}, u32[]{:S(2)}) %collective-permute-start.19) | collective-permute-done | bytes 262176 | tf_op jit(solution)/shard_map/ppermute | solution.py:70
  51.7 1.5 %collective-permute-start.20 = (f32[64,512]{1,0:T(8,128)S(1)}, f32[64,512]{1,0:T(8,128)S(1)}, u32[]{:S(2)}, u32[]{:S(2)}) collective-permute-start(f32[64,512]{1,0:T(8,128)S(1)} %constant_dynamic-slice_fusion.5), channel_id=1, source_target_pairs={{0,2},{2,0},{4,6},{6,4},{8,10},{10,8},{12,14},{14,12},{1,3},{3,1},... | collective-permute-start | bytes 393224 | tf_op jit(solution)/shard_map/ppermute | solution.py:70
  55.5 1.8 %collective-permute-done.8 = f32[64,512]{1,0:T(8,128)S(1)} collective-permute-done((f32[64,512]{1,0:T(8,128)S(1)}, f32[64,512]{1,0:T(8,128)S(1)}, u32[]{:S(2)}, u32[]{:S(2)}) %collective-permute-start.8) | collective-permute-done | bytes 131104 | tf_op jit(solution)/shard_map/ppermute | solution.py:70
  58.7 1.7 %collective-permute-start.21 = (f32[64,256]{1,0:T(8,128)S(1)}, f32[64,256]{1,0:T(8,128)S(1)}, u32[]{:S(2)}, u32[]{:S(2)}) collective-permute-start(f32[64,256]{1,0:T(8,128)S(1)} %constant_dynamic-slice_fusion.10), channel_id=1, source_target_pairs={{0,8},{2,10},{4,12},{6,14},{8,0},{10,2},{12,4},{14,6},{1,9},{3,11}... | collective-permute-start | bytes 196616 | tf_op jit(solution)/shard_map/ppermute | solution.py:70
  61.9 1.7 %collective-permute-start.3 = (f32[64,256]{1,0:T(8,128)S(1)}, f32[64,256]{1,0:T(8,128)S(1)}, u32[]{:S(2)}, u32[]{:S(2)}) collective-permute-start(f32[64,256]{1,0:T(8,128)S(1)} %constant_dynamic-slice_fusion.13), channel_id=1, source_target_pairs={{0,8},{2,10},{4,12},{6,14},{8,0},{10,2},{12,4},{14,6},{1,9},{3,11}... | collective-permute-start | bytes 196616 | tf_op jit(solution)/shard_map/ppermute | solution.py:70
  63.6 4.8 %collective-permute-done.9 = f32[64,256]{1,0:T(8,128)S(1)} collective-permute-done((f32[64,256]{1,0:T(8,128)S(1)}, f32[64,256]{1,0:T(8,128)S(1)}, u32[]{:S(2)}, u32[]{:S(2)}) %collective-permute-start.9) | collective-permute-done | bytes 65568 | tf_op jit(solution)/shard_map/ppermute | solution.py:70
  68.4 1.4 %collective-permute-done.21 = f32[64,256]{1,0:T(8,128)S(1)} collective-permute-done((f32[64,256]{1,0:T(8,128)S(1)}, f32[64,256]{1,0:T(8,128)S(1)}, u32[]{:S(2)}, u32[]{:S(2)}) %collective-permute-start.21) | collective-permute-done | bytes 65568 | tf_op jit(solution)/shard_map/ppermute | solution.py:70
  69.9 2.9 %collective-permute-start.22 = (bf16[64,256]{1,0:T(8,128)(2,1)S(1)}, bf16[64,256]{1,0:T(8,128)(2,1)S(1)}, u32[]{:S(2)}, u32[]{:S(2)}) collective-permute-start(bf16[64,256]{1,0:T(8,128)(2,1)S(1)} %get-tuple-element.52), channel_id=1, source_target_pairs={{0,8},{2,10},{4,12},{6,14},{8,0},{10,2},{12,4},{14,6},{1,9},{3,11}... | collective-permute-start | bytes 98312 | tf_op jit(solution)/shard_map/ppermute | solution.py:70
  73.0 2.8 %collective-permute-start.16 = (bf16[64,256]{1,0:T(8,128)(2,1)S(1)}, bf16[64,256]{1,0:T(8,128)(2,1)S(1)}, u32[]{:S(2)}, u32[]{:S(2)}) collective-permute-start(bf16[64,256]{1,0:T(8,128)(2,1)S(1)} %get-tuple-element.50), channel_id=1, source_target_pairs={{0,8},{2,10},{4,12},{6,14},{8,0},{10,2},{12,4},{14,6},{1,9},{3,11}... | collective-permute-start | bytes 98312 | tf_op jit(solution)/shard_map/ppermute | solution.py:70
  78.5 2.1 %collective-permute-start.17 = (bf16[2,64,256]{2,1,0:T(8,128)(2,1)S(1)}, bf16[2,64,256]{2,1,0:T(8,128)(2,1)S(1)}, u32[]{:S(2)}, u32[]{:S(2)}) collective-permute-start(bf16[2,64,256]{2,1,0:T(8,128)(2,1)S(1)} %pad_maximum_fusion.7), channel_id=1, source_target_pairs={{0,4},{2,6},{4,0},{6,2},{8,12},{10,14},{12,8},{14,10},{1,5},{3,7},... | collective-permute-start | bytes 196616 | tf_op jit(solution)/shard_map/ppermute | solution.py:70
  80.7 1.7 %collective-permute-done.23 = bf16[2,64,256]{2,1,0:T(8,128)(2,1)S(1)} collective-permute-done((bf16[2,64,256]{2,1,0:T(8,128)(2,1)S(1)}, bf16[2,64,256]{2,1,0:T(8,128)(2,1)S(1)}, u32[]{:S(2)}, u32[]{:S(2)}) %collective-permute-start.23) | collective-permute-done | bytes 65568 | tf_op jit(solution)/shard_map/ppermute | solution.py:70
  83.3 1.4 %collective-permute-start.6 = (bf16[2,2,64,256]{3,2,1,0:T(8,128)(2,1)S(1)}, bf16[2,2,64,256]{3,2,1,0:T(8,128)(2,1)S(1)}, u32[]{:S(2)}, u32[]{:S(2)}) collective-permute-start(bf16[2,2,64,256]{3,2,1,0:T(8,128)(2,1)S(1)} %pad_maximum_fusion.1), channel_id=1, source_target_pairs={{0,2},{2,0},{4,6},{6,4},{8,10},{10,8},{12,14},{14,12},{1,3},{3,1},... | collective-permute-start | bytes 393224 | tf_op jit(solution)/shard_map/ppermute | solution.py:70
  85.7 1.8 %collective-permute-done.24 = bf16[2,2,64,256]{3,2,1,0:T(8,128)(2,1)S(1)} collective-permute-done((bf16[2,2,64,256]{3,2,1,0:T(8,128)(2,1)S(1)}, bf16[2,2,64,256]{3,2,1,0:T(8,128)(2,1)S(1)}, u32[]{:S(2)}, u32[]{:S(2)}) %collective-permute-start.24) | collective-permute-done | bytes 131104 | tf_op jit(solution)/shard_map/ppermute | solution.py:70
  92.4 30.4 %shard_map.148 = (bf16[2048,2048]{1,0:T(8,128)(2,1)}, bf16[2048,2048]{1,0:T(8,128)(2,1)}, bf16[2048,2048]{1,0:T(8,128)(2,1)}) custom-call(bf16[2048,256]{1,0:T(8,128)(2,1)} %bitcast.98, bf16[2048,256]{1,0:T(8,128)(2,1)} %bitcast.99, bf16[256,2048]{1,0:T(8,128)(2,1)} %copy-done.1, bf16[2048,2048]{1,0:T(8,128)(2,1)} %bitcast.92, bf16[2048,2048]{1,0:T(8,128)(2,1)} %bitcast.95, ...), custom_call_target="tpu_custom_call" | custom-call | tf_op jit(solution)/shard_map/pallas_call | solution.py:51
  (121 shorter events, 20.2 us)
Async XLA Ops:
  2.4 21.7 %all-to-all-start = ((bf16[8,128,256]{2,1,0:T(8,128)(2,1)}), bf16[8,128,256]{2,1,0:T(8,128)(2,1)S(1)}, u32[]{:S(2)}, u32[]{:S(2)}) async-start(bf16[8,128,256]{2,1,0:T(8,128)(2,1)} %broadcast_in_dim.46), calls=%async_computation | async-start | bytes 1048576 | tf_op jit(solution)/shard_map/all_to_all | solution.py:173
  37.6 9.2 %collective-permute-start.7 = (f32[64,1024]{1,0:T(8,128)S(1)}, f32[64,1024]{1,0:T(8,128)S(1)}, u32[]{:S(2)}, u32[]{:S(2)}) collective-permute-start(f32[64,1024]{1,0:T(8,128)S(1)} %constant_dynamic-slice_fusion.9), channel_id=1, source_target_pairs={{0,4},{2,6},{4,0},{6,2},{8,12},{10,14},{12,8},{14,10},{1,5},{3,7},... | collective-permute-start | bytes 786440 | tf_op jit(solution)/shard_map/ppermute | solution.py:70
  38.4 13.2 %collective-permute-start.19 = (f32[64,1024]{1,0:T(8,128)S(1)}, f32[64,1024]{1,0:T(8,128)S(1)}, u32[]{:S(2)}, u32[]{:S(2)}) collective-permute-start(f32[64,1024]{1,0:T(8,128)S(1)} %constant_dynamic-slice_fusion), channel_id=1, source_target_pairs={{0,4},{2,6},{4,0},{6,2},{8,12},{10,14},{12,8},{14,10},{1,5},{3,7},... | collective-permute-start | bytes 786440 | tf_op jit(solution)/shard_map/ppermute | solution.py:70
  39.6 13.5 %collective-permute-start.13 = (f32[64,1024]{1,0:T(8,128)S(1)}, f32[64,1024]{1,0:T(8,128)S(1)}, u32[]{:S(2)}, u32[]{:S(2)}) collective-permute-start(f32[64,1024]{1,0:T(8,128)S(1)} %constant_dynamic-slice_fusion.3), channel_id=1, source_target_pairs={{0,2},{2,0},{4,6},{6,4},{8,10},{10,8},{12,14},{14,12},{1,3},{3,1},... | collective-permute-start | bytes 786440 | tf_op jit(solution)/shard_map/ppermute | solution.py:70
  41.1 13.4 %collective-permute-start.1 = (f32[64,1024]{1,0:T(8,128)S(1)}, f32[64,1024]{1,0:T(8,128)S(1)}, u32[]{:S(2)}, u32[]{:S(2)}) collective-permute-start(f32[64,1024]{1,0:T(8,128)S(1)} %constant_dynamic-slice_fusion.15), channel_id=1, source_target_pairs={{0,2},{2,0},{4,6},{6,4},{8,10},{10,8},{12,14},{14,12},{1,3},{3,1},... | collective-permute-start | bytes 786440 | tf_op jit(solution)/shard_map/ppermute | solution.py:70
  46.8 10.4 %collective-permute-start.8 = (f32[64,512]{1,0:T(8,128)S(1)}, f32[64,512]{1,0:T(8,128)S(1)}, u32[]{:S(2)}, u32[]{:S(2)}) collective-permute-start(f32[64,512]{1,0:T(8,128)S(1)} %constant_dynamic-slice_fusion.8), channel_id=1, source_target_pairs={{0,2},{2,0},{4,6},{6,4},{8,10},{10,8},{12,14},{14,12},{1,3},{3,1},... | collective-permute-start | bytes 393224 | tf_op jit(solution)/shard_map/ppermute | solution.py:70
  51.7 7.0 %collective-permute-start.20 = (f32[64,512]{1,0:T(8,128)S(1)}, f32[64,512]{1,0:T(8,128)S(1)}, u32[]{:S(2)}, u32[]{:S(2)}) collective-permute-start(f32[64,512]{1,0:T(8,128)S(1)} %constant_dynamic-slice_fusion.5), channel_id=1, source_target_pairs={{0,2},{2,0},{4,6},{6,4},{8,10},{10,8},{12,14},{14,12},{1,3},{3,1},... | collective-permute-start | bytes 393224 | tf_op jit(solution)/shard_map/ppermute | solution.py:70
  53.2 7.2 %collective-permute-start.14 = (f32[64,512]{1,0:T(8,128)S(1)}, f32[64,512]{1,0:T(8,128)S(1)}, u32[]{:S(2)}, u32[]{:S(2)}) collective-permute-start(f32[64,512]{1,0:T(8,128)S(1)} %constant_dynamic-slice_fusion.2), channel_id=1, source_target_pairs={{0,4},{2,6},{4,0},{6,2},{8,12},{10,14},{12,8},{14,10},{1,5},{3,7},... | collective-permute-start | bytes 393224 | tf_op jit(solution)/shard_map/ppermute | solution.py:70
  54.6 7.3 %collective-permute-start.2 = (f32[64,512]{1,0:T(8,128)S(1)}, f32[64,512]{1,0:T(8,128)S(1)}, u32[]{:S(2)}, u32[]{:S(2)}) collective-permute-start(f32[64,512]{1,0:T(8,128)S(1)} %constant_dynamic-slice_fusion.14), channel_id=1, source_target_pairs={{0,4},{2,6},{4,0},{6,2},{8,12},{10,14},{12,8},{14,10},{1,5},{3,7},... | collective-permute-start | bytes 393224 | tf_op jit(solution)/shard_map/ppermute | solution.py:70
  57.3 11.1 %collective-permute-start.9 = (f32[64,256]{1,0:T(8,128)S(1)}, f32[64,256]{1,0:T(8,128)S(1)}, u32[]{:S(2)}, u32[]{:S(2)}) collective-permute-start(f32[64,256]{1,0:T(8,128)S(1)} %constant_dynamic-slice_fusion.7), channel_id=1, source_target_pairs={{0,8},{2,10},{4,12},{6,14},{8,0},{10,2},{12,4},{14,6},{1,9},{3,11}... | collective-permute-start | bytes 196616 | tf_op jit(solution)/shard_map/ppermute | solution.py:70
  58.7 11.1 %collective-permute-start.21 = (f32[64,256]{1,0:T(8,128)S(1)}, f32[64,256]{1,0:T(8,128)S(1)}, u32[]{:S(2)}, u32[]{:S(2)}) collective-permute-start(f32[64,256]{1,0:T(8,128)S(1)} %constant_dynamic-slice_fusion.10), channel_id=1, source_target_pairs={{0,8},{2,10},{4,12},{6,14},{8,0},{10,2},{12,4},{14,6},{1,9},{3,11}... | collective-permute-start | bytes 196616 | tf_op jit(solution)/shard_map/ppermute | solution.py:70
  60.5 12.4 %collective-permute-start.15 = (f32[64,256]{1,0:T(8,128)S(1)}, f32[64,256]{1,0:T(8,128)S(1)}, u32[]{:S(2)}, u32[]{:S(2)}) collective-permute-start(f32[64,256]{1,0:T(8,128)S(1)} %constant_dynamic-slice_fusion.1), channel_id=1, source_target_pairs={{0,8},{2,10},{4,12},{6,14},{8,0},{10,2},{12,4},{14,6},{1,9},{3,11}... | collective-permute-start | bytes 196616 | tf_op jit(solution)/shard_map/ppermute | solution.py:70
  61.9 11.0 %collective-permute-start.3 = (f32[64,256]{1,0:T(8,128)S(1)}, f32[64,256]{1,0:T(8,128)S(1)}, u32[]{:S(2)}, u32[]{:S(2)}) collective-permute-start(f32[64,256]{1,0:T(8,128)S(1)} %constant_dynamic-slice_fusion.13), channel_id=1, source_target_pairs={{0,8},{2,10},{4,12},{6,14},{8,0},{10,2},{12,4},{14,6},{1,9},{3,11}... | collective-permute-start | bytes 196616 | tf_op jit(solution)/shard_map/ppermute | solution.py:70
  69.8 6.3 %collective-permute-start.10 = (bf16[64,256]{1,0:T(8,128)(2,1)S(1)}, bf16[64,256]{1,0:T(8,128)(2,1)S(1)}, u32[]{:S(2)}, u32[]{:S(2)}) collective-permute-start(bf16[64,256]{1,0:T(8,128)(2,1)S(1)} %get-tuple-element.51), channel_id=1, source_target_pairs={{0,8},{2,10},{4,12},{6,14},{8,0},{10,2},{12,4},{14,6},{1,9},{3,11}... | collective-permute-start | bytes 98312 | tf_op jit(solution)/shard_map/ppermute | solution.py:70
  69.9 7.6 %collective-permute-start.22 = (bf16[64,256]{1,0:T(8,128)(2,1)S(1)}, bf16[64,256]{1,0:T(8,128)(2,1)S(1)}, u32[]{:S(2)}, u32[]{:S(2)}) collective-permute-start(bf16[64,256]{1,0:T(8,128)(2,1)S(1)} %get-tuple-element.52), channel_id=1, source_target_pairs={{0,8},{2,10},{4,12},{6,14},{8,0},{10,2},{12,4},{14,6},{1,9},{3,11}... | collective-permute-start | bytes 98312 | tf_op jit(solution)/shard_map/ppermute | solution.py:70
  72.9 5.5 %collective-permute-start.4 = (bf16[64,256]{1,0:T(8,128)(2,1)S(1)}, bf16[64,256]{1,0:T(8,128)(2,1)S(1)}, u32[]{:S(2)}, u32[]{:S(2)}) collective-permute-start(bf16[64,256]{1,0:T(8,128)(2,1)S(1)} %get-tuple-element.49), channel_id=1, source_target_pairs={{0,8},{2,10},{4,12},{6,14},{8,0},{10,2},{12,4},{14,6},{1,9},{3,11}... | collective-permute-start | bytes 98312 | tf_op jit(solution)/shard_map/ppermute | solution.py:70
  73.0 5.4 %collective-permute-start.16 = (bf16[64,256]{1,0:T(8,128)(2,1)S(1)}, bf16[64,256]{1,0:T(8,128)(2,1)S(1)}, u32[]{:S(2)}, u32[]{:S(2)}) collective-permute-start(bf16[64,256]{1,0:T(8,128)(2,1)S(1)} %get-tuple-element.50), channel_id=1, source_target_pairs={{0,8},{2,10},{4,12},{6,14},{8,0},{10,2},{12,4},{14,6},{1,9},{3,11}... | collective-permute-start | bytes 98312 | tf_op jit(solution)/shard_map/ppermute | solution.py:70
  77.5 4.9 %collective-permute-start.23 = (bf16[2,64,256]{2,1,0:T(8,128)(2,1)S(1)}, bf16[2,64,256]{2,1,0:T(8,128)(2,1)S(1)}, u32[]{:S(2)}, u32[]{:S(2)}) collective-permute-start(bf16[2,64,256]{2,1,0:T(8,128)(2,1)S(1)} %pad_maximum_fusion.8), channel_id=1, source_target_pairs={{0,2},{2,0},{4,6},{6,4},{8,10},{10,8},{12,14},{14,12},{1,3},{3,1},... | collective-permute-start | bytes 196616 | tf_op jit(solution)/shard_map/ppermute | solution.py:70
  78.4 4.9 %collective-permute-start.5 = (bf16[2,64,256]{2,1,0:T(8,128)(2,1)S(1)}, bf16[2,64,256]{2,1,0:T(8,128)(2,1)S(1)}, u32[]{:S(2)}, u32[]{:S(2)}) collective-permute-start(bf16[2,64,256]{2,1,0:T(8,128)(2,1)S(1)} %pad_maximum_fusion.5), channel_id=1, source_target_pairs={{0,4},{2,6},{4,0},{6,2},{8,12},{10,14},{12,8},{14,10},{1,5},{3,7},... | collective-permute-start | bytes 196616 | tf_op jit(solution)/shard_map/ppermute | solution.py:70
  78.5 6.2 %collective-permute-start.17 = (bf16[2,64,256]{2,1,0:T(8,128)(2,1)S(1)}, bf16[2,64,256]{2,1,0:T(8,128)(2,1)S(1)}, u32[]{:S(2)}, u32[]{:S(2)}) collective-permute-start(bf16[2,64,256]{2,1,0:T(8,128)(2,1)S(1)} %pad_maximum_fusion.7), channel_id=1, source_target_pairs={{0,4},{2,6},{4,0},{6,2},{8,12},{10,14},{12,8},{14,10},{1,5},{3,7},... | collective-permute-start | bytes 196616 | tf_op jit(solution)/shard_map/ppermute | solution.py:70
  80.6 5.0 %collective-permute-start.12 = (bf16[2,2,64,256]{3,2,1,0:T(8,128)(2,1)S(1)}, bf16[2,2,64,256]{3,2,1,0:T(8,128)(2,1)S(1)}, u32[]{:S(2)}, u32[]{:S(2)}) collective-permute-start(bf16[2,2,64,256]{3,2,1,0:T(8,128)(2,1)S(1)} %pad_maximum_fusion.2), channel_id=1, source_target_pairs={{0,4},{2,6},{4,0},{6,2},{8,12},{10,14},{12,8},{14,10},{1,5},{3,7},... | collective-permute-start | bytes 393224 | tf_op jit(solution)/shard_map/ppermute | solution.py:70
  82.5 5.0 %collective-permute-start.24 = (bf16[2,2,64,256]{3,2,1,0:T(8,128)(2,1)S(1)}, bf16[2,2,64,256]{3,2,1,0:T(8,128)(2,1)S(1)}, u32[]{:S(2)}, u32[]{:S(2)}) collective-permute-start(bf16[2,2,64,256]{3,2,1,0:T(8,128)(2,1)S(1)} %pad_maximum_fusion.4), channel_id=1, source_target_pairs={{0,4},{2,6},{4,0},{6,2},{8,12},{10,14},{12,8},{14,10},{1,5},{3,7},... | collective-permute-start | bytes 393224 | tf_op jit(solution)/shard_map/ppermute | solution.py:70
  83.3 5.0 %collective-permute-start.6 = (bf16[2,2,64,256]{3,2,1,0:T(8,128)(2,1)S(1)}, bf16[2,2,64,256]{3,2,1,0:T(8,128)(2,1)S(1)}, u32[]{:S(2)}, u32[]{:S(2)}) collective-permute-start(bf16[2,2,64,256]{3,2,1,0:T(8,128)(2,1)S(1)} %pad_maximum_fusion.1), channel_id=1, source_target_pairs={{0,2},{2,0},{4,6},{6,4},{8,10},{10,8},{12,14},{14,12},{1,3},{3,1},... | collective-permute-start | bytes 393224 | tf_op jit(solution)/shard_map/ppermute | solution.py:70
  84.8 5.0 %collective-permute-start.18 = (bf16[2,2,64,256]{3,2,1,0:T(8,128)(2,1)S(1)}, bf16[2,2,64,256]{3,2,1,0:T(8,128)(2,1)S(1)}, u32[]{:S(2)}, u32[]{:S(2)}) collective-permute-start(bf16[2,2,64,256]{3,2,1,0:T(8,128)(2,1)S(1)} %pad_maximum_fusion.3), channel_id=1, source_target_pairs={{0,2},{2,0},{4,6},{6,4},{8,10},{10,8},{12,14},{14,12},{1,3},{3,1},... | collective-permute-start | bytes 393224 | tf_op jit(solution)/shard_map/ppermute | solution.py:70
  (11 other events, 124.5 us)

commit v19 on v18

--- a/solution.py
+++ b/solution.py
@@ -1,3 +1,4 @@
+import functools
 import jax
 import jax.numpy as jnp
 from jax import lax
@@ -16,13 +17,27 @@
 
 
 def _tail_kernel(
+    stacked,
     pre_ref, err_ref, cen_ref, dec_ref, enc_ref, m1_ref, m2_ref, w_out, m1_out, m2_out
 ):
     dec = dec_ref[...]
     dec32 = dec.astype(jnp.float32)
     row_norm = jnp.sqrt(jnp.sum(dec32 * dec32, axis=1, keepdims=True) + 1e-06)
-    back_t = jnp.dot(dec, err_ref[...], preferred_element_type=jnp.float32)
-    tokens = err_ref.shape[1]
+    if stacked:
+        blocks, tokens, part = err_ref.shape
+        back_t = lax.dot_general(
+            dec[:, :part], err_ref[0], (((1,), (1,)), ((), ())), preferred_element_type=jnp.float32
+        )
+        for b in range(1, blocks):
+            back_t = back_t + lax.dot_general(
+                dec[:, b * part : (b + 1) * part],
+                err_ref[b],
+                (((1,), (1,)), ((), ())),
+                preferred_element_type=jnp.float32,
+            )
+    else:
+        back_t = jnp.dot(dec, err_ref[...], preferred_element_type=jnp.float32)
+        tokens = err_ref.shape[1]
     d_pre = (
         jnp.where(pre_ref[...].astype(jnp.float32) > 0, 2.0 * back_t + sparsity * row_norm, 0.0) / tokens
     ).astype(jnp.bfloat16)
@@ -39,21 +54,27 @@
     m2_out[...] = moment_two.astype(jnp.bfloat16)
 
 
-def tail(pre_t, error, centered, decoder, weight_in, first, second, tile=128):
+def tail(pre_t, error_blocks, centered, decoder, weight_in, first, second, tile=512):
     n_lat, width = decoder.shape
     if n_lat % tile:
         tile = n_lat
-    tokens = error.shape[0]
-    error_t = error.T
+    tokens = error_blocks.shape[1]
+    stacked = error_blocks.shape[0] <= 8
+    if stacked:
+        error_in = error_blocks
+        error_spec = pl.BlockSpec(error_blocks.shape, lambda i: (0, 0, 0))
+    else:
+        error_in = jnp.transpose(error_blocks, (0, 2, 1)).reshape(width, tokens)
+        error_spec = pl.BlockSpec((width, tokens), lambda i: (0, 0))
     row_block = pl.BlockSpec((tile, width), lambda i: (i, 0))
     whole = pl.BlockSpec((tokens, width), lambda i: (0, 0))
     out = jax.ShapeDtypeStruct((n_lat, width), jnp.bfloat16)
     return pl.pallas_call(
-        _tail_kernel,
+        functools.partial(_tail_kernel, stacked),
         grid=(n_lat // tile,),
         in_specs=[
             pl.BlockSpec((tile, tokens), lambda i: (i, 0)),
-            pl.BlockSpec((width, tokens), lambda i: (0, 0)),
+            error_spec,
             whole,
             row_block,
             row_block,
@@ -63,7 +84,7 @@
         out_specs=[row_block, row_block, row_block],
         out_shape=[out, out, out],
         compiler_params=pltpu.CompilerParams(vmem_limit_bytes=56 * 1024 * 1024),
-    )(pre_t, error_t, centered, decoder, weight_in, first, second)
+    )(pre_t, error_in, centered, decoder, weight_in, first, second)
 
 
 def _pair_swap(value, axis, mask, size):
@@ -210,9 +231,8 @@
         stacked = _doubling_gather(error_cols, "lat", lat_size, order[::-1])
         error_parts.append(stacked[jnp.array(_block_owners(lat_size, order))])
     error_blocks = jnp.concatenate(error_parts, axis=1)
-    error = jnp.transpose(error_blocks, (1, 0, 2)).reshape(error_blocks.shape[1], -1)
     updated, moment_one, moment_two = tail(
-        latent_t, error, centered, decoder, weight_in, first_moment[0], second_moment[0]
+        latent_t, error_blocks, centered, decoder, weight_in, first_moment[0], second_moment[0]
     )
     return updated[None], moment_one[None], moment_two[None]
 

time: 124 us -> 120 us (0.968)
  Pallas kernels: 30.4 us -> 27.7 us
  local copies, waits for them, and re-layouts: 7.57 us -> 6.26 us
    pallas_call x1, Pallas kernels: 30.4 us -> 27.7 us  [tail(): pl.pallas_call(functools.partial(_tail_kernel, stacked), grid=(n_lat // t...]
    transpose x1 -> x0, local copies, waits for them, and re-layouts: 1.31 us -> none  [local(): jnp.transpose(error_blocks, (1, 0, 2)).reshape(error_blocks.shape[1], -1)]
where the time goes in v19:
time: 120 us
  waiting for transfers between devices  38.6 us (32%)
  starting transfers between devices  33.5 us (28%)
  Pallas kernels  27.7 us (23%)
  matrix products  8.84 us (7%)
  local copies, waits for them, and re-layouts  6.26 us (5%)
  other arithmetic  3.64 us (3%)
  between operations  1.24 us (1%)
    pallas_call x1, Pallas kernels, tail(): pl.pallas_call(functools.partial(_tail_kernel, stacked), grid=(n_lat // t...  27.7 us
    ppermute x24, starting transfers between devices, _pair_swap(): return lax.ppermute(value, axis, [(i, i ^ mask) for i in range(size)])  26.2 us
    ppermute x24, waiting for transfers between devices, _pair_swap(): return lax.ppermute(value, axis, [(i, i ^ mask) for i in range(size)])  23.7 us
    all_to_all x1, waiting for transfers between devices, local(): act_blocks = lax.all_to_all(copies, 'lat', 0, 0, tiled=True)  13.1 us
    all_to_all x1, starting transfers between devices, local(): act_blocks = lax.all_to_all(copies, 'lat', 0, 0, tiled=True)  7.25 us
    dot_general x1, matrix products, local(): lax.dot_general(weight_in, centered, (((1,), (1,)), ((), ())), preferred_...  6.5 us
  transfers between devices with their start and end apart: 26, of which 16 were waited for; matrix products, arithmetic and copies ran while one was open for 3% of the time, Pallas kernels for 0%

profile of v19, /device:TPU:0, one launch (start us, length us, event | category | flops | bytes accessed | tf_op | source)
XLA Modules:
  0.0 119.7 jit_solution(14981943035717570287)
XLA Ops:
  0.7 1.7 %broadcast_in_dim.46 = bf16[8,128,256]{2,1,0:T(8,128)(2,1)} broadcast(bf16[128,256]{1,0:T(8,128)(2,1)} %param.13), dimensions={1,2} | broadcast | bytes 589824 | tf_op jit(solution)/shard_map/broadcast_in_dim | solution.py:193
  2.4 7.3 %all-to-all-start = ((bf16[8,128,256]{2,1,0:T(8,128)(2,1)}), bf16[8,128,256]{2,1,0:T(8,128)(2,1)S(1)}, u32[]{:S(2)}, u32[]{:S(2)}) async-start(bf16[8,128,256]{2,1,0:T(8,128)(2,1)} %broadcast_in_dim.46), calls=%async_computation | async-start | bytes 1048576 | tf_op jit(solution)/shard_map/all_to_all | solution.py:194
  11.0 13.1 %all-to-all-done = bf16[8,128,256]{2,1,0:T(8,128)(2,1)S(1)} async-done(((bf16[8,128,256]{2,1,0:T(8,128)(2,1)}), bf16[8,128,256]{2,1,0:T(8,128)(2,1)S(1)}, u32[]{:S(2)}, u32[]{:S(2)}) %all-to-all-start) | async-done | bytes 524320 | tf_op jit(solution)/shard_map/all_to_all | solution.py:194
  24.3 1.8 %collective-permute-done = bf16[128,2048]{1,0:T(8,128)(2,1)S(1)} collective-permute-done((bf16[128,2048]{1,0:T(8,128)(2,1)S(1)}, bf16[128,2048]{1,0:T(8,128)(2,1)S(1)}, u32[]{:S(2)}, u32[]{:S(2)}) %collective-permute-start) | collective-permute-done | bytes 524320 | tf_op jit(solution)/shard_map/ppermute | solution.py:196
  26.3 1.4 %gather_fusion = bf16[256,2048]{1,0:T(8,128)(2,1)S(1)} fusion(bf16[256,2048]{1,0:T(8,128)(2,1)S(1)} %pad_maximum_fusion, s32[1024]{0:T(1024)S(1)} %pad_clamp_fusion.2), kind=kCustom, calls=%fused_computation | custom fusion | bytes 2098176 | tf_op jit(solution)/shard_map/jit(_take)/gather | solution.py:203
  28.4 6.5 %fusion.1 = bf16[256,2048]{0,1:T(8,128)(2,1)S(1)} fusion(bf16[256,2048]{1,0:T(8,128)(2,1)S(1)} %get-tuple-element.9.cen_ref, f32[2048]{0:T(1024)S(1)} %bitcast.111, bf16[1,2048,2048]{2,1,0:T(8,128)(2,1)} %param.16), kind=kOutput, calls=%fused_computation.7 | convolution fusion | flops 2149056512 | bytes 10493952 | tf_op jit(solution)/shard_map/dot_general | solution.py:209
  34.9 2.3 %fusion.2 = f32[256,2048]{1,0:T(8,128)S(1)} fusion(bf16[256,2048]{0,1:T(8,128)(2,1)S(1)} %fusion.1, bf16[1,2048,2048]{2,1,0:T(8,128)(2,1)S(1)} %bitcast.89), kind=kOutput, calls=%fused_computation.84 | convolution fusion | flops 2147483648 | bytes 11534336 | tf_op jit(solution)/shard_map/dot_general | solution.py:215
  39.6 1.5 %collective-permute-start.13 = (f32[64,1024]{1,0:T(8,128)S(1)}, f32[64,1024]{1,0:T(8,128)S(1)}, u32[]{:S(2)}, u32[]{:S(2)}) collective-permute-start(f32[64,1024]{1,0:T(8,128)S(1)} %constant_dynamic-slice_fusion.3), channel_id=1, source_target_pairs={{0,2},{2,0},{4,6},{6,4},{8,10},{10,8},{12,14},{14,12},{1,3},{3,1},... | collective-permute-start | bytes 786440 | tf_op jit(solution)/shard_map/ppermute | solution.py:91
  41.8 5.0 %collective-permute-done.7 = f32[64,1024]{1,0:T(8,128)S(1)} collective-permute-done((f32[64,1024]{1,0:T(8,128)S(1)}, f32[64,1024]{1,0:T(8,128)S(1)}, u32[]{:S(2)}, u32[]{:S(2)}) %collective-permute-start.7) | collective-permute-done | bytes 262176 | tf_op jit(solution)/shard_map/ppermute | solution.py:91
  46.8 1.5 %collective-permute-start.8 = (f32[64,512]{1,0:T(8,128)S(1)}, f32[64,512]{1,0:T(8,128)S(1)}, u32[]{:S(2)}, u32[]{:S(2)}) collective-permute-start(f32[64,512]{1,0:T(8,128)S(1)} %constant_dynamic-slice_fusion.8), channel_id=1, source_target_pairs={{0,2},{2,0},{4,6},{6,4},{8,10},{10,8},{12,14},{14,12},{1,3},{3,1},... | collective-permute-start | bytes 393224 | tf_op jit(solution)/shard_map/ppermute | solution.py:91
  48.4 3.2 %collective-permute-done.19 = f32[64,1024]{1,0:T(8,128)S(1)} collective-permute-done((f32[64,1024]{1,0:T(8,128)S(1)}, f32[64,1024]{1,0:T(8,128)S(1)}, u32[]{:S(2)}, u32[]{:S(2)}) %collective-permute-start.19) | collective-permute-done | bytes 262176 | tf_op jit(solution)/shard_map/ppermute | solution.py:91
  51.6 1.5 %collective-permute-start.20 = (f32[64,512]{1,0:T(8,128)S(1)}, f32[64,512]{1,0:T(8,128)S(1)}, u32[]{:S(2)}, u32[]{:S(2)}) collective-permute-start(f32[64,512]{1,0:T(8,128)S(1)} %constant_dynamic-slice_fusion.5), channel_id=1, source_target_pairs={{0,2},{2,0},{4,6},{6,4},{8,10},{10,8},{12,14},{14,12},{1,3},{3,1},... | collective-permute-start | bytes 393224 | tf_op jit(solution)/shard_map/ppermute | solution.py:91
  55.5 1.8 %collective-permute-done.8 = f32[64,512]{1,0:T(8,128)S(1)} collective-permute-done((f32[64,512]{1,0:T(8,128)S(1)}, f32[64,512]{1,0:T(8,128)S(1)}, u32[]{:S(2)}, u32[]{:S(2)}) %collective-permute-start.8) | collective-permute-done | bytes 131104 | tf_op jit(solution)/shard_map/ppermute | solution.py:91
  58.7 1.7 %collective-permute-start.21 = (f32[64,256]{1,0:T(8,128)S(1)}, f32[64,256]{1,0:T(8,128)S(1)}, u32[]{:S(2)}, u32[]{:S(2)}) collective-permute-start(f32[64,256]{1,0:T(8,128)S(1)} %constant_dynamic-slice_fusion.10), channel_id=1, source_target_pairs={{0,8},{2,10},{4,12},{6,14},{8,0},{10,2},{12,4},{14,6},{1,9},{3,11}... | collective-permute-start | bytes 196616 | tf_op jit(solution)/shard_map/ppermute | solution.py:91
  61.9 1.7 %collective-permute-start.3 = (f32[64,256]{1,0:T(8,128)S(1)}, f32[64,256]{1,0:T(8,128)S(1)}, u32[]{:S(2)}, u32[]{:S(2)}) collective-permute-start(f32[64,256]{1,0:T(8,128)S(1)} %constant_dynamic-slice_fusion.13), channel_id=1, source_target_pairs={{0,8},{2,10},{4,12},{6,14},{8,0},{10,2},{12,4},{14,6},{1,9},{3,11}... | collective-permute-start | bytes 196616 | tf_op jit(solution)/shard_map/ppermute | solution.py:91
  63.6 4.8 %collective-permute-done.9 = f32[64,256]{1,0:T(8,128)S(1)} collective-permute-done((f32[64,256]{1,0:T(8,128)S(1)}, f32[64,256]{1,0:T(8,128)S(1)}, u32[]{:S(2)}, u32[]{:S(2)}) %collective-permute-start.9) | collective-permute-done | bytes 65568 | tf_op jit(solution)/shard_map/ppermute | solution.py:91
  68.4 1.4 %collective-permute-done.21 = f32[64,256]{1,0:T(8,128)S(1)} collective-permute-done((f32[64,256]{1,0:T(8,128)S(1)}, f32[64,256]{1,0:T(8,128)S(1)}, u32[]{:S(2)}, u32[]{:S(2)}) %collective-permute-start.21) | collective-permute-done | bytes 65568 | tf_op jit(solution)/shard_map/ppermute | solution.py:91
  69.9 2.9 %collective-permute-start.22 = (bf16[64,256]{1,0:T(8,128)(2,1)S(1)}, bf16[64,256]{1,0:T(8,128)(2,1)S(1)}, u32[]{:S(2)}, u32[]{:S(2)}) collective-permute-start(bf16[64,256]{1,0:T(8,128)(2,1)S(1)} %get-tuple-element.52), channel_id=1, source_target_pairs={{0,8},{2,10},{4,12},{6,14},{8,0},{10,2},{12,4},{14,6},{1,9},{3,11}... | collective-permute-start | bytes 98312 | tf_op jit(solution)/shard_map/ppermute | solution.py:91
  73.0 2.8 %collective-permute-start.16 = (bf16[64,256]{1,0:T(8,128)(2,1)S(1)}, bf16[64,256]{1,0:T(8,128)(2,1)S(1)}, u32[]{:S(2)}, u32[]{:S(2)}) collective-permute-start(bf16[64,256]{1,0:T(8,128)(2,1)S(1)} %get-tuple-element.50), channel_id=1, source_target_pairs={{0,8},{2,10},{4,12},{6,14},{8,0},{10,2},{12,4},{14,6},{1,9},{3,11}... | collective-permute-start | bytes 98312 | tf_op jit(solution)/shard_map/ppermute | solution.py:91
  78.5 2.1 %collective-permute-start.17 = (bf16[2,64,256]{2,1,0:T(8,128)(2,1)S(1)}, bf16[2,64,256]{2,1,0:T(8,128)(2,1)S(1)}, u32[]{:S(2)}, u32[]{:S(2)}) collective-permute-start(bf16[2,64,256]{2,1,0:T(8,128)(2,1)S(1)} %pad_maximum_fusion.8), channel_id=1, source_target_pairs={{0,4},{2,6},{4,0},{6,2},{8,12},{10,14},{12,8},{14,10},{1,5},{3,7},... | collective-permute-start | bytes 196616 | tf_op jit(solution)/shard_map/ppermute | solution.py:91
  80.7 1.8 %collective-permute-done.23 = bf16[2,64,256]{2,1,0:T(8,128)(2,1)S(1)} collective-permute-done((bf16[2,64,256]{2,1,0:T(8,128)(2,1)S(1)}, bf16[2,64,256]{2,1,0:T(8,128)(2,1)S(1)}, u32[]{:S(2)}, u32[]{:S(2)}) %collective-permute-start.23) | collective-permute-done | bytes 65568 | tf_op jit(solution)/shard_map/ppermute | solution.py:91
  83.2 1.5 %collective-permute-start.6 = (bf16[2,2,64,256]{3,2,1,0:T(8,128)(2,1)S(1)}, bf16[2,2,64,256]{3,2,1,0:T(8,128)(2,1)S(1)}, u32[]{:S(2)}, u32[]{:S(2)}) collective-permute-start(bf16[2,2,64,256]{3,2,1,0:T(8,128)(2,1)S(1)} %pad_maximum_fusion.2), channel_id=1, source_target_pairs={{0,2},{2,0},{4,6},{6,4},{8,10},{10,8},{12,14},{14,12},{1,3},{3,1},... | collective-permute-start | bytes 393224 | tf_op jit(solution)/shard_map/ppermute | solution.py:91
  85.7 1.9 %collective-permute-done.24 = bf16[2,2,64,256]{3,2,1,0:T(8,128)(2,1)S(1)} collective-permute-done((bf16[2,2,64,256]{3,2,1,0:T(8,128)(2,1)S(1)}, bf16[2,2,64,256]{3,2,1,0:T(8,128)(2,1)S(1)}, u32[]{:S(2)}, u32[]{:S(2)}) %collective-permute-start.24) | collective-permute-done | bytes 131104 | tf_op jit(solution)/shard_map/ppermute | solution.py:91
  92.1 27.7 %shard_map.148 = (bf16[2048,2048]{1,0:T(8,128)(2,1)}, bf16[2048,2048]{1,0:T(8,128)(2,1)}, bf16[2048,2048]{1,0:T(8,128)(2,1)}) custom-call(bf16[2048,256]{1,0:T(8,128)(2,1)} %bitcast.93, bf16[8,256,256]{2,1,0:T(8,128)(2,1)} %pad_maximum_fusion.1.err_ref, bf16[256,2048]{1,0:T(8,128)(2,1)} %copy-done.1, bf16[2048,2048]{1,0:T(8,128)(2,1)} %bitcast.87, ...), custom_call_target="tpu_custom_call" | custom-call | tf_op jit(solution)/shard_map/pallas_call | solution.py:72
  (120 shorter events, 19.7 us)
Async XLA Ops:
  2.4 21.7 %all-to-all-start = ((bf16[8,128,256]{2,1,0:T(8,128)(2,1)}), bf16[8,128,256]{2,1,0:T(8,128)(2,1)S(1)}, u32[]{:S(2)}, u32[]{:S(2)}) async-start(bf16[8,128,256]{2,1,0:T(8,128)(2,1)} %broadcast_in_dim.46), calls=%async_computation | async-start | bytes 1048576 | tf_op jit(solution)/shard_map/all_to_all | solution.py:194
  37.6 9.2 %collective-permute-start.7 = (f32[64,1024]{1,0:T(8,128)S(1)}, f32[64,1024]{1,0:T(8,128)S(1)}, u32[]{:S(2)}, u32[]{:S(2)}) collective-permute-start(f32[64,1024]{1,0:T(8,128)S(1)} %constant_dynamic-slice_fusion.9), channel_id=1, source_target_pairs={{0,4},{2,6},{4,0},{6,2},{8,12},{10,14},{12,8},{14,10},{1,5},{3,7},... | collective-permute-start | bytes 786440 | tf_op jit(solution)/shard_map/ppermute | solution.py:91
  38.4 13.2 %collective-permute-start.19 = (f32[64,1024]{1,0:T(8,128)S(1)}, f32[64,1024]{1,0:T(8,128)S(1)}, u32[]{:S(2)}, u32[]{:S(2)}) collective-permute-start(f32[64,1024]{1,0:T(8,128)S(1)} %constant_dynamic-slice_fusion), channel_id=1, source_target_pairs={{0,4},{2,6},{4,0},{6,2},{8,12},{10,14},{12,8},{14,10},{1,5},{3,7},... | collective-permute-start | bytes 786440 | tf_op jit(solution)/shard_map/ppermute | solution.py:91
  39.6 13.5 %collective-permute-start.13 = (f32[64,1024]{1,0:T(8,128)S(1)}, f32[64,1024]{1,0:T(8,128)S(1)}, u32[]{:S(2)}, u32[]{:S(2)}) collective-permute-start(f32[64,1024]{1,0:T(8,128)S(1)} %constant_dynamic-slice_fusion.3), channel_id=1, source_target_pairs={{0,2},{2,0},{4,6},{6,4},{8,10},{10,8},{12,14},{14,12},{1,3},{3,1},... | collective-permute-start | bytes 786440 | tf_op jit(solution)/shard_map/ppermute | solution.py:91
  41.1 13.4 %collective-permute-start.1 = (f32[64,1024]{1,0:T(8,128)S(1)}, f32[64,1024]{1,0:T(8,128)S(1)}, u32[]{:S(2)}, u32[]{:S(2)}) collective-permute-start(f32[64,1024]{1,0:T(8,128)S(1)} %constant_dynamic-slice_fusion.15), channel_id=1, source_target_pairs={{0,2},{2,0},{4,6},{6,4},{8,10},{10,8},{12,14},{14,12},{1,3},{3,1},... | collective-permute-start | bytes 786440 | tf_op jit(solution)/shard_map/ppermute | solution.py:91
  46.8 10.4 %collective-permute-start.8 = (f32[64,512]{1,0:T(8,128)S(1)}, f32[64,512]{1,0:T(8,128)S(1)}, u32[]{:S(2)}, u32[]{:S(2)}) collective-permute-start(f32[64,512]{1,0:T(8,128)S(1)} %constant_dynamic-slice_fusion.8), channel_id=1, source_target_pairs={{0,2},{2,0},{4,6},{6,4},{8,10},{10,8},{12,14},{14,12},{1,3},{3,1},... | collective-permute-start | bytes 393224 | tf_op jit(solution)/shard_map/ppermute | solution.py:91
  51.6 7.0 %collective-permute-start.20 = (f32[64,512]{1,0:T(8,128)S(1)}, f32[64,512]{1,0:T(8,128)S(1)}, u32[]{:S(2)}, u32[]{:S(2)}) collective-permute-start(f32[64,512]{1,0:T(8,128)S(1)} %constant_dynamic-slice_fusion.5), channel_id=1, source_target_pairs={{0,2},{2,0},{4,6},{6,4},{8,10},{10,8},{12,14},{14,12},{1,3},{3,1},... | collective-permute-start | bytes 393224 | tf_op jit(solution)/shard_map/ppermute | solution.py:91
  53.2 7.2 %collective-permute-start.14 = (f32[64,512]{1,0:T(8,128)S(1)}, f32[64,512]{1,0:T(8,128)S(1)}, u32[]{:S(2)}, u32[]{:S(2)}) collective-permute-start(f32[64,512]{1,0:T(8,128)S(1)} %constant_dynamic-slice_fusion.2), channel_id=1, source_target_pairs={{0,4},{2,6},{4,0},{6,2},{8,12},{10,14},{12,8},{14,10},{1,5},{3,7},... | collective-permute-start | bytes 393224 | tf_op jit(solution)/shard_map/ppermute | solution.py:91
  54.6 7.3 %collective-permute-start.2 = (f32[64,512]{1,0:T(8,128)S(1)}, f32[64,512]{1,0:T(8,128)S(1)}, u32[]{:S(2)}, u32[]{:S(2)}) collective-permute-start(f32[64,512]{1,0:T(8,128)S(1)} %constant_dynamic-slice_fusion.14), channel_id=1, source_target_pairs={{0,4},{2,6},{4,0},{6,2},{8,12},{10,14},{12,8},{14,10},{1,5},{3,7},... | collective-permute-start | bytes 393224 | tf_op jit(solution)/shard_map/ppermute | solution.py:91
  57.3 11.1 %collective-permute-start.9 = (f32[64,256]{1,0:T(8,128)S(1)}, f32[64,256]{1,0:T(8,128)S(1)}, u32[]{:S(2)}, u32[]{:S(2)}) collective-permute-start(f32[64,256]{1,0:T(8,128)S(1)} %constant_dynamic-slice_fusion.7), channel_id=1, source_target_pairs={{0,8},{2,10},{4,12},{6,14},{8,0},{10,2},{12,4},{14,6},{1,9},{3,11}... | collective-permute-start | bytes 196616 | tf_op jit(solution)/shard_map/ppermute | solution.py:91
  58.7 11.1 %collective-permute-start.21 = (f32[64,256]{1,0:T(8,128)S(1)}, f32[64,256]{1,0:T(8,128)S(1)}, u32[]{:S(2)}, u32[]{:S(2)}) collective-permute-start(f32[64,256]{1,0:T(8,128)S(1)} %constant_dynamic-slice_fusion.10), channel_id=1, source_target_pairs={{0,8},{2,10},{4,12},{6,14},{8,0},{10,2},{12,4},{14,6},{1,9},{3,11}... | collective-permute-start | bytes 196616 | tf_op jit(solution)/shard_map/ppermute | solution.py:91
  60.5 12.4 %collective-permute-start.15 = (f32[64,256]{1,0:T(8,128)S(1)}, f32[64,256]{1,0:T(8,128)S(1)}, u32[]{:S(2)}, u32[]{:S(2)}) collective-permute-start(f32[64,256]{1,0:T(8,128)S(1)} %constant_dynamic-slice_fusion.1), channel_id=1, source_target_pairs={{0,8},{2,10},{4,12},{6,14},{8,0},{10,2},{12,4},{14,6},{1,9},{3,11}... | collective-permute-start | bytes 196616 | tf_op jit(solution)/shard_map/ppermute | solution.py:91
  61.9 11.0 %collective-permute-start.3 = (f32[64,256]{1,0:T(8,128)S(1)}, f32[64,256]{1,0:T(8,128)S(1)}, u32[]{:S(2)}, u32[]{:S(2)}) collective-permute-start(f32[64,256]{1,0:T(8,128)S(1)} %constant_dynamic-slice_fusion.13), channel_id=1, source_target_pairs={{0,8},{2,10},{4,12},{6,14},{8,0},{10,2},{12,4},{14,6},{1,9},{3,11}... | collective-permute-start | bytes 196616 | tf_op jit(solution)/shard_map/ppermute | solution.py:91
  69.8 6.3 %collective-permute-start.10 = (bf16[64,256]{1,0:T(8,128)(2,1)S(1)}, bf16[64,256]{1,0:T(8,128)(2,1)S(1)}, u32[]{:S(2)}, u32[]{:S(2)}) collective-permute-start(bf16[64,256]{1,0:T(8,128)(2,1)S(1)} %get-tuple-element.51), channel_id=1, source_target_pairs={{0,8},{2,10},{4,12},{6,14},{8,0},{10,2},{12,4},{14,6},{1,9},{3,11}... | collective-permute-start | bytes 98312 | tf_op jit(solution)/shard_map/ppermute | solution.py:91
  69.9 7.5 %collective-permute-start.22 = (bf16[64,256]{1,0:T(8,128)(2,1)S(1)}, bf16[64,256]{1,0:T(8,128)(2,1)S(1)}, u32[]{:S(2)}, u32[]{:S(2)}) collective-permute-start(bf16[64,256]{1,0:T(8,128)(2,1)S(1)} %get-tuple-element.52), channel_id=1, source_target_pairs={{0,8},{2,10},{4,12},{6,14},{8,0},{10,2},{12,4},{14,6},{1,9},{3,11}... | collective-permute-start | bytes 98312 | tf_op jit(solution)/shard_map/ppermute | solution.py:91
  72.9 5.5 %collective-permute-start.4 = (bf16[64,256]{1,0:T(8,128)(2,1)S(1)}, bf16[64,256]{1,0:T(8,128)(2,1)S(1)}, u32[]{:S(2)}, u32[]{:S(2)}) collective-permute-start(bf16[64,256]{1,0:T(8,128)(2,1)S(1)} %get-tuple-element.49), channel_id=1, source_target_pairs={{0,8},{2,10},{4,12},{6,14},{8,0},{10,2},{12,4},{14,6},{1,9},{3,11}... | collective-permute-start | bytes 98312 | tf_op jit(solution)/shard_map/ppermute | solution.py:91
  73.0 5.4 %collective-permute-start.16 = (bf16[64,256]{1,0:T(8,128)(2,1)S(1)}, bf16[64,256]{1,0:T(8,128)(2,1)S(1)}, u32[]{:S(2)}, u32[]{:S(2)}) collective-permute-start(bf16[64,256]{1,0:T(8,128)(2,1)S(1)} %get-tuple-element.50), channel_id=1, source_target_pairs={{0,8},{2,10},{4,12},{6,14},{8,0},{10,2},{12,4},{14,6},{1,9},{3,11}... | collective-permute-start | bytes 98312 | tf_op jit(solution)/shard_map/ppermute | solution.py:91
  77.5 5.0 %collective-permute-start.23 = (bf16[2,64,256]{2,1,0:T(8,128)(2,1)S(1)}, bf16[2,64,256]{2,1,0:T(8,128)(2,1)S(1)}, u32[]{:S(2)}, u32[]{:S(2)}) collective-permute-start(bf16[2,64,256]{2,1,0:T(8,128)(2,1)S(1)} %pad_maximum_fusion.9), channel_id=1, source_target_pairs={{0,2},{2,0},{4,6},{6,4},{8,10},{10,8},{12,14},{14,12},{1,3},{3,1},... | collective-permute-start | bytes 196616 | tf_op jit(solution)/shard_map/ppermute | solution.py:91
  78.4 4.8 %collective-permute-start.5 = (bf16[2,64,256]{2,1,0:T(8,128)(2,1)S(1)}, bf16[2,64,256]{2,1,0:T(8,128)(2,1)S(1)}, u32[]{:S(2)}, u32[]{:S(2)}) collective-permute-start(bf16[2,64,256]{2,1,0:T(8,128)(2,1)S(1)} %pad_maximum_fusion.6), channel_id=1, source_target_pairs={{0,4},{2,6},{4,0},{6,2},{8,12},{10,14},{12,8},{14,10},{1,5},{3,7},... | collective-permute-start | bytes 196616 | tf_op jit(solution)/shard_map/ppermute | solution.py:91
  78.5 6.2 %collective-permute-start.17 = (bf16[2,64,256]{2,1,0:T(8,128)(2,1)S(1)}, bf16[2,64,256]{2,1,0:T(8,128)(2,1)S(1)}, u32[]{:S(2)}, u32[]{:S(2)}) collective-permute-start(bf16[2,64,256]{2,1,0:T(8,128)(2,1)S(1)} %pad_maximum_fusion.8), channel_id=1, source_target_pairs={{0,4},{2,6},{4,0},{6,2},{8,12},{10,14},{12,8},{14,10},{1,5},{3,7},... | collective-permute-start | bytes 196616 | tf_op jit(solution)/shard_map/ppermute | solution.py:91
  80.6 5.0 %collective-permute-start.12 = (bf16[2,2,64,256]{3,2,1,0:T(8,128)(2,1)S(1)}, bf16[2,2,64,256]{3,2,1,0:T(8,128)(2,1)S(1)}, u32[]{:S(2)}, u32[]{:S(2)}) collective-permute-start(bf16[2,2,64,256]{3,2,1,0:T(8,128)(2,1)S(1)} %pad_maximum_fusion.3), channel_id=1, source_target_pairs={{0,4},{2,6},{4,0},{6,2},{8,12},{10,14},{12,8},{14,10},{1,5},{3,7},... | collective-permute-start | bytes 393224 | tf_op jit(solution)/shard_map/ppermute | solution.py:91
  82.5 5.0 %collective-permute-start.24 = (bf16[2,2,64,256]{3,2,1,0:T(8,128)(2,1)S(1)}, bf16[2,2,64,256]{3,2,1,0:T(8,128)(2,1)S(1)}, u32[]{:S(2)}, u32[]{:S(2)}) collective-permute-start(bf16[2,2,64,256]{3,2,1,0:T(8,128)(2,1)S(1)} %pad_maximum_fusion.5), channel_id=1, source_target_pairs={{0,4},{2,6},{4,0},{6,2},{8,12},{10,14},{12,8},{14,10},{1,5},{3,7},... | collective-permute-start | bytes 393224 | tf_op jit(solution)/shard_map/ppermute | solution.py:91
  83.2 5.0 %collective-permute-start.6 = (bf16[2,2,64,256]{3,2,1,0:T(8,128)(2,1)S(1)}, bf16[2,2,64,256]{3,2,1,0:T(8,128)(2,1)S(1)}, u32[]{:S(2)}, u32[]{:S(2)}) collective-permute-start(bf16[2,2,64,256]{3,2,1,0:T(8,128)(2,1)S(1)} %pad_maximum_fusion.2), channel_id=1, source_target_pairs={{0,2},{2,0},{4,6},{6,4},{8,10},{10,8},{12,14},{14,12},{1,3},{3,1},... | collective-permute-start | bytes 393224 | tf_op jit(solution)/shard_map/ppermute | solution.py:91
  84.8 5.0 %collective-permute-start.18 = (bf16[2,2,64,256]{3,2,1,0:T(8,128)(2,1)S(1)}, bf16[2,2,64,256]{3,2,1,0:T(8,128)(2,1)S(1)}, u32[]{:S(2)}, u32[]{:S(2)}) collective-permute-start(bf16[2,2,64,256]{3,2,1,0:T(8,128)(2,1)S(1)} %pad_maximum_fusion.4), channel_id=1, source_target_pairs={{0,2},{2,0},{4,6},{6,4},{8,10},{10,8},{12,14},{14,12},{1,3},{3,1},... | collective-permute-start | bytes 393224 | tf_op jit(solution)/shard_map/ppermute | solution.py:91
  (11 other events, 124.5 us)

commit v20 on v19

--- a/solution.py
+++ b/solution.py
@@ -24,17 +24,21 @@
     dec32 = dec.astype(jnp.float32)
     row_norm = jnp.sqrt(jnp.sum(dec32 * dec32, axis=1, keepdims=True) + 1e-06)
     if stacked:
-        blocks, tokens, part = err_ref.shape
-        back_t = lax.dot_general(
-            dec[:, :part], err_ref[0], (((1,), (1,)), ((), ())), preferred_element_type=jnp.float32
-        )
-        for b in range(1, blocks):
-            back_t = back_t + lax.dot_general(
-                dec[:, b * part : (b + 1) * part],
-                err_ref[b],
-                (((1,), (1,)), ((), ())),
-                preferred_element_type=jnp.float32,
-            )
+        groups, blocks, group_tokens, part = err_ref.shape
+        tokens = groups * group_tokens
+        pieces = []
+        for g in range(groups):
+            piece = None
+            for k in range(blocks):
+                term = lax.dot_general(
+                    dec[:, k * part : (k + 1) * part],
+                    err_ref[g, stacked[g][k]],
+                    (((1,), (1,)), ((), ())),
+                    preferred_element_type=jnp.float32,
+                )
+                piece = term if piece is None else piece + term
+            pieces.append(piece)
+        back_t = jnp.concatenate(pieces, axis=1)
     else:
         back_t = jnp.dot(dec, err_ref[...], preferred_element_type=jnp.float32)
         tokens = err_ref.shape[1]
@@ -54,17 +58,20 @@
     m2_out[...] = moment_two.astype(jnp.bfloat16)
 
 
-def tail(pre_t, error_blocks, centered, decoder, weight_in, first, second, tile=512):
+def tail(pre_t, error_blocks, owners, centered, decoder, weight_in, first, second, tile=512):
     n_lat, width = decoder.shape
     if n_lat % tile:
         tile = n_lat
-    tokens = error_blocks.shape[1]
-    stacked = error_blocks.shape[0] <= 8
-    if stacked:
+    groups, blocks, group_tokens, part = error_blocks.shape
+    tokens = groups * group_tokens
+    if blocks <= 8:
+        stacked = tuple(tuple(o) for o in owners)
         error_in = error_blocks
-        error_spec = pl.BlockSpec(error_blocks.shape, lambda i: (0, 0, 0))
+        error_spec = pl.BlockSpec(error_blocks.shape, lambda i: (0, 0, 0, 0))
     else:
-        error_in = jnp.transpose(error_blocks, (0, 2, 1)).reshape(width, tokens)
+        stacked = None
+        ordered = jnp.stack([error_blocks[g][jnp.array(owners[g])] for g in range(groups)])
+        error_in = jnp.transpose(ordered, (1, 3, 0, 2)).reshape(width, tokens)
         error_spec = pl.BlockSpec((width, tokens), lambda i: (0, 0))
     row_block = pl.BlockSpec((tile, width), lambda i: (i, 0))
     whole = pl.BlockSpec((tokens, width), lambda i: (0, 0))
@@ -219,7 +226,7 @@
     error_parts = []
     for part in range(4):
         rows = slice(part * chunk, (part + 1) * chunk)
-        order = (first, second)[part % 2]
+        order = (first, second)[part // 2]
         total, block = _halving_cols(partial_sum[rows], "lat", lat_size, order)
         start = block * width
         sample_cols = lax.dynamic_slice_in_dim(sample[rows], start, width, axis=1)
@@ -228,11 +235,20 @@
         error_cols = (
             (total + bias_cols - sample_cols.astype(jnp.float32)) * keep_cols_f
         ).astype(jnp.bfloat16)
-        stacked = _doubling_gather(error_cols, "lat", lat_size, order[::-1])
-        error_parts.append(stacked[jnp.array(_block_owners(lat_size, order))])
-    error_blocks = jnp.concatenate(error_parts, axis=1)
+        error_parts.append(_doubling_gather(error_cols, "lat", lat_size, order[::-1]))
+    error_blocks = jnp.stack(
+        [jnp.concatenate(error_parts[0:2], axis=1), jnp.concatenate(error_parts[2:4], axis=1)]
+    )
+    owners = [_block_owners(lat_size, first), _block_owners(lat_size, second)]
     updated, moment_one, moment_two = tail(
-        latent_t, error_blocks, centered, decoder, weight_in, first_moment[0], second_moment[0]
+        latent_t,
+        error_blocks,
+        owners,
+        centered,
+        decoder,
+        weight_in,
+        first_moment[0],
+        second_moment[0],
     )
     return updated[None], moment_one[None], moment_two[None]
 

time: 120 us -> 118 us (0.983)
  blocking collectives: 0 us -> 21.6 us
  waiting for transfers between devices: 38.6 us -> 23.5 us
  starting transfers between devices: 33.5 us -> 29.1 us
  local copies, waits for them, and re-layouts: 6.26 us -> 3.22 us
  other arithmetic: 3.64 us -> 2.33 us
    all_to_all x0 -> x1, blocking collectives: none -> 21.6 us  [local(): act_blocks = lax.all_to_all(copies, 'lat', 0, 0, tiled=True)]
    all_to_all x1 -> x0, waiting for transfers between devices: 13.1 us -> none  [local(): act_blocks = lax.all_to_all(copies, 'lat', 0, 0, tiled=True)]
    all_to_all x1 -> x0, starting transfers between devices: 7.25 us -> none  [local(): act_blocks = lax.all_to_all(copies, 'lat', 0, 0, tiled=True)]
    ppermute x24, starting transfers between devices: 26.2 us -> 29 us  [_pair_swap(): return lax.ppermute(value, axis, [(i, i ^ mask) for i in range(size)])]
    gather x4 -> x0, local copies, waits for them, and re-layouts: 2.25 us -> none  [local(): error_parts.append(stacked[jnp.array(_block_owners(lat_size, order))])]
    ppermute x24, waiting for transfers between devices: 23.7 us -> 21.8 us  [_pair_swap(): return lax.ppermute(value, axis, [(i, i ^ mask) for i in range(size)])]
  transfers between devices with their start and end apart: 26 -> 25, of which waited for: 16 -> 13; matrix products, arithmetic and copies ran while one was open for 3% -> 1% of each run, Pallas kernels for 0% -> 0%
where the time goes in v20:
time: 118 us
  starting transfers between devices  29.1 us (25%)
  Pallas kernels  27.7 us (23%)
  waiting for transfers between devices  23.5 us (20%)
  blocking collectives  21.6 us (18%)
  matrix products  8.84 us (7%)
  local copies, waits for them, and re-layouts  3.22 us (3%)
  other arithmetic  2.33 us (2%)
  between operations  1.25 us (1%)
    ppermute x24, starting transfers between devices, _pair_swap(): return lax.ppermute(value, axis, [(i, i ^ mask) for i in range(size)])  29 us
    pallas_call x1, Pallas kernels, tail(): pl.pallas_call(functools.partial(_tail_kernel, stacked), grid=(n_lat // t...  27.7 us
    ppermute x24, waiting for transfers between devices, _pair_swap(): return lax.ppermute(value, axis, [(i, i ^ mask) for i in range(size)])  21.8 us
    all_to_all x1, blocking collectives, local(): act_blocks = lax.all_to_all(copies, 'lat', 0, 0, tiled=True)  21.6 us
    dot_general x1, matrix products, local(): lax.dot_general(weight_in, centered, (((1,), (1,)), ((), ())), preferred_...  6.5 us
  transfers between devices with their start and end apart: 25, of which 13 were waited for; matrix products, arithmetic and copies ran while one was open for 1% of the time, Pallas kernels for 0%

profile of v20, /device:TPU:0, one launch (start us, length us, event | category | flops | bytes accessed | tf_op | source)
XLA Modules:
  0.0 117.6 jit_solution(4055404186755656039)
XLA Ops:
  1.6 21.6 %all_to_all.5 = bf16[8,128,256]{2,1,0:T(8,128)(2,1)S(1)} all-to-all(bf16[8,128,256]{2,1,0:T(8,128)(2,1)S(1)} %broadcast_in_dim.19), channel_id=1, replica_groups=mesh['groups'=2,'lat'=8,'seed'=2] {'lat'}, dimensions={0} | all-to-all | bytes 1048576 | tf_op jit(solution)/shard_map/all_to_all | solution.py:201
  23.4 1.8 %collective-permute-done = bf16[128,2048]{1,0:T(8,128)(2,1)S(1)} collective-permute-done((bf16[128,2048]{1,0:T(8,128)(2,1)S(1)}, bf16[128,2048]{1,0:T(8,128)(2,1)S(1)}, u32[]{:S(2)}, u32[]{:S(2)}) %collective-permute-start) | collective-permute-done | bytes 524320 | tf_op jit(solution)/shard_map/ppermute | solution.py:203
  25.3 1.4 %gather_fusion = bf16[256,2048]{1,0:T(8,128)(2,1)S(1)} fusion(bf16[256,2048]{1,0:T(8,128)(2,1)S(1)} %pad_maximum_fusion, s32[1024]{0:T(1024)S(1)} %pad_clamp_fusion), kind=kCustom, calls=%fused_computation | custom fusion | bytes 2098176 | tf_op jit(solution)/shard_map/jit(_take)/gather | solution.py:210
  27.4 6.5 %fusion.1 = bf16[256,2048]{0,1:T(8,128)(2,1)S(1)} fusion(bf16[256,2048]{1,0:T(8,128)(2,1)S(1)} %get-tuple-element.9.cen_ref, f32[2048]{0:T(1024)S(1)} %bitcast.115, bf16[1,2048,2048]{2,1,0:T(8,128)(2,1)} %param.12), kind=kOutput, calls=%fused_computation.3 | convolution fusion | flops 2149056512 | bytes 10493952 | tf_op jit(solution)/shard_map/dot_general | solution.py:216
  33.9 2.3 %fusion.2 = f32[256,2048]{1,0:T(8,128)S(1)} fusion(bf16[256,2048]{0,1:T(8,128)(2,1)S(1)} %fusion.1, bf16[1,2048,2048]{2,1,0:T(8,128)(2,1)S(1)} %bitcast.93), kind=kOutput, calls=%fused_computation.80 | convolution fusion | flops 2147483648 | bytes 11534336 | tf_op jit(solution)/shard_map/dot_general | solution.py:222
  36.6 1.2 %collective-permute-start.13 = (f32[64,1024]{1,0:T(8,128)S(1)}, f32[64,1024]{1,0:T(8,128)S(1)}, u32[]{:S(2)}, u32[]{:S(2)}) collective-permute-start(f32[64,1024]{1,0:T(8,128)S(1)} %constant_dynamic-slice_fusion.6), channel_id=1, source_target_pairs={{0,4},{2,6},{4,0},{6,2},{8,12},{10,14},{12,8},{14,10},{1,5},{3,7},... | collective-permute-start | bytes 786440 | tf_op jit(solution)/shard_map/ppermute | solution.py:98
  38.7 1.5 %collective-permute-start.7 = (f32[64,1024]{1,0:T(8,128)S(1)}, f32[64,1024]{1,0:T(8,128)S(1)}, u32[]{:S(2)}, u32[]{:S(2)}) collective-permute-start(f32[64,1024]{1,0:T(8,128)S(1)} %constant_dynamic-slice_fusion.9), channel_id=1, source_target_pairs={{0,2},{2,0},{4,6},{6,4},{8,10},{10,8},{12,14},{14,12},{1,3},{3,1},... | collective-permute-start | bytes 786440 | tf_op jit(solution)/shard_map/ppermute | solution.py:98
  40.8 5.0 %collective-permute-done.13 = f32[64,1024]{1,0:T(8,128)S(1)} collective-permute-done((f32[64,1024]{1,0:T(8,128)S(1)}, f32[64,1024]{1,0:T(8,128)S(1)}, u32[]{:S(2)}, u32[]{:S(2)}) %collective-permute-start.13) | collective-permute-done | bytes 262176 | tf_op jit(solution)/shard_map/ppermute | solution.py:98
  45.9 1.5 %collective-permute-start.14 = (f32[64,512]{1,0:T(8,128)S(1)}, f32[64,512]{1,0:T(8,128)S(1)}, u32[]{:S(2)}, u32[]{:S(2)}) collective-permute-start(f32[64,512]{1,0:T(8,128)S(1)} %constant_dynamic-slice_fusion.5), channel_id=1, source_target_pairs={{0,2},{2,0},{4,6},{6,4},{8,10},{10,8},{12,14},{14,12},{1,3},{3,1},... | collective-permute-start | bytes 393224 | tf_op jit(solution)/shard_map/ppermute | solution.py:98
  47.4 3.2 %collective-permute-done.19 = f32[64,1024]{1,0:T(8,128)S(1)} collective-permute-done((f32[64,1024]{1,0:T(8,128)S(1)}, f32[64,1024]{1,0:T(8,128)S(1)}, u32[]{:S(2)}, u32[]{:S(2)}) %collective-permute-start.19) | collective-permute-done | bytes 262176 | tf_op jit(solution)/shard_map/ppermute | solution.py:98
  50.7 1.5 %collective-permute-start.20 = (f32[64,512]{1,0:T(8,128)S(1)}, f32[64,512]{1,0:T(8,128)S(1)}, u32[]{:S(2)}, u32[]{:S(2)}) collective-permute-start(f32[64,512]{1,0:T(8,128)S(1)} %constant_dynamic-slice_fusion.11), channel_id=1, source_target_pairs={{0,2},{2,0},{4,6},{6,4},{8,10},{10,8},{12,14},{14,12},{1,3},{3,1},... | collective-permute-start | bytes 393224 | tf_op jit(solution)/shard_map/ppermute | solution.py:98
  54.8 1.5 %collective-permute-done.14 = f32[64,512]{1,0:T(8,128)S(1)} collective-permute-done((f32[64,512]{1,0:T(8,128)S(1)}, f32[64,512]{1,0:T(8,128)S(1)}, u32[]{:S(2)}, u32[]{:S(2)}) %collective-permute-start.14) | collective-permute-done | bytes 131104 | tf_op jit(solution)/shard_map/ppermute | solution.py:98
  57.8 1.7 %collective-permute-start.21 = (f32[64,256]{1,0:T(8,128)S(1)}, f32[64,256]{1,0:T(8,128)S(1)}, u32[]{:S(2)}, u32[]{:S(2)}) collective-permute-start(f32[64,256]{1,0:T(8,128)S(1)} %constant_dynamic-slice_fusion.2), channel_id=1, source_target_pairs={{0,8},{2,10},{4,12},{6,14},{8,0},{10,2},{12,4},{14,6},{1,9},{3,11}... | collective-permute-start | bytes 196616 | tf_op jit(solution)/shard_map/ppermute | solution.py:98
  59.5 1.4 %collective-permute-start.9 = (f32[64,256]{1,0:T(8,128)S(1)}, f32[64,256]{1,0:T(8,128)S(1)}, u32[]{:S(2)}, u32[]{:S(2)}) collective-permute-start(f32[64,256]{1,0:T(8,128)S(1)} %constant_dynamic-slice_fusion.7), channel_id=1, source_target_pairs={{0,8},{2,10},{4,12},{6,14},{8,0},{10,2},{12,4},{14,6},{1,9},{3,11}... | collective-permute-start | bytes 196616 | tf_op jit(solution)/shard_map/ppermute | solution.py:98
  60.9 1.7 %collective-permute-start.3 = (f32[64,256]{1,0:T(8,128)S(1)}, f32[64,256]{1,0:T(8,128)S(1)}, u32[]{:S(2)}, u32[]{:S(2)}) collective-permute-start(f32[64,256]{1,0:T(8,128)S(1)} %constant_dynamic-slice_fusion.13), channel_id=1, source_target_pairs={{0,8},{2,10},{4,12},{6,14},{8,0},{10,2},{12,4},{14,6},{1,9},{3,11}... | collective-permute-start | bytes 196616 | tf_op jit(solution)/shard_map/ppermute | solution.py:98
  62.6 5.0 %collective-permute-done.15 = f32[64,256]{1,0:T(8,128)S(1)} collective-permute-done((f32[64,256]{1,0:T(8,128)S(1)}, f32[64,256]{1,0:T(8,128)S(1)}, u32[]{:S(2)}, u32[]{:S(2)}) %collective-permute-start.15) | collective-permute-done | bytes 65568 | tf_op jit(solution)/shard_map/ppermute | solution.py:98
  67.6 1.4 %collective-permute-done.21 = f32[64,256]{1,0:T(8,128)S(1)} collective-permute-done((f32[64,256]{1,0:T(8,128)S(1)}, f32[64,256]{1,0:T(8,128)S(1)}, u32[]{:S(2)}, u32[]{:S(2)}) %collective-permute-start.21) | collective-permute-done | bytes 65568 | tf_op jit(solution)/shard_map/ppermute | solution.py:98
  69.1 2.9 %collective-permute-start.22 = (bf16[64,256]{1,0:T(8,128)(2,1)S(1)}, bf16[64,256]{1,0:T(8,128)(2,1)S(1)}, u32[]{:S(2)}, u32[]{:S(2)}) collective-permute-start(bf16[64,256]{1,0:T(8,128)(2,1)S(1)} %get-tuple-element.52), channel_id=1, source_target_pairs={{0,8},{2,10},{4,12},{6,14},{8,0},{10,2},{12,4},{14,6},{1,9},{3,11}... | collective-permute-start | bytes 98312 | tf_op jit(solution)/shard_map/ppermute | solution.py:98
  72.3 2.9 %collective-permute-start.10 = (bf16[64,256]{1,0:T(8,128)(2,1)S(1)}, bf16[64,256]{1,0:T(8,128)(2,1)S(1)}, u32[]{:S(2)}, u32[]{:S(2)}) collective-permute-start(bf16[64,256]{1,0:T(8,128)(2,1)S(1)} %get-tuple-element.50), channel_id=1, source_target_pairs={{0,8},{2,10},{4,12},{6,14},{8,0},{10,2},{12,4},{14,6},{1,9},{3,11}... | collective-permute-start | bytes 98312 | tf_op jit(solution)/shard_map/ppermute | solution.py:98
  77.5 2.1 %collective-permute-start.11 = (bf16[2,64,256]{2,1,0:T(8,128)(2,1)S(1)}, bf16[2,64,256]{2,1,0:T(8,128)(2,1)S(1)}, u32[]{:S(2)}, u32[]{:S(2)}) collective-permute-start(bf16[2,64,256]{2,1,0:T(8,128)(2,1)S(1)} %pad_maximum_fusion.7), channel_id=1, source_target_pairs={{0,4},{2,6},{4,0},{6,2},{8,12},{10,14},{12,8},{14,10},{1,5},{3,7},... | collective-permute-start | bytes 196616 | tf_op jit(solution)/shard_map/ppermute | solution.py:98
  81.9 1.6 %collective-permute-start.6 = (bf16[2,2,64,256]{3,2,1,0:T(8,128)(2,1)S(1)}, bf16[2,2,64,256]{3,2,1,0:T(8,128)(2,1)S(1)}, u32[]{:S(2)}, u32[]{:S(2)}) collective-permute-start(bf16[2,2,64,256]{3,2,1,0:T(8,128)(2,1)S(1)} %pad_maximum_fusion.2), channel_id=1, source_target_pairs={{0,2},{2,0},{4,6},{6,4},{8,10},{10,8},{12,14},{14,12},{1,3},{3,1},... | collective-permute-start | bytes 393224 | tf_op jit(solution)/shard_map/ppermute | solution.py:98
  83.6 1.4 %collective-permute-start.12 = (bf16[2,2,64,256]{3,2,1,0:T(8,128)(2,1)S(1)}, bf16[2,2,64,256]{3,2,1,0:T(8,128)(2,1)S(1)}, u32[]{:S(2)}, u32[]{:S(2)}) collective-permute-start(bf16[2,2,64,256]{3,2,1,0:T(8,128)(2,1)S(1)} %pad_maximum_fusion.3), channel_id=1, source_target_pairs={{0,2},{2,0},{4,6},{6,4},{8,10},{10,8},{12,14},{14,12},{1,3},{3,1},... | collective-permute-start | bytes 393224 | tf_op jit(solution)/shard_map/ppermute | solution.py:98
  87.1 1.5 %collective-permute-done.12 = bf16[2,2,64,256]{3,2,1,0:T(8,128)(2,1)S(1)} collective-permute-done((bf16[2,2,64,256]{3,2,1,0:T(8,128)(2,1)S(1)}, bf16[2,2,64,256]{3,2,1,0:T(8,128)(2,1)S(1)}, u32[]{:S(2)}, u32[]{:S(2)}) %collective-permute-start.12) | collective-permute-done | bytes 131104 | tf_op jit(solution)/shard_map/ppermute | solution.py:98
  89.9 27.7 %shard_map.112 = (bf16[2048,2048]{1,0:T(8,128)(2,1)}, bf16[2048,2048]{1,0:T(8,128)(2,1)}, bf16[2048,2048]{1,0:T(8,128)(2,1)}) custom-call(bf16[2048,256]{1,0:T(8,128)(2,1)} %bitcast.97, bf16[2,8,128,256]{3,2,1,0:T(8,128)(2,1)} %pad_maximum_fusion.1.err_ref, bf16[256,2048]{1,0:T(8,128)(2,1)} %copy-done.1, bf16[2048,2048]{1,0:T(8,128)(2,1)} %bitcast.91, ...), custom_call_target="tpu_custom_call" | custom-call | tf_op jit(solution)/shard_map/pallas_call | solution.py:79
  (113 shorter events, 16.2 us)
Async XLA Ops:
  36.6 9.2 %collective-permute-start.13 = (f32[64,1024]{1,0:T(8,128)S(1)}, f32[64,1024]{1,0:T(8,128)S(1)}, u32[]{:S(2)}, u32[]{:S(2)}) collective-permute-start(f32[64,1024]{1,0:T(8,128)S(1)} %constant_dynamic-slice_fusion.6), channel_id=1, source_target_pairs={{0,4},{2,6},{4,0},{6,2},{8,12},{10,14},{12,8},{14,10},{1,5},{3,7},... | collective-permute-start | bytes 786440 | tf_op jit(solution)/shard_map/ppermute | solution.py:98
  37.8 12.9 %collective-permute-start.19 = (f32[64,1024]{1,0:T(8,128)S(1)}, f32[64,1024]{1,0:T(8,128)S(1)}, u32[]{:S(2)}, u32[]{:S(2)}) collective-permute-start(f32[64,1024]{1,0:T(8,128)S(1)} %constant_dynamic-slice_fusion), channel_id=1, source_target_pairs={{0,4},{2,6},{4,0},{6,2},{8,12},{10,14},{12,8},{14,10},{1,5},{3,7},... | collective-permute-start | bytes 786440 | tf_op jit(solution)/shard_map/ppermute | solution.py:98
  38.7 13.5 %collective-permute-start.7 = (f32[64,1024]{1,0:T(8,128)S(1)}, f32[64,1024]{1,0:T(8,128)S(1)}, u32[]{:S(2)}, u32[]{:S(2)}) collective-permute-start(f32[64,1024]{1,0:T(8,128)S(1)} %constant_dynamic-slice_fusion.9), channel_id=1, source_target_pairs={{0,2},{2,0},{4,6},{6,4},{8,10},{10,8},{12,14},{14,12},{1,3},{3,1},... | collective-permute-start | bytes 786440 | tf_op jit(solution)/shard_map/ppermute | solution.py:98
  40.2 13.4 %collective-permute-start.1 = (f32[64,1024]{1,0:T(8,128)S(1)}, f32[64,1024]{1,0:T(8,128)S(1)}, u32[]{:S(2)}, u32[]{:S(2)}) collective-permute-start(f32[64,1024]{1,0:T(8,128)S(1)} %constant_dynamic-slice_fusion.15), channel_id=1, source_target_pairs={{0,2},{2,0},{4,6},{6,4},{8,10},{10,8},{12,14},{14,12},{1,3},{3,1},... | collective-permute-start | bytes 786440 | tf_op jit(solution)/shard_map/ppermute | solution.py:98
  45.9 10.4 %collective-permute-start.14 = (f32[64,512]{1,0:T(8,128)S(1)}, f32[64,512]{1,0:T(8,128)S(1)}, u32[]{:S(2)}, u32[]{:S(2)}) collective-permute-start(f32[64,512]{1,0:T(8,128)S(1)} %constant_dynamic-slice_fusion.5), channel_id=1, source_target_pairs={{0,2},{2,0},{4,6},{6,4},{8,10},{10,8},{12,14},{14,12},{1,3},{3,1},... | collective-permute-start | bytes 393224 | tf_op jit(solution)/shard_map/ppermute | solution.py:98
  50.7 7.0 %collective-permute-start.20 = (f32[64,512]{1,0:T(8,128)S(1)}, f32[64,512]{1,0:T(8,128)S(1)}, u32[]{:S(2)}, u32[]{:S(2)}) collective-permute-start(f32[64,512]{1,0:T(8,128)S(1)} %constant_dynamic-slice_fusion.11), channel_id=1, source_target_pairs={{0,2},{2,0},{4,6},{6,4},{8,10},{10,8},{12,14},{14,12},{1,3},{3,1},... | collective-permute-start | bytes 393224 | tf_op jit(solution)/shard_map/ppermute | solution.py:98
  52.3 7.2 %collective-permute-start.8 = (f32[64,512]{1,0:T(8,128)S(1)}, f32[64,512]{1,0:T(8,128)S(1)}, u32[]{:S(2)}, u32[]{:S(2)}) collective-permute-start(f32[64,512]{1,0:T(8,128)S(1)} %constant_dynamic-slice_fusion.8), channel_id=1, source_target_pairs={{0,4},{2,6},{4,0},{6,2},{8,12},{10,14},{12,8},{14,10},{1,5},{3,7},... | collective-permute-start | bytes 393224 | tf_op jit(solution)/shard_map/ppermute | solution.py:98
  53.6 7.3 %collective-permute-start.2 = (f32[64,512]{1,0:T(8,128)S(1)}, f32[64,512]{1,0:T(8,128)S(1)}, u32[]{:S(2)}, u32[]{:S(2)}) collective-permute-start(f32[64,512]{1,0:T(8,128)S(1)} %constant_dynamic-slice_fusion.14), channel_id=1, source_target_pairs={{0,4},{2,6},{4,0},{6,2},{8,12},{10,14},{12,8},{14,10},{1,5},{3,7},... | collective-permute-start | bytes 393224 | tf_op jit(solution)/shard_map/ppermute | solution.py:98
  56.4 11.3 %collective-permute-start.15 = (f32[64,256]{1,0:T(8,128)S(1)}, f32[64,256]{1,0:T(8,128)S(1)}, u32[]{:S(2)}, u32[]{:S(2)}) collective-permute-start(f32[64,256]{1,0:T(8,128)S(1)} %constant_dynamic-slice_fusion.4), channel_id=1, source_target_pairs={{0,8},{2,10},{4,12},{6,14},{8,0},{10,2},{12,4},{14,6},{1,9},{3,11}... | collective-permute-start | bytes 196616 | tf_op jit(solution)/shard_map/ppermute | solution.py:98
  57.8 11.3 %collective-permute-start.21 = (f32[64,256]{1,0:T(8,128)S(1)}, f32[64,256]{1,0:T(8,128)S(1)}, u32[]{:S(2)}, u32[]{:S(2)}) collective-permute-start(f32[64,256]{1,0:T(8,128)S(1)} %constant_dynamic-slice_fusion.2), channel_id=1, source_target_pairs={{0,8},{2,10},{4,12},{6,14},{8,0},{10,2},{12,4},{14,6},{1,9},{3,11}... | collective-permute-start | bytes 196616 | tf_op jit(solution)/shard_map/ppermute | solution.py:98
  59.5 12.6 %collective-permute-start.9 = (f32[64,256]{1,0:T(8,128)S(1)}, f32[64,256]{1,0:T(8,128)S(1)}, u32[]{:S(2)}, u32[]{:S(2)}) collective-permute-start(f32[64,256]{1,0:T(8,128)S(1)} %constant_dynamic-slice_fusion.7), channel_id=1, source_target_pairs={{0,8},{2,10},{4,12},{6,14},{8,0},{10,2},{12,4},{14,6},{1,9},{3,11}... | collective-permute-start | bytes 196616 | tf_op jit(solution)/shard_map/ppermute | solution.py:98
  60.9 11.1 %collective-permute-start.3 = (f32[64,256]{1,0:T(8,128)S(1)}, f32[64,256]{1,0:T(8,128)S(1)}, u32[]{:S(2)}, u32[]{:S(2)}) collective-permute-start(f32[64,256]{1,0:T(8,128)S(1)} %constant_dynamic-slice_fusion.13), channel_id=1, source_target_pairs={{0,8},{2,10},{4,12},{6,14},{8,0},{10,2},{12,4},{14,6},{1,9},{3,11}... | collective-permute-start | bytes 196616 | tf_op jit(solution)/shard_map/ppermute | solution.py:98
  69.1 6.0 %collective-permute-start.16 = (bf16[64,256]{1,0:T(8,128)(2,1)S(1)}, bf16[64,256]{1,0:T(8,128)(2,1)S(1)}, u32[]{:S(2)}, u32[]{:S(2)}) collective-permute-start(bf16[64,256]{1,0:T(8,128)(2,1)S(1)} %get-tuple-element.51), channel_id=1, source_target_pairs={{0,8},{2,10},{4,12},{6,14},{8,0},{10,2},{12,4},{14,6},{1,9},{3,11}... | collective-permute-start | bytes 98312 | tf_op jit(solution)/shard_map/ppermute | solution.py:98
  69.1 7.1 %collective-permute-start.22 = (bf16[64,256]{1,0:T(8,128)(2,1)S(1)}, bf16[64,256]{1,0:T(8,128)(2,1)S(1)}, u32[]{:S(2)}, u32[]{:S(2)}) collective-permute-start(bf16[64,256]{1,0:T(8,128)(2,1)S(1)} %get-tuple-element.52), channel_id=1, source_target_pairs={{0,8},{2,10},{4,12},{6,14},{8,0},{10,2},{12,4},{14,6},{1,9},{3,11}... | collective-permute-start | bytes 98312 | tf_op jit(solution)/shard_map/ppermute | solution.py:98
  72.1 5.2 %collective-permute-start.4 = (bf16[64,256]{1,0:T(8,128)(2,1)S(1)}, bf16[64,256]{1,0:T(8,128)(2,1)S(1)}, u32[]{:S(2)}, u32[]{:S(2)}) collective-permute-start(bf16[64,256]{1,0:T(8,128)(2,1)S(1)} %get-tuple-element.49), channel_id=1, source_target_pairs={{0,8},{2,10},{4,12},{6,14},{8,0},{10,2},{12,4},{14,6},{1,9},{3,11}... | collective-permute-start | bytes 98312 | tf_op jit(solution)/shard_map/ppermute | solution.py:98
  72.3 5.2 %collective-permute-start.10 = (bf16[64,256]{1,0:T(8,128)(2,1)S(1)}, bf16[64,256]{1,0:T(8,128)(2,1)S(1)}, u32[]{:S(2)}, u32[]{:S(2)}) collective-permute-start(bf16[64,256]{1,0:T(8,128)(2,1)S(1)} %get-tuple-element.50), channel_id=1, source_target_pairs={{0,8},{2,10},{4,12},{6,14},{8,0},{10,2},{12,4},{14,6},{1,9},{3,11}... | collective-permute-start | bytes 98312 | tf_op jit(solution)/shard_map/ppermute | solution.py:98
  75.1 4.4 %collective-permute-start.17 = (bf16[2,64,256]{2,1,0:T(8,128)(2,1)S(1)}, bf16[2,64,256]{2,1,0:T(8,128)(2,1)S(1)}, u32[]{:S(2)}, u32[]{:S(2)}) collective-permute-start(bf16[2,64,256]{2,1,0:T(8,128)(2,1)S(1)} %pad_maximum_fusion.8), channel_id=1, source_target_pairs={{0,2},{2,0},{4,6},{6,4},{8,10},{10,8},{12,14},{14,12},{1,3},{3,1},... | collective-permute-start | bytes 196616 | tf_op jit(solution)/shard_map/ppermute | solution.py:98
  76.3 4.3 %collective-permute-start.23 = (bf16[2,64,256]{2,1,0:T(8,128)(2,1)S(1)}, bf16[2,64,256]{2,1,0:T(8,128)(2,1)S(1)}, u32[]{:S(2)}, u32[]{:S(2)}) collective-permute-start(bf16[2,64,256]{2,1,0:T(8,128)(2,1)S(1)} %pad_maximum_fusion.9), channel_id=1, source_target_pairs={{0,2},{2,0},{4,6},{6,4},{8,10},{10,8},{12,14},{14,12},{1,3},{3,1},... | collective-permute-start | bytes 196616 | tf_op jit(solution)/shard_map/ppermute | solution.py:98
  77.4 4.5 %collective-permute-start.5 = (bf16[2,64,256]{2,1,0:T(8,128)(2,1)S(1)}, bf16[2,64,256]{2,1,0:T(8,128)(2,1)S(1)}, u32[]{:S(2)}, u32[]{:S(2)}) collective-permute-start(bf16[2,64,256]{2,1,0:T(8,128)(2,1)S(1)} %pad_maximum_fusion.6), channel_id=1, source_target_pairs={{0,4},{2,6},{4,0},{6,2},{8,12},{10,14},{12,8},{14,10},{1,5},{3,7},... | collective-permute-start | bytes 196616 | tf_op jit(solution)/shard_map/ppermute | solution.py:98
  77.5 6.0 %collective-permute-start.11 = (bf16[2,64,256]{2,1,0:T(8,128)(2,1)S(1)}, bf16[2,64,256]{2,1,0:T(8,128)(2,1)S(1)}, u32[]{:S(2)}, u32[]{:S(2)}) collective-permute-start(bf16[2,64,256]{2,1,0:T(8,128)(2,1)S(1)} %pad_maximum_fusion.7), channel_id=1, source_target_pairs={{0,4},{2,6},{4,0},{6,2},{8,12},{10,14},{12,8},{14,10},{1,5},{3,7},... | collective-permute-start | bytes 196616 | tf_op jit(solution)/shard_map/ppermute | solution.py:98
  79.6 5.3 %collective-permute-start.18 = (bf16[2,2,64,256]{3,2,1,0:T(8,128)(2,1)S(1)}, bf16[2,2,64,256]{3,2,1,0:T(8,128)(2,1)S(1)}, u32[]{:S(2)}, u32[]{:S(2)}) collective-permute-start(bf16[2,2,64,256]{3,2,1,0:T(8,128)(2,1)S(1)} %pad_maximum_fusion.4), channel_id=1, source_target_pairs={{0,4},{2,6},{4,0},{6,2},{8,12},{10,14},{12,8},{14,10},{1,5},{3,7},... | collective-permute-start | bytes 393224 | tf_op jit(solution)/shard_map/ppermute | solution.py:98
  80.6 5.4 %collective-permute-start.24 = (bf16[2,2,64,256]{3,2,1,0:T(8,128)(2,1)S(1)}, bf16[2,2,64,256]{3,2,1,0:T(8,128)(2,1)S(1)}, u32[]{:S(2)}, u32[]{:S(2)}) collective-permute-start(bf16[2,2,64,256]{3,2,1,0:T(8,128)(2,1)S(1)} %pad_maximum_fusion.5), channel_id=1, source_target_pairs={{0,4},{2,6},{4,0},{6,2},{8,12},{10,14},{12,8},{14,10},{1,5},{3,7},... | collective-permute-start | bytes 393224 | tf_op jit(solution)/shard_map/ppermute | solution.py:98
  81.9 5.0 %collective-permute-start.6 = (bf16[2,2,64,256]{3,2,1,0:T(8,128)(2,1)S(1)}, bf16[2,2,64,256]{3,2,1,0:T(8,128)(2,1)S(1)}, u32[]{:S(2)}, u32[]{:S(2)}) collective-permute-start(bf16[2,2,64,256]{3,2,1,0:T(8,128)(2,1)S(1)} %pad_maximum_fusion.2), channel_id=1, source_target_pairs={{0,2},{2,0},{4,6},{6,4},{8,10},{10,8},{12,14},{14,12},{1,3},{3,1},... | collective-permute-start | bytes 393224 | tf_op jit(solution)/shard_map/ppermute | solution.py:98
  83.6 5.0 %collective-permute-start.12 = (bf16[2,2,64,256]{3,2,1,0:T(8,128)(2,1)S(1)}, bf16[2,2,64,256]{3,2,1,0:T(8,128)(2,1)S(1)}, u32[]{:S(2)}, u32[]{:S(2)}) collective-permute-start(bf16[2,2,64,256]{3,2,1,0:T(8,128)(2,1)S(1)} %pad_maximum_fusion.3), channel_id=1, source_target_pairs={{0,2},{2,0},{4,6},{6,4},{8,10},{10,8},{12,14},{14,12},{1,3},{3,1},... | collective-permute-start | bytes 393224 | tf_op jit(solution)/shard_map/ppermute | solution.py:98
  (9 other events, 93.6 us)

commit v21 on v20

--- a/solution.py
+++ b/solution.py
@@ -197,8 +197,11 @@
 ):
     lat_size = LAT_SIZE[0]
     first, second = _orders(lat_size)
-    copies = jnp.broadcast_to(activations[None], (lat_size,) + activations.shape)
-    act_blocks = lax.all_to_all(copies, "lat", 0, 0, tiled=True)
+    if lat_size <= 8:
+        act_blocks = _direct_gather(activations, "lat", lat_size)
+    else:
+        copies = jnp.broadcast_to(activations[None], (lat_size,) + activations.shape)
+        act_blocks = lax.all_to_all(copies, "lat", 0, 0, tiled=True)
     half_rows = jnp.transpose(act_blocks, (1, 0, 2)).reshape(activations.shape[0], -1)
     other_rows = lax.ppermute(half_rows, "seed", [(0, 1), (1, 0)])
     seed_first = lax.axis_index("seed") == 0

time: 118 us -> 118 us (level)
  blocking collectives: 21.6 us -> 0 us
  starting transfers between devices: 29.1 us -> 44.1 us
  waiting for transfers between devices: 23.5 us -> 29.8 us
    all_to_all x1 -> x0, blocking collectives: 21.6 us -> none  [local(): act_blocks = lax.all_to_all(copies, 'lat', 0, 0, tiled=True)]
    ppermute x0 -> x7, starting transfers between devices: none -> 12.3 us  [_direct_gather(): lax.ppermute(value, axis, [(i, (i + k) % size) for i in range(size)])]
    ppermute x0 -> x7, waiting for transfers between devices: none -> 8.33 us  [_direct_gather(): lax.ppermute(value, axis, [(i, (i + k) % size) for i in range(size)])]
    ppermute x24, starting transfers between devices: 29 us -> 31.7 us  [_pair_swap(): return lax.ppermute(value, axis, [(i, i ^ mask) for i in range(size)])]
    ppermute x24, waiting for transfers between devices: 21.8 us -> 19.7 us  [_pair_swap(): return lax.ppermute(value, axis, [(i, i ^ mask) for i in range(size)])]
  transfers between devices with their start and end apart: 25 -> 32, of which waited for: 13 -> 14; matrix products, arithmetic and copies ran while one was open for 1% -> 2% of each run, Pallas kernels for 0% -> 0%
where the time goes in v21:
time: 118 us
  starting transfers between devices  44.1 us (37%)
  waiting for transfers between devices  29.8 us (25%)
  Pallas kernels  27.7 us (23%)
  matrix products  8.85 us (8%)
  local copies, waits for them, and re-layouts  3.83 us (3%)
  other arithmetic  2.5 us (2%)
  between operations  1.31 us (1%)
    ppermute x24, starting transfers between devices, _pair_swap(): return lax.ppermute(value, axis, [(i, i ^ mask) for i in range(size)])  31.7 us
    pallas_call x1, Pallas kernels, tail(): pl.pallas_call(functools.partial(_tail_kernel, stacked), grid=(n_lat // t...  27.7 us
    ppermute x24, waiting for transfers between devices, _pair_swap(): return lax.ppermute(value, axis, [(i, i ^ mask) for i in range(size)])  19.7 us
    ppermute x7, starting transfers between devices, _direct_gather(): lax.ppermute(value, axis, [(i, (i + k) % size) for i in range(size)])  12.3 us
    ppermute x7, waiting for transfers between devices, _direct_gather(): lax.ppermute(value, axis, [(i, (i + k) % size) for i in range(size)])  8.33 us
    dot_general x1, matrix products, local(): lax.dot_general(weight_in, centered, (((1,), (1,)), ((), ())), preferred_...  6.51 us
  transfers between devices with their start and end apart: 32, of which 14 were waited for; matrix products, arithmetic and copies ran while one was open for 2% of the time, Pallas kernels for 0%

profile of v21, /device:TPU:0, one launch (start us, length us, event | category | flops | bytes accessed | tf_op | source)
XLA Modules:
  0.0 118.2 jit_solution(11410002688711744865)
XLA Ops:
  0.6 5.0 %collective-permute-start.4 = (bf16[128,256]{1,0:T(8,128)(2,1)}, bf16[128,256]{1,0:T(8,128)(2,1)S(1)}, u32[]{:S(2)}, u32[]{:S(2)}) collective-permute-start(bf16[128,256]{1,0:T(8,128)(2,1)} %param.9), channel_id=1, source_target_pairs={{0,10},{2,12},{4,14},{6,0},{8,2},{10,4},{12,6},{14,8},{1,11},{3,13... | collective-permute-start | bytes 196616 | tf_op jit(solution)/shard_map/ppermute | solution.py:135
  6.0 1.7 %collective-permute-start.2 = (bf16[128,256]{1,0:T(8,128)(2,1)}, bf16[128,256]{1,0:T(8,128)(2,1)S(1)}, u32[]{:S(2)}, u32[]{:S(2)}) collective-permute-start(bf16[128,256]{1,0:T(8,128)(2,1)} %param.9), channel_id=1, source_target_pairs={{0,6},{2,8},{4,10},{6,12},{8,14},{10,0},{12,2},{14,4},{1,7},{3,9},... | collective-permute-start | bytes 196616 | tf_op jit(solution)/shard_map/ppermute | solution.py:135
  7.6 2.5 %collective-permute-start.1 = (bf16[128,256]{1,0:T(8,128)(2,1)}, bf16[128,256]{1,0:T(8,128)(2,1)S(1)}, u32[]{:S(2)}, u32[]{:S(2)}) collective-permute-start(bf16[128,256]{1,0:T(8,128)(2,1)} %param.9), channel_id=1, source_target_pairs={{0,4},{2,6},{4,8},{6,10},{8,12},{10,14},{12,0},{14,2},{1,5},{3,7},... | collective-permute-start | bytes 196616 | tf_op jit(solution)/shard_map/ppermute | solution.py:135
  12.5 4.8 %collective-permute-done = bf16[128,256]{1,0:T(8,128)(2,1)S(1)} collective-permute-done((bf16[128,256]{1,0:T(8,128)(2,1)}, bf16[128,256]{1,0:T(8,128)(2,1)S(1)}, u32[]{:S(2)}, u32[]{:S(2)}) %collective-permute-start) | collective-permute-done | bytes 65568 | tf_op jit(solution)/shard_map/ppermute | solution.py:135
  18.8 3.5 %collective-permute-done.5 = bf16[128,256]{1,0:T(8,128)(2,1)S(1)} collective-permute-done((bf16[128,256]{1,0:T(8,128)(2,1)}, bf16[128,256]{1,0:T(8,128)(2,1)S(1)}, u32[]{:S(2)}, u32[]{:S(2)}) %collective-permute-start.5) | collective-permute-done | bytes 65568 | tf_op jit(solution)/shard_map/ppermute | solution.py:135
  23.3 1.7 %collective-permute-done.7 = bf16[128,2048]{1,0:T(8,128)(2,1)S(1)} collective-permute-done((bf16[128,2048]{1,0:T(8,128)(2,1)S(1)}, bf16[128,2048]{1,0:T(8,128)(2,1)S(1)}, u32[]{:S(2)}, u32[]{:S(2)}) %collective-permute-start.7) | collective-permute-done | bytes 524320 | tf_op jit(solution)/shard_map/ppermute | solution.py:206
  27.3 6.5 %fusion.1 = bf16[256,2048]{0,1:T(8,128)(2,1)S(1)} fusion(bf16[256,2048]{1,0:T(8,128)(2,1)S(1)} %get-tuple-element.9.cen_ref, f32[2048]{0:T(1024)S(1)} %bitcast.133, bf16[1,2048,2048]{2,1,0:T(8,128)(2,1)} %param.12), kind=kOutput, calls=%fused_computation.4 | convolution fusion | flops 2149056512 | bytes 10493952 | tf_op jit(solution)/shard_map/dot_general | solution.py:219
  33.9 2.3 %fusion.5 = f32[256,2048]{1,0:T(8,128)S(1)} fusion(bf16[256,2048]{0,1:T(8,128)(2,1)S(1)} %fusion.1, bf16[1,2048,2048]{2,1,0:T(8,128)(2,1)S(1)} %bitcast.112), kind=kOutput, calls=%fused_computation.103 | convolution fusion | flops 2147483648 | bytes 11534336 | tf_op jit(solution)/shard_map/dot_general | solution.py:225
  38.6 1.6 %collective-permute-start.14 = (f32[64,1024]{1,0:T(8,128)S(1)}, f32[64,1024]{1,0:T(8,128)S(1)}, u32[]{:S(2)}, u32[]{:S(2)}) collective-permute-start(f32[64,1024]{1,0:T(8,128)S(1)} %constant_dynamic-slice_fusion.9), channel_id=1, source_target_pairs={{0,2},{2,0},{4,6},{6,4},{8,10},{10,8},{12,14},{14,12},{1,3},{3,1},... | collective-permute-start | bytes 786440 | tf_op jit(solution)/shard_map/ppermute | solution.py:98
  40.7 5.0 %collective-permute-done.20 = f32[64,1024]{1,0:T(8,128)S(1)} collective-permute-done((f32[64,1024]{1,0:T(8,128)S(1)}, f32[64,1024]{1,0:T(8,128)S(1)}, u32[]{:S(2)}, u32[]{:S(2)}) %collective-permute-start.20) | collective-permute-done | bytes 262176 | tf_op jit(solution)/shard_map/ppermute | solution.py:98
  45.8 1.7 %collective-permute-start.21 = (f32[64,512]{1,0:T(8,128)S(1)}, f32[64,512]{1,0:T(8,128)S(1)}, u32[]{:S(2)}, u32[]{:S(2)}) collective-permute-start(f32[64,512]{1,0:T(8,128)S(1)} %constant_dynamic-slice_fusion.5), channel_id=1, source_target_pairs={{0,2},{2,0},{4,6},{6,4},{8,10},{10,8},{12,14},{14,12},{1,3},{3,1},... | collective-permute-start | bytes 393224 | tf_op jit(solution)/shard_map/ppermute | solution.py:98
  47.5 3.0 %collective-permute-done.26 = f32[64,1024]{1,0:T(8,128)S(1)} collective-permute-done((f32[64,1024]{1,0:T(8,128)S(1)}, f32[64,1024]{1,0:T(8,128)S(1)}, u32[]{:S(2)}, u32[]{:S(2)}) %collective-permute-start.26) | collective-permute-done | bytes 262176 | tf_op jit(solution)/shard_map/ppermute | solution.py:98
  50.6 1.7 %collective-permute-start.27 = (f32[64,512]{1,0:T(8,128)S(1)}, f32[64,512]{1,0:T(8,128)S(1)}, u32[]{:S(2)}, u32[]{:S(2)}) collective-permute-start(f32[64,512]{1,0:T(8,128)S(1)} %constant_dynamic-slice_fusion.11), channel_id=1, source_target_pairs={{0,2},{2,0},{4,6},{6,4},{8,10},{10,8},{12,14},{14,12},{1,3},{3,1},... | collective-permute-start | bytes 393224 | tf_op jit(solution)/shard_map/ppermute | solution.py:98
  54.6 1.6 %collective-permute-done.21 = f32[64,512]{1,0:T(8,128)S(1)} collective-permute-done((f32[64,512]{1,0:T(8,128)S(1)}, f32[64,512]{1,0:T(8,128)S(1)}, u32[]{:S(2)}, u32[]{:S(2)}) %collective-permute-start.21) | collective-permute-done | bytes 131104 | tf_op jit(solution)/shard_map/ppermute | solution.py:98
  56.3 1.6 %collective-permute-start.22 = (f32[64,256]{1,0:T(8,128)S(1)}, f32[64,256]{1,0:T(8,128)S(1)}, u32[]{:S(2)}, u32[]{:S(2)}) collective-permute-start(f32[64,256]{1,0:T(8,128)S(1)} %constant_dynamic-slice_fusion.4), channel_id=1, source_target_pairs={{0,8},{2,10},{4,12},{6,14},{8,0},{10,2},{12,4},{14,6},{1,9},{3,11}... | collective-permute-start | bytes 196616 | tf_op jit(solution)/shard_map/ppermute | solution.py:98
  57.9 1.6 %collective-permute-start.28 = (f32[64,256]{1,0:T(8,128)S(1)}, f32[64,256]{1,0:T(8,128)S(1)}, u32[]{:S(2)}, u32[]{:S(2)}) collective-permute-start(f32[64,256]{1,0:T(8,128)S(1)} %constant_dynamic-slice_fusion.2), channel_id=1, source_target_pairs={{0,8},{2,10},{4,12},{6,14},{8,0},{10,2},{12,4},{14,6},{1,9},{3,11}... | collective-permute-start | bytes 196616 | tf_op jit(solution)/shard_map/ppermute | solution.py:98
  61.1 2.0 %collective-permute-start.10 = (f32[64,256]{1,0:T(8,128)S(1)}, f32[64,256]{1,0:T(8,128)S(1)}, u32[]{:S(2)}, u32[]{:S(2)}) collective-permute-start(f32[64,256]{1,0:T(8,128)S(1)} %constant_dynamic-slice_fusion.13), channel_id=1, source_target_pairs={{0,8},{2,10},{4,12},{6,14},{8,0},{10,2},{12,4},{14,6},{1,9},{3,11}... | collective-permute-start | bytes 196616 | tf_op jit(solution)/shard_map/ppermute | solution.py:98
  63.1 3.1 %collective-permute-done.22 = f32[64,256]{1,0:T(8,128)S(1)} collective-permute-done((f32[64,256]{1,0:T(8,128)S(1)}, f32[64,256]{1,0:T(8,128)S(1)}, u32[]{:S(2)}, u32[]{:S(2)}) %collective-permute-start.22) | collective-permute-done | bytes 65568 | tf_op jit(solution)/shard_map/ppermute | solution.py:98
  66.2 2.1 %collective-permute-done.28 = f32[64,256]{1,0:T(8,128)S(1)} collective-permute-done((f32[64,256]{1,0:T(8,128)S(1)}, f32[64,256]{1,0:T(8,128)S(1)}, u32[]{:S(2)}, u32[]{:S(2)}) %collective-permute-start.28) | collective-permute-done | bytes 65568 | tf_op jit(solution)/shard_map/ppermute | solution.py:98
  68.4 2.9 %collective-permute-start.29 = (bf16[64,256]{1,0:T(8,128)(2,1)S(1)}, bf16[64,256]{1,0:T(8,128)(2,1)S(1)}, u32[]{:S(2)}, u32[]{:S(2)}) collective-permute-start(bf16[64,256]{1,0:T(8,128)(2,1)S(1)} %get-tuple-element.52), channel_id=1, source_target_pairs={{0,8},{2,10},{4,12},{6,14},{8,0},{10,2},{12,4},{14,6},{1,9},{3,11}... | collective-permute-start | bytes 98312 | tf_op jit(solution)/shard_map/ppermute | solution.py:98
  71.5 2.8 %collective-permute-start.17 = (bf16[64,256]{1,0:T(8,128)(2,1)S(1)}, bf16[64,256]{1,0:T(8,128)(2,1)S(1)}, u32[]{:S(2)}, u32[]{:S(2)}) collective-permute-start(bf16[64,256]{1,0:T(8,128)(2,1)S(1)} %get-tuple-element.50), channel_id=1, source_target_pairs={{0,8},{2,10},{4,12},{6,14},{8,0},{10,2},{12,4},{14,6},{1,9},{3,11}... | collective-permute-start | bytes 98312 | tf_op jit(solution)/shard_map/ppermute | solution.py:98
  78.2 2.2 %collective-permute-start.18 = (bf16[2,64,256]{2,1,0:T(8,128)(2,1)S(1)}, bf16[2,64,256]{2,1,0:T(8,128)(2,1)S(1)}, u32[]{:S(2)}, u32[]{:S(2)}) collective-permute-start(bf16[2,64,256]{2,1,0:T(8,128)(2,1)S(1)} %pad_maximum_fusion.7), channel_id=1, source_target_pairs={{0,4},{2,6},{4,0},{6,2},{8,12},{10,14},{12,8},{14,10},{1,5},{3,7},... | collective-permute-start | bytes 196616 | tf_op jit(solution)/shard_map/ppermute | solution.py:98
  80.6 2.1 %collective-permute-start.31 = (bf16[2,2,64,256]{3,2,1,0:T(8,128)(2,1)S(1)}, bf16[2,2,64,256]{3,2,1,0:T(8,128)(2,1)S(1)}, u32[]{:S(2)}, u32[]{:S(2)}) collective-permute-start(bf16[2,2,64,256]{3,2,1,0:T(8,128)(2,1)S(1)} %pad_maximum_fusion.5), channel_id=1, source_target_pairs={{0,4},{2,6},{4,0},{6,2},{8,12},{10,14},{12,8},{14,10},{1,5},{3,7},... | collective-permute-start | bytes 393224 | tf_op jit(solution)/shard_map/ppermute | solution.py:98
  90.4 27.7 %shard_map.112 = (bf16[2048,2048]{1,0:T(8,128)(2,1)}, bf16[2048,2048]{1,0:T(8,128)(2,1)}, bf16[2048,2048]{1,0:T(8,128)(2,1)}) custom-call(bf16[2048,256]{1,0:T(8,128)(2,1)} %bitcast.116, bf16[2,8,128,256]{3,2,1,0:T(8,128)(2,1)} %pad_maximum_fusion.1.err_ref, bf16[256,2048]{1,0:T(8,128)(2,1)} %copy-done.1, bf16[2048,2048]{1,0:T(8,128)(2,1)} %bitcast.110, ...), custom_call_target="tpu_custom_call" | custom-call | tf_op jit(solution)/shard_map/pallas_call | solution.py:79
  (138 shorter events, 25.9 us)
Async XLA Ops:
  0.6 18.2 %collective-permute-start.4 = (bf16[128,256]{1,0:T(8,128)(2,1)}, bf16[128,256]{1,0:T(8,128)(2,1)S(1)}, u32[]{:S(2)}, u32[]{:S(2)}) collective-permute-start(bf16[128,256]{1,0:T(8,128)(2,1)} %param.9), channel_id=1, source_target_pairs={{0,10},{2,12},{4,14},{6,0},{8,2},{10,4},{12,6},{14,8},{1,11},{3,13... | collective-permute-start | bytes 196616 | tf_op jit(solution)/shard_map/ppermute | solution.py:135
  5.6 13.1 %collective-permute-start.3 = (bf16[128,256]{1,0:T(8,128)(2,1)}, bf16[128,256]{1,0:T(8,128)(2,1)S(1)}, u32[]{:S(2)}, u32[]{:S(2)}) collective-permute-start(bf16[128,256]{1,0:T(8,128)(2,1)} %param.9), channel_id=1, source_target_pairs={{0,8},{2,10},{4,12},{6,14},{8,0},{10,2},{12,4},{14,6},{1,9},{3,11}... | collective-permute-start | bytes 196616 | tf_op jit(solution)/shard_map/ppermute | solution.py:135
  6.0 12.8 %collective-permute-start.2 = (bf16[128,256]{1,0:T(8,128)(2,1)}, bf16[128,256]{1,0:T(8,128)(2,1)S(1)}, u32[]{:S(2)}, u32[]{:S(2)}) collective-permute-start(bf16[128,256]{1,0:T(8,128)(2,1)} %param.9), channel_id=1, source_target_pairs={{0,6},{2,8},{4,10},{6,12},{8,14},{10,0},{12,2},{14,4},{1,7},{3,9},... | collective-permute-start | bytes 196616 | tf_op jit(solution)/shard_map/ppermute | solution.py:135
  7.6 10.1 %collective-permute-start.1 = (bf16[128,256]{1,0:T(8,128)(2,1)}, bf16[128,256]{1,0:T(8,128)(2,1)S(1)}, u32[]{:S(2)}, u32[]{:S(2)}) collective-permute-start(bf16[128,256]{1,0:T(8,128)(2,1)} %param.9), channel_id=1, source_target_pairs={{0,4},{2,6},{4,8},{6,10},{8,12},{10,14},{12,0},{14,2},{1,5},{3,7},... | collective-permute-start | bytes 196616 | tf_op jit(solution)/shard_map/ppermute | solution.py:135
  10.1 7.3 %collective-permute-start = (bf16[128,256]{1,0:T(8,128)(2,1)}, bf16[128,256]{1,0:T(8,128)(2,1)S(1)}, u32[]{:S(2)}, u32[]{:S(2)}) collective-permute-start(bf16[128,256]{1,0:T(8,128)(2,1)} %param.9), channel_id=1, source_target_pairs={{0,2},{2,4},{4,6},{6,8},{8,10},{10,12},{12,14},{14,0},{1,3},{3,5},... | collective-permute-start | bytes 196616 | tf_op jit(solution)/shard_map/ppermute | solution.py:135
  36.5 9.2 %collective-permute-start.20 = (f32[64,1024]{1,0:T(8,128)S(1)}, f32[64,1024]{1,0:T(8,128)S(1)}, u32[]{:S(2)}, u32[]{:S(2)}) collective-permute-start(f32[64,1024]{1,0:T(8,128)S(1)} %constant_dynamic-slice_fusion.6), channel_id=1, source_target_pairs={{0,4},{2,6},{4,0},{6,2},{8,12},{10,14},{12,8},{14,10},{1,5},{3,7},... | collective-permute-start | bytes 786440 | tf_op jit(solution)/shard_map/ppermute | solution.py:98
  37.5 13.0 %collective-permute-start.26 = (f32[64,1024]{1,0:T(8,128)S(1)}, f32[64,1024]{1,0:T(8,128)S(1)}, u32[]{:S(2)}, u32[]{:S(2)}) collective-permute-start(f32[64,1024]{1,0:T(8,128)S(1)} %constant_dynamic-slice_fusion), channel_id=1, source_target_pairs={{0,4},{2,6},{4,0},{6,2},{8,12},{10,14},{12,8},{14,10},{1,5},{3,7},... | collective-permute-start | bytes 786440 | tf_op jit(solution)/shard_map/ppermute | solution.py:98
  38.6 13.7 %collective-permute-start.14 = (f32[64,1024]{1,0:T(8,128)S(1)}, f32[64,1024]{1,0:T(8,128)S(1)}, u32[]{:S(2)}, u32[]{:S(2)}) collective-permute-start(f32[64,1024]{1,0:T(8,128)S(1)} %constant_dynamic-slice_fusion.9), channel_id=1, source_target_pairs={{0,2},{2,0},{4,6},{6,4},{8,10},{10,8},{12,14},{14,12},{1,3},{3,1},... | collective-permute-start | bytes 786440 | tf_op jit(solution)/shard_map/ppermute | solution.py:98
  40.3 13.2 %collective-permute-start.8 = (f32[64,1024]{1,0:T(8,128)S(1)}, f32[64,1024]{1,0:T(8,128)S(1)}, u32[]{:S(2)}, u32[]{:S(2)}) collective-permute-start(f32[64,1024]{1,0:T(8,128)S(1)} %constant_dynamic-slice_fusion.15), channel_id=1, source_target_pairs={{0,2},{2,0},{4,6},{6,4},{8,10},{10,8},{12,14},{14,12},{1,3},{3,1},... | collective-permute-start | bytes 786440 | tf_op jit(solution)/shard_map/ppermute | solution.py:98
  45.8 10.4 %collective-permute-start.21 = (f32[64,512]{1,0:T(8,128)S(1)}, f32[64,512]{1,0:T(8,128)S(1)}, u32[]{:S(2)}, u32[]{:S(2)}) collective-permute-start(f32[64,512]{1,0:T(8,128)S(1)} %constant_dynamic-slice_fusion.5), channel_id=1, source_target_pairs={{0,2},{2,0},{4,6},{6,4},{8,10},{10,8},{12,14},{14,12},{1,3},{3,1},... | collective-permute-start | bytes 393224 | tf_op jit(solution)/shard_map/ppermute | solution.py:98
  50.6 7.3 %collective-permute-start.27 = (f32[64,512]{1,0:T(8,128)S(1)}, f32[64,512]{1,0:T(8,128)S(1)}, u32[]{:S(2)}, u32[]{:S(2)}) collective-permute-start(f32[64,512]{1,0:T(8,128)S(1)} %constant_dynamic-slice_fusion.11), channel_id=1, source_target_pairs={{0,2},{2,0},{4,6},{6,4},{8,10},{10,8},{12,14},{14,12},{1,3},{3,1},... | collective-permute-start | bytes 393224 | tf_op jit(solution)/shard_map/ppermute | solution.py:98
  52.4 7.2 %collective-permute-start.15 = (f32[64,512]{1,0:T(8,128)S(1)}, f32[64,512]{1,0:T(8,128)S(1)}, u32[]{:S(2)}, u32[]{:S(2)}) collective-permute-start(f32[64,512]{1,0:T(8,128)S(1)} %constant_dynamic-slice_fusion.8), channel_id=1, source_target_pairs={{0,4},{2,6},{4,0},{6,2},{8,12},{10,14},{12,8},{14,10},{1,5},{3,7},... | collective-permute-start | bytes 393224 | tf_op jit(solution)/shard_map/ppermute | solution.py:98
  53.5 7.5 %collective-permute-start.9 = (f32[64,512]{1,0:T(8,128)S(1)}, f32[64,512]{1,0:T(8,128)S(1)}, u32[]{:S(2)}, u32[]{:S(2)}) collective-permute-start(f32[64,512]{1,0:T(8,128)S(1)} %constant_dynamic-slice_fusion.14), channel_id=1, source_target_pairs={{0,4},{2,6},{4,0},{6,2},{8,12},{10,14},{12,8},{14,10},{1,5},{3,7},... | collective-permute-start | bytes 393224 | tf_op jit(solution)/shard_map/ppermute | solution.py:98
  56.3 9.9 %collective-permute-start.22 = (f32[64,256]{1,0:T(8,128)S(1)}, f32[64,256]{1,0:T(8,128)S(1)}, u32[]{:S(2)}, u32[]{:S(2)}) collective-permute-start(f32[64,256]{1,0:T(8,128)S(1)} %constant_dynamic-slice_fusion.4), channel_id=1, source_target_pairs={{0,8},{2,10},{4,12},{6,14},{8,0},{10,2},{12,4},{14,6},{1,9},{3,11}... | collective-permute-start | bytes 196616 | tf_op jit(solution)/shard_map/ppermute | solution.py:98
  57.9 10.4 %collective-permute-start.28 = (f32[64,256]{1,0:T(8,128)S(1)}, f32[64,256]{1,0:T(8,128)S(1)}, u32[]{:S(2)}, u32[]{:S(2)}) collective-permute-start(f32[64,256]{1,0:T(8,128)S(1)} %constant_dynamic-slice_fusion.2), channel_id=1, source_target_pairs={{0,8},{2,10},{4,12},{6,14},{8,0},{10,2},{12,4},{14,6},{1,9},{3,11}... | collective-permute-start | bytes 196616 | tf_op jit(solution)/shard_map/ppermute | solution.py:98
  59.6 11.7 %collective-permute-start.16 = (f32[64,256]{1,0:T(8,128)S(1)}, f32[64,256]{1,0:T(8,128)S(1)}, u32[]{:S(2)}, u32[]{:S(2)}) collective-permute-start(f32[64,256]{1,0:T(8,128)S(1)} %constant_dynamic-slice_fusion.7), channel_id=1, source_target_pairs={{0,8},{2,10},{4,12},{6,14},{8,0},{10,2},{12,4},{14,6},{1,9},{3,11}... | collective-permute-start | bytes 196616 | tf_op jit(solution)/shard_map/ppermute | solution.py:98
  61.1 10.2 %collective-permute-start.10 = (f32[64,256]{1,0:T(8,128)S(1)}, f32[64,256]{1,0:T(8,128)S(1)}, u32[]{:S(2)}, u32[]{:S(2)}) collective-permute-start(f32[64,256]{1,0:T(8,128)S(1)} %constant_dynamic-slice_fusion.13), channel_id=1, source_target_pairs={{0,8},{2,10},{4,12},{6,14},{8,0},{10,2},{12,4},{14,6},{1,9},{3,11}... | collective-permute-start | bytes 196616 | tf_op jit(solution)/shard_map/ppermute | solution.py:98
  68.3 6.0 %collective-permute-start.23 = (bf16[64,256]{1,0:T(8,128)(2,1)S(1)}, bf16[64,256]{1,0:T(8,128)(2,1)S(1)}, u32[]{:S(2)}, u32[]{:S(2)}) collective-permute-start(bf16[64,256]{1,0:T(8,128)(2,1)S(1)} %get-tuple-element.51), channel_id=1, source_target_pairs={{0,8},{2,10},{4,12},{6,14},{8,0},{10,2},{12,4},{14,6},{1,9},{3,11}... | collective-permute-start | bytes 98312 | tf_op jit(solution)/shard_map/ppermute | solution.py:98
  68.4 7.5 %collective-permute-start.29 = (bf16[64,256]{1,0:T(8,128)(2,1)S(1)}, bf16[64,256]{1,0:T(8,128)(2,1)S(1)}, u32[]{:S(2)}, u32[]{:S(2)}) collective-permute-start(bf16[64,256]{1,0:T(8,128)(2,1)S(1)} %get-tuple-element.52), channel_id=1, source_target_pairs={{0,8},{2,10},{4,12},{6,14},{8,0},{10,2},{12,4},{14,6},{1,9},{3,11}... | collective-permute-start | bytes 98312 | tf_op jit(solution)/shard_map/ppermute | solution.py:98
  71.5 6.7 %collective-permute-start.17 = (bf16[64,256]{1,0:T(8,128)(2,1)S(1)}, bf16[64,256]{1,0:T(8,128)(2,1)S(1)}, u32[]{:S(2)}, u32[]{:S(2)}) collective-permute-start(bf16[64,256]{1,0:T(8,128)(2,1)S(1)} %get-tuple-element.50), channel_id=1, source_target_pairs={{0,8},{2,10},{4,12},{6,14},{8,0},{10,2},{12,4},{14,6},{1,9},{3,11}... | collective-permute-start | bytes 98312 | tf_op jit(solution)/shard_map/ppermute | solution.py:98
  74.4 6.0 %collective-permute-start.24 = (bf16[2,64,256]{2,1,0:T(8,128)(2,1)S(1)}, bf16[2,64,256]{2,1,0:T(8,128)(2,1)S(1)}, u32[]{:S(2)}, u32[]{:S(2)}) collective-permute-start(bf16[2,64,256]{2,1,0:T(8,128)(2,1)S(1)} %pad_maximum_fusion.8), channel_id=1, source_target_pairs={{0,2},{2,0},{4,6},{6,4},{8,10},{10,8},{12,14},{14,12},{1,3},{3,1},... | collective-permute-start | bytes 196616 | tf_op jit(solution)/shard_map/ppermute | solution.py:98
  77.0 5.7 %collective-permute-start.12 = (bf16[2,64,256]{2,1,0:T(8,128)(2,1)S(1)}, bf16[2,64,256]{2,1,0:T(8,128)(2,1)S(1)}, u32[]{:S(2)}, u32[]{:S(2)}) collective-permute-start(bf16[2,64,256]{2,1,0:T(8,128)(2,1)S(1)} %pad_maximum_fusion.6), channel_id=1, source_target_pairs={{0,4},{2,6},{4,0},{6,2},{8,12},{10,14},{12,8},{14,10},{1,5},{3,7},... | collective-permute-start | bytes 196616 | tf_op jit(solution)/shard_map/ppermute | solution.py:98
  78.2 5.6 %collective-permute-start.18 = (bf16[2,64,256]{2,1,0:T(8,128)(2,1)S(1)}, bf16[2,64,256]{2,1,0:T(8,128)(2,1)S(1)}, u32[]{:S(2)}, u32[]{:S(2)}) collective-permute-start(bf16[2,64,256]{2,1,0:T(8,128)(2,1)S(1)} %pad_maximum_fusion.7), channel_id=1, source_target_pairs={{0,4},{2,6},{4,0},{6,2},{8,12},{10,14},{12,8},{14,10},{1,5},{3,7},... | collective-permute-start | bytes 196616 | tf_op jit(solution)/shard_map/ppermute | solution.py:98
  80.6 6.3 %collective-permute-start.31 = (bf16[2,2,64,256]{3,2,1,0:T(8,128)(2,1)S(1)}, bf16[2,2,64,256]{3,2,1,0:T(8,128)(2,1)S(1)}, u32[]{:S(2)}, u32[]{:S(2)}) collective-permute-start(bf16[2,2,64,256]{3,2,1,0:T(8,128)(2,1)S(1)} %pad_maximum_fusion.5), channel_id=1, source_target_pairs={{0,4},{2,6},{4,0},{6,2},{8,12},{10,14},{12,8},{14,10},{1,5},{3,7},... | collective-permute-start | bytes 393224 | tf_op jit(solution)/shard_map/ppermute | solution.py:98
  (16 other events, 93.7 us)
